TPU v7x, 32 devices: a whole 2x2x4 slice. The times are simulated.
32 devices in a mesh: px: 4 (over z), py: 8 (over y, x, core).
Axes of the slice: x: 2, y: 2, z: 4, core: 2. Of those that a mesh axis runs over, the one named last changes fastest.
Arguments:
- right_side: float32 [8, 2048, 2048], P(None, 'py', 'px'), may hold values from -6 to 6
- solution_in: float32 [8, 2048, 2048], P(None, 'py', 'px'), may hold values from -4 to 4
- classes: int32 [8, 2048, 2048], P(None, 'py', 'px'), may hold values from 0 to 15
- coeff_table: float32 [16], replicated, may hold values from 0.2 to 5
- eigenvectors: bfloat16 [2048, 2048], replicated, may hold values from -0.053880558 to 0.053880558, as said below
- eigenvalues: float32 [2048], replicated, may hold values from 0.01 to 4
- level_shift: float32 [8], replicated, may hold values from 0.3 to 3
Outputs:
- solution: float32 [8, 2048, 2048], P(None, 'py', 'px')
- residual: float32 [8, 2048, 2048], P(None, 'py', 'px')
- direction: float32 [8, 2048, 2048], P(None, 'py', 'px')
Inputs may be any that keep to these rules, and one draw needn't show every extreme that they name: eigenvectors is a symmetric matrix.
All inputs are finite; a program needn't handle non-finite values.
Results may differ from a plain program's by a relative error of at most 0.034.
Values may be sent and summed in bfloat16 or wider, within the bound.
No kernel may reach another device: no remote copies, remote signals or barrier semaphores. Data moves between devices by JAX's collectives and lax.ppermute only.
A program may use at most 128 MiB of HBM per device.

v0:
```python
import jax
import jax.numpy as jnp
from jax import lax
from jax.sharding import PartitionSpec as P

ITERS = 2


def padded_2(array, sides, width):
    for axis, dim in sides:
        size, length = (lax.axis_size(axis), array.shape[dim])
        up = [(i, (i + 1) % size) for i in range(size - 1)]
        down = [(j, i) for i, j in up]
        last = lax.slice_in_dim(array, length - width, length, axis=dim)
        initial = lax.slice_in_dim(array, 0, width, axis=dim)
        before = lax.ppermute(last, axis, up)
        after = lax.ppermute(initial, axis, down)
        array = jnp.concatenate([before, array, after], axis=dim)
    return array


def for_sending(array):

    def short(part):
        return part.astype(jnp.bfloat16) if part.dtype == jnp.float32 else part

    return jax.tree.map(short, array)


def face_sum(padded, coeff_pad):
    values = padded[:, 1:-1, 1:-1]
    coeff = coeff_pad[:, 1:-1, 1:-1]
    height = values.shape[1]
    width = values.shape[2]
    result = jnp.zeros_like(values)
    for shift_y, shift_x in ((0, 1), (2, 1), (1, 0), (1, 2)):
        neighbour = padded[:, shift_y : shift_y + height, shift_x : shift_x + width]
        other = coeff_pad[:, shift_y : shift_y + height, shift_x : shift_x + width]
        result = result + 0.5 * (coeff + other) * (values - neighbour)
    vertical = 0.5 * (coeff[:-1] + coeff[1:]) * (values[:-1] - values[1:])
    zero_layer = jnp.zeros_like(values[:1])
    result = (
        result
        + jnp.concatenate((vertical, zero_layer), 0)
        - jnp.concatenate((zero_layer, vertical), 0)
    )
    return result


def precondition(residual, eigenvectors, eigenvalues, level_shift):
    rounded = residual.astype(jnp.bfloat16)
    levels_here = residual.shape[0] // lax.axis_size("px")
    first = jnp.einsum(
        "kyx,xi->kyi",
        lax.all_to_all(rounded, "px", split_axis=0, concat_axis=2, tiled=True),
        eigenvectors,
        preferred_element_type=jnp.float32,
    ).astype(jnp.bfloat16)
    second = jnp.einsum(
        "kyi,yj->kji",
        lax.all_to_all(first, "py", split_axis=2, concat_axis=1, tiled=True),
        eigenvectors,
        preferred_element_type=jnp.float32,
    )
    spectral_cols = second.shape[2]
    eigen_cols = lax.dynamic_slice_in_dim(
        eigenvalues, lax.axis_index("py") * spectral_cols, spectral_cols, 0
    )
    shift_here = lax.dynamic_slice_in_dim(
        level_shift, lax.axis_index("px") * levels_here, levels_here, 0
    )
    denom = eigenvalues[None, :, None] + eigen_cols[None, None, :] + shift_here[:, None, None]
    scaled = (second / denom).astype(jnp.bfloat16)
    fourth = jnp.einsum(
        "kji,yj->kyi", scaled, eigenvectors, preferred_element_type=jnp.float32
    ).astype(jnp.bfloat16)
    returned = lax.all_to_all(fourth, "py", split_axis=1, concat_axis=2, tiled=True)
    pencil = jnp.einsum("kyi,xi->kyx", returned, eigenvectors, preferred_element_type=jnp.float32)
    return lax.all_to_all(
        pencil.astype(jnp.bfloat16), "px", split_axis=2, concat_axis=0, tiled=True
    ).astype(pencil.dtype)


def shards(right_side, solution_in, classes, coeff_table, eigenvectors, eigenvalues, level_shift):
    coeff = jnp.zeros(classes.shape, jnp.float32)
    for label in range(coeff_table.shape[0]):
        coeff = jnp.where(classes == label, coeff_table[label], coeff)
    stacked = padded_2(
        jnp.stack((solution_in, coeff)).astype(jnp.bfloat16), (("px", 3), ("py", 2)), 1
    ).astype(jnp.float32)
    coeff_pad = stacked[1]
    solution = solution_in
    residual = right_side - face_sum(stacked[0], coeff_pad)
    direction = jnp.zeros_like(residual)
    gamma_prev = jnp.float32(1.0)
    for iteration in range(ITERS):
        precond = precondition(residual, eigenvectors, eigenvalues, level_shift)
        gamma = lax.psum(jnp.sum(residual * precond), ("px", "py"))
        if iteration == 0:
            direction = precond
        else:
            direction = precond + gamma / gamma_prev * direction
        padded = padded_2(for_sending(direction), (("px", 2), ("py", 1)), 1).astype(direction.dtype)
        image = face_sum(padded, coeff_pad)
        alpha = gamma / lax.psum(jnp.sum(direction * image), ("px", "py"))
        solution = solution + alpha * direction
        residual = residual - alpha * image
        gamma_prev = gamma
    return (solution, residual, direction)


def solution(mesh):
    in_specs = (P(None, "py", "px"), P(None, "py", "px"), P(None, "py", "px"), P(), P(), P(), P())
    out_specs = (P(None, "py", "px"), P(None, "py", "px"), P(None, "py", "px"))
    return jax.shard_map(shards, mesh=mesh, in_specs=in_specs, out_specs=out_specs, check_vma=False)
```

profile of v0, /device:TPU:0, one launch (start us, length us, event | category | flops | bytes accessed | tf_op | source)
XLA Modules:
  0.0 880.4 jit_solution(9970656240773987177)
XLA Ops:
  2.6 5.4 copy.101
  8.0 5.4 copy.136
  16.9 14.5 %fusion.87 = bf16[1,8,256,512]{2,1,3,0:T(8,128)(2,1)S(1)} fusion(bf16[]{:T(256)} %bitcast.16, s32[8,256,512]{1,0,2:T(8,128)S(1)} %copy-done.7, bf16[]{:T(256)} %bitcast.15, bf16[]{:T(256)} %bitcast.14, bf16[]{:T(256)} %bitcast.13, bf16[]{:T(256)} %bitcast.12, bf16[]{:T(256)} %bitcast.11, bf16[]{:T(256)} %bitcast.10, bf16[]{:T(256)} %bitcast.9, bf16[]{:T(256)} %bitcast.8, ...), kind=kLoop, calls=%fused_computation.110 | loop fusion | flops 33554432 | bytes 6291488 | tf_op jit(solution)/shard_map/stack | solution.py:89
  31.4 4.9 collective-permute-start
  37.7 4.2 collective-permute-done.1
  54.2 5.4 copy.121
  64.4 11.0 %maximum_convert_fusion = f32[2,8,258,514]{2,1,3,0:T(8,128)} fusion(bf16[2,8,1,514]{2,1,3,0:T(8,128)(2,1)} %copy.120, bf16[2,8,256,1]{2,1,3,0:T(8,128)(2,1)S(1)} %collective-permute-done.1, bf16[1,8,256,512]{2,1,3,0:T(8,128)(2,1)} %copy-done.5, bf16[1,8,256,512]{2,1,3,0:T(8,128)(2,1)S(1)} %convert_bitcast_fusion, ...), kind=kLoop, calls=%fused_computation.22 | loop fusion | flops 25461504 | bytes 12730752 | tf_op jit(solution)/shard_map/convert_element_type | solution.py:90
  75.4 8.0 slice_bitcast_fusion.1
  86.1 10.6 %fusion.43 = f32[7,256,512]{1,0,2:T(8,128)} fusion(f32[8,258,514]{1,0,2:T(8,128)} %get-tuple-element.26, f32[8,258,514]{1,0,2:T(8,128)S(1)} %get-tuple-element.25), kind=kLoop, calls=%fused_computation.64 | loop fusion | flops 3670016 | bytes 18350080 | tf_op jit(solution)/shard_map/mul | solution.py:40
  96.7 29.4 %fusion.93 = (bf16[8,256,512]{1,0,2:T(8,128)(2,1)S(1)}, f32[8,256,512]{1,0,2:T(8,128)}) fusion(f32[8,256,512]{1,0,2:T(8,128)} %copy.121, f32[7,256,512]{1,0,2:T(8,128)} %fusion.43, f32[8,258,514]{1,0,2:T(8,128)} %get-tuple-element.26, f32[8,258,514]{1,0,2:T(8,128)} %copy-done), kind=kLoop, calls=%fused_computation.119 | loop fusion | flops 24117248 | bytes 56098816 | tf_op jit(solution)/shard_map/convert_element_type | solution.py:51
  126.5 52.1 %all_to_all.135 = bf16[8,256,512]{1,2,0:T(8,128)(2,1)S(1)} all-to-all(bf16[8,256,512]{1,2,0:T(8,128)(2,1)S(1)} %copy.122), channel_id=1, replica_groups=mesh['px'=4,'py'=8] {'px'}, dimensions={0} | all-to-all | bytes 4194304 | tf_op jit(solution)/shard_map/all_to_all | solution.py:55
  185.0 9.0 %fusion.63 = bf16[2,256,2048]{2,1,0:T(8,128)(2,1)} fusion(bf16[2,256,2048]{2,1,0:T(8,128)(2,1)S(1)} %all_to_all.101, bf16[2048,2048]{1,0:T(8,128)(2,1)} %param.11), kind=kOutput, calls=%fused_computation.97 | convolution fusion | flops 4296015872 | bytes 12582912 | tf_op jit(solution)/shard_map/kyx,xi->kyi/dot_general | solution.py:53
  194.0 6.2 copy.124
  200.2 5.7 all-to-all-start.1
  207.6 24.9 %all-to-all-done.1 = bf16[2,256,2048]{1,0,2:T(2,128)(2,1)S(1)} async-done(((bf16[2,256,2048]{1,0,2:T(2,128)(2,1)}), bf16[2,256,2048]{1,0,2:T(2,128)(2,1)S(1)}, u32[]{:S(2)}, u32[]{:S(2)}) %all-to-all-start.1) | async-done | bytes 2097184 | tf_op jit(solution)/shard_map/all_to_all | solution.py:61
  238.3 16.8 %fusion.84 = bf16[2,2048,256]{1,2,0:T(8,128)(2,1)} fusion(bf16[2048,2048]{1,0:T(8,128)(2,1)} %param.11, bf16[2,2048,256]{2,1,0:T(8,128)(2,1)} %bitcast.155, f32[2]{0:T(128)S(1)} %dynamic_slice.9, f32[2048,256]{0,1:T(8,128)S(1)} %copy-done.9), kind=kOutput, calls=%fused_computation.104 | convolution fusion | flops 8594128896 | bytes 14680072 | tf_op jit(solution)/shard_map/kji,yj->kyi/dot_general | solution.py:74
  255.0 4.8 copy.128
  259.9 29.3 %all_to_all.136 = bf16[2,2048,256]{2,0,1:T(2,128)(2,1)S(1)} all-to-all(bf16[2,2048,256]{2,0,1:T(2,128)(2,1)S(1)} %copy.128), channel_id=1, replica_groups=mesh['px'=4,'py'=8] {'py'}, dimensions={1} | all-to-all | bytes 4194304 | tf_op jit(solution)/shard_map/all_to_all | solution.py:77
  292.7 9.9 %fusion.69 = bf16[2,256,2048]{2,1,0:T(8,128)(2,1)} fusion(bf16[2,256,2048]{2,1,0:T(8,128)(2,1)} %all_to_all.109, bf16[2048,2048]{1,0:T(8,128)(2,1)} %param.11), kind=kOutput, calls=%fused_computation.99 | convolution fusion | flops 4296015872 | bytes 12582912 | tf_op jit(solution)/shard_map/kyi,xi->kyx/dot_general | solution.py:78
  302.6 4.8 copy.130
  307.4 50.3 %all_to_all.137 = bf16[2,256,2048]{1,0,2:T(2,128)(2,1)S(1)} all-to-all(bf16[2,256,2048]{1,0,2:T(2,128)(2,1)S(1)} %copy.130), channel_id=1, replica_groups=mesh['px'=4,'py'=8] {'px'}, dimensions={2} | all-to-all | bytes 4194304 | tf_op jit(solution)/shard_map/all_to_all | solution.py:79
  387.7 5.9 fusion.33
  393.5 31.0 %fusion.19 = (f32[]{:T(128)}, f32[]{:T(128)}, f32[8,256,512]{1,0,2:T(8,128)}) fusion(bf16[8,256,512]{1,0,2:T(8,128)(2,1)} %copy-done.3, f32[8,256,512]{1,0,2:T(8,128)} %get-tuple-element.24, f32[7,256,512]{1,0,2:T(8,128)} %fusion.33, f32[8,258,514]{1,0,2:T(8,128)} %copy-done.2, f32[8,258,514]{1,0,2:T(8,128)} %copy-done), kind=kLoop, calls=%fused_computation.29 | loop fusion | flops 27262976 | bytes 56098824 | tf_op jit(solution)/shard_map/reduce_sum | solution.py:105
  424.5 40.9 %all-reduce.6 = (f32[]{:T(128)}, f32[]{:T(128)}) all-reduce(f32[]{:T(128)} %get-tuple-element.13, f32[]{:T(128)} %get-tuple-element.12), channel_id=1, replica_groups=mesh['px'=4,'py'=8] {'px','py'}, use_global_device_ids=true, to_apply=%region_1.2 | all-reduce | flops 2 | bytes 16 | tf_op jit(solution)/shard_map/psum | solution.py:98
  466.7 6.1 fusion.91
  473.2 51.2 %all_to_all.138 = bf16[8,256,512]{1,2,0:T(8,128)(2,1)S(1)} all-to-all(bf16[8,256,512]{1,2,0:T(8,128)(2,1)S(1)} %copy.137), channel_id=1, replica_groups=mesh['px'=4,'py'=8] {'px'}, dimensions={0} | all-to-all | bytes 4194304 | tf_op jit(solution)/shard_map/all_to_all | solution.py:55
  530.7 9.0 %fusion.72 = bf16[2,256,2048]{2,1,0:T(8,128)(2,1)} fusion(bf16[2,256,2048]{2,1,0:T(8,128)(2,1)S(1)} %all_to_all.117, bf16[2048,2048]{1,0:T(8,128)(2,1)} %param.11), kind=kOutput, calls=%fused_computation.100 | convolution fusion | flops 4296015872 | bytes 12582912 | tf_op jit(solution)/shard_map/kyx,xi->kyi/dot_general | solution.py:53
  539.7 4.8 copy.139
  544.6 29.9 %all_to_all.139 = bf16[2,256,2048]{1,0,2:T(2,128)(2,1)S(1)} all-to-all(bf16[2,256,2048]{1,0,2:T(2,128)(2,1)S(1)} %copy.139), channel_id=1, replica_groups=mesh['px'=4,'py'=8] {'py'}, dimensions={2} | all-to-all | bytes 4194304 | tf_op jit(solution)/shard_map/all_to_all | solution.py:61
  577.1 17.4 %fusion.81 = bf16[2,2048,256]{1,2,0:T(8,128)(2,1)} fusion(bf16[2048,2048]{1,0:T(8,128)(2,1)} %param.11, bf16[2,2048,256]{2,1,0:T(8,128)(2,1)} %bitcast.154, f32[2]{0:T(128)S(1)} %dynamic_slice.9, f32[2048,256]{0,1:T(8,128)} %broadcast_add_fusion), kind=kOutput, calls=%fused_computation.103 | convolution fusion | flops 8594128896 | bytes 14680072 | tf_op jit(solution)/shard_map/kji,yj->kyi/dot_general | solution.py:74
  594.4 4.8 copy.143
  599.3 29.3 %all_to_all.140 = bf16[2,2048,256]{2,0,1:T(2,128)(2,1)S(1)} all-to-all(bf16[2,2048,256]{2,0,1:T(2,128)(2,1)S(1)} %copy.143), channel_id=1, replica_groups=mesh['px'=4,'py'=8] {'py'}, dimensions={1} | all-to-all | bytes 4194304 | tf_op jit(solution)/shard_map/all_to_all | solution.py:77
  632.1 9.9 %fusion.78 = bf16[2,256,2048]{2,1,0:T(8,128)(2,1)} fusion(bf16[2,256,2048]{2,1,0:T(8,128)(2,1)} %all_to_all.125, bf16[2048,2048]{1,0:T(8,128)(2,1)} %param.11), kind=kOutput, calls=%fused_computation.102 | convolution fusion | flops 4296015872 | bytes 12582912 | tf_op jit(solution)/shard_map/kyi,xi->kyx/dot_general | solution.py:78
  642.0 4.8 copy.145
  646.9 50.3 %all_to_all.141 = bf16[2,256,2048]{1,0,2:T(2,128)(2,1)S(1)} all-to-all(bf16[2,256,2048]{1,0,2:T(2,128)(2,1)S(1)} %copy.145), channel_id=1, replica_groups=mesh['px'=4,'py'=8] {'px'}, dimensions={2} | all-to-all | bytes 4194304 | tf_op jit(solution)/shard_map/all_to_all | solution.py:79
  700.6 6.0 reshape.43
  706.6 5.3 multiply_reduce_fusion.1
  711.9 38.1 %psum.30 = f32[]{:T(128)} all-reduce(f32[]{:T(128)} %multiply_reduce_fusion.1), channel_id=1, replica_groups=mesh['px'=4,'py'=8] {'px','py'}, use_global_device_ids=true, to_apply=%region_5.6 | all-reduce | flops 1 | bytes 8 | tf_op jit(solution)/shard_map/psum | solution.py:98
  751.3 4.7 fusion.89
  761.0 4.2 collective-permute-done.9
  770.4 5.2 copy.153
  779.1 4.8 maximum_convert_fusion.2
  786.5 5.8 fusion.23
  792.3 21.4 %multiply_reduce_fusion = (f32[]{:T(128)}, f32[8,256,512]{1,0,2:T(8,128)}) fusion(f32[8,256,512]{1,0,2:T(8,128)} %get-tuple-element.19, f32[7,256,512]{1,0,2:T(8,128)} %fusion.23, f32[8,258,514]{1,0,2:T(8,128)} %copy-done.1, f32[8,258,514]{1,0,2:T(8,128)S(1)} %bitcast.140), kind=kLoop, calls=%fused_computation.91 | loop fusion | flops 24117248 | bytes 54001668 | tf_op jit(solution)/shard_map/reduce_sum | solution.py:105
  813.7 43.4 %psum.31 = f32[]{:T(128)} all-reduce(f32[]{:T(128)} %get-tuple-element.16), channel_id=1, replica_groups=mesh['px'=4,'py'=8] {'px','py'}, use_global_device_ids=true, to_apply=%region_7.8 | all-reduce | flops 1 | bytes 8 | tf_op jit(solution)/shard_map/psum | solution.py:105
  858.5 11.0 %fusion.21 = (f32[8,256,512]{1,0,2:T(8,128)}, f32[8,256,512]{1,0,2:T(8,128)}) fusion(f32[8,256,512]{1,0,2:T(8,128)} %copy.136, bf16[8,256,512]{1,0,2:T(8,128)(2,1)} %copy-done.3, f32[8,256,512]{1,0,2:T(8,128)} %get-tuple-element.19, f32[]{:T(128)S(6)} %div.19, f32[]{:T(128)S(6)} %div.16, f32[8,256,512]{1,0,2:T(8,128)} %get-tuple-element.21, ...), kind=kLoop, calls=%fused_computation.31 | loop fusion | flops 7340032 | bytes 27262984 | tf_op jit(solution)/shard_map/add | solution.py:106
  869.5 5.2 copy.151
  874.8 5.2 copy.152
  (101 shorter events, 106.6 us)
Async XLA Ops:
  13.5 3.4 copy-start.7
  31.4 10.5 %copy-start.5 = (bf16[1,8,256,512]{2,1,3,0:T(8,128)(2,1)}, bf16[1,8,256,512]{2,1,3,0:T(8,128)(2,1)S(1)}, u32[]{:S(2)}) copy-start(bf16[1,8,256,512]{2,1,3,0:T(8,128)(2,1)S(1)} %fusion.87) | copy-start | bytes 6291460
  31.4 6.3 collective-permute-start
  36.3 5.5 collective-permute-start.1
  48.5 11.1 %collective-permute-start.2 = (bf16[2,8,1,514]{3,1,2,0:T(8,128)(2,1)S(1)}, bf16[2,8,1,514]{3,1,2,0:T(8,128)(2,1)S(1)}, u32[]{:S(2)}, u32[]{:S(2)}) collective-permute-start(bf16[2,8,1,514]{3,1,2,0:T(8,128)(2,1)S(1)} %copy.117), channel_id=1, source_target_pairs={{0,1},{1,2},{2,3},{3,4},{4,5},{5,6},{6,7},{8,9},{9,10},{10,11},{11... | collective-permute-start | bytes 49352 | tf_op jit(solution)/shard_map/ppermute | solution.py:16
  52.4 9.6 %collective-permute-start.3 = (bf16[2,8,1,514]{3,1,2,0:T(8,128)(2,1)S(1)}, bf16[2,8,1,514]{3,1,2,0:T(8,128)(2,1)S(1)}, u32[]{:S(2)}, u32[]{:S(2)}) collective-permute-start(bf16[2,8,1,514]{3,1,2,0:T(8,128)(2,1)S(1)} %copy.118), channel_id=1, source_target_pairs={{1,0},{2,1},{3,2},{4,3},{5,4},{6,5},{7,6},{9,8},{10,9},{11,10},{12... | collective-permute-start | bytes 49352 | tf_op jit(solution)/shard_map/ppermute | solution.py:17
  83.4 2.6 copy-start
  194.0 11.9 %copy-start.10 = (f32[2048]{0:T(1024)S(1)}, f32[2048]{0:T(1024)}, u32[]{:S(2)}) copy-start(f32[2048]{0:T(1024)} %param.12) | copy-start | bytes 24580
  194.0 12.0 %copy-start.11 = (f32[8]{0:T(128)S(1)}, f32[8]{0:T(128)}, u32[]{:S(2)}) copy-start(f32[8]{0:T(128)} %param.13) | copy-start | bytes 100
  200.2 32.3 %all-to-all-start.1 = ((bf16[2,256,2048]{1,0,2:T(2,128)(2,1)}), bf16[2,256,2048]{1,0,2:T(2,128)(2,1)S(1)}, u32[]{:S(2)}, u32[]{:S(2)}) async-start(bf16[2,256,2048]{1,0,2:T(2,128)(2,1)} %copy.124), calls=%async_computation.1 | async-start | bytes 4194304 | tf_op jit(solution)/shard_map/all_to_all | solution.py:61
  234.1 4.1 copy-start.9
  363.2 10.5 %copy-start.3 = (bf16[8,256,512]{1,0,2:T(8,128)(2,1)}, bf16[8,256,512]{1,0,2:T(8,128)(2,1)S(1)}, u32[]{:S(2)}) copy-start(bf16[8,256,512]{1,0,2:T(8,128)(2,1)S(1)} %all_to_all.113) | copy-start | bytes 6291460
  363.3 3.4 collective-permute-start.4
  365.4 5.5 collective-permute-start.5
  370.9 1.3 copy-start.8
  375.6 3.8 collective-permute-start.6
  377.7 4.6 collective-permute-start.7
  382.3 5.3 slice-start
  384.0 3.7 slice-start.1
  387.7 5.9 copy-start.2
  706.6 44.7 %copy-start.4 = (bf16[8,256,512]{1,0,2:T(8,128)(2,1)S(1)}, bf16[8,256,512]{1,0,2:T(8,128)(2,1)}, u32[]{:S(2)}) copy-start(bf16[8,256,512]{1,0,2:T(8,128)(2,1)} %copy-done.3) | copy-start | bytes 6291460
  756.0 10.0 %copy-start.6 = (bf16[8,256,512]{1,0,2:T(8,128)(2,1)}, bf16[8,256,512]{1,0,2:T(8,128)(2,1)S(1)}, u32[]{:S(2)}) copy-start(bf16[8,256,512]{1,0,2:T(8,128)(2,1)S(1)} %get-tuple-element.18) | copy-start | bytes 6291460
  756.0 5.0 collective-permute-start.8
  759.7 5.5 collective-permute-start.9
  766.7 8.9 %collective-permute-start.10 = (bf16[8,1,514]{2,0,1:T(8,128)(2,1)S(1)}, bf16[8,1,514]{2,0,1:T(8,128)(2,1)S(1)}, u32[]{:S(2)}, u32[]{:S(2)}) collective-permute-start(bf16[8,1,514]{2,0,1:T(8,128)(2,1)S(1)} %copy.147), channel_id=1, source_target_pairs={{0,1},{1,2},{2,3},{3,4},{4,5},{5,6},{6,7},{8,9},{9,10},{10,11},{11... | collective-permute-start | bytes 24680 | tf_op jit(solution)/shard_map/ppermute | solution.py:16
  769.1 8.2 collective-permute-start.11
  777.3 9.2 %slice-start.2 = ((s8[6316032]{0:T(1024)(128)(4,1)}), s8[2121728]{0:T(1024)(128)(4,1)S(1)}, s32[]{:S(2)}) async-start(s8[6316032]{0:T(1024)(128)(4,1)} %bitcast.139), calls=%async_computation.10 | async-start | bytes 4243456
  779.1 7.4 slice-start.3
  783.8 2.6 copy-start.1
where the time goes:
time: 887 us; the launch traced here: 880 us
  blocking collectives  415 us (47%)
  other arithmetic  174 us (20%)
  local copies, waits for them, and re-layouts  146 us (16%)
  matrix products  72.1 us (8%)
  waiting for transfers between devices  39.6 us (4%)
  starting transfers between devices  29.2 us (3%)
    all_to_all x2, blocking collectives, precondition(): lax.all_to_all(rounded, 'px', split_axis=0, concat_axis=2, tiled=True)  103 us
    all_to_all x2, blocking collectives, precondition(): lax.all_to_all(pencil.astype(jnp.bfloat16), 'px', split_axis=2, concat_ax...  101 us
    psum x2, blocking collectives, shards(): gamma = lax.psum(jnp.sum(residual * precond), ('px', 'py'))  79 us
    all_to_all x2, blocking collectives, precondition(): lax.all_to_all(fourth, 'py', split_axis=1, concat_axis=2, tiled=True)  58.5 us
    reduce_sum x2, other arithmetic, shards(): alpha = gamma / lax.psum(jnp.sum(direction * image), ('px', 'py'))  52.4 us
    psum x1, blocking collectives, shards(): alpha = gamma / lax.psum(jnp.sum(direction * image), ('px', 'py'))  43.4 us
    unnamed x40, local copies, waits for them, and re-layouts  39.7 us
    convert_element_type x2, other arithmetic, precondition(): rounded = residual.astype(jnp.bfloat16)  35.5 us
  transfers between devices with their start and end apart: 13, of which 5 were waited for; matrix products, arithmetic and copies ran while one was open for 2% of the time, Pallas kernels for 0%

commit v1 on v0

--- a/solution.py
+++ b/solution.py
@@ -25,6 +25,17 @@
         return part.astype(jnp.bfloat16) if part.dtype == jnp.float32 else part
 
     return jax.tree.map(short, array)
+
+
+def all_sum(values):
+    for axis in ("px", "py"):
+        size = lax.axis_size(axis)
+        step = 1
+        while step < size:
+            pairs = [(i, i ^ step) for i in range(size)]
+            values = values + lax.ppermute(values, axis, pairs)
+            step *= 2
+    return values
 
 
 def face_sum(padded, coeff_pad):
@@ -81,6 +92,11 @@
     ).astype(pencil.dtype)
 
 
+def operator(field, coeff_pad):
+    padded = padded_2(for_sending(field), (("px", 2), ("py", 1)), 1).astype(field.dtype)
+    return face_sum(padded, coeff_pad)
+
+
 def shards(right_side, solution_in, classes, coeff_table, eigenvectors, eigenvalues, level_shift):
     coeff = jnp.zeros(classes.shape, jnp.float32)
     for label in range(coeff_table.shape[0]):
@@ -91,21 +107,35 @@
     coeff_pad = stacked[1]
     solution = solution_in
     residual = right_side - face_sum(stacked[0], coeff_pad)
-    direction = jnp.zeros_like(residual)
-    gamma_prev = jnp.float32(1.0)
+    direction = image = None
+    gamma_prev = curvature_prev = None
     for iteration in range(ITERS):
         precond = precondition(residual, eigenvectors, eigenvalues, level_shift)
-        gamma = lax.psum(jnp.sum(residual * precond), ("px", "py"))
+        precond_image = operator(precond, coeff_pad)
         if iteration == 0:
-            direction = precond
+            sums = all_sum(jnp.stack((jnp.sum(residual * precond), jnp.sum(precond * precond_image))))
+            gamma, curvature = sums[0], sums[1]
+            direction, image = precond, precond_image
         else:
-            direction = precond + gamma / gamma_prev * direction
-        padded = padded_2(for_sending(direction), (("px", 2), ("py", 1)), 1).astype(direction.dtype)
-        image = face_sum(padded, coeff_pad)
-        alpha = gamma / lax.psum(jnp.sum(direction * image), ("px", "py"))
+            sums = all_sum(
+                jnp.stack(
+                    (
+                        jnp.sum(residual * precond),
+                        jnp.sum(precond * precond_image),
+                        jnp.sum(precond * image),
+                        jnp.sum(direction * precond_image),
+                    )
+                )
+            )
+            gamma = sums[0]
+            beta = gamma / gamma_prev
+            curvature = sums[1] + beta * (sums[2] + sums[3]) + beta * beta * curvature_prev
+            direction = precond + beta * direction
+            image = precond_image + beta * image
+        alpha = gamma / curvature
         solution = solution + alpha * direction
         residual = residual - alpha * image
-        gamma_prev = gamma
+        gamma_prev, curvature_prev = gamma, curvature
     return (solution, residual, direction)
 
 

time: 887 us -> 810 us (0.913)
  blocking collectives: 415 us -> 290 us
  waiting for transfers between devices: 39.6 us -> 61 us
  starting transfers between devices: 29.2 us -> 41.6 us
    psum x3 -> x0, blocking collectives: 122 us -> none  [the longest x2 79 us: shards(): gamma = lax.psum(jnp.sum(residual * precond), ('px', 'py'))]
    ppermute x0 -> x10, waiting for transfers between devices: none -> 19.3 us  [all_sum(): values = values + lax.ppermute(values, axis, pairs)]
    ppermute x0 -> x10, starting transfers between devices: none -> 14 us  [all_sum(): values = values + lax.ppermute(values, axis, pairs)]
    convert_element_type x4 -> x2, other arithmetic: 16.5 us -> 7.28 us  [operator(): padded_2(for_sending(field), (('px', 2), ('py', 1)), 1).astype(field.dtype)]
    add x1 -> x11, other arithmetic: 11 us -> 19.5 us  [the longest x1 12.2 us: shards(): direction = precond + beta * direction]
    reduce_sum x3 -> x2, other arithmetic: 57.6 us -> 64.2 us  [shards(): jnp.sum(residual * precond)]
    unnamed x40 -> x42, local copies, waits for them, and re-layouts: 39.7 us -> 40.2 us
  transfers between devices with their start and end apart: 13 -> 23, of which waited for: 5 -> 16; matrix products, arithmetic and copies ran while one was open for 2% -> 2% of each run, Pallas kernels for 0% -> 0%
where the time goes in v1:
time: 810 us; the launch traced here: 802 us
  blocking collectives  290 us (36%)
  other arithmetic  182 us (22%)
  local copies, waits for them, and re-layouts  148 us (18%)
  matrix products  72.1 us (9%)
  waiting for transfers between devices  61 us (8%)
  starting transfers between devices  41.6 us (5%)
    all_to_all x2, blocking collectives, precondition(): lax.all_to_all(rounded, 'px', split_axis=0, concat_axis=2, tiled=True)  102 us
    all_to_all x2, blocking collectives, precondition(): lax.all_to_all(pencil.astype(jnp.bfloat16), 'px', split_axis=2, concat_ax...  101 us
    reduce_sum x2, other arithmetic, shards(): jnp.sum(residual * precond)  64.2 us
    all_to_all x2, blocking collectives, precondition(): lax.all_to_all(fourth, 'py', split_axis=1, concat_axis=2, tiled=True)  58.5 us
    unnamed x42, local copies, waits for them, and re-layouts  40.2 us
    dot_general x2, matrix products, precondition(): jnp.einsum('kji,yj->kyi', scaled, eigenvectors, preferred_element_type=jn...  34.1 us
    convert_element_type x2, other arithmetic, precondition(): rounded = residual.astype(jnp.bfloat16)  33.6 us
    all_to_all x1, blocking collectives, precondition(): lax.all_to_all(first, 'py', split_axis=2, concat_axis=1, tiled=True)  29.4 us
  transfers between devices with their start and end apart: 23, of which 16 were waited for; matrix products, arithmetic and copies ran while one was open for 2% of the time, Pallas kernels for 0%

profile of v1, /device:TPU:0, one launch (start us, length us, event | category | flops | bytes accessed | tf_op | source)
XLA Modules:
  0.0 802.4 jit_solution(18386760164336173728)
XLA Ops:
  2.6 5.4 copy.136
  10.4 5.4 copy.101
  15.8 15.7 %fusion.90 = bf16[1,8,256,512]{2,1,3,0:T(8,128)(2,1)S(1)} fusion(bf16[]{:T(256)} %bitcast.16, s32[8,256,512]{1,0,2:T(8,128)} %copy.101, bf16[]{:T(256)} %bitcast.15, bf16[]{:T(256)} %bitcast.14, bf16[]{:T(256)} %bitcast.13, bf16[]{:T(256)} %bitcast.12, bf16[]{:T(256)} %bitcast.11, bf16[]{:T(256)} %bitcast.10, bf16[]{:T(256)} %bitcast.9, bf16[]{:T(256)} %bitcast.8, ...), kind=kLoop, calls=%fused_computation.115 | loop fusion | flops 33554432 | bytes 6291488 | tf_op jit(solution)/shard_map/stack | solution.py:105
  31.5 4.9 collective-permute-start
  37.8 4.2 collective-permute-done.1
  54.3 5.4 copy.121
  64.6 11.0 %maximum_convert_fusion = f32[2,8,258,514]{2,1,3,0:T(8,128)} fusion(bf16[2,8,1,514]{2,1,3,0:T(8,128)(2,1)} %copy.120, bf16[2,8,256,1]{2,1,3,0:T(8,128)(2,1)S(1)} %collective-permute-done.1, bf16[1,8,256,512]{2,1,3,0:T(8,128)(2,1)} %copy-done.6, bf16[1,8,256,512]{2,1,3,0:T(8,128)(2,1)S(1)} %convert_bitcast_fusion, ...), kind=kLoop, calls=%fused_computation.27 | loop fusion | flops 25461504 | bytes 12730752 | tf_op jit(solution)/shard_map/convert_element_type | solution.py:106
  75.6 8.0 %slice_bitcast_fusion.1 = (f32[8,258,514]{1,0,2:T(8,128)S(1)}, f32[8,258,514]{1,0,2:T(8,128)}) fusion(f32[2,8,258,514]{2,1,3,0:T(8,128)} %maximum_convert_fusion), kind=kLoop, calls=%fused_computation.26 | loop fusion | bytes 16974336 | tf_op jit(solution)/shard_map/squeeze | solution.py:107
  86.2 10.5 %fusion.46 = f32[7,256,512]{1,0,2:T(8,128)} fusion(f32[8,258,514]{1,0,2:T(8,128)} %get-tuple-element.25, f32[8,258,514]{1,0,2:T(8,128)S(1)} %get-tuple-element.24), kind=kLoop, calls=%fused_computation.72 | loop fusion | flops 3670016 | bytes 18350080 | tf_op jit(solution)/shard_map/mul | solution.py:51
  96.7 29.5 %fusion.94 = (bf16[8,256,512]{1,0,2:T(8,128)(2,1)S(1)}, f32[8,256,512]{1,0,2:T(8,128)}) fusion(f32[8,256,512]{1,0,2:T(8,128)} %copy.121, f32[7,256,512]{1,0,2:T(8,128)} %fusion.46, f32[8,258,514]{1,0,2:T(8,128)} %get-tuple-element.25, f32[8,258,514]{1,0,2:T(8,128)} %copy-done), kind=kLoop, calls=%fused_computation.128 | loop fusion | flops 24117248 | bytes 56098816 | tf_op jit(solution)/shard_map/convert_element_type | solution.py:62
  126.6 52.1 %all_to_all.144 = bf16[8,256,512]{1,2,0:T(8,128)(2,1)S(1)} all-to-all(bf16[8,256,512]{1,2,0:T(8,128)(2,1)S(1)} %copy.122), channel_id=1, replica_groups=mesh['px'=4,'py'=8] {'px'}, dimensions={0} | all-to-all | bytes 4194304 | tf_op jit(solution)/shard_map/all_to_all | solution.py:66
  178.8 3.1 copy.123
  181.8 3.3 all_to_all.107
  185.1 9.0 %fusion.66 = bf16[2,256,2048]{2,1,0:T(8,128)(2,1)} fusion(bf16[2,256,2048]{2,1,0:T(8,128)(2,1)S(1)} %all_to_all.107, bf16[2048,2048]{1,0:T(8,128)(2,1)} %param.11), kind=kOutput, calls=%fused_computation.102 | convolution fusion | flops 4296015872 | bytes 12582912 | tf_op jit(solution)/shard_map/kyx,xi->kyi/dot_general | solution.py:64
  194.2 6.2 copy.124
  200.3 5.7 all-to-all-start.1
  207.8 24.9 %all-to-all-done.1 = bf16[2,256,2048]{1,0,2:T(2,128)(2,1)S(1)} async-done(((bf16[2,256,2048]{1,0,2:T(2,128)(2,1)}), bf16[2,256,2048]{1,0,2:T(2,128)(2,1)S(1)}, u32[]{:S(2)}, u32[]{:S(2)}) %all-to-all-start.1) | async-done | bytes 2097184 | tf_op jit(solution)/shard_map/all_to_all | solution.py:72
  234.3 4.1 copy.126
  238.4 16.8 %fusion.87 = bf16[2,2048,256]{1,2,0:T(8,128)(2,1)} fusion(bf16[2048,2048]{1,0:T(8,128)(2,1)} %param.11, bf16[2,2048,256]{2,1,0:T(8,128)(2,1)} %bitcast.167, f32[2]{0:T(128)S(1)} %dynamic_slice.9, f32[2048,256]{0,1:T(8,128)S(1)} %copy-done.9), kind=kOutput, calls=%fused_computation.109 | convolution fusion | flops 8594128896 | bytes 14680072 | tf_op jit(solution)/shard_map/kji,yj->kyi/dot_general | solution.py:85
  255.1 4.8 copy.128
  260.0 29.3 %all_to_all.145 = bf16[2,2048,256]{2,0,1:T(2,128)(2,1)S(1)} all-to-all(bf16[2,2048,256]{2,0,1:T(2,128)(2,1)S(1)} %copy.128), channel_id=1, replica_groups=mesh['px'=4,'py'=8] {'py'}, dimensions={1} | all-to-all | bytes 4194304 | tf_op jit(solution)/shard_map/all_to_all | solution.py:88
  292.8 10.0 %fusion.72 = bf16[2,256,2048]{2,1,0:T(8,128)(2,1)} fusion(bf16[2,256,2048]{2,1,0:T(8,128)(2,1)} %all_to_all.115, bf16[2048,2048]{1,0:T(8,128)(2,1)} %param.11), kind=kOutput, calls=%fused_computation.104 | convolution fusion | flops 4296015872 | bytes 12582912 | tf_op jit(solution)/shard_map/kyi,xi->kyx/dot_general | solution.py:89
  302.7 4.8 copy.130
  307.6 50.3 %all_to_all.146 = bf16[2,256,2048]{1,0,2:T(2,128)(2,1)S(1)} all-to-all(bf16[2,256,2048]{1,0,2:T(2,128)(2,1)S(1)} %copy.130), channel_id=1, replica_groups=mesh['px'=4,'py'=8] {'px'}, dimensions={2} | all-to-all | bytes 4194304 | tf_op jit(solution)/shard_map/all_to_all | solution.py:90
  367.0 4.0 collective-permute-done.5
  384.1 3.6 maximum_convert_fusion.1
  387.8 5.9 fusion.36
  393.6 31.1 %fusion.21 = (f32[]{:T(128)}, f32[]{:T(128)}, f32[8,256,512]{1,0,2:T(8,128)}) fusion(f32[8,256,512]{1,0,2:T(8,128)} %get-tuple-element.23, bf16[8,256,512]{1,0,2:T(8,128)(2,1)} %copy-done.3, f32[7,256,512]{1,0,2:T(8,128)} %fusion.36, f32[8,258,514]{1,0,2:T(8,128)} %copy-done.2, f32[8,258,514]{1,0,2:T(8,128)} %copy-done), kind=kLoop, calls=%fused_computation.36 | loop fusion | flops 27262976 | bytes 56098824 | tf_op jit(solution)/shard_map/reduce_sum | solution.py:116
  447.4 4.1 fusion.91
  451.9 49.6 %all_to_all.147 = bf16[8,256,512]{1,2,0:T(8,128)(2,1)S(1)} all-to-all(bf16[8,256,512]{1,2,0:T(8,128)(2,1)S(1)} %copy.137), channel_id=1, replica_groups=mesh['px'=4,'py'=8] {'px'}, dimensions={0} | all-to-all | bytes 4194304 | tf_op jit(solution)/shard_map/all_to_all | solution.py:66
  504.6 3.3 all_to_all.123
  507.9 9.0 %fusion.75 = bf16[2,256,2048]{2,1,0:T(8,128)(2,1)} fusion(bf16[2,256,2048]{2,1,0:T(8,128)(2,1)S(1)} %all_to_all.123, bf16[2048,2048]{1,0:T(8,128)(2,1)} %param.11), kind=kOutput, calls=%fused_computation.105 | convolution fusion | flops 4296015872 | bytes 12582912 | tf_op jit(solution)/shard_map/kyx,xi->kyi/dot_general | solution.py:64
  516.9 4.8 copy.139
  521.7 29.4 %all_to_all.148 = bf16[2,256,2048]{1,0,2:T(2,128)(2,1)S(1)} all-to-all(bf16[2,256,2048]{1,0,2:T(2,128)(2,1)S(1)} %copy.139), channel_id=1, replica_groups=mesh['px'=4,'py'=8] {'py'}, dimensions={2} | all-to-all | bytes 4194304 | tf_op jit(solution)/shard_map/all_to_all | solution.py:72
  553.8 17.4 %fusion.84 = bf16[2,2048,256]{1,2,0:T(8,128)(2,1)} fusion(bf16[2048,2048]{1,0:T(8,128)(2,1)} %param.11, bf16[2,2048,256]{2,1,0:T(8,128)(2,1)} %bitcast.166, f32[2]{0:T(128)S(1)} %dynamic_slice.9, f32[2048,256]{0,1:T(8,128)} %broadcast_add_fusion), kind=kOutput, calls=%fused_computation.108 | convolution fusion | flops 8594128896 | bytes 14680072 | tf_op jit(solution)/shard_map/kji,yj->kyi/dot_general | solution.py:85
  571.2 4.8 copy.143
  576.0 29.3 %all_to_all.149 = bf16[2,2048,256]{2,0,1:T(2,128)(2,1)S(1)} all-to-all(bf16[2,2048,256]{2,0,1:T(2,128)(2,1)S(1)} %copy.143), channel_id=1, replica_groups=mesh['px'=4,'py'=8] {'py'}, dimensions={1} | all-to-all | bytes 4194304 | tf_op jit(solution)/shard_map/all_to_all | solution.py:88
  608.8 9.9 %fusion.81 = bf16[2,256,2048]{2,1,0:T(8,128)(2,1)} fusion(bf16[2,256,2048]{2,1,0:T(8,128)(2,1)} %all_to_all.131, bf16[2048,2048]{1,0:T(8,128)(2,1)} %param.11), kind=kOutput, calls=%fused_computation.107 | convolution fusion | flops 4296015872 | bytes 12582912 | tf_op jit(solution)/shard_map/kyi,xi->kyx/dot_general | solution.py:89
  618.7 4.8 copy.145
  623.5 50.3 %all_to_all.150 = bf16[2,256,2048]{1,0,2:T(2,128)(2,1)S(1)} all-to-all(bf16[2,256,2048]{1,0,2:T(2,128)(2,1)S(1)} %copy.145), channel_id=1, replica_groups=mesh['px'=4,'py'=8] {'px'}, dimensions={2} | all-to-all | bytes 4194304 | tf_op jit(solution)/shard_map/all_to_all | solution.py:90
  682.9 4.0 collective-permute-done.14
  700.1 3.6 maximum_convert_fusion.2
  706.4 5.8 fusion.26
  712.2 33.1 %fusion.18 = (f32[]{:T(128)}, f32[]{:T(128)}, f32[]{:T(128)}, f32[]{:T(128)}, f32[8,256,512]{1,0,2:T(8,128)}) fusion(bf16[8,256,512]{1,0,2:T(8,128)(2,1)} %copy-done.5, f32[8,256,512]{1,0,2:T(8,128)} %get-tuple-element.23, f32[8,256,512]{1,0,2:T(8,128)} %get-tuple-element.21, f32[]{:T(128)S(6)} %div.16, bf16[8,256,512]{1,0,2:T(8,128)(2,1)} %copy-done.3, ...), kind=kLoop, calls=%fused_computation.33 | loop fusion | flops 34603004 | bytes 62390292 | tf_op jit(solution)/shard_map/reduce_sum | solution.py:123
  774.1 12.2 %convert_add_fusion = (f32[8,256,512]{1,0,2:T(8,128)}, f32[8,256,512]{1,0,2:T(8,128)}, f32[8,256,512]{1,0,2:T(8,128)}) fusion(bf16[8,256,512]{1,0,2:T(8,128)(2,1)} %copy-done.5, bf16[8,256,512]{1,0,2:T(8,128)(2,1)S(1)} %copy-done.4, f32[]{:T(128)S(6)} %div.18, f32[]{:T(128)S(6)} %div.19, f32[8,256,512]{1,0,2:T(8,128)} %copy.136, f32[]{:T(128)S(6)} %div.16, ...), kind=kLoop, calls=%fused_computation.21 | loop fusion | flops 14680064 | bytes 33554444 | tf_op jit(solution)/shard_map/add | solution.py:133
  786.3 5.2 copy.153
  791.5 5.2 copy.151
  796.8 5.2 copy.152
  (132 shorter events, 134.9 us)
Async XLA Ops:
  31.5 10.5 %copy-start.6 = (bf16[1,8,256,512]{2,1,3,0:T(8,128)(2,1)}, bf16[1,8,256,512]{2,1,3,0:T(8,128)(2,1)S(1)}, u32[]{:S(2)}) copy-start(bf16[1,8,256,512]{2,1,3,0:T(8,128)(2,1)S(1)} %fusion.90) | copy-start | bytes 6291460
  31.5 6.3 collective-permute-start
  36.5 5.5 collective-permute-start.1
  48.7 11.1 %collective-permute-start.2 = (bf16[2,8,1,514]{3,1,2,0:T(8,128)(2,1)S(1)}, bf16[2,8,1,514]{3,1,2,0:T(8,128)(2,1)S(1)}, u32[]{:S(2)}, u32[]{:S(2)}) collective-permute-start(bf16[2,8,1,514]{3,1,2,0:T(8,128)(2,1)S(1)} %copy.117), channel_id=1, source_target_pairs={{0,1},{1,2},{2,3},{3,4},{4,5},{5,6},{6,7},{8,9},{9,10},{10,11},{11... | collective-permute-start | bytes 49352 | tf_op jit(solution)/shard_map/ppermute | solution.py:16
  52.6 9.6 %collective-permute-start.3 = (bf16[2,8,1,514]{3,1,2,0:T(8,128)(2,1)S(1)}, bf16[2,8,1,514]{3,1,2,0:T(8,128)(2,1)S(1)}, u32[]{:S(2)}, u32[]{:S(2)}) collective-permute-start(bf16[2,8,1,514]{3,1,2,0:T(8,128)(2,1)S(1)} %copy.118), channel_id=1, source_target_pairs={{1,0},{2,1},{3,2},{4,3},{5,4},{6,5},{7,6},{9,8},{10,9},{11,10},{12... | collective-permute-start | bytes 49352 | tf_op jit(solution)/shard_map/ppermute | solution.py:17
  83.6 2.6 copy-start
  194.2 11.9 %copy-start.11 = (f32[8]{0:T(128)S(1)}, f32[8]{0:T(128)}, u32[]{:S(2)}) copy-start(f32[8]{0:T(128)} %param.13) | copy-start | bytes 100
  194.2 12.0 %copy-start.10 = (f32[2048]{0:T(1024)S(1)}, f32[2048]{0:T(1024)}, u32[]{:S(2)}) copy-start(f32[2048]{0:T(1024)} %param.12) | copy-start | bytes 24580
  200.3 32.3 %all-to-all-start.1 = ((bf16[2,256,2048]{1,0,2:T(2,128)(2,1)}), bf16[2,256,2048]{1,0,2:T(2,128)(2,1)S(1)}, u32[]{:S(2)}, u32[]{:S(2)}) async-start(bf16[2,256,2048]{1,0,2:T(2,128)(2,1)} %copy.124), calls=%async_computation.1 | async-start | bytes 4194304 | tf_op jit(solution)/shard_map/all_to_all | solution.py:72
  234.3 4.1 copy-start.9
  363.4 10.4 %copy-start.3 = (bf16[8,256,512]{1,0,2:T(8,128)(2,1)}, bf16[8,256,512]{1,0,2:T(8,128)(2,1)S(1)}, u32[]{:S(2)}) copy-start(bf16[8,256,512]{1,0,2:T(8,128)(2,1)S(1)} %all_to_all.119) | copy-start | bytes 6291460
  363.4 3.4 collective-permute-start.4
  365.5 5.5 collective-permute-start.5
  371.0 1.3 copy-start.7
  375.7 3.8 collective-permute-start.6
  377.8 4.6 collective-permute-start.7
  382.4 5.3 slice-start
  384.1 3.7 slice-start.1
  387.8 5.9 copy-start.2
  426.0 3.5 collective-permute-start.8
  430.9 4.4 collective-permute-start.9
  436.7 1.1 collective-permute-start.10
  437.8 3.9 collective-permute-start.11
  441.7 3.7 collective-permute-start.12
  679.3 10.5 %copy-start.5 = (bf16[8,256,512]{1,0,2:T(8,128)(2,1)}, bf16[8,256,512]{1,0,2:T(8,128)(2,1)S(1)}, u32[]{:S(2)}) copy-start(bf16[8,256,512]{1,0,2:T(8,128)(2,1)S(1)} %all_to_all.135) | copy-start | bytes 6291460
  679.3 3.4 collective-permute-start.13
  681.5 5.5 collective-permute-start.14
  687.0 1.3 copy-start.8
  691.7 3.6 collective-permute-start.15
  693.7 4.6 collective-permute-start.16
  698.4 8.0 slice-start.2
  700.1 6.3 slice-start.3
  703.7 2.7 copy-start.1
  712.2 61.9 %copy-start.4 = (bf16[8,256,512]{1,0,2:T(8,128)(2,1)S(1)}, bf16[8,256,512]{1,0,2:T(8,128)(2,1)}, u32[]{:S(2)}) copy-start(bf16[8,256,512]{1,0,2:T(8,128)(2,1)} %copy-done.3) | copy-start | bytes 6291460
  747.7 3.5 collective-permute-start.17
  753.6 4.4 collective-permute-start.18
  760.4 1.1 collective-permute-start.19
  761.5 3.9 collective-permute-start.20
  765.4 3.7 collective-permute-start.21

commit v2 on v1

--- a/solution.py
+++ b/solution.py
@@ -58,12 +58,31 @@
     return result
 
 
-def precondition(residual, eigenvectors, eigenvalues, level_shift):
+def exchange(block, axis, split_axis, concat_axis):
+    size = lax.axis_size(axis)
+    me = lax.axis_index(axis)
+    piece = block.shape[split_axis] // size
+    width = block.shape[concat_axis]
+    shape = list(block.shape)
+    shape[split_axis] = piece
+    shape[concat_axis] = width * size
+    result = jnp.zeros(shape, block.dtype)
+    for shift in range(size):
+        part = lax.dynamic_slice_in_dim(block, ((me + shift) % size) * piece, piece, split_axis)
+        if shift:
+            part = lax.ppermute(part, axis, [(i, (i + shift) % size) for i in range(size)])
+        result = lax.dynamic_update_slice_in_dim(
+            result, part, ((me - shift) % size) * width, concat_axis
+        )
+    return result
+
+
+def precondition_levels(residual, first_level, eigenvectors, eigenvalues, level_shift):
     rounded = residual.astype(jnp.bfloat16)
     levels_here = residual.shape[0] // lax.axis_size("px")
     first = jnp.einsum(
         "kyx,xi->kyi",
-        lax.all_to_all(rounded, "px", split_axis=0, concat_axis=2, tiled=True),
+        exchange(rounded, "px", 0, 2),
         eigenvectors,
         preferred_element_type=jnp.float32,
     ).astype(jnp.bfloat16)
@@ -78,7 +97,7 @@
         eigenvalues, lax.axis_index("py") * spectral_cols, spectral_cols, 0
     )
     shift_here = lax.dynamic_slice_in_dim(
-        level_shift, lax.axis_index("px") * levels_here, levels_here, 0
+        level_shift, first_level + lax.axis_index("px") * levels_here, levels_here, 0
     )
     denom = eigenvalues[None, :, None] + eigen_cols[None, None, :] + shift_here[:, None, None]
     scaled = (second / denom).astype(jnp.bfloat16)
@@ -87,9 +106,21 @@
     ).astype(jnp.bfloat16)
     returned = lax.all_to_all(fourth, "py", split_axis=1, concat_axis=2, tiled=True)
     pencil = jnp.einsum("kyi,xi->kyx", returned, eigenvectors, preferred_element_type=jnp.float32)
-    return lax.all_to_all(
-        pencil.astype(jnp.bfloat16), "px", split_axis=2, concat_axis=0, tiled=True
-    ).astype(pencil.dtype)
+    return exchange(pencil.astype(jnp.bfloat16), "px", 2, 0).astype(pencil.dtype)
+
+
+def precondition(residual, eigenvectors, eigenvalues, level_shift):
+    levels = residual.shape[0]
+    chunk = lax.axis_size("px")
+    if levels % chunk or levels == chunk:
+        chunk = levels
+    parts = [
+        precondition_levels(
+            residual[start : start + chunk], start, eigenvectors, eigenvalues, level_shift
+        )
+        for start in range(0, levels, chunk)
+    ]
+    return jnp.concatenate(parts, 0)
 
 
 def operator(field, coeff_pad):

time: 810 us -> 738 us (0.911)
  blocking collectives: 290 us -> 0 us
  starting transfers between devices: 41.6 us -> 160 us
  waiting for transfers between devices: 61 us -> 160 us
  local copies, waits for them, and re-layouts: 148 us -> 103 us
  other arithmetic: 182 us -> 211 us
  matrix products: 72.1 us -> 90.7 us
    all_to_all x7 -> x0, blocking collectives: 290 us -> none  [the longest x2 102 us: precondition(): lax.all_to_all(rounded, 'px', split_axis=0, concat_axis=2, tiled=True)]
    ppermute x0 -> x24, waiting for transfers between devices: none -> 89.5 us  [exchange(): lax.ppermute(part, axis, [(i, (i + shift) % size) for i in range(size)])]
    unnamed x2 -> x11, other arithmetic: 0.01 us -> 89 us
    ppermute x0 -> x24, starting transfers between devices: none -> 76.5 us  [exchange(): lax.ppermute(part, axis, [(i, (i + shift) % size) for i in range(size)])]
    reduce_sum x2, other arithmetic: 64.2 us -> 27.6 us  [shards(): jnp.sum(residual * precond)]
    all_to_all x1 -> x8, starting transfers between devices: 5.7 us -> 41.3 us  [the longest x4 24.5 us: precondition_levels(): lax.all_to_all(first, 'py', split_axis=2, concat_axis=1, tiled=True)]
    convert_element_type x2 -> x0, other arithmetic: 33.6 us -> none  [precondition(): rounded = residual.astype(jnp.bfloat16)]
    all_to_all x16 -> x8, local copies, waits for them, and re-layouts: 39 us -> 6.88 us  [the longest x4 3.83 us: precondition_levels(): lax.all_to_all(first, 'py', split_axis=2, concat_axis=1, tiled=True)]
  transfers between devices with their start and end apart: 23 -> 54, of which waited for: 16 -> 32; matrix products, arithmetic and copies ran while one was open for 2% -> 30% of each run, Pallas kernels for 0% -> 0%
where the time goes in v2:
time: 738 us; the launch traced here: 732 us
  other arithmetic  211 us (29%)
  starting transfers between devices  160 us (22%)
  waiting for transfers between devices  160 us (22%)
  local copies, waits for them, and re-layouts  103 us (14%)
  matrix products  90.7 us (12%)
  between operations  8.16 us (1%)
    ppermute x24, waiting for transfers between devices, exchange(): lax.ppermute(part, axis, [(i, (i + shift) % size) for i in range(size)])  89.5 us
    unnamed x11, other arithmetic  89 us
    ppermute x24, starting transfers between devices, exchange(): lax.ppermute(part, axis, [(i, (i + shift) % size) for i in range(size)])  76.5 us
    dot_general x4, matrix products, precondition_levels(): jnp.einsum('kji,yj->kyi', scaled, eigenvectors, preferred_element_type=jn...  46 us
    unnamed x79, local copies, waits for them, and re-layouts  45.6 us
    reduce_sum x2, other arithmetic, shards(): jnp.sum(residual * precond)  27.6 us
    all_to_all x4, starting transfers between devices, precondition_levels(): lax.all_to_all(first, 'py', split_axis=2, concat_axis=1, tiled=True)  24.5 us
    dot_general x4, matrix products, precondition_levels(): jnp.einsum('kyi,xi->kyx', returned, eigenvectors, preferred_element_type=...  23.1 us
  transfers between devices with their start and end apart: 54, of which 32 were waited for; matrix products, arithmetic and copies ran while one was open for 30% of the time, Pallas kernels for 0%

profile of v2, /device:TPU:0, one launch (start us, length us, event | category | flops | bytes accessed | tf_op | source)
XLA Modules:
  0.0 732.1 jit_solution(7143578503204085190)
XLA Ops:
  5.1 14.5 %fusion.60 = bf16[1,8,256,512]{3,2,1,0:T(8,128)(2,1)S(1)} fusion(bf16[]{:T(256)} %bitcast.16, s32[8,256,512]{2,1,0:T(8,128)S(1)} %copy-done.10, bf16[]{:T(256)} %bitcast.15, bf16[]{:T(256)} %bitcast.14, bf16[]{:T(256)} %bitcast.13, bf16[]{:T(256)} %bitcast.12, bf16[]{:T(256)} %bitcast.11, bf16[]{:T(256)} %bitcast.10, bf16[]{:T(256)} %bitcast.9, ...), kind=kLoop, calls=%fused_computation.126 | loop fusion | flops 33554432 | bytes 6291488 | tf_op jit(solution)/shard_map/stack | solution.py:136
  24.0 4.9 collective-permute-start
  43.6 11.7 %maximum_convert_fusion = f32[2,8,258,514]{3,2,1,0:T(8,128)} fusion(bf16[2,8,1,514]{3,2,1,0:T(2,128)(2,1)S(1)} %collective-permute-done.3, bf16[2,8,256,1]{3,2,1,0:T(8,128)(2,1)} %copy.51, bf16[1,8,256,512]{3,2,1,0:T(8,128)(2,1)} %copy-done.7, bf16[1,8,256,512]{3,2,1,0:T(8,128)(2,1)S(1)} %convert_bitcast_fusion, bf16[2,8,256,1]{3,2,1,0:T(8,128)(2,1)S(1)} %copy.50, ...), kind=kLoop, calls=%fused_computation.11 | loop fusion | flops 25461504 | bytes 12730752 | tf_op jit(solution)/shard_map/convert_element_type | solution.py:137
  55.3 4.8 slice_bitcast_fusion.1
  60.2 5.9 fusion.42
  66.1 12.7 %fusion.68 = (bf16[8,256,512]{2,1,0:T(8,128)(2,1)S(1)}, f32[8,256,512]{2,1,0:T(8,128)}) fusion(f32[8,256,512]{2,1,0:T(8,128)} %param.7, f32[7,256,512]{2,1,0:T(8,128)} %fusion.42, f32[8,258,514]{2,1,0:T(8,128)S(1)} %get-tuple-element.21, f32[8,258,514]{2,1,0:T(8,128)S(1)} %get-tuple-element.20), kind=kLoop, calls=%fused_computation.204 | loop fusion | flops 24117248 | bytes 56098816 | tf_op jit(solution)/shard_map/convert.5
  87.4 6.9 collective-permute-done.4
  94.5 4.8 collective-permute-done.5
  99.4 17.4 %collective-permute-done.6 = bf16[1,256,512]{2,1,0:T(8,128)(2,1)S(1)} collective-permute-done((bf16[1,256,512]{2,1,0:T(8,128)(2,1)S(1)}, bf16[1,256,512]{2,1,0:T(8,128)(2,1)S(1)}, u32[]{:S(2)}, u32[]{:S(2)}) %collective-permute-start.6) | collective-permute-done | bytes 262176 | tf_op jit(solution)/shard_map/ppermute | solution.py:73
  116.8 5.7 fusion.48
  124.9 10.6 %reduce.2 = bf16[2048,256]{1,0:T(8,128)(2,1)S(1)} reduce(bf16[2048,1,256]{2,1,0:T(2,128)(2,1)S(1)} %bitcast.245, bf16[]{:T(256)} %broadcast.89), dimensions={1}, to_apply=%bitcast.189.reduce_sub_computation | reduce | bytes 2097154
  136.6 11.8 %all-to-all-start = ((bf16[8,2,32768]{2,1,0:T(2,128)(2,1)}), bf16[8,2,32768]{2,1,0:T(2,128)(2,1)S(1)}, u32[]{:S(2)}, u32[]{:S(2)}) async-start(bf16[8,2,32768]{2,1,0:T(2,128)(2,1)} %reshape.214), calls=%async_computation | async-start | bytes 2097152 | tf_op jit(solution)/shard_map/all_to_all | solution.py:91
  151.5 6.7 fusion.50
  162.8 11.6 %reduce = bf16[2048,256]{1,0:T(8,128)(2,1)} reduce(bf16[2048,1,256]{2,1,0:T(2,128)(2,1)S(1)} %bitcast.247, bf16[]{:T(256)} %broadcast.89), dimensions={1}, to_apply=%bitcast.193.reduce_sub_computation | reduce | bytes 2097154
  183.0 11.1 %fusion.49 = bf16[1,2048,256]{1,2,0:T(8,128)(2,1)S(1)} fusion(bf16[2048,2048]{1,0:T(8,128)(2,1)} %param.11, bf16[2048,256]{1,0:T(8,128)(2,1)S(1)} %bitcast.264, f32[]{:T(128)} %bitcast.28, f32[256]{0:T(256)S(1)} %dynamic_slice.114, f32[2048]{0:T(1024)S(1)} %copy-done.20), kind=kOutput, calls=%fused_computation.114 | convolution fusion | flops 4297588736 | bytes 10494980 | tf_op jit(solution)/shard_map/kji,yj->kyi/dot_general | solution.py:104
  195.7 10.6 %reduce.3 = bf16[2048,256]{1,0:T(8,128)(2,1)S(1)} reduce(bf16[2048,1,256]{2,1,0:T(2,128)(2,1)S(1)} %bitcast.248, bf16[]{:T(256)} %broadcast.89), dimensions={1}, to_apply=%bitcast.191.reduce_sub_computation | reduce | bytes 2097154
  218.9 12.0 %fusion.51 = bf16[1,2048,256]{1,2,0:T(8,128)(2,1)} fusion(bf16[2048,2048]{1,0:T(8,128)(2,1)} %param.11, bf16[2048,256]{1,0:T(8,128)(2,1)S(1)} %bitcast.262, f32[]{:T(128)} %bitcast.45, f32[256]{0:T(256)S(1)} %dynamic_slice.114, f32[2048]{0:T(1024)S(1)} %copy-done.20), kind=kOutput, calls=%fused_computation.116 | convolution fusion | flops 4297588736 | bytes 10494980 | tf_op jit(solution)/shard_map/kji,yj->kyi/dot_general | solution.py:104
  235.5 11.6 %reduce.1 = bf16[2048,256]{1,0:T(8,128)(2,1)} reduce(bf16[2048,1,256]{2,1,0:T(2,128)(2,1)S(1)} %bitcast.249, bf16[]{:T(256)} %broadcast.89), dimensions={1}, to_apply=%bitcast.195.reduce_sub_computation | reduce | bytes 2097154
  255.3 5.8 convolution_convert_fusion.9
  262.9 5.1 collective-permute-start.7
  274.0 5.8 convolution_convert_fusion.6
  279.9 5.1 collective-permute-start.13
  291.8 20.8 %collective-permute-done.8 = bf16[1,256,512]{2,1,0:T(8,128)(2,1)S(1)} collective-permute-done((bf16[1,256,512]{2,1,0:T(8,128)(2,1)S(1)}, bf16[1,256,512]{2,1,0:T(8,128)(2,1)S(1)}, u32[]{:S(2)}, u32[]{:S(2)}) %collective-permute-start.8) | collective-permute-done | bytes 262176 | tf_op jit(solution)/shard_map/ppermute | solution.py:73
  312.6 10.2 %collective-permute-done.14 = bf16[1,256,512]{2,1,0:T(8,128)(2,1)S(1)} collective-permute-done((bf16[1,256,512]{2,1,0:T(8,128)(2,1)S(1)}, bf16[1,256,512]{2,1,0:T(8,128)(2,1)S(1)}, u32[]{:S(2)}, u32[]{:S(2)}) %collective-permute-start.14) | collective-permute-done | bytes 262176 | tf_op jit(solution)/shard_map/ppermute | solution.py:73
  325.8 9.4 %collective-permute-done.16 = bf16[8,256,1]{2,1,0:T(8,128)(2,1)S(1)} collective-permute-done((bf16[8,256,1]{2,1,0:T(8,128)(2,1)S(1)}, bf16[8,256,1]{2,1,0:T(8,128)(2,1)S(1)}, u32[]{:S(2)}, u32[]{:S(2)}) %collective-permute-start.16) | collective-permute-done | bytes 4128 | tf_op jit(solution)/shard_map/ppermute | solution.py:16
  342.9 4.8 collective-permute-done.19
  350.1 5.9 fusion.41
  356.0 13.4 %fusion.3 = (f32[]{:T(128)}, f32[]{:T(128)}, f32[8,256,512]{2,1,0:T(8,128)}) fusion(f32[8,256,512]{2,1,0:T(8,128)} %get-tuple-element.19, bf16[4,256,512]{2,1,0:T(8,128)(2,1)} %copy-done.4, bf16[4,256,512]{2,1,0:T(8,128)(2,1)} %copy-done.3, f32[7,256,512]{2,1,0:T(8,128)} %fusion.41, f32[8,258,514]{2,1,0:T(8,128)S(1)} %maximum_convert_fusion.1, ...), kind=kLoop, calls=%fused_computation.15 | loop fusion | flops 28311552 | bytes 56098824 | tf_op jit(solution)/shard_map/reduce_sum | solution.py:147
  392.3 4.8 fusion.61
  404.7 9.8 %collective-permute-done.31 = bf16[1,256,512]{2,1,0:T(8,128)(2,1)S(1)} collective-permute-done((bf16[1,256,512]{2,1,0:T(8,128)(2,1)S(1)}, bf16[1,256,512]{2,1,0:T(8,128)(2,1)S(1)}, u32[]{:S(2)}, u32[]{:S(2)}) %collective-permute-start.31) | collective-permute-done | bytes 262176 | tf_op jit(solution)/shard_map/ppermute | solution.py:73
  414.4 19.7 %collective-permute-start.25 = (bf16[1,256,512]{2,1,0:T(8,128)(2,1)S(1)}, bf16[1,256,512]{2,1,0:T(8,128)(2,1)S(1)}, u32[]{:S(2)}, u32[]{:S(2)}) collective-permute-start(bf16[1,256,512]{2,1,0:T(8,128)(2,1)S(1)} %get-tuple-element.43), channel_id=1, source_target_pairs={{0,8},{8,16},{16,24},{24,0},{1,9},{9,17},{17,25},{25,1},{2,10},{10... | collective-permute-start | bytes 786440 | tf_op jit(solution)/shard_map/ppermute | solution.py:73
  438.1 6.3 collective-permute-done.26
  449.6 10.6 %reduce.4 = bf16[2048,256]{1,0:T(8,128)(2,1)S(1)} reduce(bf16[2048,1,256]{2,1,0:T(2,128)(2,1)S(1)} %bitcast.250, bf16[]{:T(256)} %broadcast.89), dimensions={1}, to_apply=%bitcast.197.reduce_sub_computation | reduce | bytes 2097154
  464.9 6.7 fusion.52
  476.2 11.6 %reduce.6 = bf16[2048,256]{1,0:T(8,128)(2,1)} reduce(bf16[2048,1,256]{2,1,0:T(2,128)(2,1)S(1)} %bitcast.251, bf16[]{:T(256)} %broadcast.89), dimensions={1}, to_apply=%bitcast.201.reduce_sub_computation | reduce | bytes 2097154
  497.0 12.9 %all-to-all-done.4 = bf16[8,2,32768]{2,1,0:T(2,128)(2,1)} async-done(((bf16[8,2,32768]{2,1,0:T(2,128)(2,1)}), bf16[8,2,32768]{2,1,0:T(2,128)(2,1)}, u32[]{:S(2)}, u32[]{:S(2)}) %all-to-all-start.4) | async-done | bytes 1048608 | tf_op jit(solution)/shard_map/all_to_all | solution.py:91
  514.9 11.1 %fusion.53 = bf16[1,2048,256]{1,2,0:T(8,128)(2,1)S(1)} fusion(bf16[2048,2048]{1,0:T(8,128)(2,1)} %param.11, bf16[2048,256]{1,0:T(8,128)(2,1)S(1)} %bitcast.263, f32[]{:T(128)} %bitcast.28, f32[256]{0:T(256)S(1)} %dynamic_slice.114, f32[2048]{0:T(1024)S(1)} %copy-done.20), kind=kOutput, calls=%fused_computation.118 | convolution fusion | flops 4297588736 | bytes 10494980 | tf_op jit(solution)/shard_map/kji,yj->kyi/dot_general | solution.py:104
  527.7 10.6 %reduce.7 = bf16[2048,256]{1,0:T(8,128)(2,1)S(1)} reduce(bf16[2048,1,256]{2,1,0:T(2,128)(2,1)S(1)} %bitcast.252, bf16[]{:T(256)} %broadcast.89), dimensions={1}, to_apply=%bitcast.203.reduce_sub_computation | reduce | bytes 2097154
  543.5 12.0 %fusion.55 = bf16[1,2048,256]{1,2,0:T(8,128)(2,1)} fusion(bf16[2048,2048]{1,0:T(8,128)(2,1)} %param.11, bf16[2048,256]{1,0:T(8,128)(2,1)S(1)} %bitcast.261, f32[]{:T(128)} %bitcast.45, f32[256]{0:T(256)S(1)} %dynamic_slice.114, f32[2048]{0:T(1024)S(1)} %copy-done.20), kind=kOutput, calls=%fused_computation.120 | convolution fusion | flops 4297588736 | bytes 10494980 | tf_op jit(solution)/shard_map/kji,yj->kyi/dot_general | solution.py:104
  560.0 11.6 %reduce.5 = bf16[2048,256]{1,0:T(8,128)(2,1)} reduce(bf16[2048,1,256]{2,1,0:T(2,128)(2,1)S(1)} %bitcast.246, bf16[]{:T(256)} %broadcast.89), dimensions={1}, to_apply=%bitcast.199.reduce_sub_computation | reduce | bytes 2097154
  585.9 5.8 convolution_convert_fusion.3
  596.3 5.8 convolution_convert_fusion
  607.2 22.4 %collective-permute-start.34 = (bf16[1,256,512]{2,1,0:T(8,128)(2,1)S(1)}, bf16[1,256,512]{2,1,0:T(8,128)(2,1)S(1)}, u32[]{:S(2)}, u32[]{:S(2)}) collective-permute-start(bf16[1,256,512]{2,1,0:T(8,128)(2,1)S(1)} %get-tuple-element.46), channel_id=1, source_target_pairs={{0,8},{8,16},{16,24},{24,0},{1,9},{9,17},{17,25},{25,1},{2,10},{10... | collective-permute-start | bytes 786440 | tf_op jit(solution)/shard_map/ppermute | solution.py:73
  634.7 6.0 collective-permute-done.35
  643.9 10.0 %collective-permute-done.37 = bf16[8,256,1]{2,1,0:T(8,128)(2,1)S(1)} collective-permute-done((bf16[8,256,1]{2,1,0:T(8,128)(2,1)S(1)}, bf16[8,256,1]{2,1,0:T(8,128)(2,1)S(1)}, u32[]{:S(2)}, u32[]{:S(2)}) %collective-permute-start.37) | collective-permute-done | bytes 4128 | tf_op jit(solution)/shard_map/ppermute | solution.py:16
  667.3 5.9 fusion.40
  673.2 14.2 %fusion = (f32[]{:T(128)}, f32[]{:T(128)}, f32[]{:T(128)}, f32[]{:T(128)}, f32[8,256,512]{2,1,0:T(8,128)}) fusion(f32[8,256,512]{2,1,0:T(8,128)} %get-tuple-element.19, f32[8,256,512]{2,1,0:T(8,128)} %get-tuple-element.17, f32[]{:T(128)S(6)} %div.27, bf16[4,256,512]{2,1,0:T(8,128)(2,1)} %copy-done.5, bf16[4,256,512]{2,1,0:T(8,128)(2,1)} %copy-done.6, ...), kind=kLoop, calls=%fused_computation.12 | loop fusion | flops 36700156 | bytes 62390292 | tf_op jit(solution)/shard_map/reduce_sum | solution.py:154
  718.3 7.2 fusion.6
  (269 shorter events, 257.3 us)
Async XLA Ops:
  24.0 6.8 collective-permute-start
  29.3 5.7 collective-permute-start.1
  38.8 4.8 collective-permute-start.3
  79.0 20.3 %collective-permute-start.5 = (bf16[1,256,512]{2,1,0:T(8,128)(2,1)S(1)}, bf16[1,256,512]{2,1,0:T(8,128)(2,1)S(1)}, u32[]{:S(2)}, u32[]{:S(2)}) collective-permute-start(bf16[1,256,512]{2,1,0:T(8,128)(2,1)S(1)} %get-tuple-element.54), channel_id=1, source_target_pairs={{0,16},{8,24},{16,0},{24,8},{1,17},{9,25},{17,1},{25,9},{2,18},{10... | collective-permute-start | bytes 786440 | tf_op jit(solution)/shard_map/ppermute | solution.py:73
  81.7 12.6 %collective-permute-start.4 = (bf16[1,256,512]{2,1,0:T(8,128)(2,1)S(1)}, bf16[1,256,512]{2,1,0:T(8,128)(2,1)S(1)}, u32[]{:S(2)}, u32[]{:S(2)}) collective-permute-start(bf16[1,256,512]{2,1,0:T(8,128)(2,1)S(1)} %get-tuple-element.55), channel_id=1, source_target_pairs={{0,8},{8,16},{16,24},{24,0},{1,9},{9,17},{17,25},{25,1},{2,10},{10... | collective-permute-start | bytes 786440 | tf_op jit(solution)/shard_map/ppermute | solution.py:73
  82.9 67.6 %collective-permute-start.12 = (bf16[1,256,512]{2,1,0:T(8,128)(2,1)S(1)}, bf16[1,256,512]{2,1,0:T(8,128)(2,1)}, u32[]{:S(2)}, u32[]{:S(2)}) collective-permute-start(bf16[1,256,512]{2,1,0:T(8,128)(2,1)S(1)} %get-tuple-element.59), channel_id=1, source_target_pairs={{0,24},{8,0},{16,8},{24,16},{1,25},{9,1},{17,9},{25,17},{2,26},{10... | collective-permute-start | bytes 786440 | tf_op jit(solution)/shard_map/ppermute | solution.py:73
  86.7 62.7 %collective-permute-start.11 = (bf16[1,256,512]{2,1,0:T(8,128)(2,1)}, bf16[1,256,512]{2,1,0:T(8,128)(2,1)}, u32[]{:S(2)}, u32[]{:S(2)}) collective-permute-start(bf16[1,256,512]{2,1,0:T(8,128)(2,1)} %get-tuple-element.60), channel_id=1, source_target_pairs={{0,16},{8,24},{16,0},{24,8},{1,17},{9,25},{17,1},{25,9},{2,18},{10... | collective-permute-start | bytes 786440 | tf_op jit(solution)/shard_map/ppermute | solution.py:73
  86.7 61.7 %collective-permute-start.10 = (bf16[1,256,512]{2,1,0:T(8,128)(2,1)}, bf16[1,256,512]{2,1,0:T(8,128)(2,1)}, u32[]{:S(2)}, u32[]{:S(2)}) collective-permute-start(bf16[1,256,512]{2,1,0:T(8,128)(2,1)} %get-tuple-element.61), channel_id=1, source_target_pairs={{0,8},{8,16},{16,24},{24,0},{1,9},{9,17},{17,25},{25,1},{2,10},{10... | collective-permute-start | bytes 786440 | tf_op jit(solution)/shard_map/ppermute | solution.py:73
  94.3 22.5 %collective-permute-start.6 = (bf16[1,256,512]{2,1,0:T(8,128)(2,1)S(1)}, bf16[1,256,512]{2,1,0:T(8,128)(2,1)S(1)}, u32[]{:S(2)}, u32[]{:S(2)}) collective-permute-start(bf16[1,256,512]{2,1,0:T(8,128)(2,1)S(1)} %get-tuple-element.53), channel_id=1, source_target_pairs={{0,24},{8,0},{16,8},{24,16},{1,25},{9,1},{17,9},{25,17},{2,26},{10... | collective-permute-start | bytes 786440 | tf_op jit(solution)/shard_map/ppermute | solution.py:73
  136.6 39.9 %all-to-all-start = ((bf16[8,2,32768]{2,1,0:T(2,128)(2,1)}), bf16[8,2,32768]{2,1,0:T(2,128)(2,1)S(1)}, u32[]{:S(2)}, u32[]{:S(2)}) async-start(bf16[8,2,32768]{2,1,0:T(2,128)(2,1)} %reshape.214), calls=%async_computation | async-start | bytes 2097152 | tf_op jit(solution)/shard_map/all_to_all | solution.py:91
  176.5 31.1 %all-to-all-start.2 = ((bf16[8,2,32768]{2,1,0:T(2,128)(2,1)}), bf16[8,2,32768]{2,1,0:T(2,128)(2,1)}, u32[]{:S(2)}, u32[]{:S(2)}) async-start(bf16[8,2,32768]{2,1,0:T(2,128)(2,1)} %reshape.218), calls=%async_computation.2 | async-start | bytes 2097152 | tf_op jit(solution)/shard_map/all_to_all | solution.py:91
  207.6 41.7 %all-to-all-start.1 = ((bf16[8,2,32768]{2,1,0:T(2,128)(2,1)}), bf16[8,2,32768]{2,1,0:T(2,128)(2,1)S(1)}, u32[]{:S(2)}, u32[]{:S(2)}) async-start(bf16[8,2,32768]{2,1,0:T(2,128)(2,1)} %reshape.216), calls=%async_computation.1 | async-start | bytes 2097152 | tf_op jit(solution)/shard_map/all_to_all | solution.py:107
  249.2 19.7 %all-to-all-start.3 = ((bf16[8,2,32768]{2,1,0:T(2,128)(2,1)}), bf16[8,2,32768]{2,1,0:T(2,128)(2,1)}, u32[]{:S(2)}, u32[]{:S(2)}) async-start(bf16[8,2,32768]{2,1,0:T(2,128)(2,1)} %reshape.220), calls=%async_computation.3 | async-start | bytes 2097152 | tf_op jit(solution)/shard_map/all_to_all | solution.py:107
  262.9 27.8 %collective-permute-start.7 = (bf16[1,256,512]{2,1,0:T(8,128)(2,1)}, bf16[1,256,512]{2,1,0:T(8,128)(2,1)}, u32[]{:S(2)}, u32[]{:S(2)}) collective-permute-start(bf16[1,256,512]{2,1,0:T(8,128)(2,1)} %get-tuple-element.52), channel_id=1, source_target_pairs={{0,8},{8,16},{16,24},{24,0},{1,9},{9,17},{17,25},{25,1},{2,10},{10... | collective-permute-start | bytes 786440 | tf_op jit(solution)/shard_map/ppermute | solution.py:73
  279.9 11.9 %collective-permute-start.13 = (bf16[1,256,512]{2,1,0:T(8,128)(2,1)S(1)}, bf16[1,256,512]{2,1,0:T(8,128)(2,1)S(1)}, u32[]{:S(2)}, u32[]{:S(2)}) collective-permute-start(bf16[1,256,512]{2,1,0:T(8,128)(2,1)S(1)} %get-tuple-element.58), channel_id=1, source_target_pairs={{0,8},{8,16},{16,24},{24,0},{1,9},{9,17},{17,25},{25,1},{2,10},{10... | collective-permute-start | bytes 786440 | tf_op jit(solution)/shard_map/ppermute | solution.py:73
  286.1 36.8 %collective-permute-start.9 = (bf16[1,256,512]{2,1,0:T(8,128)(2,1)S(1)}, bf16[1,256,512]{2,1,0:T(8,128)(2,1)S(1)}, u32[]{:S(2)}, u32[]{:S(2)}) collective-permute-start(bf16[1,256,512]{2,1,0:T(8,128)(2,1)S(1)} %get-tuple-element.50), channel_id=1, source_target_pairs={{0,24},{8,0},{16,8},{24,16},{1,25},{9,1},{17,9},{25,17},{2,26},{10... | collective-permute-start | bytes 786440 | tf_op jit(solution)/shard_map/ppermute | solution.py:73
  286.1 26.5 %collective-permute-start.8 = (bf16[1,256,512]{2,1,0:T(8,128)(2,1)S(1)}, bf16[1,256,512]{2,1,0:T(8,128)(2,1)S(1)}, u32[]{:S(2)}, u32[]{:S(2)}) collective-permute-start(bf16[1,256,512]{2,1,0:T(8,128)(2,1)S(1)} %copy-done.18), channel_id=1, source_target_pairs={{0,16},{8,24},{16,0},{24,8},{1,17},{9,25},{17,1},{25,9},{2,18},{10... | collective-permute-start | bytes 786440 | tf_op jit(solution)/shard_map/ppermute | solution.py:73
  287.7 35.2 %collective-permute-start.15 = (bf16[1,256,512]{2,1,0:T(8,128)(2,1)S(1)}, bf16[1,256,512]{2,1,0:T(8,128)(2,1)S(1)}, u32[]{:S(2)}, u32[]{:S(2)}) collective-permute-start(bf16[1,256,512]{2,1,0:T(8,128)(2,1)S(1)} %get-tuple-element.56), channel_id=1, source_target_pairs={{0,24},{8,0},{16,8},{24,16},{1,25},{9,1},{17,9},{25,17},{2,26},{10... | collective-permute-start | bytes 786440 | tf_op jit(solution)/shard_map/ppermute | solution.py:73
  290.7 32.2 %collective-permute-start.14 = (bf16[1,256,512]{2,1,0:T(8,128)(2,1)S(1)}, bf16[1,256,512]{2,1,0:T(8,128)(2,1)S(1)}, u32[]{:S(2)}, u32[]{:S(2)}) collective-permute-start(bf16[1,256,512]{2,1,0:T(8,128)(2,1)S(1)} %get-tuple-element.57), channel_id=1, source_target_pairs={{0,16},{8,24},{16,0},{24,8},{1,17},{9,25},{17,1},{25,9},{2,18},{10... | collective-permute-start | bytes 786440 | tf_op jit(solution)/shard_map/ppermute | solution.py:73
  323.2 12.0 %collective-permute-start.16 = (bf16[8,256,1]{2,1,0:T(8,128)(2,1)S(1)}, bf16[8,256,1]{2,1,0:T(8,128)(2,1)S(1)}, u32[]{:S(2)}, u32[]{:S(2)}) collective-permute-start(bf16[8,256,1]{2,1,0:T(8,128)(2,1)S(1)} %get-tuple-element.34), channel_id=1, source_target_pairs={{0,8},{8,16},{16,24},{1,9},{9,17},{17,25},{2,10},{10,18},{18,26},{... | collective-permute-start | bytes 12296 | tf_op jit(solution)/shard_map/ppermute | solution.py:16
  324.5 14.8 %collective-permute-start.17 = (bf16[8,256,1]{2,1,0:T(8,128)(2,1)S(1)}, bf16[8,256,1]{2,1,0:T(8,128)(2,1)S(1)}, u32[]{:S(2)}, u32[]{:S(2)}) collective-permute-start(bf16[8,256,1]{2,1,0:T(8,128)(2,1)S(1)} %get-tuple-element.35), channel_id=1, source_target_pairs={{8,0},{16,8},{24,16},{9,1},{17,9},{25,17},{10,2},{18,10},{26,18},{... | collective-permute-start | bytes 12296 | tf_op jit(solution)/shard_map/ppermute | solution.py:17
  341.1 6.7 collective-permute-start.19
  370.7 3.7 collective-permute-start.20
  375.7 4.7 collective-permute-start.21
  383.0 3.7 collective-permute-start.23
  397.4 36.8 %collective-permute-start.32 = (bf16[1,256,512]{2,1,0:T(8,128)(2,1)S(1)}, bf16[1,256,512]{2,1,0:T(8,128)(2,1)S(1)}, u32[]{:S(2)}, u32[]{:S(2)}) collective-permute-start(bf16[1,256,512]{2,1,0:T(8,128)(2,1)S(1)} %get-tuple-element.48), channel_id=1, source_target_pairs={{0,16},{8,24},{16,0},{24,8},{1,17},{9,25},{17,1},{25,9},{2,18},{10... | collective-permute-start | bytes 786440 | tf_op jit(solution)/shard_map/ppermute | solution.py:73
  400.4 14.1 %collective-permute-start.31 = (bf16[1,256,512]{2,1,0:T(8,128)(2,1)S(1)}, bf16[1,256,512]{2,1,0:T(8,128)(2,1)S(1)}, u32[]{:S(2)}, u32[]{:S(2)}) collective-permute-start(bf16[1,256,512]{2,1,0:T(8,128)(2,1)S(1)} %get-tuple-element.49), channel_id=1, source_target_pairs={{0,8},{8,16},{16,24},{24,0},{1,9},{9,17},{17,25},{25,1},{2,10},{10... | collective-permute-start | bytes 786440 | tf_op jit(solution)/shard_map/ppermute | solution.py:73
  400.7 43.7 %collective-permute-start.33 = (bf16[1,256,512]{2,1,0:T(8,128)(2,1)S(1)}, bf16[1,256,512]{2,1,0:T(8,128)(2,1)S(1)}, u32[]{:S(2)}, u32[]{:S(2)}) collective-permute-start(bf16[1,256,512]{2,1,0:T(8,128)(2,1)S(1)} %get-tuple-element.47), channel_id=1, source_target_pairs={{0,24},{8,0},{16,8},{24,16},{1,25},{9,1},{17,9},{25,17},{2,26},{10... | collective-permute-start | bytes 786440 | tf_op jit(solution)/shard_map/ppermute | solution.py:73
  404.6 39.8 %collective-permute-start.27 = (bf16[1,256,512]{2,1,0:T(8,128)(2,1)S(1)}, bf16[1,256,512]{2,1,0:T(8,128)(2,1)S(1)}, u32[]{:S(2)}, u32[]{:S(2)}) collective-permute-start(bf16[1,256,512]{2,1,0:T(8,128)(2,1)S(1)} %get-tuple-element.41), channel_id=1, source_target_pairs={{0,24},{8,0},{16,8},{24,16},{1,25},{9,1},{17,9},{25,17},{2,26},{10... | collective-permute-start | bytes 786440 | tf_op jit(solution)/shard_map/ppermute | solution.py:73
  404.7 39.7 %collective-permute-start.26 = (bf16[1,256,512]{2,1,0:T(8,128)(2,1)S(1)}, bf16[1,256,512]{2,1,0:T(8,128)(2,1)S(1)}, u32[]{:S(2)}, u32[]{:S(2)}) collective-permute-start(bf16[1,256,512]{2,1,0:T(8,128)(2,1)S(1)} %get-tuple-element.42), channel_id=1, source_target_pairs={{0,16},{8,24},{16,0},{24,8},{1,17},{9,25},{17,1},{25,9},{2,18},{10... | collective-permute-start | bytes 786440 | tf_op jit(solution)/shard_map/ppermute | solution.py:73
  414.4 23.6 %collective-permute-start.25 = (bf16[1,256,512]{2,1,0:T(8,128)(2,1)S(1)}, bf16[1,256,512]{2,1,0:T(8,128)(2,1)S(1)}, u32[]{:S(2)}, u32[]{:S(2)}) collective-permute-start(bf16[1,256,512]{2,1,0:T(8,128)(2,1)S(1)} %get-tuple-element.43), channel_id=1, source_target_pairs={{0,8},{8,16},{16,24},{24,0},{1,9},{9,17},{17,25},{25,1},{2,10},{10... | collective-permute-start | bytes 786440 | tf_op jit(solution)/shard_map/ppermute | solution.py:73
  461.3 28.6 %all-to-all-start.6 = ((bf16[8,2,32768]{2,1,0:T(2,128)(2,1)}), bf16[8,2,32768]{2,1,0:T(2,128)(2,1)S(1)}, u32[]{:S(2)}, u32[]{:S(2)}) async-start(bf16[8,2,32768]{2,1,0:T(2,128)(2,1)} %reshape.222), calls=%async_computation.6 | async-start | bytes 2097152 | tf_op jit(solution)/shard_map/all_to_all | solution.py:91
  490.0 19.9 %all-to-all-start.4 = ((bf16[8,2,32768]{2,1,0:T(2,128)(2,1)}), bf16[8,2,32768]{2,1,0:T(2,128)(2,1)}, u32[]{:S(2)}, u32[]{:S(2)}) async-start(bf16[8,2,32768]{2,1,0:T(2,128)(2,1)} %reshape.226), calls=%async_computation.4 | async-start | bytes 2097152 | tf_op jit(solution)/shard_map/all_to_all | solution.py:91
  539.5 34.3 %all-to-all-start.5 = ((bf16[8,2,32768]{2,1,0:T(2,128)(2,1)}), bf16[8,2,32768]{2,1,0:T(2,128)(2,1)S(1)}, u32[]{:S(2)}, u32[]{:S(2)}) async-start(bf16[8,2,32768]{2,1,0:T(2,128)(2,1)} %reshape.228), calls=%async_computation.5 | async-start | bytes 2097152 | tf_op jit(solution)/shard_map/all_to_all | solution.py:107
  574.8 19.8 %all-to-all-start.7 = ((bf16[8,2,32768]{2,1,0:T(2,128)(2,1)}), bf16[8,2,32768]{2,1,0:T(2,128)(2,1)S(1)}, u32[]{:S(2)}, u32[]{:S(2)}) async-start(bf16[8,2,32768]{2,1,0:T(2,128)(2,1)} %reshape.224), calls=%async_computation.7 | async-start | bytes 2097152 | tf_op jit(solution)/shard_map/all_to_all | solution.py:107
  592.7 37.9 %collective-permute-start.29 = (bf16[1,256,512]{2,1,0:T(8,128)(2,1)}, bf16[1,256,512]{2,1,0:T(8,128)(2,1)}, u32[]{:S(2)}, u32[]{:S(2)}) collective-permute-start(bf16[1,256,512]{2,1,0:T(8,128)(2,1)} %get-tuple-element.39), channel_id=1, source_target_pairs={{0,16},{8,24},{16,0},{24,8},{1,17},{9,25},{17,1},{25,9},{2,18},{10... | collective-permute-start | bytes 786440 | tf_op jit(solution)/shard_map/ppermute | solution.py:73
  593.9 13.3 %collective-permute-start.28 = (bf16[1,256,512]{2,1,0:T(8,128)(2,1)}, bf16[1,256,512]{2,1,0:T(8,128)(2,1)}, u32[]{:S(2)}, u32[]{:S(2)}) collective-permute-start(bf16[1,256,512]{2,1,0:T(8,128)(2,1)} %get-tuple-element.40), channel_id=1, source_target_pairs={{0,8},{8,16},{16,24},{24,0},{1,9},{9,17},{17,25},{25,1},{2,10},{10... | collective-permute-start | bytes 786440 | tf_op jit(solution)/shard_map/ppermute | solution.py:73
  603.2 28.3 %collective-permute-start.30 = (bf16[1,256,512]{2,1,0:T(8,128)(2,1)S(1)}, bf16[1,256,512]{2,1,0:T(8,128)(2,1)S(1)}, u32[]{:S(2)}, u32[]{:S(2)}) collective-permute-start(bf16[1,256,512]{2,1,0:T(8,128)(2,1)S(1)} %get-tuple-element.38), channel_id=1, source_target_pairs={{0,24},{8,0},{16,8},{24,16},{1,25},{9,1},{17,9},{25,17},{2,26},{10... | collective-permute-start | bytes 786440 | tf_op jit(solution)/shard_map/ppermute | solution.py:73
  606.6 34.1 %collective-permute-start.36 = (bf16[1,256,512]{2,1,0:T(8,128)(2,1)S(1)}, bf16[1,256,512]{2,1,0:T(8,128)(2,1)S(1)}, u32[]{:S(2)}, u32[]{:S(2)}) collective-permute-start(bf16[1,256,512]{2,1,0:T(8,128)(2,1)S(1)} %get-tuple-element.44), channel_id=1, source_target_pairs={{0,24},{8,0},{16,8},{24,16},{1,25},{9,1},{17,9},{25,17},{2,26},{10... | collective-permute-start | bytes 786440 | tf_op jit(solution)/shard_map/ppermute | solution.py:73
  606.6 34.0 %collective-permute-start.35 = (bf16[1,256,512]{2,1,0:T(8,128)(2,1)S(1)}, bf16[1,256,512]{2,1,0:T(8,128)(2,1)S(1)}, u32[]{:S(2)}, u32[]{:S(2)}) collective-permute-start(bf16[1,256,512]{2,1,0:T(8,128)(2,1)S(1)} %get-tuple-element.45), channel_id=1, source_target_pairs={{0,16},{8,24},{16,0},{24,8},{1,17},{9,25},{17,1},{25,9},{2,18},{10... | collective-permute-start | bytes 786440 | tf_op jit(solution)/shard_map/ppermute | solution.py:73
  607.2 27.5 %collective-permute-start.34 = (bf16[1,256,512]{2,1,0:T(8,128)(2,1)S(1)}, bf16[1,256,512]{2,1,0:T(8,128)(2,1)S(1)}, u32[]{:S(2)}, u32[]{:S(2)}) collective-permute-start(bf16[1,256,512]{2,1,0:T(8,128)(2,1)S(1)} %get-tuple-element.46), channel_id=1, source_target_pairs={{0,8},{8,16},{16,24},{24,0},{1,9},{9,17},{17,25},{25,1},{2,10},{10... | collective-permute-start | bytes 786440 | tf_op jit(solution)/shard_map/ppermute | solution.py:73
  640.9 13.0 %collective-permute-start.37 = (bf16[8,256,1]{2,1,0:T(8,128)(2,1)S(1)}, bf16[8,256,1]{2,1,0:T(8,128)(2,1)S(1)}, u32[]{:S(2)}, u32[]{:S(2)}) collective-permute-start(bf16[8,256,1]{2,1,0:T(8,128)(2,1)S(1)} %get-tuple-element.30), channel_id=1, source_target_pairs={{0,8},{8,16},{16,24},{1,9},{9,17},{17,25},{2,10},{10,18},{18,26},{... | collective-permute-start | bytes 12296 | tf_op jit(solution)/shard_map/ppermute | solution.py:16
  642.6 15.9 %collective-permute-start.38 = (bf16[8,256,1]{2,1,0:T(8,128)(2,1)S(1)}, bf16[8,256,1]{2,1,0:T(8,128)(2,1)S(1)}, u32[]{:S(2)}, u32[]{:S(2)}) collective-permute-start(bf16[8,256,1]{2,1,0:T(8,128)(2,1)S(1)} %get-tuple-element.31), channel_id=1, source_target_pairs={{8,0},{16,8},{24,16},{9,1},{17,9},{25,17},{10,2},{18,10},{26,18},{... | collective-permute-start | bytes 12296 | tf_op jit(solution)/shard_map/ppermute | solution.py:17
  660.2 4.7 collective-permute-start.40
  690.1 3.6 collective-permute-start.41
  696.3 4.7 collective-permute-start.42
  704.9 3.9 collective-permute-start.44
  708.8 4.3 collective-permute-start.45
  (33 other events, 394.9 us)

commit v3 on v2

--- a/solution.py
+++ b/solution.py
@@ -78,35 +78,36 @@
 
 
 def precondition_levels(residual, first_level, eigenvectors, eigenvalues, level_shift):
-    rounded = residual.astype(jnp.bfloat16)
-    levels_here = residual.shape[0] // lax.axis_size("px")
-    first = jnp.einsum(
-        "kyx,xi->kyi",
-        exchange(rounded, "px", 0, 2),
-        eigenvectors,
-        preferred_element_type=jnp.float32,
+    across = lax.axis_size("py")
+    lines = exchange(residual.astype(jnp.bfloat16), "px", 0, 2)
+    levels_here, rows, width = lines.shape
+    cols = width // across
+    first = jnp.dot(
+        lines.reshape(levels_here * rows, width), eigenvectors, preferred_element_type=jnp.float32
     ).astype(jnp.bfloat16)
-    second = jnp.einsum(
-        "kyi,yj->kji",
-        lax.all_to_all(first, "py", split_axis=2, concat_axis=1, tiled=True),
-        eigenvectors,
-        preferred_element_type=jnp.float32,
-    )
-    spectral_cols = second.shape[2]
-    eigen_cols = lax.dynamic_slice_in_dim(
-        eigenvalues, lax.axis_index("py") * spectral_cols, spectral_cols, 0
-    )
+    outgoing = first.reshape(levels_here * rows, across, cols).transpose(1, 0, 2)
+    incoming = lax.all_to_all(outgoing, "py", 0, 0, tiled=True)
+    spectral = incoming.reshape(across, levels_here, rows, cols).transpose(1, 0, 2, 3)
+    spectral = spectral.reshape(levels_here, across * rows, cols)
+    second = jnp.einsum("jy,kyi->kji", eigenvectors, spectral, preferred_element_type=jnp.float32)
+    eigen_cols = lax.dynamic_slice_in_dim(eigenvalues, lax.axis_index("py") * cols, cols, 0)
     shift_here = lax.dynamic_slice_in_dim(
         level_shift, first_level + lax.axis_index("px") * levels_here, levels_here, 0
     )
     denom = eigenvalues[None, :, None] + eigen_cols[None, None, :] + shift_here[:, None, None]
     scaled = (second / denom).astype(jnp.bfloat16)
     fourth = jnp.einsum(
-        "kji,yj->kyi", scaled, eigenvectors, preferred_element_type=jnp.float32
+        "yj,kji->kyi", eigenvectors, scaled, preferred_element_type=jnp.float32
     ).astype(jnp.bfloat16)
-    returned = lax.all_to_all(fourth, "py", split_axis=1, concat_axis=2, tiled=True)
-    pencil = jnp.einsum("kyi,xi->kyx", returned, eigenvectors, preferred_element_type=jnp.float32)
-    return exchange(pencil.astype(jnp.bfloat16), "px", 2, 0).astype(pencil.dtype)
+    outgoing = fourth.reshape(levels_here, across, rows, cols).transpose(1, 0, 2, 3)
+    returned = lax.all_to_all(outgoing, "py", 0, 0, tiled=True)
+    pencil = jnp.einsum(
+        "qkyi,qix->kyx",
+        returned,
+        eigenvectors.reshape(across, cols, width),
+        preferred_element_type=jnp.float32,
+    )
+    return exchange(pencil.astype(jnp.bfloat16), "px", 2, 0).astype(jnp.float32)
 
 
 def precondition(residual, eigenvectors, eigenvalues, level_shift):

time: 738 us -> 589 us (0.80)
  other arithmetic: 211 us -> 122 us
  local copies, waits for them, and re-layouts: 103 us -> 29.5 us
  waiting for transfers between devices: 160 us -> 207 us
  starting transfers between devices: 160 us -> 132 us
    unnamed x11 -> x3, other arithmetic: 89 us -> 0.01 us
    unnamed x79 -> x36, local copies, waits for them, and re-layouts: 45.6 us -> 4.22 us
    all_to_all x8, waiting for transfers between devices: 13.9 us -> 44.6 us  [the longest x4 22.5 us: precondition_levels(): returned = lax.all_to_all(outgoing, 'py', 0, 0, tiled=True)]
    convert_element_type x8 -> x0, local copies, waits for them, and re-layouts: 25.1 us -> none  [the longest x4 12.6 us: precondition_levels(): first = jnp.einsum('kyx,xi->kyi', exchange(rounded, 'px', 0, 2), eigenvec...]
    ppermute x24, starting transfers between devices: 76.5 us -> 66.7 us  [exchange(): lax.ppermute(part, axis, [(i, (i + shift) % size) for i in range(size)])]
    ppermute x10, starting transfers between devices: 20.9 us -> 11.5 us  [all_sum(): values = values + lax.ppermute(values, axis, pairs)]
    all_to_all x8, starting transfers between devices: 41.3 us -> 32.4 us  [the longest x4 17.4 us: precondition_levels(): incoming = lax.all_to_all(outgoing, 'py', 0, 0, tiled=True)]
    ppermute x10, waiting for transfers between devices: 14 us -> 21.7 us  [all_sum(): values = values + lax.ppermute(values, axis, pairs)]
  transfers between devices with their start and end apart: 54 -> 54, of which waited for: 32 -> 37; matrix products, arithmetic and copies ran while one was open for 30% -> 17% of each run, Pallas kernels for 0% -> 0%
where the time goes in v3:
time: 589 us; the launch traced here: 584 us
  waiting for transfers between devices  207 us (35%)
  starting transfers between devices  132 us (22%)
  other arithmetic  122 us (21%)
  matrix products  86.6 us (15%)
  local copies, waits for them, and re-layouts  29.5 us (5%)
  between operations  7.92 us (1%)
    ppermute x24, waiting for transfers between devices, exchange(): lax.ppermute(part, axis, [(i, (i + shift) % size) for i in range(size)])  94.8 us
    ppermute x24, starting transfers between devices, exchange(): lax.ppermute(part, axis, [(i, (i + shift) % size) for i in range(size)])  66.7 us
    dot_general x4, matrix products, precondition_levels(): jnp.einsum('yj,kji->kyi', eigenvectors, scaled, preferred_element_type=jn...  44.2 us
    ppermute x6, waiting for transfers between devices, padded_2(): after = lax.ppermute(initial, axis, down)  27.6 us
    reduce_sum x2, other arithmetic, shards(): jnp.sum(residual * precond)  27.6 us
    dot_general x4, matrix products, precondition_levels(): jnp.einsum('qkyi,qix->kyx', returned, eigenvectors.reshape(across, cols,...  22.8 us
    all_to_all x4, waiting for transfers between devices, precondition_levels(): returned = lax.all_to_all(outgoing, 'py', 0, 0, tiled=True)  22.5 us
    all_to_all x4, waiting for transfers between devices, precondition_levels(): incoming = lax.all_to_all(outgoing, 'py', 0, 0, tiled=True)  22.1 us
  transfers between devices with their start and end apart: 54, of which 37 were waited for; matrix products, arithmetic and copies ran while one was open for 17% of the time, Pallas kernels for 0%

profile of v3, /device:TPU:0, one launch (start us, length us, event | category | flops | bytes accessed | tf_op | source)
XLA Modules:
  0.0 584.4 jit_solution(4398794939715801199)
XLA Ops:
  5.0 14.5 %fusion.64 = bf16[1,8,256,512]{3,2,1,0:T(8,128)(2,1)S(1)} fusion(bf16[]{:T(256)} %bitcast.16, s32[8,256,512]{2,1,0:T(8,128)S(1)} %copy-done.9, bf16[]{:T(256)} %bitcast.15, bf16[]{:T(256)} %bitcast.14, bf16[]{:T(256)} %bitcast.13, bf16[]{:T(256)} %bitcast.12, bf16[]{:T(256)} %bitcast.11, bf16[]{:T(256)} %bitcast.10, bf16[]{:T(256)} %bitcast.9, bf16[]{:T(256)} %bitcast.8, ...), kind=kLoop, calls=%fused_computation.130 | loop fusion | flops 33554432 | bytes 6291488 | tf_op jit(solution)/shard_map/stack | solution.py:137
  24.0 4.9 collective-permute-start
  43.6 11.7 %maximum_convert_fusion = f32[2,8,258,514]{3,2,1,0:T(8,128)} fusion(bf16[2,8,1,514]{3,2,1,0:T(2,128)(2,1)S(1)} %collective-permute-done.3, bf16[2,8,256,1]{3,2,1,0:T(8,128)(2,1)} %copy.55, bf16[1,8,256,512]{3,2,1,0:T(8,128)(2,1)} %copy-done.7, bf16[1,8,256,512]{3,2,1,0:T(8,128)(2,1)S(1)} %convert_bitcast_fusion, bf16[2,8,256,1]{3,2,1,0:T(8,128)(2,1)S(1)} %copy.54, ...), kind=kLoop, calls=%fused_computation.11 | loop fusion | flops 25461504 | bytes 12730752 | tf_op jit(solution)/shard_map/convert_element_type | solution.py:138
  55.3 4.8 slice_bitcast_fusion.1
  60.2 5.9 %fusion.42 = f32[7,256,512]{2,1,0:T(8,128)} fusion(f32[8,258,514]{2,1,0:T(8,128)S(1)} %get-tuple-element.21, f32[8,258,514]{2,1,0:T(8,128)S(1)} %get-tuple-element.20), kind=kLoop, calls=%fused_computation.76 | loop fusion | flops 3670016 | bytes 18350080 | tf_op jit(solution)/shard_map/mul | solution.py:51
  66.1 12.7 %fusion.76 = (bf16[8,256,512]{2,1,0:T(8,128)(2,1)S(1)}, f32[8,256,512]{2,1,0:T(8,128)}) fusion(f32[8,256,512]{2,1,0:T(8,128)} %param.7, f32[7,256,512]{2,1,0:T(8,128)} %fusion.42, f32[8,258,514]{2,1,0:T(8,128)S(1)} %get-tuple-element.21, f32[8,258,514]{2,1,0:T(8,128)S(1)} %get-tuple-element.20), kind=kLoop, calls=%fused_computation.216 | loop fusion | flops 24117248 | bytes 56098816 | tf_op jit(solution)/shard_map/convert.5
  82.0 3.9 collective-permute-start.12
  86.0 8.2 %collective-permute-done.10 = bf16[1,256,512]{2,1,0:T(8,128)(2,1)S(1)} collective-permute-done((bf16[1,256,512]{2,1,0:T(8,128)(2,1)S(1)}, bf16[1,256,512]{2,1,0:T(8,128)(2,1)S(1)}, u32[]{:S(2)}, u32[]{:S(2)}) %collective-permute-start.10) | collective-permute-done | bytes 262176 | tf_op jit(solution)/shard_map/ppermute | solution.py:73
  94.2 20.4 %collective-permute-start.4 = (bf16[1,256,512]{2,1,0:T(8,128)(2,1)S(1)}, bf16[1,256,512]{2,1,0:T(8,128)(2,1)}, u32[]{:S(2)}, u32[]{:S(2)}) collective-permute-start(bf16[1,256,512]{2,1,0:T(8,128)(2,1)S(1)} %get-tuple-element.55), channel_id=1, source_target_pairs={{0,8},{8,16},{16,24},{24,0},{1,9},{9,17},{17,25},{25,1},{2,10},{10... | collective-permute-start | bytes 786440 | tf_op jit(solution)/shard_map/ppermute | solution.py:73
  114.7 5.7 convolution_convert_fusion.5
  121.5 6.7 %all-to-all-start.2 = ((bf16[8,256,256]{2,1,0:T(8,128)(2,1)}), bf16[8,256,256]{2,1,0:T(8,128)(2,1)S(1)}, u32[]{:S(2)}, u32[]{:S(2)}) async-start(bf16[8,256,256]{2,1,0:T(8,128)(2,1)} %bitcast.267), calls=%async_computation.2 | async-start | bytes 2097152 | tf_op jit(solution)/shard_map/all_to_all | solution.py:89
  129.3 5.7 convolution_convert_fusion.7
  136.0 7.6 %all-to-all-done.2 = bf16[8,256,256]{2,1,0:T(8,128)(2,1)S(1)} async-done(((bf16[8,256,256]{2,1,0:T(8,128)(2,1)}), bf16[8,256,256]{2,1,0:T(8,128)(2,1)S(1)}, u32[]{:S(2)}, u32[]{:S(2)}) %all-to-all-start.2) | async-done | bytes 1048608 | tf_op jit(solution)/shard_map/all_to_all | solution.py:89
  147.2 11.0 %fusion.53 = bf16[1,2048,256]{1,2,0:T(8,128)(2,1)S(1)} fusion(bf16[2048,2048]{1,0:T(8,128)(2,1)} %param.11, bf16[2048,256]{1,0:T(8,128)(2,1)S(1)} %bitcast.274, f32[]{:T(128)} %bitcast.48, f32[256]{0:T(256)S(1)} %dynamic_slice.114, f32[2048]{0:T(1024)S(1)} %copy-done.11), kind=kOutput, calls=%fused_computation.118 | convolution fusion | flops 4297588736 | bytes 10494980 | tf_op jit(solution)/shard_map/yj,kji->kyi/dot_general | solution.py:99
  162.5 4.0 all-to-all-start.3
  166.5 11.1 %fusion.52 = bf16[1,2048,256]{1,2,0:T(8,128)(2,1)S(1)} fusion(bf16[2048,2048]{1,0:T(8,128)(2,1)} %param.11, bf16[2048,256]{1,0:T(8,128)(2,1)S(1)} %bitcast.277, f32[]{:T(128)} %bitcast.28, f32[256]{0:T(256)S(1)} %dynamic_slice.114, f32[2048]{0:T(1024)S(1)} %copy-done.11), kind=kOutput, calls=%fused_computation.117 | convolution fusion | flops 4297588736 | bytes 10494980 | tf_op jit(solution)/shard_map/yj,kji->kyi/dot_general | solution.py:99
  185.4 5.7 fusion.49
  193.7 7.1 %all-to-all-done.1 = bf16[8,1,256,256]{3,2,1,0:T(8,128)(2,1)S(1)} async-done(((bf16[8,1,256,256]{3,2,1,0:T(8,128)(2,1)}), bf16[8,1,256,256]{3,2,1,0:T(8,128)(2,1)S(1)}, u32[]{:S(2)}, u32[]{:S(2)}) %all-to-all-start.1) | async-done | bytes 1048608 | tf_op jit(solution)/shard_map/all_to_all | solution.py:103
  200.7 5.7 fusion.48
  213.8 3.9 collective-permute-done.7
  217.7 19.7 %collective-permute-done.14 = bf16[1,256,512]{2,1,0:T(8,128)(2,1)S(1)} collective-permute-done((bf16[1,256,512]{2,1,0:T(8,128)(2,1)S(1)}, bf16[1,256,512]{2,1,0:T(8,128)(2,1)S(1)}, u32[]{:S(2)}, u32[]{:S(2)}) %collective-permute-start.14) | collective-permute-done | bytes 262176 | tf_op jit(solution)/shard_map/ppermute | solution.py:73
  237.5 9.8 %collective-permute-done.8 = bf16[1,256,512]{2,1,0:T(8,128)(2,1)S(1)} collective-permute-done((bf16[1,256,512]{2,1,0:T(8,128)(2,1)S(1)}, bf16[1,256,512]{2,1,0:T(8,128)(2,1)S(1)}, u32[]{:S(2)}, u32[]{:S(2)}) %collective-permute-start.8) | collective-permute-done | bytes 262176 | tf_op jit(solution)/shard_map/ppermute | solution.py:73
  250.3 9.0 %collective-permute-done.16 = bf16[8,256,1]{2,1,0:T(8,128)(2,1)S(1)} collective-permute-done((bf16[8,256,1]{2,1,0:T(8,128)(2,1)S(1)}, bf16[8,256,1]{2,1,0:T(8,128)(2,1)S(1)}, u32[]{:S(2)}, u32[]{:S(2)}) %collective-permute-start.16) | collective-permute-done | bytes 4128 | tf_op jit(solution)/shard_map/ppermute | solution.py:16
  259.2 4.1 collective-permute-done.17
  266.7 6.8 %collective-permute-done.19 = bf16[8,1,514]{2,1,0:T(2,128)(2,1)S(1)} collective-permute-done((bf16[8,1,514]{2,1,0:T(2,128)(2,1)S(1)}, bf16[8,1,514]{2,1,0:T(2,128)(2,1)S(1)}, u32[]{:S(2)}, u32[]{:S(2)}) %collective-permute-start.19) | collective-permute-done | bytes 8256 | tf_op jit(solution)/shard_map/ppermute | solution.py:17
  275.8 5.9 %fusion.41 = f32[7,256,512]{2,1,0:T(8,128)} fusion(f32[8,258,514]{2,1,0:T(8,128)S(1)} %maximum_convert_fusion.1, f32[8,258,514]{2,1,0:T(8,128)S(1)} %bitcast.271), kind=kLoop, calls=%fused_computation.74 | loop fusion | flops 3670016 | bytes 18350080 | tf_op jit(solution)/shard_map/mul | solution.py:51
  281.7 13.4 %fusion.3 = (f32[]{:T(128)}, f32[]{:T(128)}, f32[8,256,512]{2,1,0:T(8,128)}) fusion(f32[8,256,512]{2,1,0:T(8,128)} %get-tuple-element.19, bf16[4,256,512]{2,1,0:T(8,128)(2,1)} %copy-done.3, bf16[4,256,512]{2,1,0:T(8,128)(2,1)} %copy-done.4, f32[7,256,512]{2,1,0:T(8,128)} %fusion.41, f32[8,258,514]{2,1,0:T(8,128)S(1)} %maximum_convert_fusion.1, ...), kind=kLoop, calls=%fused_computation.15 | loop fusion | flops 28311552 | bytes 56098824 | tf_op jit(solution)/shard_map/reduce_sum | solution.py:148
  317.6 4.8 fusion.65
  328.5 9.9 %collective-permute-done.31 = bf16[1,256,512]{2,1,0:T(8,128)(2,1)S(1)} collective-permute-done((bf16[1,256,512]{2,1,0:T(8,128)(2,1)S(1)}, bf16[1,256,512]{2,1,0:T(8,128)(2,1)S(1)}, u32[]{:S(2)}, u32[]{:S(2)}) %collective-permute-start.31) | collective-permute-done | bytes 262176 | tf_op jit(solution)/shard_map/ppermute | solution.py:73
  338.4 19.6 %collective-permute-start.25 = (bf16[1,256,512]{2,1,0:T(8,128)(2,1)S(1)}, bf16[1,256,512]{2,1,0:T(8,128)(2,1)S(1)}, u32[]{:S(2)}, u32[]{:S(2)}) collective-permute-start(bf16[1,256,512]{2,1,0:T(8,128)(2,1)S(1)} %get-tuple-element.43), channel_id=1, source_target_pairs={{0,8},{8,16},{16,24},{24,0},{1,9},{9,17},{17,25},{25,1},{2,10},{10... | collective-permute-start | bytes 786440 | tf_op jit(solution)/shard_map/ppermute | solution.py:73
  362.0 7.3 %collective-permute-done.26 = bf16[1,256,512]{2,1,0:T(8,128)(2,1)S(1)} collective-permute-done((bf16[1,256,512]{2,1,0:T(8,128)(2,1)S(1)}, bf16[1,256,512]{2,1,0:T(8,128)(2,1)S(1)}, u32[]{:S(2)}, u32[]{:S(2)}) %collective-permute-start.26) | collective-permute-done | bytes 262176 | tf_op jit(solution)/shard_map/ppermute | solution.py:73
  376.5 5.7 convolution_convert_fusion.1
  383.2 8.6 %all-to-all-done.4 = bf16[8,256,256]{2,1,0:T(8,128)(2,1)S(1)} async-done(((bf16[8,256,256]{2,1,0:T(8,128)(2,1)}), bf16[8,256,256]{2,1,0:T(8,128)(2,1)S(1)}, u32[]{:S(2)}, u32[]{:S(2)}) %all-to-all-start.4) | async-done | bytes 1048608 | tf_op jit(solution)/shard_map/all_to_all | solution.py:89
  395.4 11.1 %fusion.54 = bf16[1,2048,256]{1,2,0:T(8,128)(2,1)S(1)} fusion(bf16[2048,2048]{1,0:T(8,128)(2,1)} %param.11, bf16[2048,256]{1,0:T(8,128)(2,1)S(1)} %bitcast.276, f32[]{:T(128)} %bitcast.28, f32[256]{0:T(256)S(1)} %dynamic_slice.114, f32[2048]{0:T(1024)S(1)} %copy-done.11), kind=kOutput, calls=%fused_computation.119 | convolution fusion | flops 4297588736 | bytes 10494980 | tf_op jit(solution)/shard_map/yj,kji->kyi/dot_general | solution.py:99
  410.7 4.0 all-to-all-start.5
  414.7 11.0 %fusion.55 = bf16[1,2048,256]{1,2,0:T(8,128)(2,1)S(1)} fusion(bf16[2048,2048]{1,0:T(8,128)(2,1)} %param.11, bf16[2048,256]{1,0:T(8,128)(2,1)S(1)} %bitcast.275, f32[]{:T(128)} %bitcast.48, f32[256]{0:T(256)S(1)} %dynamic_slice.114, f32[2048]{0:T(1024)S(1)} %copy-done.11), kind=kOutput, calls=%fused_computation.120 | convolution fusion | flops 4297588736 | bytes 10494980 | tf_op jit(solution)/shard_map/yj,kji->kyi/dot_general | solution.py:99
  433.6 5.7 fusion.50
  439.4 9.5 %all-to-all-done.7 = bf16[8,1,256,256]{3,2,1,0:T(8,128)(2,1)S(1)} async-done(((bf16[8,1,256,256]{3,2,1,0:T(8,128)(2,1)}), bf16[8,1,256,256]{3,2,1,0:T(8,128)(2,1)S(1)}, u32[]{:S(2)}, u32[]{:S(2)}) %all-to-all-start.7) | async-done | bytes 1048608 | tf_op jit(solution)/shard_map/all_to_all | solution.py:103
  448.9 5.7 fusion.51
  460.2 6.4 %collective-permute-done.29 = bf16[1,256,512]{2,1,0:T(8,128)(2,1)S(1)} collective-permute-done((bf16[1,256,512]{2,1,0:T(8,128)(2,1)S(1)}, bf16[1,256,512]{2,1,0:T(8,128)(2,1)S(1)}, u32[]{:S(2)}, u32[]{:S(2)}) %collective-permute-start.29) | collective-permute-done | bytes 262176 | tf_op jit(solution)/shard_map/ppermute | solution.py:73
  468.0 14.0 %collective-permute-done.34 = bf16[1,256,512]{2,1,0:T(8,128)(2,1)S(1)} collective-permute-done((bf16[1,256,512]{2,1,0:T(8,128)(2,1)S(1)}, bf16[1,256,512]{2,1,0:T(8,128)(2,1)S(1)}, u32[]{:S(2)}, u32[]{:S(2)}) %collective-permute-start.34) | collective-permute-done | bytes 262176 | tf_op jit(solution)/shard_map/ppermute | solution.py:73
  482.0 10.3 %collective-permute-done.35 = bf16[1,256,512]{2,1,0:T(8,128)(2,1)S(1)} collective-permute-done((bf16[1,256,512]{2,1,0:T(8,128)(2,1)S(1)}, bf16[1,256,512]{2,1,0:T(8,128)(2,1)S(1)}, u32[]{:S(2)}, u32[]{:S(2)}) %collective-permute-start.35) | collective-permute-done | bytes 262176 | tf_op jit(solution)/shard_map/ppermute | solution.py:73
  495.7 9.0 %collective-permute-done.37 = bf16[8,256,1]{2,1,0:T(8,128)(2,1)S(1)} collective-permute-done((bf16[8,256,1]{2,1,0:T(8,128)(2,1)S(1)}, bf16[8,256,1]{2,1,0:T(8,128)(2,1)S(1)}, u32[]{:S(2)}, u32[]{:S(2)}) %collective-permute-start.37) | collective-permute-done | bytes 4128 | tf_op jit(solution)/shard_map/ppermute | solution.py:16
  504.7 4.9 collective-permute-done.38
  512.9 5.6 collective-permute-done.40
  520.9 5.9 %fusion.40 = f32[7,256,512]{2,1,0:T(8,128)} fusion(f32[8,258,514]{2,1,0:T(8,128)S(1)} %maximum_convert_fusion.2, f32[8,258,514]{2,1,0:T(8,128)S(1)} %bitcast.273), kind=kLoop, calls=%fused_computation.72 | loop fusion | flops 3670016 | bytes 18350080 | tf_op jit(solution)/shard_map/mul | solution.py:51
  526.8 14.2 %fusion = (f32[]{:T(128)}, f32[]{:T(128)}, f32[]{:T(128)}, f32[]{:T(128)}, f32[8,256,512]{2,1,0:T(8,128)}) fusion(f32[8,256,512]{2,1,0:T(8,128)} %get-tuple-element.19, f32[8,256,512]{2,1,0:T(8,128)} %get-tuple-element.17, f32[]{:T(128)S(6)} %div.23, bf16[4,256,512]{2,1,0:T(8,128)(2,1)} %copy-done.6, bf16[4,256,512]{2,1,0:T(8,128)(2,1)} %copy-done.5, ...), kind=kLoop, calls=%fused_computation.12 | loop fusion | flops 36700156 | bytes 62390292 | tf_op jit(solution)/shard_map/reduce_sum | solution.py:155
  570.6 7.2 %fusion.6 = (f32[8,256,512]{2,1,0:T(8,128)}, f32[8,256,512]{2,1,0:T(8,128)}) fusion(f32[8,256,512]{2,1,0:T(8,128)} %param.8, f32[]{:T(128)S(6)} %div.27, f32[]{:T(128)S(6)} %div.23, bf16[4,256,512]{2,1,0:T(8,128)(2,1)} %copy-done.3, bf16[4,256,512]{2,1,0:T(8,128)(2,1)} %copy-done.4, f32[]{:T(128)S(6)} %div.26, bf16[4,256,512]{2,1,0:T(8,128)(2,1)} %copy-done.6, ...), kind=kLoop, calls=%fused_computation.18 | loop fusion | flops 10485760 | bytes 16777228 | tf_op jit(solution)/shard_map/add | solution.py:168
  (210 shorter events, 166.2 us)
Async XLA Ops:
  24.0 6.8 %collective-permute-start = (bf16[2,8,256,1]{2,1,3,0:T(8,128)(2,1)S(1)}, bf16[2,8,256,1]{2,1,3,0:T(8,128)(2,1)S(1)}, u32[]{:S(2)}, u32[]{:S(2)}) collective-permute-start(bf16[2,8,256,1]{2,1,3,0:T(8,128)(2,1)S(1)} %copy.52), channel_id=1, source_target_pairs={{0,8},{8,16},{16,24},{1,9},{9,17},{17,25},{2,10},{10,18},{18,26},{... | collective-permute-start | bytes 24584 | tf_op jit(solution)/shard_map/ppermute | solution.py:16
  29.3 5.7 collective-permute-start.1
  37.5 3.6 collective-permute-start.2
  38.8 4.8 collective-permute-start.3
  79.0 35.6 %collective-permute-start.11 = (bf16[1,256,512]{2,1,0:T(8,128)(2,1)S(1)}, bf16[1,256,512]{2,1,0:T(8,128)(2,1)S(1)}, u32[]{:S(2)}, u32[]{:S(2)}) collective-permute-start(bf16[1,256,512]{2,1,0:T(8,128)(2,1)S(1)} %get-tuple-element.60), channel_id=1, source_target_pairs={{0,16},{8,24},{16,0},{24,8},{1,17},{9,25},{17,1},{25,9},{2,18},{10... | collective-permute-start | bytes 786440 | tf_op jit(solution)/shard_map/ppermute | solution.py:73
  81.7 12.6 %collective-permute-start.10 = (bf16[1,256,512]{2,1,0:T(8,128)(2,1)S(1)}, bf16[1,256,512]{2,1,0:T(8,128)(2,1)S(1)}, u32[]{:S(2)}, u32[]{:S(2)}) collective-permute-start(bf16[1,256,512]{2,1,0:T(8,128)(2,1)S(1)} %get-tuple-element.61), channel_id=1, source_target_pairs={{0,8},{8,16},{16,24},{24,0},{1,9},{9,17},{17,25},{25,1},{2,10},{10... | collective-permute-start | bytes 786440 | tf_op jit(solution)/shard_map/ppermute | solution.py:73
  82.0 32.6 %collective-permute-start.12 = (bf16[1,256,512]{2,1,0:T(8,128)(2,1)S(1)}, bf16[1,256,512]{2,1,0:T(8,128)(2,1)S(1)}, u32[]{:S(2)}, u32[]{:S(2)}) collective-permute-start(bf16[1,256,512]{2,1,0:T(8,128)(2,1)S(1)} %get-tuple-element.59), channel_id=1, source_target_pairs={{0,24},{8,0},{16,8},{24,16},{1,25},{9,1},{17,9},{25,17},{2,26},{10... | collective-permute-start | bytes 786440 | tf_op jit(solution)/shard_map/ppermute | solution.py:73
  85.9 43.3 %collective-permute-start.6 = (bf16[1,256,512]{2,1,0:T(8,128)(2,1)S(1)}, bf16[1,256,512]{2,1,0:T(8,128)(2,1)S(1)}, u32[]{:S(2)}, u32[]{:S(2)}) collective-permute-start(bf16[1,256,512]{2,1,0:T(8,128)(2,1)S(1)} %get-tuple-element.53), channel_id=1, source_target_pairs={{0,24},{8,0},{16,8},{24,16},{1,25},{9,1},{17,9},{25,17},{2,26},{10... | collective-permute-start | bytes 786440 | tf_op jit(solution)/shard_map/ppermute | solution.py:73
  86.0 43.2 %collective-permute-start.5 = (bf16[1,256,512]{2,1,0:T(8,128)(2,1)S(1)}, bf16[1,256,512]{2,1,0:T(8,128)(2,1)S(1)}, u32[]{:S(2)}, u32[]{:S(2)}) collective-permute-start(bf16[1,256,512]{2,1,0:T(8,128)(2,1)S(1)} %get-tuple-element.54), channel_id=1, source_target_pairs={{0,16},{8,24},{16,0},{24,8},{1,17},{9,25},{17,1},{25,9},{2,18},{10... | collective-permute-start | bytes 786440 | tf_op jit(solution)/shard_map/ppermute | solution.py:73
  94.2 34.0 %collective-permute-start.4 = (bf16[1,256,512]{2,1,0:T(8,128)(2,1)S(1)}, bf16[1,256,512]{2,1,0:T(8,128)(2,1)}, u32[]{:S(2)}, u32[]{:S(2)}) collective-permute-start(bf16[1,256,512]{2,1,0:T(8,128)(2,1)S(1)} %get-tuple-element.55), channel_id=1, source_target_pairs={{0,8},{8,16},{16,24},{24,0},{1,9},{9,17},{17,25},{25,1},{2,10},{10... | collective-permute-start | bytes 786440 | tf_op jit(solution)/shard_map/ppermute | solution.py:73
  121.5 22.1 %all-to-all-start.2 = ((bf16[8,256,256]{2,1,0:T(8,128)(2,1)}), bf16[8,256,256]{2,1,0:T(8,128)(2,1)S(1)}, u32[]{:S(2)}, u32[]{:S(2)}) async-start(bf16[8,256,256]{2,1,0:T(8,128)(2,1)} %bitcast.267), calls=%async_computation.2 | async-start | bytes 2097152 | tf_op jit(solution)/shard_map/all_to_all | solution.py:89
  143.6 18.9 %all-to-all-start = ((bf16[8,256,256]{2,1,0:T(8,128)(2,1)}), bf16[8,256,256]{2,1,0:T(8,128)(2,1)S(1)}, u32[]{:S(2)}, u32[]{:S(2)}) async-start(bf16[8,256,256]{2,1,0:T(8,128)(2,1)} %bitcast.269), calls=%async_computation | async-start | bytes 2097152 | tf_op jit(solution)/shard_map/all_to_all | solution.py:89
  162.5 19.3 %all-to-all-start.3 = ((bf16[8,1,256,256]{3,2,1,0:T(8,128)(2,1)}), bf16[8,1,256,256]{3,2,1,0:T(8,128)(2,1)S(1)}, u32[]{:S(2)}, u32[]{:S(2)}) async-start(bf16[8,1,256,256]{3,2,1,0:T(8,128)(2,1)} %bitcast.52), calls=%async_computation.3 | async-start | bytes 2097152 | tf_op jit(solution)/shard_map/all_to_all | solution.py:103
  181.8 18.9 %all-to-all-start.1 = ((bf16[8,1,256,256]{3,2,1,0:T(8,128)(2,1)}), bf16[8,1,256,256]{3,2,1,0:T(8,128)(2,1)S(1)}, u32[]{:S(2)}, u32[]{:S(2)}) async-start(bf16[8,1,256,256]{3,2,1,0:T(8,128)(2,1)} %bitcast.32), calls=%async_computation.1 | async-start | bytes 2097152 | tf_op jit(solution)/shard_map/all_to_all | solution.py:103
  191.2 22.4 %collective-permute-start.13 = (bf16[1,256,512]{2,1,0:T(8,128)(2,1)S(1)}, bf16[1,256,512]{2,1,0:T(8,128)(2,1)S(1)}, u32[]{:S(2)}, u32[]{:S(2)}) collective-permute-start(bf16[1,256,512]{2,1,0:T(8,128)(2,1)S(1)} %get-tuple-element.58), channel_id=1, source_target_pairs={{0,8},{8,16},{16,24},{24,0},{1,9},{9,17},{17,25},{25,1},{2,10},{10... | collective-permute-start | bytes 786440 | tf_op jit(solution)/shard_map/ppermute | solution.py:73
  206.5 11.2 %collective-permute-start.7 = (bf16[1,256,512]{2,1,0:T(8,128)(2,1)S(1)}, bf16[1,256,512]{2,1,0:T(8,128)(2,1)S(1)}, u32[]{:S(2)}, u32[]{:S(2)}) collective-permute-start(bf16[1,256,512]{2,1,0:T(8,128)(2,1)S(1)} %get-tuple-element.52), channel_id=1, source_target_pairs={{0,8},{8,16},{16,24},{24,0},{1,9},{9,17},{17,25},{25,1},{2,10},{10... | collective-permute-start | bytes 786440 | tf_op jit(solution)/shard_map/ppermute | solution.py:73
  209.1 38.2 %collective-permute-start.15 = (bf16[1,256,512]{2,1,0:T(8,128)(2,1)S(1)}, bf16[1,256,512]{2,1,0:T(8,128)(2,1)S(1)}, u32[]{:S(2)}, u32[]{:S(2)}) collective-permute-start(bf16[1,256,512]{2,1,0:T(8,128)(2,1)S(1)} %get-tuple-element.56), channel_id=1, source_target_pairs={{0,24},{8,0},{16,8},{24,16},{1,25},{9,1},{17,9},{25,17},{2,26},{10... | collective-permute-start | bytes 786440 | tf_op jit(solution)/shard_map/ppermute | solution.py:73
  210.6 26.9 %collective-permute-start.14 = (bf16[1,256,512]{2,1,0:T(8,128)(2,1)S(1)}, bf16[1,256,512]{2,1,0:T(8,128)(2,1)S(1)}, u32[]{:S(2)}, u32[]{:S(2)}) collective-permute-start(bf16[1,256,512]{2,1,0:T(8,128)(2,1)S(1)} %get-tuple-element.57), channel_id=1, source_target_pairs={{0,16},{8,24},{16,0},{24,8},{1,17},{9,25},{17,1},{25,9},{2,18},{10... | collective-permute-start | bytes 786440 | tf_op jit(solution)/shard_map/ppermute | solution.py:73
  210.8 36.5 %collective-permute-start.9 = (bf16[1,256,512]{2,1,0:T(8,128)(2,1)S(1)}, bf16[1,256,512]{2,1,0:T(8,128)(2,1)S(1)}, u32[]{:S(2)}, u32[]{:S(2)}) collective-permute-start(bf16[1,256,512]{2,1,0:T(8,128)(2,1)S(1)} %get-tuple-element.50), channel_id=1, source_target_pairs={{0,24},{8,0},{16,8},{24,16},{1,25},{9,1},{17,9},{25,17},{2,26},{10... | collective-permute-start | bytes 786440 | tf_op jit(solution)/shard_map/ppermute | solution.py:73
  213.7 33.6 %collective-permute-start.8 = (bf16[1,256,512]{2,1,0:T(8,128)(2,1)S(1)}, bf16[1,256,512]{2,1,0:T(8,128)(2,1)S(1)}, u32[]{:S(2)}, u32[]{:S(2)}) collective-permute-start(bf16[1,256,512]{2,1,0:T(8,128)(2,1)S(1)} %get-tuple-element.51), channel_id=1, source_target_pairs={{0,16},{8,24},{16,0},{24,8},{1,17},{9,25},{17,1},{25,9},{2,18},{10... | collective-permute-start | bytes 786440 | tf_op jit(solution)/shard_map/ppermute | solution.py:73
  247.6 11.6 %collective-permute-start.16 = (bf16[8,256,1]{2,1,0:T(8,128)(2,1)S(1)}, bf16[8,256,1]{2,1,0:T(8,128)(2,1)S(1)}, u32[]{:S(2)}, u32[]{:S(2)}) collective-permute-start(bf16[8,256,1]{2,1,0:T(8,128)(2,1)S(1)} %get-tuple-element.34), channel_id=1, source_target_pairs={{0,8},{8,16},{16,24},{1,9},{9,17},{17,25},{2,10},{10,18},{18,26},{... | collective-permute-start | bytes 12296 | tf_op jit(solution)/shard_map/ppermute | solution.py:16
  249.0 14.4 %collective-permute-start.17 = (bf16[8,256,1]{2,1,0:T(8,128)(2,1)S(1)}, bf16[8,256,1]{2,1,0:T(8,128)(2,1)S(1)}, u32[]{:S(2)}, u32[]{:S(2)}) collective-permute-start(bf16[8,256,1]{2,1,0:T(8,128)(2,1)S(1)} %get-tuple-element.35), channel_id=1, source_target_pairs={{8,0},{16,8},{24,16},{9,1},{17,9},{25,17},{10,2},{18,10},{26,18},{... | collective-permute-start | bytes 12296 | tf_op jit(solution)/shard_map/ppermute | solution.py:17
  265.1 8.4 %collective-permute-start.19 = (bf16[8,1,514]{2,1,0:T(2,128)(2,1)S(1)}, bf16[8,1,514]{2,1,0:T(2,128)(2,1)S(1)}, u32[]{:S(2)}, u32[]{:S(2)}) collective-permute-start(bf16[8,1,514]{2,1,0:T(2,128)(2,1)S(1)} %get-tuple-element.29), channel_id=1, source_target_pairs={{1,0},{2,1},{3,2},{4,3},{5,4},{6,5},{7,6},{9,8},{10,9},{11,10},{12... | collective-permute-start | bytes 24680 | tf_op jit(solution)/shard_map/ppermute | solution.py:17
  296.4 3.5 collective-permute-start.20
  301.3 4.4 collective-permute-start.21
  308.2 3.9 collective-permute-start.23
  322.7 35.4 %collective-permute-start.32 = (bf16[1,256,512]{2,1,0:T(8,128)(2,1)S(1)}, bf16[1,256,512]{2,1,0:T(8,128)(2,1)S(1)}, u32[]{:S(2)}, u32[]{:S(2)}) collective-permute-start(bf16[1,256,512]{2,1,0:T(8,128)(2,1)S(1)} %get-tuple-element.48), channel_id=1, source_target_pairs={{0,16},{8,24},{16,0},{24,8},{1,17},{9,25},{17,1},{25,9},{2,18},{10... | collective-permute-start | bytes 786440 | tf_op jit(solution)/shard_map/ppermute | solution.py:73
  324.2 14.2 %collective-permute-start.31 = (bf16[1,256,512]{2,1,0:T(8,128)(2,1)S(1)}, bf16[1,256,512]{2,1,0:T(8,128)(2,1)S(1)}, u32[]{:S(2)}, u32[]{:S(2)}) collective-permute-start(bf16[1,256,512]{2,1,0:T(8,128)(2,1)S(1)} %get-tuple-element.49), channel_id=1, source_target_pairs={{0,8},{8,16},{16,24},{24,0},{1,9},{9,17},{17,25},{25,1},{2,10},{10... | collective-permute-start | bytes 786440 | tf_op jit(solution)/shard_map/ppermute | solution.py:73
  324.6 44.7 %collective-permute-start.33 = (bf16[1,256,512]{2,1,0:T(8,128)(2,1)S(1)}, bf16[1,256,512]{2,1,0:T(8,128)(2,1)S(1)}, u32[]{:S(2)}, u32[]{:S(2)}) collective-permute-start(bf16[1,256,512]{2,1,0:T(8,128)(2,1)S(1)} %get-tuple-element.47), channel_id=1, source_target_pairs={{0,24},{8,0},{16,8},{24,16},{1,25},{9,1},{17,9},{25,17},{2,26},{10... | collective-permute-start | bytes 786440 | tf_op jit(solution)/shard_map/ppermute | solution.py:73
  328.5 40.9 %collective-permute-start.27 = (bf16[1,256,512]{2,1,0:T(8,128)(2,1)S(1)}, bf16[1,256,512]{2,1,0:T(8,128)(2,1)S(1)}, u32[]{:S(2)}, u32[]{:S(2)}) collective-permute-start(bf16[1,256,512]{2,1,0:T(8,128)(2,1)S(1)} %get-tuple-element.41), channel_id=1, source_target_pairs={{0,24},{8,0},{16,8},{24,16},{1,25},{9,1},{17,9},{25,17},{2,26},{10... | collective-permute-start | bytes 786440 | tf_op jit(solution)/shard_map/ppermute | solution.py:73
  328.5 40.7 %collective-permute-start.26 = (bf16[1,256,512]{2,1,0:T(8,128)(2,1)S(1)}, bf16[1,256,512]{2,1,0:T(8,128)(2,1)S(1)}, u32[]{:S(2)}, u32[]{:S(2)}) collective-permute-start(bf16[1,256,512]{2,1,0:T(8,128)(2,1)S(1)} %get-tuple-element.42), channel_id=1, source_target_pairs={{0,16},{8,24},{16,0},{24,8},{1,17},{9,25},{17,1},{25,9},{2,18},{10... | collective-permute-start | bytes 786440 | tf_op jit(solution)/shard_map/ppermute | solution.py:73
  338.4 23.5 %collective-permute-start.25 = (bf16[1,256,512]{2,1,0:T(8,128)(2,1)S(1)}, bf16[1,256,512]{2,1,0:T(8,128)(2,1)S(1)}, u32[]{:S(2)}, u32[]{:S(2)}) collective-permute-start(bf16[1,256,512]{2,1,0:T(8,128)(2,1)S(1)} %get-tuple-element.43), channel_id=1, source_target_pairs={{0,8},{8,16},{16,24},{24,0},{1,9},{9,17},{17,25},{25,1},{2,10},{10... | collective-permute-start | bytes 786440 | tf_op jit(solution)/shard_map/ppermute | solution.py:73
  372.9 18.9 %all-to-all-start.4 = ((bf16[8,256,256]{2,1,0:T(8,128)(2,1)}), bf16[8,256,256]{2,1,0:T(8,128)(2,1)S(1)}, u32[]{:S(2)}, u32[]{:S(2)}) async-start(bf16[8,256,256]{2,1,0:T(8,128)(2,1)} %bitcast.265), calls=%async_computation.4 | async-start | bytes 2097152 | tf_op jit(solution)/shard_map/all_to_all | solution.py:89
  391.8 18.9 %all-to-all-start.6 = ((bf16[8,256,256]{2,1,0:T(8,128)(2,1)}), bf16[8,256,256]{2,1,0:T(8,128)(2,1)S(1)}, u32[]{:S(2)}, u32[]{:S(2)}) async-start(bf16[8,256,256]{2,1,0:T(8,128)(2,1)} %bitcast.263), calls=%async_computation.6 | async-start | bytes 2097152 | tf_op jit(solution)/shard_map/all_to_all | solution.py:89
  410.7 19.3 %all-to-all-start.5 = ((bf16[8,1,256,256]{3,2,1,0:T(8,128)(2,1)}), bf16[8,1,256,256]{3,2,1,0:T(8,128)(2,1)S(1)}, u32[]{:S(2)}, u32[]{:S(2)}) async-start(bf16[8,1,256,256]{3,2,1,0:T(8,128)(2,1)} %bitcast.74), calls=%async_computation.5 | async-start | bytes 2097152 | tf_op jit(solution)/shard_map/all_to_all | solution.py:103
  430.0 18.9 %all-to-all-start.7 = ((bf16[8,1,256,256]{3,2,1,0:T(8,128)(2,1)}), bf16[8,1,256,256]{3,2,1,0:T(8,128)(2,1)S(1)}, u32[]{:S(2)}, u32[]{:S(2)}) async-start(bf16[8,1,256,256]{3,2,1,0:T(8,128)(2,1)} %bitcast.92), calls=%async_computation.7 | async-start | bytes 2097152 | tf_op jit(solution)/shard_map/all_to_all | solution.py:103
  439.4 20.1 %collective-permute-start.28 = (bf16[1,256,512]{2,1,0:T(8,128)(2,1)S(1)}, bf16[1,256,512]{2,1,0:T(8,128)(2,1)S(1)}, u32[]{:S(2)}, u32[]{:S(2)}) collective-permute-start(bf16[1,256,512]{2,1,0:T(8,128)(2,1)S(1)} %get-tuple-element.40), channel_id=1, source_target_pairs={{0,8},{8,16},{16,24},{24,0},{1,9},{9,17},{17,25},{25,1},{2,10},{10... | collective-permute-start | bytes 786440 | tf_op jit(solution)/shard_map/ppermute | solution.py:73
  454.7 11.9 %collective-permute-start.29 = (bf16[1,256,512]{2,1,0:T(8,128)(2,1)S(1)}, bf16[1,256,512]{2,1,0:T(8,128)(2,1)S(1)}, u32[]{:S(2)}, u32[]{:S(2)}) collective-permute-start(bf16[1,256,512]{2,1,0:T(8,128)(2,1)S(1)} %get-tuple-element.39), channel_id=1, source_target_pairs={{0,16},{8,24},{16,0},{24,8},{1,17},{9,25},{17,1},{25,9},{2,18},{10... | collective-permute-start | bytes 786440 | tf_op jit(solution)/shard_map/ppermute | solution.py:73
  455.1 12.9 %collective-permute-start.30 = (bf16[1,256,512]{2,1,0:T(8,128)(2,1)S(1)}, bf16[1,256,512]{2,1,0:T(8,128)(2,1)S(1)}, u32[]{:S(2)}, u32[]{:S(2)}) collective-permute-start(bf16[1,256,512]{2,1,0:T(8,128)(2,1)S(1)} %get-tuple-element.38), channel_id=1, source_target_pairs={{0,24},{8,0},{16,8},{24,16},{1,25},{9,1},{17,9},{25,17},{2,26},{10... | collective-permute-start | bytes 786440 | tf_op jit(solution)/shard_map/ppermute | solution.py:73
  455.7 36.6 %collective-permute-start.36 = (bf16[1,256,512]{2,1,0:T(8,128)(2,1)S(1)}, bf16[1,256,512]{2,1,0:T(8,128)(2,1)S(1)}, u32[]{:S(2)}, u32[]{:S(2)}) collective-permute-start(bf16[1,256,512]{2,1,0:T(8,128)(2,1)S(1)} %get-tuple-element.44), channel_id=1, source_target_pairs={{0,24},{8,0},{16,8},{24,16},{1,25},{9,1},{17,9},{25,17},{2,26},{10... | collective-permute-start | bytes 786440 | tf_op jit(solution)/shard_map/ppermute | solution.py:73
  459.5 32.8 %collective-permute-start.35 = (bf16[1,256,512]{2,1,0:T(8,128)(2,1)S(1)}, bf16[1,256,512]{2,1,0:T(8,128)(2,1)S(1)}, u32[]{:S(2)}, u32[]{:S(2)}) collective-permute-start(bf16[1,256,512]{2,1,0:T(8,128)(2,1)S(1)} %get-tuple-element.45), channel_id=1, source_target_pairs={{0,16},{8,24},{16,0},{24,8},{1,17},{9,25},{17,1},{25,9},{2,18},{10... | collective-permute-start | bytes 786440 | tf_op jit(solution)/shard_map/ppermute | solution.py:73
  459.5 22.5 %collective-permute-start.34 = (bf16[1,256,512]{2,1,0:T(8,128)(2,1)S(1)}, bf16[1,256,512]{2,1,0:T(8,128)(2,1)S(1)}, u32[]{:S(2)}, u32[]{:S(2)}) collective-permute-start(bf16[1,256,512]{2,1,0:T(8,128)(2,1)S(1)} %get-tuple-element.46), channel_id=1, source_target_pairs={{0,8},{8,16},{16,24},{24,0},{1,9},{9,17},{17,25},{25,1},{2,10},{10... | collective-permute-start | bytes 786440 | tf_op jit(solution)/shard_map/ppermute | solution.py:73
  492.6 12.1 %collective-permute-start.37 = (bf16[8,256,1]{2,1,0:T(8,128)(2,1)S(1)}, bf16[8,256,1]{2,1,0:T(8,128)(2,1)S(1)}, u32[]{:S(2)}, u32[]{:S(2)}) collective-permute-start(bf16[8,256,1]{2,1,0:T(8,128)(2,1)S(1)} %get-tuple-element.30), channel_id=1, source_target_pairs={{0,8},{8,16},{16,24},{1,9},{9,17},{17,25},{2,10},{10,18},{18,26},{... | collective-permute-start | bytes 12296 | tf_op jit(solution)/shard_map/ppermute | solution.py:16
  494.4 15.2 %collective-permute-start.38 = (bf16[8,256,1]{2,1,0:T(8,128)(2,1)S(1)}, bf16[8,256,1]{2,1,0:T(8,128)(2,1)S(1)}, u32[]{:S(2)}, u32[]{:S(2)}) collective-permute-start(bf16[8,256,1]{2,1,0:T(8,128)(2,1)S(1)} %get-tuple-element.31), channel_id=1, source_target_pairs={{8,0},{16,8},{24,16},{9,1},{17,9},{25,17},{10,2},{18,10},{26,18},{... | collective-permute-start | bytes 12296 | tf_op jit(solution)/shard_map/ppermute | solution.py:17
  511.3 7.2 %collective-permute-start.40 = (bf16[8,1,514]{2,1,0:T(2,128)(2,1)S(1)}, bf16[8,1,514]{2,1,0:T(2,128)(2,1)S(1)}, u32[]{:S(2)}, u32[]{:S(2)}) collective-permute-start(bf16[8,1,514]{2,1,0:T(2,128)(2,1)S(1)} %get-tuple-element.27), channel_id=1, source_target_pairs={{1,0},{2,1},{3,2},{4,3},{5,4},{6,5},{7,6},{9,8},{10,9},{11,10},{12... | collective-permute-start | bytes 24680 | tf_op jit(solution)/shard_map/ppermute | solution.py:17
  543.6 3.5 collective-permute-start.41
  549.7 4.4 collective-permute-start.42
  557.9 3.9 collective-permute-start.44
  (24 other events, 347.2 us)

commit v4 on v3

--- a/solution.py
+++ b/solution.py
@@ -77,9 +77,12 @@
     return result
 
 
-def precondition_levels(residual, first_level, eigenvectors, eigenvalues, level_shift):
+def to_lines(residual):
+    return exchange(residual.astype(jnp.bfloat16), "px", 0, 2)
+
+
+def transform_lines(lines, first_level, eigenvectors, eigenvalues, level_shift):
     across = lax.axis_size("py")
-    lines = exchange(residual.astype(jnp.bfloat16), "px", 0, 2)
     levels_here, rows, width = lines.shape
     cols = width // across
     first = jnp.dot(
@@ -107,7 +110,7 @@
         eigenvectors.reshape(across, cols, width),
         preferred_element_type=jnp.float32,
     )
-    return exchange(pencil.astype(jnp.bfloat16), "px", 2, 0).astype(jnp.float32)
+    return pencil.astype(jnp.bfloat16)
 
 
 def precondition(residual, eigenvectors, eigenvalues, level_shift):
@@ -115,13 +118,15 @@
     chunk = lax.axis_size("px")
     if levels % chunk or levels == chunk:
         chunk = levels
-    parts = [
-        precondition_levels(
-            residual[start : start + chunk], start, eigenvectors, eigenvalues, level_shift
-        )
-        for start in range(0, levels, chunk)
-    ]
-    return jnp.concatenate(parts, 0)
+    starts = list(range(0, levels, chunk))
+    lines = [to_lines(residual[start : start + chunk]) for start in starts]
+    parts = []
+    for index, start in enumerate(starts):
+        pencil = transform_lines(lines[index], start, eigenvectors, eigenvalues, level_shift)
+        if index + 1 < len(starts):
+            pencil, lines[index + 1] = lax.optimization_barrier((pencil, lines[index + 1]))
+        parts.append(exchange(pencil, "px", 2, 0))
+    return jnp.concatenate(parts, 0).astype(jnp.float32)
 
 
 def operator(field, coeff_pad):

time: 589 us -> 643 us (1.092)
  blocking collectives: 0 us -> 57.4 us
  starting transfers between devices: 132 us -> 103 us
  waiting for transfers between devices: 207 us -> 219 us
  other arithmetic: 122 us -> 129 us
    all_to_all x0 -> x3, blocking collectives: none -> 57.4 us  [transform_lines(): incoming = lax.all_to_all(outgoing, 'py', 0, 0, tiled=True)]
    ppermute x24, waiting for transfers between devices: 94.8 us -> 141 us  [exchange(): lax.ppermute(part, axis, [(i, (i + shift) % size) for i in range(size)])]
    all_to_all x8 -> x5, waiting for transfers between devices: 44.6 us -> 17.4 us  [the longest x1 14.7 us: transform_lines(): incoming = lax.all_to_all(outgoing, 'py', 0, 0, tiled=True)]
    ppermute x24, starting transfers between devices: 66.7 us -> 45 us  [exchange(): lax.ppermute(part, axis, [(i, (i + shift) % size) for i in range(size)])]
    all_to_all x8 -> x5, starting transfers between devices: 32.4 us -> 18.9 us  [the longest x4 14.2 us: transform_lines(): returned = lax.all_to_all(outgoing, 'py', 0, 0, tiled=True)]
    convert_element_type x2, other arithmetic: 4.68 us -> 11.4 us  [operator(): padded_2(for_sending(field), (('px', 2), ('py', 1)), 1).astype(field.dtype)]
  transfers between devices with their start and end apart: 54 -> 51, of which waited for: 37 -> 37; matrix products, arithmetic and copies ran while one was open for 17% -> 4% of each run, Pallas kernels for 0% -> 0%
where the time goes in v4:
time: 643 us; the launch traced here: 638 us
  waiting for transfers between devices  219 us (34%)
  other arithmetic  129 us (20%)
  starting transfers between devices  103 us (16%)
  matrix products  87.2 us (14%)
  blocking collectives  57.4 us (9%)
  local copies, waits for them, and re-layouts  34.9 us (5%)
  between operations  7.46 us (1%)
    ppermute x24, waiting for transfers between devices, exchange(): lax.ppermute(part, axis, [(i, (i + shift) % size) for i in range(size)])  141 us
    all_to_all x3, blocking collectives, transform_lines(): incoming = lax.all_to_all(outgoing, 'py', 0, 0, tiled=True)  57.4 us
    ppermute x24, starting transfers between devices, exchange(): lax.ppermute(part, axis, [(i, (i + shift) % size) for i in range(size)])  45 us
    dot_general x4, matrix products, transform_lines(): jnp.einsum('yj,kji->kyi', eigenvectors, scaled, preferred_element_type=jn...  44.1 us
    reduce_sum x2, other arithmetic, shards(): jnp.sum(residual * precond)  27.6 us
    dot_general x4, matrix products, transform_lines(): jnp.einsum('qkyi,qix->kyx', returned, eigenvectors.reshape(across, cols,...  22.8 us
    ppermute x6, waiting for transfers between devices, padded_2(): after = lax.ppermute(initial, axis, down)  22.2 us
    ppermute x10, waiting for transfers between devices, all_sum(): values = values + lax.ppermute(values, axis, pairs)  20.5 us
  transfers between devices with their start and end apart: 51, of which 37 were waited for; matrix products, arithmetic and copies ran while one was open for 4% of the time, Pallas kernels for 0%

profile of v4, /device:TPU:0, one launch (start us, length us, event | category | flops | bytes accessed | tf_op | source)
XLA Modules:
  0.0 638.3 jit_solution(12984670231692842378)
XLA Ops:
  5.1 14.3 %fusion.66 = bf16[1,8,256,512]{3,2,1,0:T(8,128)(2,1)S(1)} fusion(bf16[]{:T(256)} %bitcast.16, s32[8,256,512]{2,1,0:T(8,128)S(1)} %copy-done.9, bf16[]{:T(256)} %bitcast.15, bf16[]{:T(256)} %bitcast.14, bf16[]{:T(256)} %bitcast.13, bf16[]{:T(256)} %bitcast.12, bf16[]{:T(256)} %bitcast.11, bf16[]{:T(256)} %bitcast.10, bf16[]{:T(256)} %bitcast.9, bf16[]{:T(256)} %bitcast.8, ...), kind=kLoop, calls=%fused_computation.132 | loop fusion | flops 33554432 | bytes 6291488 | tf_op jit(solution)/shard_map/stack | solution.py:142
  23.8 4.9 collective-permute-start
  43.3 11.7 %maximum_convert_fusion = f32[2,8,258,514]{3,2,1,0:T(8,128)} fusion(bf16[2,8,1,514]{3,2,1,0:T(2,128)(2,1)S(1)} %collective-permute-done.3, bf16[2,8,256,1]{3,2,1,0:T(8,128)(2,1)} %copy.63, bf16[1,8,256,512]{3,2,1,0:T(8,128)(2,1)} %copy-done.7, bf16[1,8,256,512]{3,2,1,0:T(8,128)(2,1)S(1)} %convert_bitcast_fusion, bf16[2,8,256,1]{3,2,1,0:T(8,128)(2,1)S(1)} %copy.62, ...), kind=kLoop, calls=%fused_computation.11 | loop fusion | flops 25461504 | bytes 12730752 | tf_op jit(solution)/shard_map/convert_element_type | solution.py:143
  55.1 4.8 slice_bitcast_fusion.1
  59.9 5.9 fusion.42
  65.8 12.5 %fusion.80 = (bf16[8,256,512]{2,1,0:T(8,128)(2,1)S(1)}, f32[8,256,512]{2,1,0:T(8,128)}) fusion(f32[8,256,512]{2,1,0:T(8,128)} %param.7, f32[7,256,512]{2,1,0:T(8,128)} %fusion.42, f32[8,258,514]{2,1,0:T(8,128)S(1)} %get-tuple-element.29, f32[8,258,514]{2,1,0:T(8,128)S(1)} %get-tuple-element.28), kind=kLoop, calls=%fused_computation.220 | loop fusion | flops 24117248 | bytes 56098816 | tf_op jit(solution)/shard_map/convert.3
  88.1 18.3 %collective-permute-done.5 = bf16[1,256,512]{2,1,0:T(8,128)(2,1)S(1)} collective-permute-done((bf16[1,256,512]{2,1,0:T(8,128)(2,1)S(1)}, bf16[1,256,512]{2,1,0:T(8,128)(2,1)S(1)}, u32[]{:S(2)}, u32[]{:S(2)}) %collective-permute-start.5) | collective-permute-done | bytes 262176 | tf_op jit(solution)/shard_map/ppermute | solution.py:73
  106.5 5.7 convolution_convert_fusion.7
  118.7 14.7 %all-to-all-done = bf16[8,256,256]{2,1,0:T(8,128)(2,1)S(1)} async-done(((bf16[8,256,256]{2,1,0:T(8,128)(2,1)}), bf16[8,256,256]{2,1,0:T(8,128)(2,1)S(1)}, u32[]{:S(2)}, u32[]{:S(2)}) %all-to-all-start) | async-done | bytes 1048608 | tf_op jit(solution)/shard_map/all_to_all | solution.py:92
  133.4 11.0 %fusion.52 = bf16[1,2048,256]{1,2,0:T(8,128)(2,1)S(1)} fusion(bf16[2048,2048]{1,0:T(8,128)(2,1)} %param.11, bf16[2048,256]{1,0:T(8,128)(2,1)S(1)} %bitcast.257, f32[]{:T(128)} %bitcast.28, f32[256]{0:T(256)S(1)} %dynamic_slice.114, f32[2048]{0:T(1024)S(1)} %copy-done.11), kind=kOutput, calls=%fused_computation.117 | convolution fusion | flops 4297588736 | bytes 10494980 | tf_op jit(solution)/shard_map/yj,kji->kyi/dot_general | solution.py:102
  155.0 7.2 %collective-permute-done.7 = bf16[1,256,512]{2,1,0:T(8,128)(2,1)S(1)} collective-permute-done((bf16[1,256,512]{2,1,0:T(8,128)(2,1)S(1)}, bf16[1,256,512]{2,1,0:T(8,128)(2,1)S(1)}, u32[]{:S(2)}, u32[]{:S(2)}) %collective-permute-start.7) | collective-permute-done | bytes 262176 | tf_op jit(solution)/shard_map/ppermute | solution.py:73
  162.9 9.5 %collective-permute-done.8 = bf16[1,256,512]{2,1,0:T(8,128)(2,1)S(1)} collective-permute-done((bf16[1,256,512]{2,1,0:T(8,128)(2,1)S(1)}, bf16[1,256,512]{2,1,0:T(8,128)(2,1)S(1)}, u32[]{:S(2)}, u32[]{:S(2)}) %collective-permute-start.8) | collective-permute-done | bytes 262176 | tf_op jit(solution)/shard_map/ppermute | solution.py:73
  173.9 5.7 fusion.57
  179.6 6.0 convolution_convert_fusion.5
  185.8 19.7 %all_to_all.40 = bf16[8,256,256]{2,1,0:T(8,128)(2,1)S(1)} all-to-all(bf16[8,256,256]{2,1,0:T(8,128)(2,1)S(1)} %bitcast.254), channel_id=1, replica_groups=mesh['px'=4,'py'=8] {'py'}, dimensions={0} | all-to-all | bytes 2097152 | tf_op jit(solution)/shard_map/all_to_all | solution.py:92
  205.5 11.0 %fusion.53 = bf16[1,2048,256]{1,2,0:T(8,128)(2,1)S(1)} fusion(bf16[2048,2048]{1,0:T(8,128)(2,1)} %param.11, bf16[2048,256]{1,0:T(8,128)(2,1)S(1)} %bitcast.259, f32[]{:T(128)} %bitcast.42, f32[256]{0:T(256)S(1)} %dynamic_slice.114, f32[2048]{0:T(1024)S(1)} %copy-done.11), kind=kOutput, calls=%fused_computation.118 | convolution fusion | flops 4297588736 | bytes 10494980 | tf_op jit(solution)/shard_map/yj,kji->kyi/dot_general | solution.py:102
  228.6 5.6 collective-permute-done.10
  236.8 5.7 fusion.49
  242.6 4.7 collective-permute-start.13
  247.3 14.6 %collective-permute-done.11 = bf16[1,256,512]{2,1,0:T(8,128)(2,1)S(1)} collective-permute-done((bf16[1,256,512]{2,1,0:T(8,128)(2,1)}, bf16[1,256,512]{2,1,0:T(8,128)(2,1)S(1)}, u32[]{:S(2)}, u32[]{:S(2)}) %collective-permute-start.11) | collective-permute-done | bytes 262176 | tf_op jit(solution)/shard_map/ppermute | solution.py:73
  262.3 9.8 %collective-permute-done.14 = bf16[1,256,512]{2,1,0:T(8,128)(2,1)S(1)} collective-permute-done((bf16[1,256,512]{2,1,0:T(8,128)(2,1)S(1)}, bf16[1,256,512]{2,1,0:T(8,128)(2,1)S(1)}, u32[]{:S(2)}, u32[]{:S(2)}) %collective-permute-start.14) | collective-permute-done | bytes 262176 | tf_op jit(solution)/shard_map/ppermute | solution.py:73
  280.9 9.2 %collective-permute-done.16 = bf16[8,256,1]{2,1,0:T(8,128)(2,1)S(1)} collective-permute-done((bf16[8,256,1]{2,1,0:T(8,128)(2,1)S(1)}, bf16[8,256,1]{2,1,0:T(8,128)(2,1)S(1)}, u32[]{:S(2)}, u32[]{:S(2)}) %collective-permute-start.16) | collective-permute-done | bytes 4128 | tf_op jit(solution)/shard_map/ppermute | solution.py:16
  301.1 5.7 maximum_convert_fusion.1
  306.8 5.9 fusion.41
  312.7 13.4 %fusion.3 = (f32[]{:T(128)}, f32[]{:T(128)}, f32[8,256,512]{2,1,0:T(8,128)}) fusion(f32[8,256,512]{2,1,0:T(8,128)} %get-tuple-element.27, bf16[4,256,512]{2,1,0:T(8,128)(2,1)} %copy-done.4, bf16[4,256,512]{2,1,0:T(8,128)(2,1)} %copy-done.3, f32[7,256,512]{2,1,0:T(8,128)} %fusion.41, f32[8,258,514]{2,1,0:T(8,128)S(1)} %maximum_convert_fusion.1, ...), kind=kLoop, calls=%fused_computation.15 | loop fusion | flops 28311552 | bytes 56098824 | tf_op jit(solution)/shard_map/reduce_sum | solution.py:153
  349.7 4.8 fusion.67
  359.7 6.4 collective-permute-done.25
  366.1 8.5 %collective-permute-done.26 = bf16[1,256,512]{2,1,0:T(8,128)(2,1)S(1)} collective-permute-done((bf16[1,256,512]{2,1,0:T(8,128)(2,1)S(1)}, bf16[1,256,512]{2,1,0:T(8,128)(2,1)S(1)}, u32[]{:S(2)}, u32[]{:S(2)}) %collective-permute-start.26) | collective-permute-done | bytes 262176 | tf_op jit(solution)/shard_map/ppermute | solution.py:73
  377.2 18.2 %all_to_all.41 = bf16[8,256,256]{2,1,0:T(8,128)(2,1)S(1)} all-to-all(bf16[8,256,256]{2,1,0:T(8,128)(2,1)S(1)} %bitcast.255), channel_id=1, replica_groups=mesh['px'=4,'py'=8] {'py'}, dimensions={0} | all-to-all | bytes 2097152 | tf_op jit(solution)/shard_map/all_to_all | solution.py:92
  395.4 11.0 %fusion.54 = bf16[1,2048,256]{1,2,0:T(8,128)(2,1)S(1)} fusion(bf16[2048,2048]{1,0:T(8,128)(2,1)} %param.11, bf16[2048,256]{1,0:T(8,128)(2,1)S(1)} %bitcast.260, f32[]{:T(128)} %bitcast.28, f32[256]{0:T(256)S(1)} %dynamic_slice.114, f32[2048]{0:T(1024)S(1)} %copy-done.11), kind=kOutput, calls=%fused_computation.119 | convolution fusion | flops 4297588736 | bytes 10494980 | tf_op jit(solution)/shard_map/yj,kji->kyi/dot_general | solution.py:102
  413.1 5.2 collective-permute-start.28
  420.7 5.7 collective-permute-done.28
  427.1 10.2 %collective-permute-done.29 = bf16[1,256,512]{2,1,0:T(8,128)(2,1)S(1)} collective-permute-done((bf16[1,256,512]{2,1,0:T(8,128)(2,1)S(1)}, bf16[1,256,512]{2,1,0:T(8,128)(2,1)S(1)}, u32[]{:S(2)}, u32[]{:S(2)}) %collective-permute-start.29) | collective-permute-done | bytes 262176 | tf_op jit(solution)/shard_map/ppermute | solution.py:73
  438.8 5.7 fusion.56
  444.5 6.0 convolution_convert_fusion.1
  450.6 19.5 %all_to_all.42 = bf16[8,256,256]{2,1,0:T(8,128)(2,1)S(1)} all-to-all(bf16[8,256,256]{2,1,0:T(8,128)(2,1)S(1)} %bitcast.256), channel_id=1, replica_groups=mesh['px'=4,'py'=8] {'py'}, dimensions={0} | all-to-all | bytes 2097152 | tf_op jit(solution)/shard_map/all_to_all | solution.py:92
  470.1 11.0 %fusion.55 = bf16[1,2048,256]{1,2,0:T(8,128)(2,1)S(1)} fusion(bf16[2048,2048]{1,0:T(8,128)(2,1)} %param.11, bf16[2048,256]{1,0:T(8,128)(2,1)S(1)} %bitcast.258, f32[]{:T(128)} %bitcast.42, f32[256]{0:T(256)S(1)} %dynamic_slice.114, f32[2048]{0:T(1024)S(1)} %copy-done.11), kind=kOutput, calls=%fused_computation.120 | convolution fusion | flops 4297588736 | bytes 10494980 | tf_op jit(solution)/shard_map/yj,kji->kyi/dot_general | solution.py:102
  486.9 5.4 collective-permute-start.31
  494.5 6.6 %collective-permute-done.31 = bf16[1,256,512]{2,1,0:T(8,128)(2,1)S(1)} collective-permute-done((bf16[1,256,512]{2,1,0:T(8,128)(2,1)S(1)}, bf16[1,256,512]{2,1,0:T(8,128)(2,1)S(1)}, u32[]{:S(2)}, u32[]{:S(2)}) %collective-permute-start.31) | collective-permute-done | bytes 262176 | tf_op jit(solution)/shard_map/ppermute | solution.py:73
  501.3 5.7 fusion.51
  507.1 5.4 collective-permute-start.34
  512.6 16.4 %collective-permute-done.32 = bf16[1,256,512]{2,1,0:T(8,128)(2,1)S(1)} collective-permute-done((bf16[1,256,512]{2,1,0:T(8,128)(2,1)}, bf16[1,256,512]{2,1,0:T(8,128)(2,1)S(1)}, u32[]{:S(2)}, u32[]{:S(2)}) %collective-permute-start.32) | collective-permute-done | bytes 262176 | tf_op jit(solution)/shard_map/ppermute | solution.py:73
  529.3 9.8 %collective-permute-done.35 = bf16[1,256,512]{2,1,0:T(8,128)(2,1)S(1)} collective-permute-done((bf16[1,256,512]{2,1,0:T(8,128)(2,1)S(1)}, bf16[1,256,512]{2,1,0:T(8,128)(2,1)S(1)}, u32[]{:S(2)}, u32[]{:S(2)}) %collective-permute-start.35) | collective-permute-done | bytes 262176 | tf_op jit(solution)/shard_map/ppermute | solution.py:73
  547.9 9.2 %collective-permute-done.37 = bf16[8,256,1]{2,1,0:T(8,128)(2,1)S(1)} collective-permute-done((bf16[8,256,1]{2,1,0:T(8,128)(2,1)S(1)}, bf16[8,256,1]{2,1,0:T(8,128)(2,1)S(1)}, u32[]{:S(2)}, u32[]{:S(2)}) %collective-permute-start.37) | collective-permute-done | bytes 4128 | tf_op jit(solution)/shard_map/ppermute | solution.py:16
  568.1 5.7 maximum_convert_fusion.2
  573.8 5.9 fusion.40
  579.7 14.2 %fusion = (f32[]{:T(128)}, f32[]{:T(128)}, f32[]{:T(128)}, f32[]{:T(128)}, f32[8,256,512]{2,1,0:T(8,128)}) fusion(f32[8,256,512]{2,1,0:T(8,128)} %get-tuple-element.27, f32[8,256,512]{2,1,0:T(8,128)} %get-tuple-element.25, f32[]{:T(128)S(6)} %div.23, bf16[4,256,512]{2,1,0:T(8,128)(2,1)} %copy-done.6, bf16[4,256,512]{2,1,0:T(8,128)(2,1)} %copy-done.5, ...), kind=kLoop, calls=%fused_computation.12 | loop fusion | flops 36700156 | bytes 62390292 | tf_op jit(solution)/shard_map/reduce_sum | solution.py:160
  624.5 7.2 %fusion.6 = (f32[8,256,512]{2,1,0:T(8,128)}, f32[8,256,512]{2,1,0:T(8,128)}) fusion(f32[8,256,512]{2,1,0:T(8,128)} %param.8, f32[]{:T(128)S(6)} %div.27, f32[]{:T(128)S(6)} %div.23, bf16[4,256,512]{2,1,0:T(8,128)(2,1)} %copy-done.4, bf16[4,256,512]{2,1,0:T(8,128)(2,1)} %copy-done.3, f32[]{:T(128)S(6)} %div.26, bf16[4,256,512]{2,1,0:T(8,128)(2,1)} %copy-done.6, ...), kind=kLoop, calls=%fused_computation.18 | loop fusion | flops 10485760 | bytes 16777228 | tf_op jit(solution)/shard_map/add | solution.py:173
  (204 shorter events, 189.1 us)
Async XLA Ops:
  23.8 6.6 %collective-permute-start = (bf16[2,8,256,1]{2,1,3,0:T(8,128)(2,1)S(1)}, bf16[2,8,256,1]{2,1,3,0:T(8,128)(2,1)S(1)}, u32[]{:S(2)}, u32[]{:S(2)}) collective-permute-start(bf16[2,8,256,1]{2,1,3,0:T(8,128)(2,1)S(1)} %copy.60), channel_id=1, source_target_pairs={{0,8},{8,16},{16,24},{1,9},{9,17},{17,25},{2,10},{10,18},{18,26},{... | collective-permute-start | bytes 24584 | tf_op jit(solution)/shard_map/ppermute | solution.py:16
  29.1 5.5 collective-permute-start.1
  38.5 4.8 collective-permute-start.3
  78.7 9.4 %collective-permute-start.4 = (bf16[1,256,512]{2,1,0:T(8,128)(2,1)S(1)}, bf16[1,256,512]{2,1,0:T(8,128)(2,1)S(1)}, u32[]{:S(2)}, u32[]{:S(2)}) collective-permute-start(bf16[1,256,512]{2,1,0:T(8,128)(2,1)S(1)} %get-tuple-element.73), channel_id=1, source_target_pairs={{0,8},{8,16},{16,24},{24,0},{1,9},{9,17},{17,25},{25,1},{2,10},{10... | collective-permute-start | bytes 786440 | tf_op jit(solution)/shard_map/ppermute | solution.py:73
  80.3 26.2 %collective-permute-start.6 = (bf16[1,256,512]{2,1,0:T(8,128)(2,1)S(1)}, bf16[1,256,512]{2,1,0:T(8,128)(2,1)S(1)}, u32[]{:S(2)}, u32[]{:S(2)}) collective-permute-start(bf16[1,256,512]{2,1,0:T(8,128)(2,1)S(1)} %get-tuple-element.71), channel_id=1, source_target_pairs={{0,24},{8,0},{16,8},{24,16},{1,25},{9,1},{17,9},{25,17},{2,26},{10... | collective-permute-start | bytes 786440 | tf_op jit(solution)/shard_map/ppermute | solution.py:73
  82.7 23.7 %collective-permute-start.5 = (bf16[1,256,512]{2,1,0:T(8,128)(2,1)S(1)}, bf16[1,256,512]{2,1,0:T(8,128)(2,1)S(1)}, u32[]{:S(2)}, u32[]{:S(2)}) collective-permute-start(bf16[1,256,512]{2,1,0:T(8,128)(2,1)S(1)} %get-tuple-element.72), channel_id=1, source_target_pairs={{0,16},{8,24},{16,0},{24,8},{1,17},{9,25},{17,1},{25,9},{2,18},{10... | collective-permute-start | bytes 786440 | tf_op jit(solution)/shard_map/ppermute | solution.py:73
  113.3 20.0 %all-to-all-start = ((bf16[8,256,256]{2,1,0:T(8,128)(2,1)}), bf16[8,256,256]{2,1,0:T(8,128)(2,1)S(1)}, u32[]{:S(2)}, u32[]{:S(2)}) async-start(bf16[8,256,256]{2,1,0:T(8,128)(2,1)} %bitcast.249), calls=%async_computation | async-start | bytes 2097152 | tf_op jit(solution)/shard_map/all_to_all | solution.py:92
  145.7 28.2 %all-to-all-start.1 = ((bf16[8,1,256,256]{3,2,1,0:T(8,128)(2,1)}), bf16[8,1,256,256]{3,2,1,0:T(8,128)(2,1)S(1)}, u32[]{:S(2)}, u32[]{:S(2)}) async-start(bf16[8,1,256,256]{3,2,1,0:T(8,128)(2,1)} %bitcast.32), calls=%async_computation.1 | async-start | bytes 2097152 | tf_op jit(solution)/shard_map/all_to_all | solution.py:106
  151.2 11.1 %collective-permute-start.7 = (bf16[1,256,512]{2,1,0:T(8,128)(2,1)S(1)}, bf16[1,256,512]{2,1,0:T(8,128)(2,1)S(1)}, u32[]{:S(2)}, u32[]{:S(2)}) collective-permute-start(bf16[1,256,512]{2,1,0:T(8,128)(2,1)S(1)} %get-tuple-element.69), channel_id=1, source_target_pairs={{0,8},{8,16},{16,24},{24,0},{1,9},{9,17},{17,25},{25,1},{2,10},{10... | collective-permute-start | bytes 786440 | tf_op jit(solution)/shard_map/ppermute | solution.py:73
  151.2 21.3 %collective-permute-start.8 = (bf16[1,256,512]{2,1,0:T(8,128)(2,1)S(1)}, bf16[1,256,512]{2,1,0:T(8,128)(2,1)S(1)}, u32[]{:S(2)}, u32[]{:S(2)}) collective-permute-start(bf16[1,256,512]{2,1,0:T(8,128)(2,1)S(1)} %get-tuple-element.68), channel_id=1, source_target_pairs={{0,16},{8,24},{16,0},{24,8},{1,17},{9,25},{17,1},{25,9},{2,18},{10... | collective-permute-start | bytes 786440 | tf_op jit(solution)/shard_map/ppermute | solution.py:73
  153.4 19.8 %collective-permute-start.9 = (bf16[1,256,512]{2,1,0:T(8,128)(2,1)S(1)}, bf16[1,256,512]{2,1,0:T(8,128)(2,1)S(1)}, u32[]{:S(2)}, u32[]{:S(2)}) collective-permute-start(bf16[1,256,512]{2,1,0:T(8,128)(2,1)S(1)} %get-tuple-element.67), channel_id=1, source_target_pairs={{0,24},{8,0},{16,8},{24,16},{1,25},{9,1},{17,9},{25,17},{2,26},{10... | collective-permute-start | bytes 786440 | tf_op jit(solution)/shard_map/ppermute | solution.py:73
  217.8 18.9 %all-to-all-start.3 = ((bf16[8,1,256,256]{3,2,1,0:T(8,128)(2,1)}), bf16[8,1,256,256]{3,2,1,0:T(8,128)(2,1)S(1)}, u32[]{:S(2)}, u32[]{:S(2)}) async-start(bf16[8,1,256,256]{3,2,1,0:T(8,128)(2,1)} %bitcast.46), calls=%async_computation.3 | async-start | bytes 2097152 | tf_op jit(solution)/shard_map/all_to_all | solution.py:106
  222.4 11.7 %collective-permute-start.10 = (bf16[1,256,512]{2,1,0:T(8,128)(2,1)}, bf16[1,256,512]{2,1,0:T(8,128)(2,1)S(1)}, u32[]{:S(2)}, u32[]{:S(2)}) collective-permute-start(bf16[1,256,512]{2,1,0:T(8,128)(2,1)} %get-tuple-element.62), channel_id=1, source_target_pairs={{0,8},{8,16},{16,24},{24,0},{1,9},{9,17},{17,25},{25,1},{2,10},{10... | collective-permute-start | bytes 786440 | tf_op jit(solution)/shard_map/ppermute | solution.py:73
  227.1 34.9 %collective-permute-start.12 = (bf16[1,256,512]{2,1,0:T(8,128)(2,1)S(1)}, bf16[1,256,512]{2,1,0:T(8,128)(2,1)S(1)}, u32[]{:S(2)}, u32[]{:S(2)}) collective-permute-start(bf16[1,256,512]{2,1,0:T(8,128)(2,1)S(1)} %get-tuple-element.60), channel_id=1, source_target_pairs={{0,24},{8,0},{16,8},{24,16},{1,25},{9,1},{17,9},{25,17},{2,26},{10... | collective-permute-start | bytes 786440 | tf_op jit(solution)/shard_map/ppermute | solution.py:73
  227.1 34.8 %collective-permute-start.11 = (bf16[1,256,512]{2,1,0:T(8,128)(2,1)}, bf16[1,256,512]{2,1,0:T(8,128)(2,1)S(1)}, u32[]{:S(2)}, u32[]{:S(2)}) collective-permute-start(bf16[1,256,512]{2,1,0:T(8,128)(2,1)} %get-tuple-element.61), channel_id=1, source_target_pairs={{0,16},{8,24},{16,0},{24,8},{1,17},{9,25},{17,1},{25,9},{2,18},{10... | collective-permute-start | bytes 786440 | tf_op jit(solution)/shard_map/ppermute | solution.py:73
  242.6 19.7 %collective-permute-start.13 = (bf16[1,256,512]{2,1,0:T(8,128)(2,1)S(1)}, bf16[1,256,512]{2,1,0:T(8,128)(2,1)S(1)}, u32[]{:S(2)}, u32[]{:S(2)}) collective-permute-start(bf16[1,256,512]{2,1,0:T(8,128)(2,1)S(1)} %get-tuple-element.66), channel_id=1, source_target_pairs={{0,8},{8,16},{16,24},{24,0},{1,9},{9,17},{17,25},{25,1},{2,10},{10... | collective-permute-start | bytes 786440 | tf_op jit(solution)/shard_map/ppermute | solution.py:73
  261.9 10.2 %collective-permute-start.14 = (bf16[1,256,512]{2,1,0:T(8,128)(2,1)S(1)}, bf16[1,256,512]{2,1,0:T(8,128)(2,1)S(1)}, u32[]{:S(2)}, u32[]{:S(2)}) collective-permute-start(bf16[1,256,512]{2,1,0:T(8,128)(2,1)S(1)} %get-tuple-element.65), channel_id=1, source_target_pairs={{0,16},{8,24},{16,0},{24,8},{1,17},{9,25},{17,1},{25,9},{2,18},{10... | collective-permute-start | bytes 786440 | tf_op jit(solution)/shard_map/ppermute | solution.py:73
  262.1 13.9 %collective-permute-start.15 = (bf16[1,256,512]{2,1,0:T(8,128)(2,1)S(1)}, bf16[1,256,512]{2,1,0:T(8,128)(2,1)S(1)}, u32[]{:S(2)}, u32[]{:S(2)}) collective-permute-start(bf16[1,256,512]{2,1,0:T(8,128)(2,1)S(1)} %get-tuple-element.64), channel_id=1, source_target_pairs={{0,24},{8,0},{16,8},{24,16},{1,25},{9,1},{17,9},{25,17},{2,26},{10... | collective-permute-start | bytes 786440 | tf_op jit(solution)/shard_map/ppermute | solution.py:73
  276.3 13.8 %collective-permute-start.16 = (bf16[8,256,1]{2,1,0:T(8,128)(2,1)S(1)}, bf16[8,256,1]{2,1,0:T(8,128)(2,1)S(1)}, u32[]{:S(2)}, u32[]{:S(2)}) collective-permute-start(bf16[8,256,1]{2,1,0:T(8,128)(2,1)S(1)} %get-tuple-element.42), channel_id=1, source_target_pairs={{0,8},{8,16},{16,24},{1,9},{9,17},{17,25},{2,10},{10,18},{18,26},{... | collective-permute-start | bytes 12296 | tf_op jit(solution)/shard_map/ppermute | solution.py:16
  279.6 14.7 %collective-permute-start.17 = (bf16[8,256,1]{2,1,0:T(8,128)(2,1)S(1)}, bf16[8,256,1]{2,1,0:T(8,128)(2,1)S(1)}, u32[]{:S(2)}, u32[]{:S(2)}) collective-permute-start(bf16[8,256,1]{2,1,0:T(8,128)(2,1)S(1)} %get-tuple-element.43), channel_id=1, source_target_pairs={{8,0},{16,8},{24,16},{9,1},{17,9},{25,17},{10,2},{18,10},{26,18},{... | collective-permute-start | bytes 12296 | tf_op jit(solution)/shard_map/ppermute | solution.py:17
  294.4 3.2 collective-permute-start.18
  296.0 5.1 collective-permute-start.19
  327.5 3.5 collective-permute-start.20
  332.5 4.4 collective-permute-start.21
  339.5 3.9 collective-permute-start.23
  343.4 4.5 collective-permute-start.24
  354.9 11.2 %collective-permute-start.25 = (bf16[1,256,512]{2,1,0:T(8,128)(2,1)S(1)}, bf16[1,256,512]{2,1,0:T(8,128)(2,1)S(1)}, u32[]{:S(2)}, u32[]{:S(2)}) collective-permute-start(bf16[1,256,512]{2,1,0:T(8,128)(2,1)S(1)} %get-tuple-element.59), channel_id=1, source_target_pairs={{0,8},{8,16},{16,24},{24,0},{1,9},{9,17},{17,25},{25,1},{2,10},{10... | collective-permute-start | bytes 786440 | tf_op jit(solution)/shard_map/ppermute | solution.py:73
  355.2 19.4 %collective-permute-start.26 = (bf16[1,256,512]{2,1,0:T(8,128)(2,1)S(1)}, bf16[1,256,512]{2,1,0:T(8,128)(2,1)S(1)}, u32[]{:S(2)}, u32[]{:S(2)}) collective-permute-start(bf16[1,256,512]{2,1,0:T(8,128)(2,1)S(1)} %get-tuple-element.58), channel_id=1, source_target_pairs={{0,16},{8,24},{16,0},{24,8},{1,17},{9,25},{17,1},{25,9},{2,18},{10... | collective-permute-start | bytes 786440 | tf_op jit(solution)/shard_map/ppermute | solution.py:73
  356.6 18.0 %collective-permute-start.27 = (bf16[1,256,512]{2,1,0:T(8,128)(2,1)S(1)}, bf16[1,256,512]{2,1,0:T(8,128)(2,1)S(1)}, u32[]{:S(2)}, u32[]{:S(2)}) collective-permute-start(bf16[1,256,512]{2,1,0:T(8,128)(2,1)S(1)} %get-tuple-element.57), channel_id=1, source_target_pairs={{0,24},{8,0},{16,8},{24,16},{1,25},{9,1},{17,9},{25,17},{2,26},{10... | collective-permute-start | bytes 786440 | tf_op jit(solution)/shard_map/ppermute | solution.py:73
  407.7 31.0 %all-to-all-start.5 = ((bf16[8,1,256,256]{3,2,1,0:T(8,128)(2,1)}), bf16[8,1,256,256]{3,2,1,0:T(8,128)(2,1)S(1)}, u32[]{:S(2)}, u32[]{:S(2)}) async-start(bf16[8,1,256,256]{3,2,1,0:T(8,128)(2,1)} %bitcast.68), calls=%async_computation.5 | async-start | bytes 2097152 | tf_op jit(solution)/shard_map/all_to_all | solution.py:106
  413.1 13.2 %collective-permute-start.28 = (bf16[1,256,512]{2,1,0:T(8,128)(2,1)S(1)}, bf16[1,256,512]{2,1,0:T(8,128)(2,1)S(1)}, u32[]{:S(2)}, u32[]{:S(2)}) collective-permute-start(bf16[1,256,512]{2,1,0:T(8,128)(2,1)S(1)} %get-tuple-element.55), channel_id=1, source_target_pairs={{0,8},{8,16},{16,24},{24,0},{1,9},{9,17},{17,25},{25,1},{2,10},{10... | collective-permute-start | bytes 786440 | tf_op jit(solution)/shard_map/ppermute | solution.py:73
  418.3 19.0 %collective-permute-start.29 = (bf16[1,256,512]{2,1,0:T(8,128)(2,1)S(1)}, bf16[1,256,512]{2,1,0:T(8,128)(2,1)S(1)}, u32[]{:S(2)}, u32[]{:S(2)}) collective-permute-start(bf16[1,256,512]{2,1,0:T(8,128)(2,1)S(1)} %get-tuple-element.54), channel_id=1, source_target_pairs={{0,16},{8,24},{16,0},{24,8},{1,17},{9,25},{17,1},{25,9},{2,18},{10... | collective-permute-start | bytes 786440 | tf_op jit(solution)/shard_map/ppermute | solution.py:73
  419.7 18.4 %collective-permute-start.30 = (bf16[1,256,512]{2,1,0:T(8,128)(2,1)S(1)}, bf16[1,256,512]{2,1,0:T(8,128)(2,1)S(1)}, u32[]{:S(2)}, u32[]{:S(2)}) collective-permute-start(bf16[1,256,512]{2,1,0:T(8,128)(2,1)S(1)} %get-tuple-element.53), channel_id=1, source_target_pairs={{0,24},{8,0},{16,8},{24,16},{1,25},{9,1},{17,9},{25,17},{2,26},{10... | collective-permute-start | bytes 786440 | tf_op jit(solution)/shard_map/ppermute | solution.py:73
  482.4 18.9 %all-to-all-start.7 = ((bf16[8,1,256,256]{3,2,1,0:T(8,128)(2,1)}), bf16[8,1,256,256]{3,2,1,0:T(8,128)(2,1)S(1)}, u32[]{:S(2)}, u32[]{:S(2)}) async-start(bf16[8,1,256,256]{3,2,1,0:T(8,128)(2,1)} %bitcast.80), calls=%async_computation.7 | async-start | bytes 2097152 | tf_op jit(solution)/shard_map/all_to_all | solution.py:106
  486.9 14.3 %collective-permute-start.31 = (bf16[1,256,512]{2,1,0:T(8,128)(2,1)S(1)}, bf16[1,256,512]{2,1,0:T(8,128)(2,1)S(1)}, u32[]{:S(2)}, u32[]{:S(2)}) collective-permute-start(bf16[1,256,512]{2,1,0:T(8,128)(2,1)S(1)} %get-tuple-element.48), channel_id=1, source_target_pairs={{0,8},{8,16},{16,24},{24,0},{1,9},{9,17},{17,25},{25,1},{2,10},{10... | collective-permute-start | bytes 786440 | tf_op jit(solution)/shard_map/ppermute | solution.py:73
  492.3 36.7 %collective-permute-start.33 = (bf16[1,256,512]{2,1,0:T(8,128)(2,1)S(1)}, bf16[1,256,512]{2,1,0:T(8,128)(2,1)S(1)}, u32[]{:S(2)}, u32[]{:S(2)}) collective-permute-start(bf16[1,256,512]{2,1,0:T(8,128)(2,1)S(1)} %get-tuple-element.46), channel_id=1, source_target_pairs={{0,24},{8,0},{16,8},{24,16},{1,25},{9,1},{17,9},{25,17},{2,26},{10... | collective-permute-start | bytes 786440 | tf_op jit(solution)/shard_map/ppermute | solution.py:73
  494.0 35.0 %collective-permute-start.32 = (bf16[1,256,512]{2,1,0:T(8,128)(2,1)}, bf16[1,256,512]{2,1,0:T(8,128)(2,1)S(1)}, u32[]{:S(2)}, u32[]{:S(2)}) collective-permute-start(bf16[1,256,512]{2,1,0:T(8,128)(2,1)} %get-tuple-element.47), channel_id=1, source_target_pairs={{0,16},{8,24},{16,0},{24,8},{1,17},{9,25},{17,1},{25,9},{2,18},{10... | collective-permute-start | bytes 786440 | tf_op jit(solution)/shard_map/ppermute | solution.py:73
  507.1 22.1 %collective-permute-start.34 = (bf16[1,256,512]{2,1,0:T(8,128)(2,1)S(1)}, bf16[1,256,512]{2,1,0:T(8,128)(2,1)S(1)}, u32[]{:S(2)}, u32[]{:S(2)}) collective-permute-start(bf16[1,256,512]{2,1,0:T(8,128)(2,1)S(1)} %get-tuple-element.52), channel_id=1, source_target_pairs={{0,8},{8,16},{16,24},{24,0},{1,9},{9,17},{17,25},{25,1},{2,10},{10... | collective-permute-start | bytes 786440 | tf_op jit(solution)/shard_map/ppermute | solution.py:73
  528.9 10.2 %collective-permute-start.35 = (bf16[1,256,512]{2,1,0:T(8,128)(2,1)S(1)}, bf16[1,256,512]{2,1,0:T(8,128)(2,1)S(1)}, u32[]{:S(2)}, u32[]{:S(2)}) collective-permute-start(bf16[1,256,512]{2,1,0:T(8,128)(2,1)S(1)} %get-tuple-element.51), channel_id=1, source_target_pairs={{0,16},{8,24},{16,0},{24,8},{1,17},{9,25},{17,1},{25,9},{2,18},{10... | collective-permute-start | bytes 786440 | tf_op jit(solution)/shard_map/ppermute | solution.py:73
  529.1 13.9 %collective-permute-start.36 = (bf16[1,256,512]{2,1,0:T(8,128)(2,1)S(1)}, bf16[1,256,512]{2,1,0:T(8,128)(2,1)S(1)}, u32[]{:S(2)}, u32[]{:S(2)}) collective-permute-start(bf16[1,256,512]{2,1,0:T(8,128)(2,1)S(1)} %get-tuple-element.50), channel_id=1, source_target_pairs={{0,24},{8,0},{16,8},{24,16},{1,25},{9,1},{17,9},{25,17},{2,26},{10... | collective-permute-start | bytes 786440 | tf_op jit(solution)/shard_map/ppermute | solution.py:73
  543.3 13.9 %collective-permute-start.37 = (bf16[8,256,1]{2,1,0:T(8,128)(2,1)S(1)}, bf16[8,256,1]{2,1,0:T(8,128)(2,1)S(1)}, u32[]{:S(2)}, u32[]{:S(2)}) collective-permute-start(bf16[8,256,1]{2,1,0:T(8,128)(2,1)S(1)} %get-tuple-element.38), channel_id=1, source_target_pairs={{0,8},{8,16},{16,24},{1,9},{9,17},{17,25},{2,10},{10,18},{18,26},{... | collective-permute-start | bytes 12296 | tf_op jit(solution)/shard_map/ppermute | solution.py:16
  546.6 14.7 %collective-permute-start.38 = (bf16[8,256,1]{2,1,0:T(8,128)(2,1)S(1)}, bf16[8,256,1]{2,1,0:T(8,128)(2,1)S(1)}, u32[]{:S(2)}, u32[]{:S(2)}) collective-permute-start(bf16[8,256,1]{2,1,0:T(8,128)(2,1)S(1)} %get-tuple-element.39), channel_id=1, source_target_pairs={{8,0},{16,8},{24,16},{9,1},{17,9},{25,17},{10,2},{18,10},{26,18},{... | collective-permute-start | bytes 12296 | tf_op jit(solution)/shard_map/ppermute | solution.py:17
  561.4 3.2 collective-permute-start.39
  563.0 5.1 collective-permute-start.40
  596.6 3.5 collective-permute-start.41
  602.8 4.4 collective-permute-start.42
  611.0 3.9 collective-permute-start.44
  614.9 4.5 collective-permute-start.45
  (21 other events, 265.4 us)

commit v5 on v3

--- a/solution.py
+++ b/solution.py
@@ -7,14 +7,21 @@
 
 
 def padded_2(array, sides, width):
+    slabs = {}
     for axis, dim in sides:
         size, length = (lax.axis_size(axis), array.shape[dim])
         up = [(i, (i + 1) % size) for i in range(size - 1)]
         down = [(j, i) for i, j in up]
         last = lax.slice_in_dim(array, length - width, length, axis=dim)
         initial = lax.slice_in_dim(array, 0, width, axis=dim)
-        before = lax.ppermute(last, axis, up)
-        after = lax.ppermute(initial, axis, down)
+        slabs[dim] = (lax.ppermute(last, axis, up), lax.ppermute(initial, axis, down))
+    for position, (axis, dim) in enumerate(sides):
+        before, after = slabs[dim]
+        for _, other in sides[:position]:
+            pad = [(0, 0)] * array.ndim
+            pad[other] = (width, width)
+            before = jnp.pad(before, pad)
+            after = jnp.pad(after, pad)
         array = jnp.concatenate([before, array, after], axis=dim)
     return array
 

time: 589 us -> 586 us (level)
  waiting for transfers between devices: 207 us -> 183 us
  starting transfers between devices: 132 us -> 148 us
  other arithmetic: 122 us -> 129 us
    ppermute x12, waiting for transfers between devices: 45.6 us -> 25.4 us  [the longest x6 12.9 us: padded_2(): lax.ppermute(last, axis, up)]
    ppermute x10, starting transfers between devices: 11.5 us -> 28.7 us  [all_sum(): values = values + lax.ppermute(values, axis, pairs)]
    convert_element_type x2, other arithmetic: 4.68 us -> 10.9 us  [operator(): padded_2(for_sending(field), (('px', 2), ('py', 1)), 1).astype(field.dtype)]
  transfers between devices with their start and end apart: 54 -> 54, of which waited for: 37 -> 34; matrix products, arithmetic and copies ran while one was open for 17% -> 17% of each run, Pallas kernels for 0% -> 0%
where the time goes in v5:
time: 586 us; the launch traced here: 582 us
  waiting for transfers between devices  183 us (31%)
  starting transfers between devices  148 us (25%)
  other arithmetic  129 us (22%)
  matrix products  86.6 us (15%)
  local copies, waits for them, and re-layouts  28.2 us (5%)
  between operations  7.97 us (1%)
    ppermute x24, waiting for transfers between devices, exchange(): lax.ppermute(part, axis, [(i, (i + shift) % size) for i in range(size)])  96.2 us
    ppermute x24, starting transfers between devices, exchange(): lax.ppermute(part, axis, [(i, (i + shift) % size) for i in range(size)])  67.1 us
    dot_general x4, matrix products, precondition_levels(): jnp.einsum('yj,kji->kyi', eigenvectors, scaled, preferred_element_type=jn...  44.2 us
    ppermute x10, starting transfers between devices, all_sum(): values = values + lax.ppermute(values, axis, pairs)  28.7 us
    reduce_sum x2, other arithmetic, shards(): jnp.sum(residual * precond)  27.6 us
    dot_general x4, matrix products, precondition_levels(): jnp.einsum('qkyi,qix->kyx', returned, eigenvectors.reshape(across, cols,...  22.8 us
    all_to_all x4, waiting for transfers between devices, precondition_levels(): returned = lax.all_to_all(outgoing, 'py', 0, 0, tiled=True)  22.4 us
    all_to_all x4, waiting for transfers between devices, precondition_levels(): incoming = lax.all_to_all(outgoing, 'py', 0, 0, tiled=True)  22.1 us
  transfers between devices with their start and end apart: 54, of which 34 were waited for; matrix products, arithmetic and copies ran while one was open for 17% of the time, Pallas kernels for 0%

profile of v5, /device:TPU:0, one launch (start us, length us, event | category | flops | bytes accessed | tf_op | source)
XLA Modules:
  0.0 582.2 jit_solution(3008254294219382936)
XLA Ops:
  5.0 14.5 %fusion.79 = bf16[1,8,256,512]{3,2,1,0:T(8,128)(2,1)S(1)} fusion(bf16[]{:T(256)} %bitcast.16, s32[8,256,512]{2,1,0:T(8,128)S(1)} %copy-done.9, bf16[]{:T(256)} %bitcast.15, bf16[]{:T(256)} %bitcast.14, bf16[]{:T(256)} %bitcast.13, bf16[]{:T(256)} %bitcast.12, bf16[]{:T(256)} %bitcast.11, bf16[]{:T(256)} %bitcast.10, bf16[]{:T(256)} %bitcast.9, bf16[]{:T(256)} %bitcast.8, ...), kind=kLoop, calls=%fused_computation.154 | loop fusion | flops 33554432 | bytes 6291488 | tf_op jit(solution)/shard_map/stack | solution.py:144
  26.4 4.3 collective-permute-start.1
  38.0 13.2 %fusion.3 = f32[2,8,258,514]{3,2,1,0:T(8,128)} fusion(bf16[2,8,1,512]{3,2,1,0:T(2,128)(2,1)S(1)} %collective-permute-done.3, bf16[2,8,1,512]{3,2,1,0:T(2,128)(2,1)S(1)} %collective-permute-done, bf16[2,8,256,1]{3,2,1,0:T(8,128)(2,1)} %copy.55, bf16[1,8,256,512]{3,2,1,0:T(8,128)(2,1)} %copy-done.7, bf16[1,8,256,512]{3,2,1,0:T(8,128)(2,1)S(1)} %convert_bitcast_fusion, ...), kind=kLoop, calls=%fused_computation.14 | loop fusion | flops 33948672 | bytes 12730624 | tf_op jit(solution)/shard_map/convert_element_type | solution.py:145
  51.3 4.8 slice_bitcast_fusion.1
  56.1 5.9 %fusion.51 = f32[7,256,512]{2,1,0:T(8,128)} fusion(f32[8,258,514]{2,1,0:T(8,128)S(1)} %get-tuple-element.21, f32[8,258,514]{2,1,0:T(8,128)S(1)} %get-tuple-element.20), kind=kLoop, calls=%fused_computation.88 | loop fusion | flops 3670016 | bytes 18350080 | tf_op jit(solution)/shard_map/mul | solution.py:58
  62.1 12.7 %fusion.95 = (bf16[8,256,512]{2,1,0:T(8,128)(2,1)S(1)}, f32[8,256,512]{2,1,0:T(8,128)}) fusion(f32[8,256,512]{2,1,0:T(8,128)} %param.7, f32[7,256,512]{2,1,0:T(8,128)} %fusion.51, f32[8,258,514]{2,1,0:T(8,128)S(1)} %get-tuple-element.21, f32[8,258,514]{2,1,0:T(8,128)S(1)} %get-tuple-element.20), kind=kLoop, calls=%fused_computation.234 | loop fusion | flops 24117248 | bytes 56098816 | tf_op jit(solution)/shard_map/convert.5
  82.2 9.8 %collective-permute-done.10 = bf16[1,256,512]{2,1,0:T(8,128)(2,1)S(1)} collective-permute-done((bf16[1,256,512]{2,1,0:T(8,128)(2,1)S(1)}, bf16[1,256,512]{2,1,0:T(8,128)(2,1)S(1)}, u32[]{:S(2)}, u32[]{:S(2)}) %collective-permute-start.10) | collective-permute-done | bytes 262176 | tf_op jit(solution)/shard_map/ppermute | solution.py:80
  92.0 19.5 %collective-permute-start.4 = (bf16[1,256,512]{2,1,0:T(8,128)(2,1)S(1)}, bf16[1,256,512]{2,1,0:T(8,128)(2,1)}, u32[]{:S(2)}, u32[]{:S(2)}) collective-permute-start(bf16[1,256,512]{2,1,0:T(8,128)(2,1)S(1)} %get-tuple-element.55), channel_id=1, source_target_pairs={{0,8},{8,16},{16,24},{24,0},{1,9},{9,17},{17,25},{25,1},{2,10},{10... | collective-permute-start | bytes 786440 | tf_op jit(solution)/shard_map/ppermute | solution.py:80
  111.6 5.7 convolution_convert_fusion.5
  118.4 5.3 all-to-all-start.2
  124.8 5.7 convolution_convert_fusion.7
  131.6 7.6 %all-to-all-done.2 = bf16[8,256,256]{2,1,0:T(8,128)(2,1)S(1)} async-done(((bf16[8,256,256]{2,1,0:T(8,128)(2,1)}), bf16[8,256,256]{2,1,0:T(8,128)(2,1)S(1)}, u32[]{:S(2)}, u32[]{:S(2)}) %all-to-all-start.2) | async-done | bytes 1048608 | tf_op jit(solution)/shard_map/all_to_all | solution.py:96
  142.7 11.0 %fusion.68 = bf16[1,2048,256]{1,2,0:T(8,128)(2,1)S(1)} fusion(bf16[2048,2048]{1,0:T(8,128)(2,1)} %param.11, bf16[2048,256]{1,0:T(8,128)(2,1)S(1)} %bitcast.274, f32[]{:T(128)} %bitcast.48, f32[256]{0:T(256)S(1)} %dynamic_slice.114, f32[2048]{0:T(1024)S(1)} %copy-done.11), kind=kOutput, calls=%fused_computation.142 | convolution fusion | flops 4297588736 | bytes 10494980 | tf_op jit(solution)/shard_map/yj,kji->kyi/dot_general | solution.py:106
  158.1 4.0 all-to-all-start.3
  162.1 11.1 %fusion.67 = bf16[1,2048,256]{1,2,0:T(8,128)(2,1)S(1)} fusion(bf16[2048,2048]{1,0:T(8,128)(2,1)} %param.11, bf16[2048,256]{1,0:T(8,128)(2,1)S(1)} %bitcast.277, f32[]{:T(128)} %bitcast.28, f32[256]{0:T(256)S(1)} %dynamic_slice.114, f32[2048]{0:T(1024)S(1)} %copy-done.11), kind=kOutput, calls=%fused_computation.141 | convolution fusion | flops 4297588736 | bytes 10494980 | tf_op jit(solution)/shard_map/yj,kji->kyi/dot_general | solution.py:106
  181.0 5.7 fusion.64
  189.4 6.9 %all-to-all-done.1 = bf16[8,1,256,256]{3,2,1,0:T(8,128)(2,1)S(1)} async-done(((bf16[8,1,256,256]{3,2,1,0:T(8,128)(2,1)}), bf16[8,1,256,256]{3,2,1,0:T(8,128)(2,1)S(1)}, u32[]{:S(2)}, u32[]{:S(2)}) %all-to-all-start.1) | async-done | bytes 1048608 | tf_op jit(solution)/shard_map/all_to_all | solution.py:110
  196.3 5.7 fusion.63
  213.3 19.7 %collective-permute-done.14 = bf16[1,256,512]{2,1,0:T(8,128)(2,1)S(1)} collective-permute-done((bf16[1,256,512]{2,1,0:T(8,128)(2,1)S(1)}, bf16[1,256,512]{2,1,0:T(8,128)(2,1)S(1)}, u32[]{:S(2)}, u32[]{:S(2)}) %collective-permute-start.14) | collective-permute-done | bytes 262176 | tf_op jit(solution)/shard_map/ppermute | solution.py:80
  233.1 9.8 %collective-permute-done.8 = bf16[1,256,512]{2,1,0:T(8,128)(2,1)S(1)} collective-permute-done((bf16[1,256,512]{2,1,0:T(8,128)(2,1)S(1)}, bf16[1,256,512]{2,1,0:T(8,128)(2,1)S(1)}, u32[]{:S(2)}, u32[]{:S(2)}) %collective-permute-start.8) | collective-permute-done | bytes 262176 | tf_op jit(solution)/shard_map/ppermute | solution.py:80
  249.1 6.3 %collective-permute-done.17 = bf16[8,256,1]{2,1,0:T(8,128)(2,1)S(1)} collective-permute-done((bf16[8,256,1]{2,1,0:T(8,128)(2,1)S(1)}, bf16[8,256,1]{2,1,0:T(8,128)(2,1)S(1)}, u32[]{:S(2)}, u32[]{:S(2)}) %collective-permute-start.17) | collective-permute-done | bytes 4128 | tf_op jit(solution)/shard_map/ppermute | solution.py:17
  255.4 4.8 collective-permute-done.18
  260.2 5.4 fusion.59
  265.7 5.9 %fusion.50 = f32[7,256,512]{2,1,0:T(8,128)} fusion(f32[8,258,514]{2,1,0:T(8,128)S(1)} %fusion.59, f32[8,258,514]{2,1,0:T(8,128)S(1)} %bitcast.271), kind=kLoop, calls=%fused_computation.86 | loop fusion | flops 3670016 | bytes 18350080 | tf_op jit(solution)/shard_map/mul | solution.py:58
  271.6 13.4 %fusion.12 = (f32[]{:T(128)}, f32[]{:T(128)}, f32[8,256,512]{2,1,0:T(8,128)}) fusion(f32[8,256,512]{2,1,0:T(8,128)} %get-tuple-element.19, bf16[4,256,512]{2,1,0:T(8,128)(2,1)} %copy-done.3, bf16[4,256,512]{2,1,0:T(8,128)(2,1)} %copy-done.4, f32[7,256,512]{2,1,0:T(8,128)} %fusion.50, f32[8,258,514]{2,1,0:T(8,128)S(1)} %fusion.59, f32[8,258,514]{2,1,0:T(8,128)S(1)} %bitcast.271), kind=kLoop, calls=%fused_computation.27 | loop fusion | flops 28311552 | bytes 56098824 | tf_op jit(solution)/shard_map/reduce_sum | solution.py:155
  299.4 7.2 %collective-permute-start.23 = (f32[2]{0:T(128)S(1)}, f32[2]{0:T(128)S(1)}, u32[]{:S(2)}, u32[]{:S(2)}) collective-permute-start(f32[2]{0:T(128)S(1)} %add.505), channel_id=1, source_target_pairs={{0,2},{1,3},{2,0},{3,1},{4,6},{5,7},{6,4},{7,5},{8,10},{9,11},{10,... | collective-permute-start | bytes 32 | tf_op jit(solution)/shard_map/ppermute | solution.py:43
  313.6 4.8 fusion.80
  325.2 9.8 %collective-permute-done.31 = bf16[1,256,512]{2,1,0:T(8,128)(2,1)S(1)} collective-permute-done((bf16[1,256,512]{2,1,0:T(8,128)(2,1)S(1)}, bf16[1,256,512]{2,1,0:T(8,128)(2,1)S(1)}, u32[]{:S(2)}, u32[]{:S(2)}) %collective-permute-start.31) | collective-permute-done | bytes 262176 | tf_op jit(solution)/shard_map/ppermute | solution.py:80
  334.9 19.7 %collective-permute-start.25 = (bf16[1,256,512]{2,1,0:T(8,128)(2,1)S(1)}, bf16[1,256,512]{2,1,0:T(8,128)(2,1)S(1)}, u32[]{:S(2)}, u32[]{:S(2)}) collective-permute-start(bf16[1,256,512]{2,1,0:T(8,128)(2,1)S(1)} %get-tuple-element.43), channel_id=1, source_target_pairs={{0,8},{8,16},{16,24},{24,0},{1,9},{9,17},{17,25},{25,1},{2,10},{10... | collective-permute-start | bytes 786440 | tf_op jit(solution)/shard_map/ppermute | solution.py:80
  358.6 6.8 %collective-permute-done.26 = bf16[1,256,512]{2,1,0:T(8,128)(2,1)S(1)} collective-permute-done((bf16[1,256,512]{2,1,0:T(8,128)(2,1)S(1)}, bf16[1,256,512]{2,1,0:T(8,128)(2,1)S(1)}, u32[]{:S(2)}, u32[]{:S(2)}) %collective-permute-start.26) | collective-permute-done | bytes 262176 | tf_op jit(solution)/shard_map/ppermute | solution.py:80
  372.5 5.7 convolution_convert_fusion.1
  379.3 8.6 %all-to-all-done.4 = bf16[8,256,256]{2,1,0:T(8,128)(2,1)S(1)} async-done(((bf16[8,256,256]{2,1,0:T(8,128)(2,1)}), bf16[8,256,256]{2,1,0:T(8,128)(2,1)S(1)}, u32[]{:S(2)}, u32[]{:S(2)}) %all-to-all-start.4) | async-done | bytes 1048608 | tf_op jit(solution)/shard_map/all_to_all | solution.py:96
  391.4 11.1 %fusion.69 = bf16[1,2048,256]{1,2,0:T(8,128)(2,1)S(1)} fusion(bf16[2048,2048]{1,0:T(8,128)(2,1)} %param.11, bf16[2048,256]{1,0:T(8,128)(2,1)S(1)} %bitcast.276, f32[]{:T(128)} %bitcast.28, f32[256]{0:T(256)S(1)} %dynamic_slice.114, f32[2048]{0:T(1024)S(1)} %copy-done.11), kind=kOutput, calls=%fused_computation.143 | convolution fusion | flops 4297588736 | bytes 10494980 | tf_op jit(solution)/shard_map/yj,kji->kyi/dot_general | solution.py:106
  406.8 4.0 all-to-all-start.5
  410.8 11.0 %fusion.70 = bf16[1,2048,256]{1,2,0:T(8,128)(2,1)S(1)} fusion(bf16[2048,2048]{1,0:T(8,128)(2,1)} %param.11, bf16[2048,256]{1,0:T(8,128)(2,1)S(1)} %bitcast.275, f32[]{:T(128)} %bitcast.48, f32[256]{0:T(256)S(1)} %dynamic_slice.114, f32[2048]{0:T(1024)S(1)} %copy-done.11), kind=kOutput, calls=%fused_computation.144 | convolution fusion | flops 4297588736 | bytes 10494980 | tf_op jit(solution)/shard_map/yj,kji->kyi/dot_general | solution.py:106
  429.7 5.7 fusion.65
  435.5 9.5 %all-to-all-done.7 = bf16[8,1,256,256]{3,2,1,0:T(8,128)(2,1)S(1)} async-done(((bf16[8,1,256,256]{3,2,1,0:T(8,128)(2,1)}), bf16[8,1,256,256]{3,2,1,0:T(8,128)(2,1)S(1)}, u32[]{:S(2)}, u32[]{:S(2)}) %all-to-all-start.7) | async-done | bytes 1048608 | tf_op jit(solution)/shard_map/all_to_all | solution.py:110
  445.0 5.7 fusion.66
  456.3 6.7 %collective-permute-done.29 = bf16[1,256,512]{2,1,0:T(8,128)(2,1)S(1)} collective-permute-done((bf16[1,256,512]{2,1,0:T(8,128)(2,1)S(1)}, bf16[1,256,512]{2,1,0:T(8,128)(2,1)S(1)}, u32[]{:S(2)}, u32[]{:S(2)}) %collective-permute-start.29) | collective-permute-done | bytes 262176 | tf_op jit(solution)/shard_map/ppermute | solution.py:80
  464.7 13.4 %collective-permute-done.34 = bf16[1,256,512]{2,1,0:T(8,128)(2,1)S(1)} collective-permute-done((bf16[1,256,512]{2,1,0:T(8,128)(2,1)S(1)}, bf16[1,256,512]{2,1,0:T(8,128)(2,1)S(1)}, u32[]{:S(2)}, u32[]{:S(2)}) %collective-permute-start.34) | collective-permute-done | bytes 262176 | tf_op jit(solution)/shard_map/ppermute | solution.py:80
  478.1 10.9 %collective-permute-done.35 = bf16[1,256,512]{2,1,0:T(8,128)(2,1)S(1)} collective-permute-done((bf16[1,256,512]{2,1,0:T(8,128)(2,1)S(1)}, bf16[1,256,512]{2,1,0:T(8,128)(2,1)S(1)}, u32[]{:S(2)}, u32[]{:S(2)}) %collective-permute-start.35) | collective-permute-done | bytes 262176 | tf_op jit(solution)/shard_map/ppermute | solution.py:80
  495.5 6.5 %collective-permute-done.38 = bf16[8,256,1]{2,1,0:T(8,128)(2,1)S(1)} collective-permute-done((bf16[8,256,1]{2,1,0:T(8,128)(2,1)S(1)}, bf16[8,256,1]{2,1,0:T(8,128)(2,1)S(1)}, u32[]{:S(2)}, u32[]{:S(2)}) %collective-permute-start.38) | collective-permute-done | bytes 4128 | tf_op jit(solution)/shard_map/ppermute | solution.py:17
  502.0 5.0 collective-permute-done.39
  507.1 5.4 fusion.62
  512.6 5.9 %fusion.49 = f32[7,256,512]{2,1,0:T(8,128)} fusion(f32[8,258,514]{2,1,0:T(8,128)S(1)} %fusion.62, f32[8,258,514]{2,1,0:T(8,128)S(1)} %bitcast.273), kind=kLoop, calls=%fused_computation.84 | loop fusion | flops 3670016 | bytes 18350080 | tf_op jit(solution)/shard_map/mul | solution.py:58
  518.5 14.2 %fusion.9 = (f32[]{:T(128)}, f32[]{:T(128)}, f32[]{:T(128)}, f32[]{:T(128)}, f32[8,256,512]{2,1,0:T(8,128)}) fusion(f32[8,256,512]{2,1,0:T(8,128)} %get-tuple-element.19, f32[8,256,512]{2,1,0:T(8,128)} %get-tuple-element.17, f32[]{:T(128)S(6)} %div.23, bf16[4,256,512]{2,1,0:T(8,128)(2,1)} %copy-done.6, bf16[4,256,512]{2,1,0:T(8,128)(2,1)} %copy-done.5, ...), kind=kLoop, calls=%fused_computation.24 | loop fusion | flops 36700156 | bytes 62390292 | tf_op jit(solution)/shard_map/reduce_sum | solution.py:162
  551.2 6.9 %collective-permute-start.44 = (f32[4]{0:T(128)S(1)}, f32[4]{0:T(128)S(1)}, u32[]{:S(2)}, u32[]{:S(2)}) collective-permute-start(f32[4]{0:T(128)S(1)} %add.515), channel_id=1, source_target_pairs={{0,2},{1,3},{2,0},{3,1},{4,6},{5,7},{6,4},{7,5},{8,10},{9,11},{10,... | collective-permute-start | bytes 56 | tf_op jit(solution)/shard_map/ppermute | solution.py:43
  568.4 7.2 %fusion.15 = (f32[8,256,512]{2,1,0:T(8,128)}, f32[8,256,512]{2,1,0:T(8,128)}) fusion(f32[8,256,512]{2,1,0:T(8,128)} %param.8, f32[]{:T(128)S(6)} %div.27, f32[]{:T(128)S(6)} %div.23, bf16[4,256,512]{2,1,0:T(8,128)(2,1)} %copy-done.3, bf16[4,256,512]{2,1,0:T(8,128)(2,1)} %copy-done.4, f32[]{:T(128)S(6)} %div.26, bf16[4,256,512]{2,1,0:T(8,128)(2,1)} %copy-done.6, ...), kind=kLoop, calls=%fused_computation.30 | loop fusion | flops 10485760 | bytes 16777228 | tf_op jit(solution)/shard_map/add | solution.py:175
  (210 shorter events, 163.6 us)
Async XLA Ops:
  19.6 18.4 %collective-permute-start = (bf16[2,8,1,512]{3,2,1,0:T(2,128)(2,1)S(1)}, bf16[2,8,1,512]{3,2,1,0:T(2,128)(2,1)S(1)}, u32[]{:S(2)}, u32[]{:S(2)}) collective-permute-start(bf16[2,8,1,512]{3,2,1,0:T(2,128)(2,1)S(1)} %get-tuple-element.24), channel_id=1, source_target_pairs={{0,1},{1,2},{2,3},{3,4},{4,5},{5,6},{6,7},{8,9},{9,10},{10,11},{11... | collective-permute-start | bytes 49160 | tf_op jit(solution)/shard_map/ppermute | solution.py:17
  22.0 16.0 %collective-permute-start.3 = (bf16[2,8,1,512]{3,2,1,0:T(2,128)(2,1)S(1)}, bf16[2,8,1,512]{3,2,1,0:T(2,128)(2,1)S(1)}, u32[]{:S(2)}, u32[]{:S(2)}) collective-permute-start(bf16[2,8,1,512]{3,2,1,0:T(2,128)(2,1)S(1)} %get-tuple-element.25), channel_id=1, source_target_pairs={{1,0},{2,1},{3,2},{4,3},{5,4},{6,5},{7,6},{9,8},{10,9},{11,10},{12... | collective-permute-start | bytes 49160 | tf_op jit(solution)/shard_map/ppermute | solution.py:17
  26.4 7.0 %collective-permute-start.1 = (bf16[2,8,256,1]{2,1,3,0:T(8,128)(2,1)S(1)}, bf16[2,8,256,1]{2,1,3,0:T(8,128)(2,1)S(1)}, u32[]{:S(2)}, u32[]{:S(2)}) collective-permute-start(bf16[2,8,256,1]{2,1,3,0:T(8,128)(2,1)S(1)} %copy.52), channel_id=1, source_target_pairs={{0,8},{8,16},{16,24},{1,9},{9,17},{17,25},{2,10},{10,18},{18,26},{... | collective-permute-start | bytes 24584 | tf_op jit(solution)/shard_map/ppermute | solution.py:17
  31.1 5.5 collective-permute-start.2
  75.0 36.6 %collective-permute-start.11 = (bf16[1,256,512]{2,1,0:T(8,128)(2,1)S(1)}, bf16[1,256,512]{2,1,0:T(8,128)(2,1)S(1)}, u32[]{:S(2)}, u32[]{:S(2)}) collective-permute-start(bf16[1,256,512]{2,1,0:T(8,128)(2,1)S(1)} %get-tuple-element.60), channel_id=1, source_target_pairs={{0,16},{8,24},{16,0},{24,8},{1,17},{9,25},{17,1},{25,9},{2,18},{10... | collective-permute-start | bytes 786440 | tf_op jit(solution)/shard_map/ppermute | solution.py:80
  77.6 14.3 %collective-permute-start.10 = (bf16[1,256,512]{2,1,0:T(8,128)(2,1)S(1)}, bf16[1,256,512]{2,1,0:T(8,128)(2,1)S(1)}, u32[]{:S(2)}, u32[]{:S(2)}) collective-permute-start(bf16[1,256,512]{2,1,0:T(8,128)(2,1)S(1)} %get-tuple-element.61), channel_id=1, source_target_pairs={{0,8},{8,16},{16,24},{24,0},{1,9},{9,17},{17,25},{25,1},{2,10},{10... | collective-permute-start | bytes 786440 | tf_op jit(solution)/shard_map/ppermute | solution.py:80
  78.2 33.4 %collective-permute-start.12 = (bf16[1,256,512]{2,1,0:T(8,128)(2,1)S(1)}, bf16[1,256,512]{2,1,0:T(8,128)(2,1)S(1)}, u32[]{:S(2)}, u32[]{:S(2)}) collective-permute-start(bf16[1,256,512]{2,1,0:T(8,128)(2,1)S(1)} %get-tuple-element.59), channel_id=1, source_target_pairs={{0,24},{8,0},{16,8},{24,16},{1,25},{9,1},{17,9},{25,17},{2,26},{10... | collective-permute-start | bytes 786440 | tf_op jit(solution)/shard_map/ppermute | solution.py:80
  82.1 42.7 %collective-permute-start.6 = (bf16[1,256,512]{2,1,0:T(8,128)(2,1)S(1)}, bf16[1,256,512]{2,1,0:T(8,128)(2,1)S(1)}, u32[]{:S(2)}, u32[]{:S(2)}) collective-permute-start(bf16[1,256,512]{2,1,0:T(8,128)(2,1)S(1)} %get-tuple-element.53), channel_id=1, source_target_pairs={{0,24},{8,0},{16,8},{24,16},{1,25},{9,1},{17,9},{25,17},{2,26},{10... | collective-permute-start | bytes 786440 | tf_op jit(solution)/shard_map/ppermute | solution.py:80
  82.2 42.6 %collective-permute-start.5 = (bf16[1,256,512]{2,1,0:T(8,128)(2,1)S(1)}, bf16[1,256,512]{2,1,0:T(8,128)(2,1)S(1)}, u32[]{:S(2)}, u32[]{:S(2)}) collective-permute-start(bf16[1,256,512]{2,1,0:T(8,128)(2,1)S(1)} %get-tuple-element.54), channel_id=1, source_target_pairs={{0,16},{8,24},{16,0},{24,8},{1,17},{9,25},{17,1},{25,9},{2,18},{10... | collective-permute-start | bytes 786440 | tf_op jit(solution)/shard_map/ppermute | solution.py:80
  92.0 31.8 %collective-permute-start.4 = (bf16[1,256,512]{2,1,0:T(8,128)(2,1)S(1)}, bf16[1,256,512]{2,1,0:T(8,128)(2,1)}, u32[]{:S(2)}, u32[]{:S(2)}) collective-permute-start(bf16[1,256,512]{2,1,0:T(8,128)(2,1)S(1)} %get-tuple-element.55), channel_id=1, source_target_pairs={{0,8},{8,16},{16,24},{24,0},{1,9},{9,17},{17,25},{25,1},{2,10},{10... | collective-permute-start | bytes 786440 | tf_op jit(solution)/shard_map/ppermute | solution.py:80
  118.4 20.8 %all-to-all-start.2 = ((bf16[8,256,256]{2,1,0:T(8,128)(2,1)}), bf16[8,256,256]{2,1,0:T(8,128)(2,1)S(1)}, u32[]{:S(2)}, u32[]{:S(2)}) async-start(bf16[8,256,256]{2,1,0:T(8,128)(2,1)} %bitcast.267), calls=%async_computation.2 | async-start | bytes 2097152 | tf_op jit(solution)/shard_map/all_to_all | solution.py:96
  139.2 18.9 %all-to-all-start = ((bf16[8,256,256]{2,1,0:T(8,128)(2,1)}), bf16[8,256,256]{2,1,0:T(8,128)(2,1)S(1)}, u32[]{:S(2)}, u32[]{:S(2)}) async-start(bf16[8,256,256]{2,1,0:T(8,128)(2,1)} %bitcast.269), calls=%async_computation | async-start | bytes 2097152 | tf_op jit(solution)/shard_map/all_to_all | solution.py:96
  158.1 19.3 %all-to-all-start.3 = ((bf16[8,1,256,256]{3,2,1,0:T(8,128)(2,1)}), bf16[8,1,256,256]{3,2,1,0:T(8,128)(2,1)S(1)}, u32[]{:S(2)}, u32[]{:S(2)}) async-start(bf16[8,1,256,256]{3,2,1,0:T(8,128)(2,1)} %bitcast.52), calls=%async_computation.3 | async-start | bytes 2097152 | tf_op jit(solution)/shard_map/all_to_all | solution.py:110
  177.4 18.9 %all-to-all-start.1 = ((bf16[8,1,256,256]{3,2,1,0:T(8,128)(2,1)}), bf16[8,1,256,256]{3,2,1,0:T(8,128)(2,1)S(1)}, u32[]{:S(2)}, u32[]{:S(2)}) async-start(bf16[8,1,256,256]{3,2,1,0:T(8,128)(2,1)} %bitcast.32), calls=%async_computation.1 | async-start | bytes 2097152 | tf_op jit(solution)/shard_map/all_to_all | solution.py:110
  186.8 22.6 %collective-permute-start.13 = (bf16[1,256,512]{2,1,0:T(8,128)(2,1)S(1)}, bf16[1,256,512]{2,1,0:T(8,128)(2,1)S(1)}, u32[]{:S(2)}, u32[]{:S(2)}) collective-permute-start(bf16[1,256,512]{2,1,0:T(8,128)(2,1)S(1)} %get-tuple-element.58), channel_id=1, source_target_pairs={{0,8},{8,16},{16,24},{24,0},{1,9},{9,17},{17,25},{25,1},{2,10},{10... | collective-permute-start | bytes 786440 | tf_op jit(solution)/shard_map/ppermute | solution.py:80
  202.1 11.2 %collective-permute-start.7 = (bf16[1,256,512]{2,1,0:T(8,128)(2,1)S(1)}, bf16[1,256,512]{2,1,0:T(8,128)(2,1)S(1)}, u32[]{:S(2)}, u32[]{:S(2)}) collective-permute-start(bf16[1,256,512]{2,1,0:T(8,128)(2,1)S(1)} %get-tuple-element.52), channel_id=1, source_target_pairs={{0,8},{8,16},{16,24},{24,0},{1,9},{9,17},{17,25},{25,1},{2,10},{10... | collective-permute-start | bytes 786440 | tf_op jit(solution)/shard_map/ppermute | solution.py:80
  204.8 38.1 %collective-permute-start.15 = (bf16[1,256,512]{2,1,0:T(8,128)(2,1)S(1)}, bf16[1,256,512]{2,1,0:T(8,128)(2,1)S(1)}, u32[]{:S(2)}, u32[]{:S(2)}) collective-permute-start(bf16[1,256,512]{2,1,0:T(8,128)(2,1)S(1)} %get-tuple-element.56), channel_id=1, source_target_pairs={{0,24},{8,0},{16,8},{24,16},{1,25},{9,1},{17,9},{25,17},{2,26},{10... | collective-permute-start | bytes 786440 | tf_op jit(solution)/shard_map/ppermute | solution.py:80
  206.1 26.9 %collective-permute-start.14 = (bf16[1,256,512]{2,1,0:T(8,128)(2,1)S(1)}, bf16[1,256,512]{2,1,0:T(8,128)(2,1)S(1)}, u32[]{:S(2)}, u32[]{:S(2)}) collective-permute-start(bf16[1,256,512]{2,1,0:T(8,128)(2,1)S(1)} %get-tuple-element.57), channel_id=1, source_target_pairs={{0,16},{8,24},{16,0},{24,8},{1,17},{9,25},{17,1},{25,9},{2,18},{10... | collective-permute-start | bytes 786440 | tf_op jit(solution)/shard_map/ppermute | solution.py:80
  206.4 36.5 %collective-permute-start.9 = (bf16[1,256,512]{2,1,0:T(8,128)(2,1)S(1)}, bf16[1,256,512]{2,1,0:T(8,128)(2,1)S(1)}, u32[]{:S(2)}, u32[]{:S(2)}) collective-permute-start(bf16[1,256,512]{2,1,0:T(8,128)(2,1)S(1)} %get-tuple-element.50), channel_id=1, source_target_pairs={{0,24},{8,0},{16,8},{24,16},{1,25},{9,1},{17,9},{25,17},{2,26},{10... | collective-permute-start | bytes 786440 | tf_op jit(solution)/shard_map/ppermute | solution.py:80
  209.4 33.5 %collective-permute-start.8 = (bf16[1,256,512]{2,1,0:T(8,128)(2,1)S(1)}, bf16[1,256,512]{2,1,0:T(8,128)(2,1)S(1)}, u32[]{:S(2)}, u32[]{:S(2)}) collective-permute-start(bf16[1,256,512]{2,1,0:T(8,128)(2,1)S(1)} %get-tuple-element.51), channel_id=1, source_target_pairs={{0,16},{8,24},{16,0},{24,8},{1,17},{9,25},{17,1},{25,9},{2,18},{10... | collective-permute-start | bytes 786440 | tf_op jit(solution)/shard_map/ppermute | solution.py:80
  243.0 17.2 %collective-permute-start.16 = (bf16[8,1,512]{2,1,0:T(2,128)(2,1)S(1)}, bf16[8,1,512]{2,1,0:T(2,128)(2,1)S(1)}, u32[]{:S(2)}, u32[]{:S(2)}) collective-permute-start(bf16[8,1,512]{2,1,0:T(2,128)(2,1)S(1)} %get-tuple-element.34), channel_id=1, source_target_pairs={{0,1},{1,2},{2,3},{3,4},{4,5},{5,6},{6,7},{8,9},{9,10},{10,11},{11... | collective-permute-start | bytes 24584 | tf_op jit(solution)/shard_map/ppermute | solution.py:17
  244.3 15.9 %collective-permute-start.19 = (bf16[8,1,512]{2,1,0:T(2,128)(2,1)S(1)}, bf16[8,1,512]{2,1,0:T(2,128)(2,1)S(1)}, u32[]{:S(2)}, u32[]{:S(2)}) collective-permute-start(bf16[8,1,512]{2,1,0:T(2,128)(2,1)S(1)} %get-tuple-element.35), channel_id=1, source_target_pairs={{1,0},{2,1},{3,2},{4,3},{5,4},{6,5},{7,6},{9,8},{10,9},{11,10},{12... | collective-permute-start | bytes 24584 | tf_op jit(solution)/shard_map/ppermute | solution.py:17
  245.9 9.5 %collective-permute-start.17 = (bf16[8,256,1]{2,1,0:T(8,128)(2,1)S(1)}, bf16[8,256,1]{2,1,0:T(8,128)(2,1)S(1)}, u32[]{:S(2)}, u32[]{:S(2)}) collective-permute-start(bf16[8,256,1]{2,1,0:T(8,128)(2,1)S(1)} %get-tuple-element.32), channel_id=1, source_target_pairs={{0,8},{8,16},{16,24},{1,9},{9,17},{17,25},{2,10},{10,18},{18,26},{... | collective-permute-start | bytes 12296 | tf_op jit(solution)/shard_map/ppermute | solution.py:17
  247.5 12.8 %collective-permute-start.18 = (bf16[8,256,1]{2,1,0:T(8,128)(2,1)S(1)}, bf16[8,256,1]{2,1,0:T(8,128)(2,1)S(1)}, u32[]{:S(2)}, u32[]{:S(2)}) collective-permute-start(bf16[8,256,1]{2,1,0:T(8,128)(2,1)S(1)} %get-tuple-element.33), channel_id=1, source_target_pairs={{8,0},{16,8},{24,16},{9,1},{17,9},{25,17},{10,2},{18,10},{26,18},{... | collective-permute-start | bytes 12296 | tf_op jit(solution)/shard_map/ppermute | solution.py:17
  291.2 4.4 collective-permute-start.21
  299.4 8.7 %collective-permute-start.23 = (f32[2]{0:T(128)S(1)}, f32[2]{0:T(128)S(1)}, u32[]{:S(2)}, u32[]{:S(2)}) collective-permute-start(f32[2]{0:T(128)S(1)} %add.505), channel_id=1, source_target_pairs={{0,2},{1,3},{2,0},{3,1},{4,6},{5,7},{6,4},{7,5},{8,10},{9,11},{10,... | collective-permute-start | bytes 32 | tf_op jit(solution)/shard_map/ppermute | solution.py:43
  318.6 36.1 %collective-permute-start.32 = (bf16[1,256,512]{2,1,0:T(8,128)(2,1)S(1)}, bf16[1,256,512]{2,1,0:T(8,128)(2,1)S(1)}, u32[]{:S(2)}, u32[]{:S(2)}) collective-permute-start(bf16[1,256,512]{2,1,0:T(8,128)(2,1)S(1)} %get-tuple-element.48), channel_id=1, source_target_pairs={{0,16},{8,24},{16,0},{24,8},{1,17},{9,25},{17,1},{25,9},{2,18},{10... | collective-permute-start | bytes 786440 | tf_op jit(solution)/shard_map/ppermute | solution.py:80
  320.9 14.1 %collective-permute-start.31 = (bf16[1,256,512]{2,1,0:T(8,128)(2,1)S(1)}, bf16[1,256,512]{2,1,0:T(8,128)(2,1)S(1)}, u32[]{:S(2)}, u32[]{:S(2)}) collective-permute-start(bf16[1,256,512]{2,1,0:T(8,128)(2,1)S(1)} %get-tuple-element.49), channel_id=1, source_target_pairs={{0,8},{8,16},{16,24},{24,0},{1,9},{9,17},{17,25},{25,1},{2,10},{10... | collective-permute-start | bytes 786440 | tf_op jit(solution)/shard_map/ppermute | solution.py:80
  321.3 44.1 %collective-permute-start.33 = (bf16[1,256,512]{2,1,0:T(8,128)(2,1)S(1)}, bf16[1,256,512]{2,1,0:T(8,128)(2,1)S(1)}, u32[]{:S(2)}, u32[]{:S(2)}) collective-permute-start(bf16[1,256,512]{2,1,0:T(8,128)(2,1)S(1)} %get-tuple-element.47), channel_id=1, source_target_pairs={{0,24},{8,0},{16,8},{24,16},{1,25},{9,1},{17,9},{25,17},{2,26},{10... | collective-permute-start | bytes 786440 | tf_op jit(solution)/shard_map/ppermute | solution.py:80
  325.1 40.3 %collective-permute-start.27 = (bf16[1,256,512]{2,1,0:T(8,128)(2,1)S(1)}, bf16[1,256,512]{2,1,0:T(8,128)(2,1)S(1)}, u32[]{:S(2)}, u32[]{:S(2)}) collective-permute-start(bf16[1,256,512]{2,1,0:T(8,128)(2,1)S(1)} %get-tuple-element.41), channel_id=1, source_target_pairs={{0,24},{8,0},{16,8},{24,16},{1,25},{9,1},{17,9},{25,17},{2,26},{10... | collective-permute-start | bytes 786440 | tf_op jit(solution)/shard_map/ppermute | solution.py:80
  325.2 40.2 %collective-permute-start.26 = (bf16[1,256,512]{2,1,0:T(8,128)(2,1)S(1)}, bf16[1,256,512]{2,1,0:T(8,128)(2,1)S(1)}, u32[]{:S(2)}, u32[]{:S(2)}) collective-permute-start(bf16[1,256,512]{2,1,0:T(8,128)(2,1)S(1)} %get-tuple-element.42), channel_id=1, source_target_pairs={{0,16},{8,24},{16,0},{24,8},{1,17},{9,25},{17,1},{25,9},{2,18},{10... | collective-permute-start | bytes 786440 | tf_op jit(solution)/shard_map/ppermute | solution.py:80
  334.9 23.6 %collective-permute-start.25 = (bf16[1,256,512]{2,1,0:T(8,128)(2,1)S(1)}, bf16[1,256,512]{2,1,0:T(8,128)(2,1)S(1)}, u32[]{:S(2)}, u32[]{:S(2)}) collective-permute-start(bf16[1,256,512]{2,1,0:T(8,128)(2,1)S(1)} %get-tuple-element.43), channel_id=1, source_target_pairs={{0,8},{8,16},{16,24},{24,0},{1,9},{9,17},{17,25},{25,1},{2,10},{10... | collective-permute-start | bytes 786440 | tf_op jit(solution)/shard_map/ppermute | solution.py:80
  369.0 18.9 %all-to-all-start.4 = ((bf16[8,256,256]{2,1,0:T(8,128)(2,1)}), bf16[8,256,256]{2,1,0:T(8,128)(2,1)S(1)}, u32[]{:S(2)}, u32[]{:S(2)}) async-start(bf16[8,256,256]{2,1,0:T(8,128)(2,1)} %bitcast.265), calls=%async_computation.4 | async-start | bytes 2097152 | tf_op jit(solution)/shard_map/all_to_all | solution.py:96
  387.9 18.9 %all-to-all-start.6 = ((bf16[8,256,256]{2,1,0:T(8,128)(2,1)}), bf16[8,256,256]{2,1,0:T(8,128)(2,1)S(1)}, u32[]{:S(2)}, u32[]{:S(2)}) async-start(bf16[8,256,256]{2,1,0:T(8,128)(2,1)} %bitcast.263), calls=%async_computation.6 | async-start | bytes 2097152 | tf_op jit(solution)/shard_map/all_to_all | solution.py:96
  406.8 19.3 %all-to-all-start.5 = ((bf16[8,1,256,256]{3,2,1,0:T(8,128)(2,1)}), bf16[8,1,256,256]{3,2,1,0:T(8,128)(2,1)S(1)}, u32[]{:S(2)}, u32[]{:S(2)}) async-start(bf16[8,1,256,256]{3,2,1,0:T(8,128)(2,1)} %bitcast.74), calls=%async_computation.5 | async-start | bytes 2097152 | tf_op jit(solution)/shard_map/all_to_all | solution.py:110
  426.1 18.9 %all-to-all-start.7 = ((bf16[8,1,256,256]{3,2,1,0:T(8,128)(2,1)}), bf16[8,1,256,256]{3,2,1,0:T(8,128)(2,1)S(1)}, u32[]{:S(2)}, u32[]{:S(2)}) async-start(bf16[8,1,256,256]{3,2,1,0:T(8,128)(2,1)} %bitcast.92), calls=%async_computation.7 | async-start | bytes 2097152 | tf_op jit(solution)/shard_map/all_to_all | solution.py:110
  435.5 20.1 %collective-permute-start.28 = (bf16[1,256,512]{2,1,0:T(8,128)(2,1)S(1)}, bf16[1,256,512]{2,1,0:T(8,128)(2,1)S(1)}, u32[]{:S(2)}, u32[]{:S(2)}) collective-permute-start(bf16[1,256,512]{2,1,0:T(8,128)(2,1)S(1)} %get-tuple-element.40), channel_id=1, source_target_pairs={{0,8},{8,16},{16,24},{24,0},{1,9},{9,17},{17,25},{25,1},{2,10},{10... | collective-permute-start | bytes 786440 | tf_op jit(solution)/shard_map/ppermute | solution.py:80
  450.8 12.1 %collective-permute-start.29 = (bf16[1,256,512]{2,1,0:T(8,128)(2,1)S(1)}, bf16[1,256,512]{2,1,0:T(8,128)(2,1)S(1)}, u32[]{:S(2)}, u32[]{:S(2)}) collective-permute-start(bf16[1,256,512]{2,1,0:T(8,128)(2,1)S(1)} %get-tuple-element.39), channel_id=1, source_target_pairs={{0,16},{8,24},{16,0},{24,8},{1,17},{9,25},{17,1},{25,9},{2,18},{10... | collective-permute-start | bytes 786440 | tf_op jit(solution)/shard_map/ppermute | solution.py:80
  451.7 12.9 %collective-permute-start.30 = (bf16[1,256,512]{2,1,0:T(8,128)(2,1)S(1)}, bf16[1,256,512]{2,1,0:T(8,128)(2,1)S(1)}, u32[]{:S(2)}, u32[]{:S(2)}) collective-permute-start(bf16[1,256,512]{2,1,0:T(8,128)(2,1)S(1)} %get-tuple-element.38), channel_id=1, source_target_pairs={{0,24},{8,0},{16,8},{24,16},{1,25},{9,1},{17,9},{25,17},{2,26},{10... | collective-permute-start | bytes 786440 | tf_op jit(solution)/shard_map/ppermute | solution.py:80
  452.4 36.6 %collective-permute-start.36 = (bf16[1,256,512]{2,1,0:T(8,128)(2,1)S(1)}, bf16[1,256,512]{2,1,0:T(8,128)(2,1)S(1)}, u32[]{:S(2)}, u32[]{:S(2)}) collective-permute-start(bf16[1,256,512]{2,1,0:T(8,128)(2,1)S(1)} %get-tuple-element.44), channel_id=1, source_target_pairs={{0,24},{8,0},{16,8},{24,16},{1,25},{9,1},{17,9},{25,17},{2,26},{10... | collective-permute-start | bytes 786440 | tf_op jit(solution)/shard_map/ppermute | solution.py:80
  455.6 33.4 %collective-permute-start.35 = (bf16[1,256,512]{2,1,0:T(8,128)(2,1)S(1)}, bf16[1,256,512]{2,1,0:T(8,128)(2,1)S(1)}, u32[]{:S(2)}, u32[]{:S(2)}) collective-permute-start(bf16[1,256,512]{2,1,0:T(8,128)(2,1)S(1)} %get-tuple-element.45), channel_id=1, source_target_pairs={{0,16},{8,24},{16,0},{24,8},{1,17},{9,25},{17,1},{25,9},{2,18},{10... | collective-permute-start | bytes 786440 | tf_op jit(solution)/shard_map/ppermute | solution.py:80
  455.6 22.5 %collective-permute-start.34 = (bf16[1,256,512]{2,1,0:T(8,128)(2,1)S(1)}, bf16[1,256,512]{2,1,0:T(8,128)(2,1)S(1)}, u32[]{:S(2)}, u32[]{:S(2)}) collective-permute-start(bf16[1,256,512]{2,1,0:T(8,128)(2,1)S(1)} %get-tuple-element.46), channel_id=1, source_target_pairs={{0,8},{8,16},{16,24},{24,0},{1,9},{9,17},{17,25},{25,1},{2,10},{10... | collective-permute-start | bytes 786440 | tf_op jit(solution)/shard_map/ppermute | solution.py:80
  489.1 18.0 %collective-permute-start.37 = (bf16[8,1,512]{2,1,0:T(2,128)(2,1)S(1)}, bf16[8,1,512]{2,1,0:T(2,128)(2,1)S(1)}, u32[]{:S(2)}, u32[]{:S(2)}) collective-permute-start(bf16[8,1,512]{2,1,0:T(2,128)(2,1)S(1)} %get-tuple-element.28), channel_id=1, source_target_pairs={{0,1},{1,2},{2,3},{3,4},{4,5},{5,6},{6,7},{8,9},{9,10},{10,11},{11... | collective-permute-start | bytes 24584 | tf_op jit(solution)/shard_map/ppermute | solution.py:17
  490.4 16.7 %collective-permute-start.40 = (bf16[8,1,512]{2,1,0:T(2,128)(2,1)S(1)}, bf16[8,1,512]{2,1,0:T(2,128)(2,1)S(1)}, u32[]{:S(2)}, u32[]{:S(2)}) collective-permute-start(bf16[8,1,512]{2,1,0:T(2,128)(2,1)S(1)} %get-tuple-element.29), channel_id=1, source_target_pairs={{1,0},{2,1},{3,2},{4,3},{5,4},{6,5},{7,6},{9,8},{10,9},{11,10},{12... | collective-permute-start | bytes 24584 | tf_op jit(solution)/shard_map/ppermute | solution.py:17
  491.9 10.1 %collective-permute-start.38 = (bf16[8,256,1]{2,1,0:T(8,128)(2,1)S(1)}, bf16[8,256,1]{2,1,0:T(8,128)(2,1)S(1)}, u32[]{:S(2)}, u32[]{:S(2)}) collective-permute-start(bf16[8,256,1]{2,1,0:T(8,128)(2,1)S(1)} %get-tuple-element.26), channel_id=1, source_target_pairs={{0,8},{8,16},{16,24},{1,9},{9,17},{17,25},{2,10},{10,18},{18,26},{... | collective-permute-start | bytes 12296 | tf_op jit(solution)/shard_map/ppermute | solution.py:17
  493.9 13.2 %collective-permute-start.39 = (bf16[8,256,1]{2,1,0:T(8,128)(2,1)S(1)}, bf16[8,256,1]{2,1,0:T(8,128)(2,1)S(1)}, u32[]{:S(2)}, u32[]{:S(2)}) collective-permute-start(bf16[8,256,1]{2,1,0:T(8,128)(2,1)S(1)} %get-tuple-element.27), channel_id=1, source_target_pairs={{8,0},{16,8},{24,16},{9,1},{17,9},{25,17},{10,2},{18,10},{26,18},{... | collective-permute-start | bytes 12296 | tf_op jit(solution)/shard_map/ppermute | solution.py:17
  541.7 4.4 collective-permute-start.42
  551.2 8.5 %collective-permute-start.44 = (f32[4]{0:T(128)S(1)}, f32[4]{0:T(128)S(1)}, u32[]{:S(2)}, u32[]{:S(2)}) collective-permute-start(f32[4]{0:T(128)S(1)} %add.515), channel_id=1, source_target_pairs={{0,2},{1,3},{2,0},{3,1},{4,6},{5,7},{6,4},{7,5},{8,10},{9,11},{10,... | collective-permute-start | bytes 56 | tf_op jit(solution)/shard_map/ppermute | solution.py:43
  (24 other events, 354.4 us)

commit v6 on v5

--- a/solution.py
+++ b/solution.py
@@ -35,14 +35,10 @@
 
 
 def all_sum(values):
-    for axis in ("px", "py"):
-        size = lax.axis_size(axis)
-        step = 1
-        while step < size:
-            pairs = [(i, i ^ step) for i in range(size)]
-            values = values + lax.ppermute(values, axis, pairs)
-            step *= 2
-    return values
+    axes = ("px", "py")
+    count = lax.axis_size(axes)
+    spread = jnp.broadcast_to(values[None], (count,) + values.shape)
+    return jnp.sum(lax.all_to_all(spread, axes, 0, 0, tiled=True), 0)
 
 
 def face_sum(padded, coeff_pad):
@@ -84,9 +80,8 @@
     return result
 
 
-def precondition_levels(residual, first_level, eigenvectors, eigenvalues, level_shift):
+def precondition_lines(lines, first_level, eigenvectors, eigenvalues, level_shift):
     across = lax.axis_size("py")
-    lines = exchange(residual.astype(jnp.bfloat16), "px", 0, 2)
     levels_here, rows, width = lines.shape
     cols = width // across
     first = jnp.dot(
@@ -122,12 +117,12 @@
     chunk = lax.axis_size("px")
     if levels % chunk or levels == chunk:
         chunk = levels
-    parts = [
-        precondition_levels(
-            residual[start : start + chunk], start, eigenvectors, eigenvalues, level_shift
-        )
-        for start in range(0, levels, chunk)
-    ]
+    parts = []
+    waiting = residual
+    for start in range(0, levels, chunk):
+        lines = exchange(waiting[start : start + chunk].astype(jnp.bfloat16), "px", 0, 2)
+        lines, waiting = lax.optimization_barrier((lines, waiting))
+        parts.append(precondition_lines(lines, start, eigenvectors, eigenvalues, level_shift))
     return jnp.concatenate(parts, 0)
 
 

time: 586 us -> 546 us (0.932)
  starting transfers between devices: 148 us -> 113 us
  waiting for transfers between devices: 183 us -> 151 us
  blocking collectives: 0 us -> 26.3 us
  local copies, waits for them, and re-layouts: 28.2 us -> 37.2 us
  other arithmetic: 129 us -> 121 us
    ppermute x10 -> x0, starting transfers between devices: 28.7 us -> none  [all_sum(): values = values + lax.ppermute(values, axis, pairs)]
    all_to_all x0 -> x2, blocking collectives: none -> 26.3 us  [all_sum(): return jnp.sum(lax.all_to_all(spread, axes, 0, 0, tiled=True), 0)]
    all_to_all x8, waiting for transfers between devices: 44.5 us -> 18.4 us  [the longest x4 12.4 us: precondition_lines(): returned = lax.all_to_all(outgoing, 'py', 0, 0, tiled=True)]
    another operation x2 -> x0, other arithmetic: 17.5 us -> none
    ppermute x10 -> x0, waiting for transfers between devices: 16.7 us -> none  [all_sum(): values = values + lax.ppermute(values, axis, pairs)]
    sub x0 -> x1, other arithmetic: none -> 11.2 us  [shards(): residual = right_side - face_sum(stacked[0], coeff_pad)]
    ppermute x24, starting transfers between devices: 67.1 us -> 56.7 us  [exchange(): lax.ppermute(part, axis, [(i, (i + shift) % size) for i in range(size)])]
    add x10 -> x0, other arithmetic: 7.84 us -> none  [all_sum(): values = values + lax.ppermute(values, axis, pairs)]
  transfers between devices with their start and end apart: 54 -> 44, of which waited for: 34 -> 25; matrix products, arithmetic and copies ran while one was open for 17% -> 20% of each run, Pallas kernels for 0% -> 0%
where the time goes in v6:
time: 546 us; the launch traced here: 542 us
  waiting for transfers between devices  151 us (28%)
  other arithmetic  121 us (22%)
  starting transfers between devices  113 us (21%)
  matrix products  86.6 us (16%)
  local copies, waits for them, and re-layouts  37.2 us (7%)
  blocking collectives  26.3 us (5%)
  between operations  7.61 us (1%)
    ppermute x24, waiting for transfers between devices, exchange(): lax.ppermute(part, axis, [(i, (i + shift) % size) for i in range(size)])  101 us
    ppermute x24, starting transfers between devices, exchange(): lax.ppermute(part, axis, [(i, (i + shift) % size) for i in range(size)])  56.7 us
    dot_general x4, matrix products, precondition_lines(): jnp.einsum('yj,kji->kyi', eigenvectors, scaled, preferred_element_type=jn...  44.2 us
    reduce_sum x2, other arithmetic, shards(): jnp.sum(residual * precond)  27.5 us
    all_to_all x2, blocking collectives, all_sum(): return jnp.sum(lax.all_to_all(spread, axes, 0, 0, tiled=True), 0)  26.3 us
    dot_general x4, matrix products, precondition_lines(): jnp.einsum('qkyi,qix->kyx', returned, eigenvectors.reshape(across, cols,...  22.8 us
    dot_general x4, matrix products, precondition_lines(): jnp.dot(lines.reshape(levels_here * rows, width), eigenvectors, preferred...  19.6 us
    ppermute x6, starting transfers between devices, padded_2(): lax.ppermute(last, axis, up)  18 us
  transfers between devices with their start and end apart: 44, of which 25 were waited for; matrix products, arithmetic and copies ran while one was open for 20% of the time, Pallas kernels for 0%

profile of v6, /device:TPU:0, one launch (start us, length us, event | category | flops | bytes accessed | tf_op | source)
XLA Modules:
  0.0 542.0 jit_solution(123476741148592540)
XLA Ops:
  5.1 14.6 %fusion.79 = bf16[1,8,256,512]{3,2,1,0:T(8,128)(2,1)S(1)} fusion(bf16[]{:T(256)} %bitcast.16, s32[8,256,512]{2,1,0:T(8,128)S(1)} %copy-done.11, bf16[]{:T(256)} %bitcast.15, bf16[]{:T(256)} %bitcast.14, bf16[]{:T(256)} %bitcast.13, bf16[]{:T(256)} %bitcast.12, bf16[]{:T(256)} %bitcast.11, bf16[]{:T(256)} %bitcast.10, bf16[]{:T(256)} %bitcast.9, ...), kind=kLoop, calls=%fused_computation.158 | loop fusion | flops 33554432 | bytes 6291488 | tf_op jit(solution)/shard_map/stack | solution.py:139
  38.2 13.2 %fusion.3 = f32[2,8,258,514]{3,2,1,0:T(8,128)} fusion(bf16[2,8,1,512]{3,2,1,0:T(2,128)(2,1)S(1)} %collective-permute-done.3, bf16[2,8,1,512]{3,2,1,0:T(2,128)(2,1)S(1)} %collective-permute-done, bf16[2,8,256,1]{3,2,1,0:T(8,128)(2,1)} %copy.79, bf16[1,8,256,512]{3,2,1,0:T(8,128)(2,1)} %copy-done.9, bf16[1,8,256,512]{3,2,1,0:T(8,128)(2,1)S(1)} %convert_bitcast_fusion, ...), kind=kLoop, calls=%fused_computation.14 | loop fusion | flops 33948672 | bytes 12730624 | tf_op jit(solution)/shard_map/convert_element_type | solution.py:140
  51.4 4.8 slice_bitcast_fusion.1
  56.2 5.9 %fusion.51 = f32[7,256,512]{2,1,0:T(8,128)} fusion(f32[8,258,514]{2,1,0:T(8,128)S(1)} %get-tuple-element.31, f32[8,258,514]{2,1,0:T(8,128)S(1)} %get-tuple-element.30), kind=kLoop, calls=%fused_computation.88 | loop fusion | flops 3670016 | bytes 18350080 | tf_op jit(solution)/shard_map/mul | solution.py:54
  62.2 11.2 %fusion.39 = f32[8,256,512]{2,1,0:T(8,128)S(1)} fusion(f32[8,256,512]{2,1,0:T(8,128)} %param.7, f32[8,258,514]{2,1,0:T(8,128)S(1)} %get-tuple-element.31, f32[7,256,512]{2,1,0:T(8,128)} %fusion.51, f32[8,258,514]{2,1,0:T(8,128)S(1)} %get-tuple-element.30), kind=kLoop, calls=%fused_computation.63 | loop fusion | flops 23068672 | bytes 54001664 | tf_op jit(solution)/shard_map/sub | solution.py:143
  82.3 4.7 collective-permute-done.4
  87.0 11.1 %collective-permute-done.5 = bf16[1,256,512]{2,1,0:T(8,128)(2,1)S(1)} collective-permute-done((bf16[1,256,512]{2,1,0:T(8,128)(2,1)S(1)}, bf16[1,256,512]{2,1,0:T(8,128)(2,1)S(1)}, u32[]{:S(2)}, u32[]{:S(2)}) %collective-permute-start.5) | collective-permute-done | bytes 262176 | tf_op jit(solution)/shard_map/ppermute | solution.py:76
  100.9 7.2 %collective-permute-start.12 = (bf16[1,256,512]{2,1,0:T(8,128)(2,1)S(1)}, bf16[1,256,512]{2,1,0:T(8,128)(2,1)S(1)}, u32[]{:S(2)}, u32[]{:S(2)}) collective-permute-start(bf16[1,256,512]{2,1,0:T(8,128)(2,1)S(1)} %get-tuple-element.64), channel_id=1, source_target_pairs={{0,24},{8,0},{16,8},{24,16},{1,25},{9,1},{17,9},{25,17},{2,26},{10... | collective-permute-start | bytes 786440 | tf_op jit(solution)/shard_map/ppermute | solution.py:76
  108.7 5.7 %convolution_convert_fusion.7 = bf16[256,2048]{1,0:T(8,128)(2,1)S(1)} fusion(bf16[2048,2048]{1,0:T(8,128)(2,1)} %param.11, bf16[1,256,2048]{2,1,0:T(8,128)(2,1)S(1)} %constant_dynamic-update-slice_fusion.20), kind=kOutput, calls=%fused_computation.140 | convolution fusion | flops 2148007936 | bytes 10485760 | tf_op jit(solution)/shard_map/dot_general | solution.py:87
  119.0 7.0 %collective-permute-done.10 = bf16[1,256,512]{2,1,0:T(8,128)(2,1)S(1)} collective-permute-done((bf16[1,256,512]{2,1,0:T(8,128)(2,1)}, bf16[1,256,512]{2,1,0:T(8,128)(2,1)S(1)}, u32[]{:S(2)}, u32[]{:S(2)}) %collective-permute-start.10) | collective-permute-done | bytes 262176 | tf_op jit(solution)/shard_map/ppermute | solution.py:76
  126.0 5.5 %collective-permute-done.11 = bf16[1,256,512]{2,1,0:T(8,128)(2,1)S(1)} collective-permute-done((bf16[1,256,512]{2,1,0:T(8,128)(2,1)S(1)}, bf16[1,256,512]{2,1,0:T(8,128)(2,1)S(1)}, u32[]{:S(2)}, u32[]{:S(2)}) %collective-permute-start.11) | collective-permute-done | bytes 262176 | tf_op jit(solution)/shard_map/ppermute | solution.py:76
  131.6 5.7 %convolution_convert_fusion.5 = bf16[256,2048]{1,0:T(8,128)(2,1)S(1)} fusion(bf16[2048,2048]{1,0:T(8,128)(2,1)} %param.11, bf16[1,256,2048]{2,1,0:T(8,128)(2,1)S(1)} %constant_dynamic-update-slice_fusion.14), kind=kOutput, calls=%fused_computation.138 | convolution fusion | flops 2148007936 | bytes 10485760 | tf_op jit(solution)/shard_map/dot_general | solution.py:87
  142.0 11.0 %fusion.67 = bf16[1,2048,256]{1,2,0:T(8,128)(2,1)S(1)} fusion(bf16[2048,2048]{1,0:T(8,128)(2,1)} %param.11, bf16[2048,256]{1,0:T(8,128)(2,1)S(1)} %bitcast.251, f32[]{:T(128)} %bitcast.25, f32[256]{0:T(256)S(1)} %dynamic_slice.114, f32[2048]{0:T(1024)S(1)} %copy-done.13), kind=kOutput, calls=%fused_computation.141 | convolution fusion | flops 4297588736 | bytes 10494980 | tf_op jit(solution)/shard_map/yj,kji->kyi/dot_general | solution.py:101
  161.3 11.1 %fusion.68 = bf16[1,2048,256]{1,2,0:T(8,128)(2,1)S(1)} fusion(bf16[2048,2048]{1,0:T(8,128)(2,1)} %param.11, bf16[2048,256]{1,0:T(8,128)(2,1)S(1)} %bitcast.253, f32[]{:T(128)} %bitcast.42, f32[256]{0:T(256)S(1)} %dynamic_slice.114, f32[2048]{0:T(1024)S(1)} %copy-done.13), kind=kOutput, calls=%fused_computation.142 | convolution fusion | flops 4297588736 | bytes 10494980 | tf_op jit(solution)/shard_map/yj,kji->kyi/dot_general | solution.py:101
  180.2 5.7 %fusion.63 = bf16[256,2048]{1,0:T(8,128)(2,1)S(1)} fusion(bf16[8,256,2048]{2,1,0:T(8,128)(2,1)} %bitcast.258, bf16[8,1,256,256]{3,2,1,0:T(8,128)(2,1)S(1)} %all-to-all-done.1), kind=kOutput, calls=%fused_computation.129 | convolution fusion | flops 2148007936 | bytes 10485760 | tf_op jit(solution)/shard_map/qkyi,qix->kyx/dot_general | solution.py:106
  190.7 7.3 %collective-permute-done.7 = bf16[1,256,512]{2,1,0:T(8,128)(2,1)} collective-permute-done((bf16[1,256,512]{2,1,0:T(8,128)(2,1)}, bf16[1,256,512]{2,1,0:T(8,128)(2,1)}, u32[]{:S(2)}, u32[]{:S(2)}) %collective-permute-start.7) | collective-permute-done | bytes 262176 | tf_op jit(solution)/shard_map/ppermute | solution.py:76
  199.0 5.7 %fusion.64 = bf16[256,2048]{1,0:T(8,128)(2,1)S(1)} fusion(bf16[8,256,2048]{2,1,0:T(8,128)(2,1)} %bitcast.259, bf16[8,1,256,256]{3,2,1,0:T(8,128)(2,1)S(1)} %all-to-all-done.3), kind=kOutput, calls=%fused_computation.130 | convolution fusion | flops 2148007936 | bytes 10485760 | tf_op jit(solution)/shard_map/qkyi,qix->kyx/dot_general | solution.py:106
  204.8 9.3 %collective-permute-start.13 = (bf16[1,256,512]{2,1,0:T(8,128)(2,1)S(1)}, bf16[1,256,512]{2,1,0:T(8,128)(2,1)S(1)}, u32[]{:S(2)}, u32[]{:S(2)}) collective-permute-start(bf16[1,256,512]{2,1,0:T(8,128)(2,1)S(1)} %get-tuple-element.63), channel_id=1, source_target_pairs={{0,8},{8,16},{16,24},{24,0},{1,9},{9,17},{17,25},{25,1},{2,10},{10... | collective-permute-start | bytes 786440 | tf_op jit(solution)/shard_map/ppermute | solution.py:76
  214.2 5.3 collective-permute-done.8
  221.8 9.1 %collective-permute-done.14 = bf16[1,256,512]{2,1,0:T(8,128)(2,1)S(1)} collective-permute-done((bf16[1,256,512]{2,1,0:T(8,128)(2,1)S(1)}, bf16[1,256,512]{2,1,0:T(8,128)(2,1)S(1)}, u32[]{:S(2)}, u32[]{:S(2)}) %collective-permute-start.14) | collective-permute-done | bytes 262176 | tf_op jit(solution)/shard_map/ppermute | solution.py:76
  237.9 5.6 %collective-permute-start.17 = (bf16[8,256,1]{2,1,0:T(8,128)(2,1)S(1)}, bf16[8,256,1]{2,1,0:T(8,128)(2,1)S(1)}, u32[]{:S(2)}, u32[]{:S(2)}) collective-permute-start(bf16[8,256,1]{2,1,0:T(8,128)(2,1)S(1)} %get-tuple-element.40), channel_id=1, source_target_pairs={{0,8},{8,16},{16,24},{1,9},{9,17},{17,25},{2,10},{10,18},{18,26},{... | collective-permute-start | bytes 12296 | tf_op jit(solution)/shard_map/ppermute | solution.py:17
  245.2 8.7 %collective-permute-done.17 = bf16[8,256,1]{2,1,0:T(8,128)(2,1)S(1)} collective-permute-done((bf16[8,256,1]{2,1,0:T(8,128)(2,1)S(1)}, bf16[8,256,1]{2,1,0:T(8,128)(2,1)S(1)}, u32[]{:S(2)}, u32[]{:S(2)}) %collective-permute-start.17) | collective-permute-done | bytes 4128 | tf_op jit(solution)/shard_map/ppermute | solution.py:17
  253.8 4.8 collective-permute-done.18
  258.7 6.4 %fusion.59 = f32[8,258,514]{2,1,0:T(8,128)S(1)} fusion(bf16[8,1,512]{2,1,0:T(2,128)(2,1)S(1)} %collective-permute-done.19, bf16[8,1,512]{2,1,0:T(2,128)(2,1)S(1)} %collective-permute-done.16, bf16[8,256,1]{2,1,0:T(8,128)(2,1)S(1)} %collective-permute-done.18, bf16[4,256,512]{2,1,0:T(8,128)(2,1)S(1)} %constant_dynamic-update-slice_fusion.10, ...), kind=kLoop, calls=%fused_computation.125 | loop fusion | flops 16974336 | bytes 6365312 | tf_op jit(solution)/shard_map/convert_element_type | solution.py:130
  265.1 5.9 %fusion.50 = f32[7,256,512]{2,1,0:T(8,128)} fusion(f32[8,258,514]{2,1,0:T(8,128)S(1)} %fusion.59, f32[8,258,514]{2,1,0:T(8,128)S(1)} %bitcast.247), kind=kLoop, calls=%fused_computation.86 | loop fusion | flops 3670016 | bytes 18350080 | tf_op jit(solution)/shard_map/mul | solution.py:54
  271.0 13.4 %fusion.12 = (f32[]{:T(128)}, f32[]{:T(128)}, f32[8,256,512]{2,1,0:T(8,128)}) fusion(f32[8,256,512]{2,1,0:T(8,128)} %copy-done.4, bf16[4,256,512]{2,1,0:T(8,128)(2,1)} %copy-done.3, bf16[4,256,512]{2,1,0:T(8,128)(2,1)} %copy-done.2, f32[7,256,512]{2,1,0:T(8,128)} %fusion.50, f32[8,258,514]{2,1,0:T(8,128)S(1)} %fusion.59, f32[8,258,514]{2,1,0:T(8,128)S(1)} %bitcast.247), kind=kLoop, calls=%fused_computation.27 | loop fusion | flops 28311552 | bytes 56098824 | tf_op jit(solution)/shard_map/reduce_sum | solution.py:150
  285.7 12.6 %all_to_all.52 = f32[32,1,2]{2,1,0:T(1,128)S(1)} all-to-all(f32[32,1,2]{2,1,0:T(1,128)S(1)} %broadcast_in_dim.93), channel_id=1, replica_groups=mesh['px'=4,'py'=8] {'px','py'}, dimensions={0} | all-to-all | bytes 512 | tf_op jit(solution)/shard_map/all_to_all | solution.py:41
  300.2 4.7 multiply_subtract_fusion.1
  309.2 7.3 %collective-permute-done.20 = bf16[1,256,512]{2,1,0:T(8,128)(2,1)S(1)} collective-permute-done((bf16[1,256,512]{2,1,0:T(8,128)(2,1)S(1)}, bf16[1,256,512]{2,1,0:T(8,128)(2,1)S(1)}, u32[]{:S(2)}, u32[]{:S(2)}) %collective-permute-start.20) | collective-permute-done | bytes 262176 | tf_op jit(solution)/shard_map/ppermute | solution.py:76
  316.5 10.2 %collective-permute-done.21 = bf16[1,256,512]{2,1,0:T(8,128)(2,1)S(1)} collective-permute-done((bf16[1,256,512]{2,1,0:T(8,128)(2,1)S(1)}, bf16[1,256,512]{2,1,0:T(8,128)(2,1)S(1)}, u32[]{:S(2)}, u32[]{:S(2)}) %collective-permute-start.21) | collective-permute-done | bytes 262176 | tf_op jit(solution)/shard_map/ppermute | solution.py:76
  327.8 5.0 collective-permute-start.28
  341.8 8.4 %collective-permute-done.26 = bf16[1,256,512]{2,1,0:T(8,128)(2,1)S(1)} collective-permute-done((bf16[1,256,512]{2,1,0:T(8,128)(2,1)}, bf16[1,256,512]{2,1,0:T(8,128)(2,1)S(1)}, u32[]{:S(2)}, u32[]{:S(2)}) %collective-permute-start.26) | collective-permute-done | bytes 262176 | tf_op jit(solution)/shard_map/ppermute | solution.py:76
  350.3 6.5 %collective-permute-done.27 = bf16[1,256,512]{2,1,0:T(8,128)(2,1)S(1)} collective-permute-done((bf16[1,256,512]{2,1,0:T(8,128)(2,1)S(1)}, bf16[1,256,512]{2,1,0:T(8,128)(2,1)S(1)}, u32[]{:S(2)}, u32[]{:S(2)}) %collective-permute-start.27) | collective-permute-done | bytes 262176 | tf_op jit(solution)/shard_map/ppermute | solution.py:76
  356.9 5.7 %convolution_convert_fusion.1 = bf16[256,2048]{1,0:T(8,128)(2,1)S(1)} fusion(bf16[2048,2048]{1,0:T(8,128)(2,1)} %param.11, bf16[1,256,2048]{2,1,0:T(8,128)(2,1)S(1)} %constant_dynamic-update-slice_fusion), kind=kOutput, calls=%fused_computation.134 | convolution fusion | flops 2148007936 | bytes 10485760 | tf_op jit(solution)/shard_map/dot_general | solution.py:87
  367.2 11.0 %fusion.69 = bf16[1,2048,256]{1,2,0:T(8,128)(2,1)S(1)} fusion(bf16[2048,2048]{1,0:T(8,128)(2,1)} %param.11, bf16[2048,256]{1,0:T(8,128)(2,1)S(1)} %bitcast.250, f32[]{:T(128)} %bitcast.25, f32[256]{0:T(256)S(1)} %dynamic_slice.114, f32[2048]{0:T(1024)S(1)} %copy-done.13), kind=kOutput, calls=%fused_computation.143 | convolution fusion | flops 4297588736 | bytes 10494980 | tf_op jit(solution)/shard_map/yj,kji->kyi/dot_general | solution.py:101
  386.5 11.1 %fusion.70 = bf16[1,2048,256]{1,2,0:T(8,128)(2,1)S(1)} fusion(bf16[2048,2048]{1,0:T(8,128)(2,1)} %param.11, bf16[2048,256]{1,0:T(8,128)(2,1)S(1)} %bitcast.252, f32[]{:T(128)} %bitcast.42, f32[256]{0:T(256)S(1)} %dynamic_slice.114, f32[2048]{0:T(1024)S(1)} %copy-done.13), kind=kOutput, calls=%fused_computation.144 | convolution fusion | flops 4297588736 | bytes 10494980 | tf_op jit(solution)/shard_map/yj,kji->kyi/dot_general | solution.py:101
  405.4 5.7 %fusion.65 = bf16[256,2048]{1,0:T(8,128)(2,1)S(1)} fusion(bf16[8,256,2048]{2,1,0:T(8,128)(2,1)} %bitcast.260, bf16[8,1,256,256]{3,2,1,0:T(8,128)(2,1)S(1)} %all-to-all-done.6), kind=kOutput, calls=%fused_computation.131 | convolution fusion | flops 2148007936 | bytes 10485760 | tf_op jit(solution)/shard_map/qkyi,qix->kyx/dot_general | solution.py:106
  414.2 6.5 %all-to-all-done.8 = bf16[8,1,256,256]{3,2,1,0:T(8,128)(2,1)S(1)} async-done(((bf16[8,1,256,256]{3,2,1,0:T(8,128)(2,1)}), bf16[8,1,256,256]{3,2,1,0:T(8,128)(2,1)S(1)}, u32[]{:S(2)}, u32[]{:S(2)}) %all-to-all-start.8) | async-done | bytes 1048608 | tf_op jit(solution)/shard_map/all_to_all | solution.py:105
  420.7 5.7 %fusion.66 = bf16[256,2048]{1,0:T(8,128)(2,1)S(1)} fusion(bf16[8,256,2048]{2,1,0:T(8,128)(2,1)} %bitcast.261, bf16[8,1,256,256]{3,2,1,0:T(8,128)(2,1)S(1)} %all-to-all-done.8), kind=kOutput, calls=%fused_computation.132 | convolution fusion | flops 2148007936 | bytes 10485760 | tf_op jit(solution)/shard_map/qkyi,qix->kyx/dot_general | solution.py:106
  432.1 15.2 %collective-permute-start.29 = (bf16[1,256,512]{2,1,0:T(8,128)(2,1)S(1)}, bf16[1,256,512]{2,1,0:T(8,128)(2,1)S(1)}, u32[]{:S(2)}, u32[]{:S(2)}) collective-permute-start(bf16[1,256,512]{2,1,0:T(8,128)(2,1)S(1)} %get-tuple-element.49), channel_id=1, source_target_pairs={{0,8},{8,16},{16,24},{24,0},{1,9},{9,17},{17,25},{25,1},{2,10},{10... | collective-permute-start | bytes 786440 | tf_op jit(solution)/shard_map/ppermute | solution.py:76
  453.1 5.3 collective-permute-done.30
  466.0 9.2 %collective-permute-done.33 = bf16[8,256,1]{2,1,0:T(8,128)(2,1)S(1)} collective-permute-done((bf16[8,256,1]{2,1,0:T(8,128)(2,1)S(1)}, bf16[8,256,1]{2,1,0:T(8,128)(2,1)S(1)}, u32[]{:S(2)}, u32[]{:S(2)}) %collective-permute-start.33) | collective-permute-done | bytes 4128 | tf_op jit(solution)/shard_map/ppermute | solution.py:17
  475.2 5.0 collective-permute-done.34
  480.2 6.4 %fusion.62 = f32[8,258,514]{2,1,0:T(8,128)S(1)} fusion(bf16[8,1,512]{2,1,0:T(2,128)(2,1)S(1)} %collective-permute-done.35, bf16[8,1,512]{2,1,0:T(2,128)(2,1)S(1)} %collective-permute-done.32, bf16[8,256,1]{2,1,0:T(8,128)(2,1)S(1)} %collective-permute-done.34, bf16[4,256,512]{2,1,0:T(8,128)(2,1)S(1)} %constant_dynamic-update-slice_fusion.23, ...), kind=kLoop, calls=%fused_computation.128 | loop fusion | flops 16974336 | bytes 6365312 | tf_op jit(solution)/shard_map/convert_element_type | solution.py:130
  486.6 5.9 %fusion.49 = f32[7,256,512]{2,1,0:T(8,128)} fusion(f32[8,258,514]{2,1,0:T(8,128)S(1)} %fusion.62, f32[8,258,514]{2,1,0:T(8,128)S(1)} %bitcast.249), kind=kLoop, calls=%fused_computation.84 | loop fusion | flops 3670016 | bytes 18350080 | tf_op jit(solution)/shard_map/mul | solution.py:54
  492.6 14.2 %fusion.9 = (f32[]{:T(128)}, f32[]{:T(128)}, f32[]{:T(128)}, f32[]{:T(128)}, f32[8,256,512]{2,1,0:T(8,128)}) fusion(f32[8,256,512]{2,1,0:T(8,128)} %copy-done.5, bf16[4,256,512]{2,1,0:T(8,128)(2,1)} %copy-done.7, bf16[4,256,512]{2,1,0:T(8,128)(2,1)} %copy-done.8, f32[8,256,512]{2,1,0:T(8,128)} %get-tuple-element.29, bf16[4,256,512]{2,1,0:T(8,128)(2,1)} %copy-done.3, ...), kind=kLoop, calls=%fused_computation.24 | loop fusion | flops 34603004 | bytes 62390288 | tf_op jit(solution)/shard_map/reduce_sum | solution.py:157
  509.3 13.7 %all_to_all.53 = f32[32,1,4]{2,1,0:T(1,128)S(1)} all-to-all(f32[32,1,4]{2,1,0:T(1,128)S(1)} %broadcast_in_dim.94), channel_id=1, replica_groups=mesh['px'=4,'py'=8] {'px','py'}, dimensions={0} | all-to-all | bytes 1024 | tf_op jit(solution)/shard_map/all_to_all | solution.py:41
  528.2 7.2 %fusion.15 = (f32[8,256,512]{2,1,0:T(8,128)}, f32[8,256,512]{2,1,0:T(8,128)}) fusion(f32[8,256,512]{2,1,0:T(8,128)} %param.8, f32[]{:T(128)S(6)} %div.27, f32[]{:T(128)S(6)} %div.23, bf16[4,256,512]{2,1,0:T(8,128)(2,1)} %copy-done.3, bf16[4,256,512]{2,1,0:T(8,128)(2,1)} %copy-done.2, f32[]{:T(128)S(6)} %div.26, bf16[4,256,512]{2,1,0:T(8,128)(2,1)} %copy-done.7, ...), kind=kLoop, calls=%fused_computation.30 | loop fusion | flops 10485760 | bytes 16777228 | tf_op jit(solution)/shard_map/add | solution.py:170
  (189 shorter events, 145.7 us)
Async XLA Ops:
  19.7 18.4 %collective-permute-start = (bf16[2,8,1,512]{3,2,1,0:T(2,128)(2,1)S(1)}, bf16[2,8,1,512]{3,2,1,0:T(2,128)(2,1)S(1)}, u32[]{:S(2)}, u32[]{:S(2)}) collective-permute-start(bf16[2,8,1,512]{3,2,1,0:T(2,128)(2,1)S(1)} %get-tuple-element.34), channel_id=1, source_target_pairs={{0,1},{1,2},{2,3},{3,4},{4,5},{5,6},{6,7},{8,9},{9,10},{10,11},{11... | collective-permute-start | bytes 49160 | tf_op jit(solution)/shard_map/ppermute | solution.py:17
  22.1 16.0 %collective-permute-start.3 = (bf16[2,8,1,512]{3,2,1,0:T(2,128)(2,1)S(1)}, bf16[2,8,1,512]{3,2,1,0:T(2,128)(2,1)S(1)}, u32[]{:S(2)}, u32[]{:S(2)}) collective-permute-start(bf16[2,8,1,512]{3,2,1,0:T(2,128)(2,1)S(1)} %get-tuple-element.35), channel_id=1, source_target_pairs={{1,0},{2,1},{3,2},{4,3},{5,4},{6,5},{7,6},{9,8},{10,9},{11,10},{12... | collective-permute-start | bytes 49160 | tf_op jit(solution)/shard_map/ppermute | solution.py:17
  26.5 6.2 %collective-permute-start.1 = (bf16[2,8,256,1]{2,1,3,0:T(8,128)(2,1)S(1)}, bf16[2,8,256,1]{2,1,3,0:T(8,128)(2,1)S(1)}, u32[]{:S(2)}, u32[]{:S(2)}) collective-permute-start(bf16[2,8,256,1]{2,1,3,0:T(8,128)(2,1)S(1)} %copy.76), channel_id=1, source_target_pairs={{0,8},{8,16},{16,24},{1,9},{9,17},{17,25},{2,10},{10,18},{18,26},{... | collective-permute-start | bytes 24584 | tf_op jit(solution)/shard_map/ppermute | solution.py:17
  31.2 5.5 %collective-permute-start.2 = (bf16[2,8,256,1]{2,1,3,0:T(8,128)(2,1)S(1)}, bf16[2,8,256,1]{2,1,3,0:T(8,128)(2,1)S(1)}, u32[]{:S(2)}, u32[]{:S(2)}) collective-permute-start(bf16[2,8,256,1]{2,1,3,0:T(8,128)(2,1)S(1)} %copy.77), channel_id=1, source_target_pairs={{8,0},{16,8},{24,16},{9,1},{17,9},{25,17},{10,2},{18,10},{26,18},{... | collective-permute-start | bytes 24584 | tf_op jit(solution)/shard_map/ppermute | solution.py:17
  75.8 11.2 %collective-permute-start.4 = (bf16[1,256,512]{2,1,0:T(8,128)(2,1)S(1)}, bf16[1,256,512]{2,1,0:T(8,128)(2,1)S(1)}, u32[]{:S(2)}, u32[]{:S(2)}) collective-permute-start(bf16[1,256,512]{2,1,0:T(8,128)(2,1)S(1)} %get-tuple-element.70), channel_id=1, source_target_pairs={{0,8},{8,16},{16,24},{24,0},{1,9},{9,17},{17,25},{25,1},{2,10},{10... | collective-permute-start | bytes 786440 | tf_op jit(solution)/shard_map/ppermute | solution.py:76
  77.4 20.7 %collective-permute-start.5 = (bf16[1,256,512]{2,1,0:T(8,128)(2,1)S(1)}, bf16[1,256,512]{2,1,0:T(8,128)(2,1)S(1)}, u32[]{:S(2)}, u32[]{:S(2)}) collective-permute-start(bf16[1,256,512]{2,1,0:T(8,128)(2,1)S(1)} %get-tuple-element.69), channel_id=1, source_target_pairs={{0,16},{8,24},{16,0},{24,8},{1,17},{9,25},{17,1},{25,9},{2,18},{10... | collective-permute-start | bytes 786440 | tf_op jit(solution)/shard_map/ppermute | solution.py:76
  78.5 19.6 %collective-permute-start.6 = (bf16[1,256,512]{2,1,0:T(8,128)(2,1)S(1)}, bf16[1,256,512]{2,1,0:T(8,128)(2,1)S(1)}, u32[]{:S(2)}, u32[]{:S(2)}) collective-permute-start(bf16[1,256,512]{2,1,0:T(8,128)(2,1)S(1)} %get-tuple-element.68), channel_id=1, source_target_pairs={{0,24},{8,0},{16,8},{24,16},{1,25},{9,1},{17,9},{25,17},{2,26},{10... | collective-permute-start | bytes 786440 | tf_op jit(solution)/shard_map/ppermute | solution.py:76
  100.9 30.7 %collective-permute-start.12 = (bf16[1,256,512]{2,1,0:T(8,128)(2,1)S(1)}, bf16[1,256,512]{2,1,0:T(8,128)(2,1)S(1)}, u32[]{:S(2)}, u32[]{:S(2)}) collective-permute-start(bf16[1,256,512]{2,1,0:T(8,128)(2,1)S(1)} %get-tuple-element.64), channel_id=1, source_target_pairs={{0,24},{8,0},{16,8},{24,16},{1,25},{9,1},{17,9},{25,17},{2,26},{10... | collective-permute-start | bytes 786440 | tf_op jit(solution)/shard_map/ppermute | solution.py:76
  108.1 23.5 %collective-permute-start.11 = (bf16[1,256,512]{2,1,0:T(8,128)(2,1)S(1)}, bf16[1,256,512]{2,1,0:T(8,128)(2,1)S(1)}, u32[]{:S(2)}, u32[]{:S(2)}) collective-permute-start(bf16[1,256,512]{2,1,0:T(8,128)(2,1)S(1)} %get-tuple-element.65), channel_id=1, source_target_pairs={{0,16},{8,24},{16,0},{24,8},{1,17},{9,25},{17,1},{25,9},{2,18},{10... | collective-permute-start | bytes 786440 | tf_op jit(solution)/shard_map/ppermute | solution.py:76
  108.4 17.6 %collective-permute-start.10 = (bf16[1,256,512]{2,1,0:T(8,128)(2,1)}, bf16[1,256,512]{2,1,0:T(8,128)(2,1)S(1)}, u32[]{:S(2)}, u32[]{:S(2)}) collective-permute-start(bf16[1,256,512]{2,1,0:T(8,128)(2,1)} %get-tuple-element.66), channel_id=1, source_target_pairs={{0,8},{8,16},{16,24},{24,0},{1,9},{9,17},{17,25},{25,1},{2,10},{10... | collective-permute-start | bytes 786440 | tf_op jit(solution)/shard_map/ppermute | solution.py:76
  115.4 23.0 %all-to-all-start = ((bf16[8,256,256]{2,1,0:T(8,128)(2,1)}), bf16[8,256,256]{2,1,0:T(8,128)(2,1)S(1)}, u32[]{:S(2)}, u32[]{:S(2)}) async-start(bf16[8,256,256]{2,1,0:T(8,128)(2,1)} %bitcast.245), calls=%async_computation | async-start | bytes 2097152 | tf_op jit(solution)/shard_map/all_to_all | solution.py:91
  138.4 18.9 %all-to-all-start.2 = ((bf16[8,256,256]{2,1,0:T(8,128)(2,1)}), bf16[8,256,256]{2,1,0:T(8,128)(2,1)S(1)}, u32[]{:S(2)}, u32[]{:S(2)}) async-start(bf16[8,256,256]{2,1,0:T(8,128)(2,1)} %bitcast.243), calls=%async_computation.2 | async-start | bytes 2097152 | tf_op jit(solution)/shard_map/all_to_all | solution.py:91
  157.3 19.3 %all-to-all-start.1 = ((bf16[8,1,256,256]{3,2,1,0:T(8,128)(2,1)}), bf16[8,1,256,256]{3,2,1,0:T(8,128)(2,1)S(1)}, u32[]{:S(2)}, u32[]{:S(2)}) async-start(bf16[8,1,256,256]{3,2,1,0:T(8,128)(2,1)} %bitcast.29), calls=%async_computation.1 | async-start | bytes 2097152 | tf_op jit(solution)/shard_map/all_to_all | solution.py:105
  176.6 22.4 %all-to-all-start.3 = ((bf16[8,1,256,256]{3,2,1,0:T(8,128)(2,1)}), bf16[8,1,256,256]{3,2,1,0:T(8,128)(2,1)S(1)}, u32[]{:S(2)}, u32[]{:S(2)}) async-start(bf16[8,1,256,256]{3,2,1,0:T(8,128)(2,1)} %bitcast.46), calls=%async_computation.3 | async-start | bytes 2097152 | tf_op jit(solution)/shard_map/all_to_all | solution.py:105
  186.8 11.3 %collective-permute-start.7 = (bf16[1,256,512]{2,1,0:T(8,128)(2,1)}, bf16[1,256,512]{2,1,0:T(8,128)(2,1)}, u32[]{:S(2)}, u32[]{:S(2)}) collective-permute-start(bf16[1,256,512]{2,1,0:T(8,128)(2,1)} %get-tuple-element.60), channel_id=1, source_target_pairs={{0,8},{8,16},{16,24},{24,0},{1,9},{9,17},{17,25},{25,1},{2,10},{10... | collective-permute-start | bytes 786440 | tf_op jit(solution)/shard_map/ppermute | solution.py:76
  186.8 33.8 %collective-permute-start.9 = (bf16[1,256,512]{2,1,0:T(8,128)(2,1)S(1)}, bf16[1,256,512]{2,1,0:T(8,128)(2,1)}, u32[]{:S(2)}, u32[]{:S(2)}) collective-permute-start(bf16[1,256,512]{2,1,0:T(8,128)(2,1)S(1)} %get-tuple-element.58), channel_id=1, source_target_pairs={{0,24},{8,0},{16,8},{24,16},{1,25},{9,1},{17,9},{25,17},{2,26},{10... | collective-permute-start | bytes 786440 | tf_op jit(solution)/shard_map/ppermute | solution.py:76
  190.6 28.9 %collective-permute-start.8 = (bf16[1,256,512]{2,1,0:T(8,128)(2,1)}, bf16[1,256,512]{2,1,0:T(8,128)(2,1)}, u32[]{:S(2)}, u32[]{:S(2)}) collective-permute-start(bf16[1,256,512]{2,1,0:T(8,128)(2,1)} %get-tuple-element.59), channel_id=1, source_target_pairs={{0,16},{8,24},{16,0},{24,8},{1,17},{9,25},{17,1},{25,9},{2,18},{10... | collective-permute-start | bytes 786440 | tf_op jit(solution)/shard_map/ppermute | solution.py:76
  204.8 16.9 %collective-permute-start.13 = (bf16[1,256,512]{2,1,0:T(8,128)(2,1)S(1)}, bf16[1,256,512]{2,1,0:T(8,128)(2,1)S(1)}, u32[]{:S(2)}, u32[]{:S(2)}) collective-permute-start(bf16[1,256,512]{2,1,0:T(8,128)(2,1)S(1)} %get-tuple-element.63), channel_id=1, source_target_pairs={{0,8},{8,16},{16,24},{24,0},{1,9},{9,17},{17,25},{25,1},{2,10},{10... | collective-permute-start | bytes 786440 | tf_op jit(solution)/shard_map/ppermute | solution.py:76
  220.5 10.4 %collective-permute-start.14 = (bf16[1,256,512]{2,1,0:T(8,128)(2,1)S(1)}, bf16[1,256,512]{2,1,0:T(8,128)(2,1)S(1)}, u32[]{:S(2)}, u32[]{:S(2)}) collective-permute-start(bf16[1,256,512]{2,1,0:T(8,128)(2,1)S(1)} %get-tuple-element.62), channel_id=1, source_target_pairs={{0,16},{8,24},{16,0},{24,8},{1,17},{9,25},{17,1},{25,9},{2,18},{10... | collective-permute-start | bytes 786440 | tf_op jit(solution)/shard_map/ppermute | solution.py:76
  221.6 13.4 %collective-permute-start.15 = (bf16[1,256,512]{2,1,0:T(8,128)(2,1)S(1)}, bf16[1,256,512]{2,1,0:T(8,128)(2,1)S(1)}, u32[]{:S(2)}, u32[]{:S(2)}) collective-permute-start(bf16[1,256,512]{2,1,0:T(8,128)(2,1)S(1)} %get-tuple-element.61), channel_id=1, source_target_pairs={{0,24},{8,0},{16,8},{24,16},{1,25},{9,1},{17,9},{25,17},{2,26},{10... | collective-permute-start | bytes 786440 | tf_op jit(solution)/shard_map/ppermute | solution.py:76
  235.1 23.6 %collective-permute-start.16 = (bf16[8,1,512]{2,1,0:T(2,128)(2,1)S(1)}, bf16[8,1,512]{2,1,0:T(2,128)(2,1)S(1)}, u32[]{:S(2)}, u32[]{:S(2)}) collective-permute-start(bf16[8,1,512]{2,1,0:T(2,128)(2,1)S(1)} %get-tuple-element.42), channel_id=1, source_target_pairs={{0,1},{1,2},{2,3},{3,4},{4,5},{5,6},{6,7},{8,9},{9,10},{10,11},{11... | collective-permute-start | bytes 24584 | tf_op jit(solution)/shard_map/ppermute | solution.py:17
  236.4 22.3 %collective-permute-start.19 = (bf16[8,1,512]{2,1,0:T(2,128)(2,1)S(1)}, bf16[8,1,512]{2,1,0:T(2,128)(2,1)S(1)}, u32[]{:S(2)}, u32[]{:S(2)}) collective-permute-start(bf16[8,1,512]{2,1,0:T(2,128)(2,1)S(1)} %get-tuple-element.43), channel_id=1, source_target_pairs={{1,0},{2,1},{3,2},{4,3},{5,4},{6,5},{7,6},{9,8},{10,9},{11,10},{12... | collective-permute-start | bytes 24584 | tf_op jit(solution)/shard_map/ppermute | solution.py:17
  237.7 27.4 %slice-start = ((s8[5406720]{0:T(1024)(128)(4,1)}), s8[4194304]{0:T(1024)(128)(4,1)S(1)}, s32[]{:S(2)}) async-start(s8[5406720]{0:T(1024)(128)(4,1)} %bitcast.246), calls=%async_computation.10 | async-start | bytes 8388608
  237.9 15.9 %collective-permute-start.17 = (bf16[8,256,1]{2,1,0:T(8,128)(2,1)S(1)}, bf16[8,256,1]{2,1,0:T(8,128)(2,1)S(1)}, u32[]{:S(2)}, u32[]{:S(2)}) collective-permute-start(bf16[8,256,1]{2,1,0:T(8,128)(2,1)S(1)} %get-tuple-element.40), channel_id=1, source_target_pairs={{0,8},{8,16},{16,24},{1,9},{9,17},{17,25},{2,10},{10,18},{18,26},{... | collective-permute-start | bytes 12296 | tf_op jit(solution)/shard_map/ppermute | solution.py:17
  243.6 15.1 %collective-permute-start.18 = (bf16[8,256,1]{2,1,0:T(8,128)(2,1)S(1)}, bf16[8,256,1]{2,1,0:T(8,128)(2,1)S(1)}, u32[]{:S(2)}, u32[]{:S(2)}) collective-permute-start(bf16[8,256,1]{2,1,0:T(8,128)(2,1)S(1)} %get-tuple-element.41), channel_id=1, source_target_pairs={{8,0},{16,8},{24,16},{9,1},{17,9},{25,17},{10,2},{18,10},{26,18},{... | collective-permute-start | bytes 12296 | tf_op jit(solution)/shard_map/ppermute | solution.py:17
  300.2 34.5 %slice-start.4 = ((s8[8388608]{0:T(1024)(128)(4,1)}), s8[4194304]{0:T(1024)(128)(4,1)S(1)}, s32[]{:S(2)}) async-start(s8[8388608]{0:T(1024)(128)(4,1)} %bitcast.262), calls=%async_computation.14 | async-start | bytes 8388608
  300.2 34.5 %slice-start.5 = ((s8[8388608]{0:T(1024)(128)(4,1)}), s8[4194304]{0:T(1024)(128)(4,1)S(1)}, s32[]{:S(2)}) async-start(s8[8388608]{0:T(1024)(128)(4,1)} %bitcast.262), calls=%async_computation.15 | async-start | bytes 8388608
  305.3 11.1 %collective-permute-start.20 = (bf16[1,256,512]{2,1,0:T(8,128)(2,1)S(1)}, bf16[1,256,512]{2,1,0:T(8,128)(2,1)S(1)}, u32[]{:S(2)}, u32[]{:S(2)}) collective-permute-start(bf16[1,256,512]{2,1,0:T(8,128)(2,1)S(1)} %get-tuple-element.56), channel_id=1, source_target_pairs={{0,8},{8,16},{16,24},{24,0},{1,9},{9,17},{17,25},{25,1},{2,10},{10... | collective-permute-start | bytes 786440 | tf_op jit(solution)/shard_map/ppermute | solution.py:76
  305.9 20.7 %collective-permute-start.21 = (bf16[1,256,512]{2,1,0:T(8,128)(2,1)S(1)}, bf16[1,256,512]{2,1,0:T(8,128)(2,1)S(1)}, u32[]{:S(2)}, u32[]{:S(2)}) collective-permute-start(bf16[1,256,512]{2,1,0:T(8,128)(2,1)S(1)} %get-tuple-element.55), channel_id=1, source_target_pairs={{0,16},{8,24},{16,0},{24,8},{1,17},{9,25},{17,1},{25,9},{2,18},{10... | collective-permute-start | bytes 786440 | tf_op jit(solution)/shard_map/ppermute | solution.py:76
  306.5 20.2 %collective-permute-start.22 = (bf16[1,256,512]{2,1,0:T(8,128)(2,1)S(1)}, bf16[1,256,512]{2,1,0:T(8,128)(2,1)S(1)}, u32[]{:S(2)}, u32[]{:S(2)}) collective-permute-start(bf16[1,256,512]{2,1,0:T(8,128)(2,1)S(1)} %get-tuple-element.54), channel_id=1, source_target_pairs={{0,24},{8,0},{16,8},{24,16},{1,25},{9,1},{17,9},{25,17},{2,26},{10... | collective-permute-start | bytes 786440 | tf_op jit(solution)/shard_map/ppermute | solution.py:76
  327.8 29.0 %collective-permute-start.28 = (bf16[1,256,512]{2,1,0:T(8,128)(2,1)S(1)}, bf16[1,256,512]{2,1,0:T(8,128)(2,1)S(1)}, u32[]{:S(2)}, u32[]{:S(2)}) collective-permute-start(bf16[1,256,512]{2,1,0:T(8,128)(2,1)S(1)} %get-tuple-element.50), channel_id=1, source_target_pairs={{0,24},{8,0},{16,8},{24,16},{1,25},{9,1},{17,9},{25,17},{2,26},{10... | collective-permute-start | bytes 786440 | tf_op jit(solution)/shard_map/ppermute | solution.py:76
  332.8 24.0 %collective-permute-start.27 = (bf16[1,256,512]{2,1,0:T(8,128)(2,1)S(1)}, bf16[1,256,512]{2,1,0:T(8,128)(2,1)S(1)}, u32[]{:S(2)}, u32[]{:S(2)}) collective-permute-start(bf16[1,256,512]{2,1,0:T(8,128)(2,1)S(1)} %get-tuple-element.51), channel_id=1, source_target_pairs={{0,16},{8,24},{16,0},{24,8},{1,17},{9,25},{17,1},{25,9},{2,18},{10... | collective-permute-start | bytes 786440 | tf_op jit(solution)/shard_map/ppermute | solution.py:76
  334.5 15.7 %collective-permute-start.26 = (bf16[1,256,512]{2,1,0:T(8,128)(2,1)}, bf16[1,256,512]{2,1,0:T(8,128)(2,1)S(1)}, u32[]{:S(2)}, u32[]{:S(2)}) collective-permute-start(bf16[1,256,512]{2,1,0:T(8,128)(2,1)} %get-tuple-element.52), channel_id=1, source_target_pairs={{0,8},{8,16},{16,24},{24,0},{1,9},{9,17},{17,25},{25,1},{2,10},{10... | collective-permute-start | bytes 786440 | tf_op jit(solution)/shard_map/ppermute | solution.py:76
  338.2 25.4 %all-to-all-start.5 = ((bf16[8,256,256]{2,1,0:T(8,128)(2,1)}), bf16[8,256,256]{2,1,0:T(8,128)(2,1)S(1)}, u32[]{:S(2)}, u32[]{:S(2)}) async-start(bf16[8,256,256]{2,1,0:T(8,128)(2,1)} %bitcast.241), calls=%async_computation.5 | async-start | bytes 2097152 | tf_op jit(solution)/shard_map/all_to_all | solution.py:91
  363.6 18.9 %all-to-all-start.7 = ((bf16[8,256,256]{2,1,0:T(8,128)(2,1)}), bf16[8,256,256]{2,1,0:T(8,128)(2,1)S(1)}, u32[]{:S(2)}, u32[]{:S(2)}) async-start(bf16[8,256,256]{2,1,0:T(8,128)(2,1)} %bitcast.239), calls=%async_computation.7 | async-start | bytes 2097152 | tf_op jit(solution)/shard_map/all_to_all | solution.py:91
  382.5 19.3 %all-to-all-start.6 = ((bf16[8,1,256,256]{3,2,1,0:T(8,128)(2,1)}), bf16[8,1,256,256]{3,2,1,0:T(8,128)(2,1)S(1)}, u32[]{:S(2)}, u32[]{:S(2)}) async-start(bf16[8,1,256,256]{3,2,1,0:T(8,128)(2,1)} %bitcast.65), calls=%async_computation.6 | async-start | bytes 2097152 | tf_op jit(solution)/shard_map/all_to_all | solution.py:105
  401.8 18.9 %all-to-all-start.8 = ((bf16[8,1,256,256]{3,2,1,0:T(8,128)(2,1)}), bf16[8,1,256,256]{3,2,1,0:T(8,128)(2,1)S(1)}, u32[]{:S(2)}, u32[]{:S(2)}) async-start(bf16[8,1,256,256]{3,2,1,0:T(8,128)(2,1)} %bitcast.80), calls=%async_computation.8 | async-start | bytes 2097152 | tf_op jit(solution)/shard_map/all_to_all | solution.py:105
  411.2 37.2 %collective-permute-start.25 = (bf16[1,256,512]{2,1,0:T(8,128)(2,1)S(1)}, bf16[1,256,512]{2,1,0:T(8,128)(2,1)S(1)}, u32[]{:S(2)}, u32[]{:S(2)}) collective-permute-start(bf16[1,256,512]{2,1,0:T(8,128)(2,1)S(1)} %get-tuple-element.44), channel_id=1, source_target_pairs={{0,24},{8,0},{16,8},{24,16},{1,25},{9,1},{17,9},{25,17},{2,26},{10... | collective-permute-start | bytes 786440 | tf_op jit(solution)/shard_map/ppermute | solution.py:76
  411.3 37.0 %collective-permute-start.24 = (bf16[1,256,512]{2,1,0:T(8,128)(2,1)S(1)}, bf16[1,256,512]{2,1,0:T(8,128)(2,1)S(1)}, u32[]{:S(2)}, u32[]{:S(2)}) collective-permute-start(bf16[1,256,512]{2,1,0:T(8,128)(2,1)S(1)} %get-tuple-element.45), channel_id=1, source_target_pairs={{0,16},{8,24},{16,0},{24,8},{1,17},{9,25},{17,1},{25,9},{2,18},{10... | collective-permute-start | bytes 786440 | tf_op jit(solution)/shard_map/ppermute | solution.py:76
  412.2 20.0 %collective-permute-start.23 = (bf16[1,256,512]{2,1,0:T(8,128)(2,1)S(1)}, bf16[1,256,512]{2,1,0:T(8,128)(2,1)}, u32[]{:S(2)}, u32[]{:S(2)}) collective-permute-start(bf16[1,256,512]{2,1,0:T(8,128)(2,1)S(1)} %get-tuple-element.46), channel_id=1, source_target_pairs={{0,8},{8,16},{16,24},{24,0},{1,9},{9,17},{17,25},{25,1},{2,10},{10... | collective-permute-start | bytes 786440 | tf_op jit(solution)/shard_map/ppermute | solution.py:76
  426.7 31.7 %collective-permute-start.31 = (bf16[1,256,512]{2,1,0:T(8,128)(2,1)S(1)}, bf16[1,256,512]{2,1,0:T(8,128)(2,1)S(1)}, u32[]{:S(2)}, u32[]{:S(2)}) collective-permute-start(bf16[1,256,512]{2,1,0:T(8,128)(2,1)S(1)} %get-tuple-element.47), channel_id=1, source_target_pairs={{0,24},{8,0},{16,8},{24,16},{1,25},{9,1},{17,9},{25,17},{2,26},{10... | collective-permute-start | bytes 786440 | tf_op jit(solution)/shard_map/ppermute | solution.py:76
  426.7 31.6 %collective-permute-start.30 = (bf16[1,256,512]{2,1,0:T(8,128)(2,1)S(1)}, bf16[1,256,512]{2,1,0:T(8,128)(2,1)S(1)}, u32[]{:S(2)}, u32[]{:S(2)}) collective-permute-start(bf16[1,256,512]{2,1,0:T(8,128)(2,1)S(1)} %get-tuple-element.48), channel_id=1, source_target_pairs={{0,16},{8,24},{16,0},{24,8},{1,17},{9,25},{17,1},{25,9},{2,18},{10... | collective-permute-start | bytes 786440 | tf_op jit(solution)/shard_map/ppermute | solution.py:76
  432.1 20.9 %collective-permute-start.29 = (bf16[1,256,512]{2,1,0:T(8,128)(2,1)S(1)}, bf16[1,256,512]{2,1,0:T(8,128)(2,1)S(1)}, u32[]{:S(2)}, u32[]{:S(2)}) collective-permute-start(bf16[1,256,512]{2,1,0:T(8,128)(2,1)S(1)} %get-tuple-element.49), channel_id=1, source_target_pairs={{0,8},{8,16},{16,24},{24,0},{1,9},{9,17},{17,25},{25,1},{2,10},{10... | collective-permute-start | bytes 786440 | tf_op jit(solution)/shard_map/ppermute | solution.py:76
  448.4 31.8 %copy-start.8 = (bf16[4,256,512]{2,1,0:T(8,128)(2,1)}, bf16[4,256,512]{2,1,0:T(8,128)(2,1)S(1)}, u32[]{:S(2)}) copy-start(bf16[4,256,512]{2,1,0:T(8,128)(2,1)S(1)} %constant_dynamic-update-slice_fusion.3) | copy-start | bytes 3145732
  458.4 21.8 %collective-permute-start.32 = (bf16[8,1,512]{2,1,0:T(2,128)(2,1)S(1)}, bf16[8,1,512]{2,1,0:T(2,128)(2,1)S(1)}, u32[]{:S(2)}, u32[]{:S(2)}) collective-permute-start(bf16[8,1,512]{2,1,0:T(2,128)(2,1)S(1)} %get-tuple-element.38), channel_id=1, source_target_pairs={{0,1},{1,2},{2,3},{3,4},{4,5},{5,6},{6,7},{8,9},{9,10},{10,11},{11... | collective-permute-start | bytes 24584 | tf_op jit(solution)/shard_map/ppermute | solution.py:17
  460.2 20.0 %collective-permute-start.35 = (bf16[8,1,512]{2,1,0:T(2,128)(2,1)S(1)}, bf16[8,1,512]{2,1,0:T(2,128)(2,1)S(1)}, u32[]{:S(2)}, u32[]{:S(2)}) collective-permute-start(bf16[8,1,512]{2,1,0:T(2,128)(2,1)S(1)} %get-tuple-element.39), channel_id=1, source_target_pairs={{1,0},{2,1},{3,2},{4,3},{5,4},{6,5},{7,6},{9,8},{10,9},{11,10},{12... | collective-permute-start | bytes 24584 | tf_op jit(solution)/shard_map/ppermute | solution.py:17
  461.7 13.5 %collective-permute-start.33 = (bf16[8,256,1]{2,1,0:T(8,128)(2,1)S(1)}, bf16[8,256,1]{2,1,0:T(8,128)(2,1)S(1)}, u32[]{:S(2)}, u32[]{:S(2)}) collective-permute-start(bf16[8,256,1]{2,1,0:T(8,128)(2,1)S(1)} %get-tuple-element.36), channel_id=1, source_target_pairs={{0,8},{8,16},{16,24},{1,9},{9,17},{17,25},{2,10},{10,18},{18,26},{... | collective-permute-start | bytes 12296 | tf_op jit(solution)/shard_map/ppermute | solution.py:17
  464.4 15.8 %collective-permute-start.34 = (bf16[8,256,1]{2,1,0:T(8,128)(2,1)S(1)}, bf16[8,256,1]{2,1,0:T(8,128)(2,1)S(1)}, u32[]{:S(2)}, u32[]{:S(2)}) collective-permute-start(bf16[8,256,1]{2,1,0:T(8,128)(2,1)S(1)} %get-tuple-element.37), channel_id=1, source_target_pairs={{8,0},{16,8},{24,16},{9,1},{17,9},{25,17},{10,2},{18,10},{26,18},{... | collective-permute-start | bytes 12296 | tf_op jit(solution)/shard_map/ppermute | solution.py:17
  (16 other events, 208.8 us)

commit v7 on v6

--- a/solution.py
+++ b/solution.py
@@ -80,7 +80,7 @@
     return result
 
 
-def precondition_lines(lines, first_level, eigenvectors, eigenvalues, level_shift):
+def spectrum(lines, first_level, eigenvectors, eigenvalues, level_shift):
     across = lax.axis_size("py")
     levels_here, rows, width = lines.shape
     cols = width // across
@@ -97,7 +97,14 @@
         level_shift, first_level + lax.axis_index("px") * levels_here, levels_here, 0
     )
     denom = eigenvalues[None, :, None] + eigen_cols[None, None, :] + shift_here[:, None, None]
-    scaled = (second / denom).astype(jnp.bfloat16)
+    return (second / denom).astype(jnp.bfloat16)
+
+
+def pencil_of(scaled, eigenvectors):
+    across = lax.axis_size("py")
+    levels_here, height, cols = scaled.shape
+    rows = height // across
+    width = cols * across
     fourth = jnp.einsum(
         "yj,kji->kyi", eigenvectors, scaled, preferred_element_type=jnp.float32
     ).astype(jnp.bfloat16)
@@ -109,7 +116,7 @@
         eigenvectors.reshape(across, cols, width),
         preferred_element_type=jnp.float32,
     )
-    return exchange(pencil.astype(jnp.bfloat16), "px", 2, 0).astype(jnp.float32)
+    return pencil.astype(jnp.bfloat16)
 
 
 def precondition(residual, eigenvectors, eigenvalues, level_shift):
@@ -117,13 +124,20 @@
     chunk = lax.axis_size("px")
     if levels % chunk or levels == chunk:
         chunk = levels
-    parts = []
+    starts = list(range(0, levels, chunk))
+    spectra = []
     waiting = residual
-    for start in range(0, levels, chunk):
+    for start in starts:
         lines = exchange(waiting[start : start + chunk].astype(jnp.bfloat16), "px", 0, 2)
         lines, waiting = lax.optimization_barrier((lines, waiting))
-        parts.append(precondition_lines(lines, start, eigenvectors, eigenvalues, level_shift))
-    return jnp.concatenate(parts, 0)
+        spectra.append(spectrum(lines, start, eigenvectors, eigenvalues, level_shift))
+    parts = []
+    for index in range(len(starts)):
+        pencil = pencil_of(spectra[index], eigenvectors)
+        if index + 1 < len(starts):
+            pencil, spectra[index + 1] = lax.optimization_barrier((pencil, spectra[index + 1]))
+        parts.append(exchange(pencil, "px", 2, 0))
+    return jnp.concatenate(parts, 0).astype(jnp.float32)
 
 
 def operator(field, coeff_pad):
@@ -135,12 +149,12 @@
     coeff = jnp.zeros(classes.shape, jnp.float32)
     for label in range(coeff_table.shape[0]):
         coeff = jnp.where(classes == label, coeff_table[label], coeff)
-    stacked = padded_2(
-        jnp.stack((solution_in, coeff)).astype(jnp.bfloat16), (("px", 3), ("py", 2)), 1
-    ).astype(jnp.float32)
-    coeff_pad = stacked[1]
+    solution_pad, coeff_pad = (
+        padded_2(array.astype(jnp.bfloat16), (("px", 2), ("py", 1)), 1).astype(jnp.float32)
+        for array in (solution_in, coeff)
+    )
     solution = solution_in
-    residual = right_side - face_sum(stacked[0], coeff_pad)
+    residual = right_side - face_sum(solution_pad, coeff_pad)
     direction = image = None
     gamma_prev = curvature_prev = None
     for iteration in range(ITERS):

time: 546 us -> 572 us (1.048)
  waiting for transfers between devices: 151 us -> 212 us
  starting transfers between devices: 113 us -> 95.2 us
  other arithmetic: 121 us -> 110 us
  local copies, waits for them, and re-layouts: 37.2 us -> 28 us
    ppermute x24, waiting for transfers between devices: 101 us -> 136 us  [exchange(): lax.ppermute(part, axis, [(i, (i + shift) % size) for i in range(size)])]
    ppermute x24, starting transfers between devices: 56.7 us -> 30.5 us  [exchange(): lax.ppermute(part, axis, [(i, (i + shift) % size) for i in range(size)])]
    another operation x2 -> x0, other arithmetic: 17.1 us -> none  [shards(): jnp.stack((solution_in, coeff)).astype(jnp.bfloat16)]
    ppermute x6 -> x8, waiting for transfers between devices: 17.9 us -> 30.6 us  [padded_2(): lax.ppermute(last, axis, up)]
    all_to_all x8, waiting for transfers between devices: 18.4 us -> 28.1 us  [the longest x4 22.1 us: pencil_of(): returned = lax.all_to_all(outgoing, 'py', 0, 0, tiled=True)]
    convert_element_type x1 -> x4, other arithmetic: 13.2 us -> 20.6 us  [the longest x2 16.3 us: shards(): array.astype(jnp.bfloat16)]
    ppermute x6 -> x8, starting transfers between devices: 18 us -> 24 us  [padded_2(): lax.ppermute(last, axis, up)]
    dot_general x12 -> x14, matrix products: 86.6 us -> 91.1 us  [the longest x4 33.5 us: pencil_of(): jnp.einsum('yj,kji->kyi', eigenvectors, scaled, preferred_element_type=jn...]
  transfers between devices with their start and end apart: 44 -> 48, of which waited for: 25 -> 30; matrix products, arithmetic and copies ran while one was open for 20% -> 15% of each run, Pallas kernels for 0% -> 0%
where the time goes in v7:
time: 572 us; the launch traced here: 568 us
  waiting for transfers between devices  212 us (37%)
  other arithmetic  110 us (19%)
  starting transfers between devices  95.2 us (17%)
  matrix products  91.1 us (16%)
  local copies, waits for them, and re-layouts  28 us (5%)
  blocking collectives  24.8 us (4%)
  between operations  7.67 us (1%)
    ppermute x24, waiting for transfers between devices, exchange(): lax.ppermute(part, axis, [(i, (i + shift) % size) for i in range(size)])  136 us
    dot_general x4, matrix products, pencil_of(): jnp.einsum('yj,kji->kyi', eigenvectors, scaled, preferred_element_type=jn...  33.5 us
    ppermute x8, waiting for transfers between devices, padded_2(): lax.ppermute(last, axis, up)  30.6 us
    ppermute x24, starting transfers between devices, exchange(): lax.ppermute(part, axis, [(i, (i + shift) % size) for i in range(size)])  30.5 us
    reduce_sum x2, other arithmetic, shards(): jnp.sum(residual * precond)  27.6 us
    all_to_all x2, blocking collectives, all_sum(): return jnp.sum(lax.all_to_all(spread, axes, 0, 0, tiled=True), 0)  24.8 us
    ppermute x8, starting transfers between devices, padded_2(): lax.ppermute(last, axis, up)  24 us
    dot_general x4, matrix products, pencil_of(): jnp.einsum('qkyi,qix->kyx', returned, eigenvectors.reshape(across, cols,...  22.9 us
  transfers between devices with their start and end apart: 48, of which 30 were waited for; matrix products, arithmetic and copies ran while one was open for 15% of the time, Pallas kernels for 0%

profile of v7, /device:TPU:0, one launch (start us, length us, event | category | flops | bytes accessed | tf_op | source)
XLA Modules:
  0.0 568.1 jit_solution(8739236026969370780)
XLA Ops:
  2.6 16.0 %select_convert_fusion = bf16[8,256,512]{2,1,0:T(8,128)(2,1)S(1)} fusion(s32[8,256,512]{2,1,0:T(8,128)} %param.9, bf16[]{:T(256)} %bitcast.15, bf16[]{:T(256)} %bitcast.14, bf16[]{:T(256)} %bitcast.13, bf16[]{:T(256)} %bitcast.12, bf16[]{:T(256)} %bitcast.11, bf16[]{:T(256)} %bitcast.10, bf16[]{:T(256)} %bitcast.9, bf16[]{:T(256)} %bitcast.8, bf16[]{:T(256)} %bitcast.7, ...), kind=kLoop, calls=%fused_computation.77 | loop fusion | flops 33554432 | bytes 6291488 | tf_op jit(solution)/shard_map/convert_element_type | solution.py:153
  50.9 8.7 %collective-permute-done.5 = bf16[8,256,1]{2,1,0:T(8,128)(2,1)S(1)} collective-permute-done((bf16[8,256,1]{2,1,0:T(8,128)(2,1)}, bf16[8,256,1]{2,1,0:T(8,128)(2,1)S(1)}, u32[]{:S(2)}, u32[]{:S(2)}) %collective-permute-start.5) | collective-permute-done | bytes 4128 | tf_op jit(solution)/shard_map/ppermute | solution.py:17
  66.1 5.9 %fusion.50 = f32[7,256,512]{2,1,0:T(8,128)} fusion(f32[8,258,514]{2,1,0:T(8,128)S(1)} %fusion.61, f32[8,258,514]{2,1,0:T(8,128)S(1)} %fusion.58), kind=kLoop, calls=%fused_computation.83 | loop fusion | flops 3670016 | bytes 18350080 | tf_op jit(solution)/shard_map/mul | solution.py:54
  72.0 11.2 %fusion.38 = f32[8,256,512]{2,1,0:T(8,128)S(1)} fusion(f32[8,256,512]{2,1,0:T(8,128)} %param.7, f32[8,258,514]{2,1,0:T(8,128)S(1)} %fusion.61, f32[7,256,512]{2,1,0:T(8,128)} %fusion.50, f32[8,258,514]{2,1,0:T(8,128)S(1)} %fusion.58), kind=kLoop, calls=%fused_computation.58 | loop fusion | flops 23068672 | bytes 54001664 | tf_op jit(solution)/shard_map/sub | solution.py:157
  90.6 6.3 %collective-permute-done.8 = bf16[1,256,512]{2,1,0:T(8,128)(2,1)S(1)} collective-permute-done((bf16[1,256,512]{2,1,0:T(8,128)(2,1)S(1)}, bf16[1,256,512]{2,1,0:T(8,128)(2,1)S(1)}, u32[]{:S(2)}, u32[]{:S(2)}) %collective-permute-start.8) | collective-permute-done | bytes 262176 | tf_op jit(solution)/shard_map/ppermute | solution.py:76
  96.9 10.1 %collective-permute-done.9 = bf16[1,256,512]{2,1,0:T(8,128)(2,1)S(1)} collective-permute-done((bf16[1,256,512]{2,1,0:T(8,128)(2,1)S(1)}, bf16[1,256,512]{2,1,0:T(8,128)(2,1)S(1)}, u32[]{:S(2)}, u32[]{:S(2)}) %collective-permute-start.9) | collective-permute-done | bytes 262176 | tf_op jit(solution)/shard_map/ppermute | solution.py:76
  109.7 6.0 %collective-permute-start.13 = (bf16[1,256,512]{2,1,0:T(8,128)(2,1)S(1)}, bf16[1,256,512]{2,1,0:T(8,128)(2,1)S(1)}, u32[]{:S(2)}, u32[]{:S(2)}) collective-permute-start(bf16[1,256,512]{2,1,0:T(8,128)(2,1)S(1)} %get-tuple-element.73), channel_id=1, source_target_pairs={{0,24},{8,0},{16,8},{24,16},{1,25},{9,1},{17,9},{25,17},{2,26},{10... | collective-permute-start | bytes 786440 | tf_op jit(solution)/shard_map/ppermute | solution.py:76
  117.2 5.7 %convolution_convert_fusion.7 = bf16[256,2048]{1,0:T(8,128)(2,1)S(1)} fusion(bf16[2048,2048]{1,0:T(8,128)(2,1)} %param.11, bf16[1,256,2048]{2,1,0:T(8,128)(2,1)S(1)} %constant_dynamic-update-slice_fusion.20), kind=kOutput, calls=%fused_computation.141 | convolution fusion | flops 2148007936 | bytes 10485760 | tf_op jit(solution)/shard_map/dot_general | solution.py:87
  127.7 6.0 %collective-permute-done.11 = bf16[1,256,512]{2,1,0:T(8,128)(2,1)S(1)} collective-permute-done((bf16[1,256,512]{2,1,0:T(8,128)(2,1)}, bf16[1,256,512]{2,1,0:T(8,128)(2,1)S(1)}, u32[]{:S(2)}, u32[]{:S(2)}) %collective-permute-start.11) | collective-permute-done | bytes 262176 | tf_op jit(solution)/shard_map/ppermute | solution.py:76
  133.7 6.5 %collective-permute-done.12 = bf16[1,256,512]{2,1,0:T(8,128)(2,1)S(1)} collective-permute-done((bf16[1,256,512]{2,1,0:T(8,128)(2,1)S(1)}, bf16[1,256,512]{2,1,0:T(8,128)(2,1)S(1)}, u32[]{:S(2)}, u32[]{:S(2)}) %collective-permute-start.12) | collective-permute-done | bytes 262176 | tf_op jit(solution)/shard_map/ppermute | solution.py:76
  140.3 5.7 %convolution_convert_fusion.5 = bf16[256,2048]{1,0:T(8,128)(2,1)S(1)} fusion(bf16[2048,2048]{1,0:T(8,128)(2,1)} %param.11, bf16[1,256,2048]{2,1,0:T(8,128)(2,1)S(1)} %constant_dynamic-update-slice_fusion.17), kind=kOutput, calls=%fused_computation.139 | convolution fusion | flops 2148007936 | bytes 10485760 | tf_op jit(solution)/shard_map/dot_general | solution.py:87
  150.7 11.0 %fusion.72 = bf16[1,2048,256]{1,2,0:T(8,128)(2,1)S(1)} fusion(bf16[2048,2048]{1,0:T(8,128)(2,1)} %param.11, bf16[2048,256]{1,0:T(8,128)(2,1)S(1)} %bitcast.225, f32[]{:T(128)} %bitcast.21, f32[256]{0:T(256)S(1)} %dynamic_slice.114, f32[2048]{0:T(1024)S(1)} %copy-done.14), kind=kOutput, calls=%fused_computation.142 | convolution fusion | flops 4297588736 | bytes 10494980 | tf_op jit(solution)/shard_map/yj,kji->kyi/dot_general | solution.py:108
  170.0 7.6 %fusion.80 = bf16[1,2048,256]{1,2,0:T(8,128)(2,1)} fusion(bf16[2048,256]{1,0:T(8,128)(2,1)S(1)} %bitcast.227, bf16[2048,2048]{1,0:T(8,128)(2,1)} %param.11, f32[]{:T(128)} %bitcast.35, f32[256]{0:T(256)S(1)} %dynamic_slice.114, f32[2048]{0:T(1024)S(1)} %copy-done.14), kind=kOutput, calls=%fused_computation.150 | convolution fusion | flops 2149580800 | bytes 10494980 | tf_op jit(solution)/shard_map/jy,kyi->kji/dot_general | solution.py:94
  177.5 7.8 %all-to-all-done.1 = bf16[8,1,256,256]{3,2,1,0:T(8,128)(2,1)S(1)} async-done(((bf16[8,1,256,256]{3,2,1,0:T(8,128)(2,1)}), bf16[8,1,256,256]{3,2,1,0:T(8,128)(2,1)S(1)}, u32[]{:S(2)}, u32[]{:S(2)}) %all-to-all-start.1) | async-done | bytes 1048608 | tf_op jit(solution)/shard_map/all_to_all | solution.py:112
  185.3 5.8 %fusion.77 = bf16[1,256,2048]{2,1,0:T(8,128)(2,1)S(1)} fusion(bf16[8,256,2048]{2,1,0:T(8,128)(2,1)} %bitcast.232, bf16[8,1,256,256]{3,2,1,0:T(8,128)(2,1)S(1)} %all-to-all-done.1), kind=kOutput, calls=%fused_computation.147 | convolution fusion | flops 2148007936 | bytes 10485760 | tf_op jit(solution)/shard_map/qkyi,qix->kyx/dot_general | solution.py:113
  191.1 5.7 %fusion.73 = bf16[1,2048,256]{1,2,0:T(8,128)(2,1)S(1)} fusion(bf16[2048,2048]{1,0:T(8,128)(2,1)} %param.11, bf16[1,2048,256]{1,2,0:T(8,128)(2,1)S(1)} %copy-done.16), kind=kOutput, calls=%fused_computation.143 | convolution fusion | flops 2148007936 | bytes 10485760 | tf_op jit(solution)/shard_map/yj,kji->kyi/dot_general | solution.py:108
  206.6 7.3 %collective-permute-done.14 = bf16[1,256,512]{2,1,0:T(8,128)(2,1)S(1)} collective-permute-done((bf16[1,256,512]{2,1,0:T(8,128)(2,1)}, bf16[1,256,512]{2,1,0:T(8,128)(2,1)S(1)}, u32[]{:S(2)}, u32[]{:S(2)}) %collective-permute-start.14) | collective-permute-done | bytes 262176 | tf_op jit(solution)/shard_map/ppermute | solution.py:76
  217.1 5.7 %fusion.69 = bf16[256,2048]{1,0:T(8,128)(2,1)S(1)} fusion(bf16[8,256,2048]{2,1,0:T(8,128)(2,1)} %bitcast.233, bf16[8,1,256,256]{3,2,1,0:T(8,128)(2,1)S(1)} %all-to-all-done.3), kind=kOutput, calls=%fused_computation.131 | convolution fusion | flops 2148007936 | bytes 10485760 | tf_op jit(solution)/shard_map/qkyi,qix->kyx/dot_general | solution.py:113
  223.0 17.0 %collective-permute-done.15 = bf16[1,256,512]{2,1,0:T(8,128)(2,1)S(1)} collective-permute-done((bf16[1,256,512]{2,1,0:T(8,128)(2,1)}, bf16[1,256,512]{2,1,0:T(8,128)(2,1)S(1)}, u32[]{:S(2)}, u32[]{:S(2)}) %collective-permute-start.15) | collective-permute-done | bytes 262176 | tf_op jit(solution)/shard_map/ppermute | solution.py:76
  240.4 9.9 %collective-permute-done.18 = bf16[1,256,512]{2,1,0:T(8,128)(2,1)S(1)} collective-permute-done((bf16[1,256,512]{2,1,0:T(8,128)(2,1)S(1)}, bf16[1,256,512]{2,1,0:T(8,128)(2,1)S(1)}, u32[]{:S(2)}, u32[]{:S(2)}) %collective-permute-start.18) | collective-permute-done | bytes 262176 | tf_op jit(solution)/shard_map/ppermute | solution.py:76
  261.4 8.8 %collective-permute-done.21 = bf16[8,256,1]{2,1,0:T(8,128)(2,1)S(1)} collective-permute-done((bf16[8,256,1]{2,1,0:T(8,128)(2,1)S(1)}, bf16[8,256,1]{2,1,0:T(8,128)(2,1)S(1)}, u32[]{:S(2)}, u32[]{:S(2)}) %collective-permute-start.21) | collective-permute-done | bytes 4128 | tf_op jit(solution)/shard_map/ppermute | solution.py:17
  270.2 4.8 collective-permute-done.22
  275.0 6.4 %fusion.64 = f32[8,258,514]{2,1,0:T(8,128)S(1)} fusion(bf16[8,1,512]{2,1,0:T(2,128)(2,1)S(1)} %collective-permute-done.23, bf16[8,1,512]{2,1,0:T(2,128)(2,1)S(1)} %collective-permute-done.20, bf16[8,256,1]{2,1,0:T(8,128)(2,1)S(1)} %collective-permute-done.22, bf16[4,256,512]{2,1,0:T(8,128)(2,1)S(1)} %constant_dynamic-update-slice_fusion.10, ...), kind=kLoop, calls=%fused_computation.126 | loop fusion | flops 16974336 | bytes 6365312 | tf_op jit(solution)/shard_map/convert_element_type | solution.py:144
  281.4 5.9 %fusion.49 = f32[7,256,512]{2,1,0:T(8,128)} fusion(f32[8,258,514]{2,1,0:T(8,128)S(1)} %fusion.64, f32[8,258,514]{2,1,0:T(8,128)S(1)} %bitcast.221), kind=kLoop, calls=%fused_computation.81 | loop fusion | flops 3670016 | bytes 18350080 | tf_op jit(solution)/shard_map/mul | solution.py:54
  287.3 13.4 %fusion.11 = (f32[]{:T(128)}, f32[]{:T(128)}, f32[8,256,512]{2,1,0:T(8,128)}) fusion(f32[8,256,512]{2,1,0:T(8,128)} %copy-done.4, bf16[4,256,512]{2,1,0:T(8,128)(2,1)} %copy-done.3, bf16[4,256,512]{2,1,0:T(8,128)(2,1)} %copy-done.2, f32[7,256,512]{2,1,0:T(8,128)} %fusion.49, f32[8,258,514]{2,1,0:T(8,128)S(1)} %fusion.64, f32[8,258,514]{2,1,0:T(8,128)S(1)} %bitcast.221), kind=kLoop, calls=%fused_computation.22 | loop fusion | flops 28311552 | bytes 56098824 | tf_op jit(solution)/shard_map/reduce_sum | solution.py:164
  302.0 12.5 %all_to_all.52 = f32[32,1,2]{2,1,0:T(1,128)S(1)} all-to-all(f32[32,1,2]{2,1,0:T(1,128)S(1)} %broadcast_in_dim.93), channel_id=1, replica_groups=mesh['px'=4,'py'=8] {'px','py'}, dimensions={0} | all-to-all | bytes 512 | tf_op jit(solution)/shard_map/all_to_all | solution.py:41
  325.5 7.3 %collective-permute-done.24 = bf16[1,256,512]{2,1,0:T(8,128)(2,1)S(1)} collective-permute-done((bf16[1,256,512]{2,1,0:T(8,128)(2,1)S(1)}, bf16[1,256,512]{2,1,0:T(8,128)(2,1)S(1)}, u32[]{:S(2)}, u32[]{:S(2)}) %collective-permute-start.24) | collective-permute-done | bytes 262176 | tf_op jit(solution)/shard_map/ppermute | solution.py:76
  332.8 10.2 %collective-permute-done.25 = bf16[1,256,512]{2,1,0:T(8,128)(2,1)S(1)} collective-permute-done((bf16[1,256,512]{2,1,0:T(8,128)(2,1)S(1)}, bf16[1,256,512]{2,1,0:T(8,128)(2,1)S(1)}, u32[]{:S(2)}, u32[]{:S(2)}) %collective-permute-start.25) | collective-permute-done | bytes 262176 | tf_op jit(solution)/shard_map/ppermute | solution.py:76
  344.1 5.0 collective-permute-start.29
  358.1 8.4 %collective-permute-done.27 = bf16[1,256,512]{2,1,0:T(8,128)(2,1)S(1)} collective-permute-done((bf16[1,256,512]{2,1,0:T(8,128)(2,1)}, bf16[1,256,512]{2,1,0:T(8,128)(2,1)S(1)}, u32[]{:S(2)}, u32[]{:S(2)}) %collective-permute-start.27) | collective-permute-done | bytes 262176 | tf_op jit(solution)/shard_map/ppermute | solution.py:76
  366.6 6.5 %collective-permute-done.28 = bf16[1,256,512]{2,1,0:T(8,128)(2,1)S(1)} collective-permute-done((bf16[1,256,512]{2,1,0:T(8,128)(2,1)S(1)}, bf16[1,256,512]{2,1,0:T(8,128)(2,1)S(1)}, u32[]{:S(2)}, u32[]{:S(2)}) %collective-permute-start.28) | collective-permute-done | bytes 262176 | tf_op jit(solution)/shard_map/ppermute | solution.py:76
  373.1 5.7 %convolution_convert_fusion.1 = bf16[256,2048]{1,0:T(8,128)(2,1)S(1)} fusion(bf16[2048,2048]{1,0:T(8,128)(2,1)} %param.11, bf16[1,256,2048]{2,1,0:T(8,128)(2,1)S(1)} %constant_dynamic-update-slice_fusion.3), kind=kOutput, calls=%fused_computation.135 | convolution fusion | flops 2148007936 | bytes 10485760 | tf_op jit(solution)/shard_map/dot_general | solution.py:87
  383.5 11.0 %fusion.74 = bf16[1,2048,256]{1,2,0:T(8,128)(2,1)S(1)} fusion(bf16[2048,2048]{1,0:T(8,128)(2,1)} %param.11, bf16[2048,256]{1,0:T(8,128)(2,1)S(1)} %bitcast.224, f32[]{:T(128)} %bitcast.21, f32[256]{0:T(256)S(1)} %dynamic_slice.114, f32[2048]{0:T(1024)S(1)} %copy-done.14), kind=kOutput, calls=%fused_computation.144 | convolution fusion | flops 4297588736 | bytes 10494980 | tf_op jit(solution)/shard_map/yj,kji->kyi/dot_general | solution.py:108
  402.8 7.6 %fusion.83 = bf16[1,2048,256]{1,2,0:T(8,128)(2,1)} fusion(bf16[2048,256]{1,0:T(8,128)(2,1)S(1)} %bitcast.226, bf16[2048,2048]{1,0:T(8,128)(2,1)} %param.11, f32[]{:T(128)} %bitcast.35, f32[256]{0:T(256)S(1)} %dynamic_slice.114, f32[2048]{0:T(1024)S(1)} %copy-done.14), kind=kOutput, calls=%fused_computation.153 | convolution fusion | flops 2149580800 | bytes 10494980 | tf_op jit(solution)/shard_map/jy,kyi->kji/dot_general | solution.py:94
  410.3 7.8 %all-to-all-done.6 = bf16[8,1,256,256]{3,2,1,0:T(8,128)(2,1)S(1)} async-done(((bf16[8,1,256,256]{3,2,1,0:T(8,128)(2,1)}), bf16[8,1,256,256]{3,2,1,0:T(8,128)(2,1)S(1)}, u32[]{:S(2)}, u32[]{:S(2)}) %all-to-all-start.6) | async-done | bytes 1048608 | tf_op jit(solution)/shard_map/all_to_all | solution.py:112
  418.1 5.7 %fusion.76 = bf16[1,256,2048]{2,1,0:T(8,128)(2,1)S(1)} fusion(bf16[8,256,2048]{2,1,0:T(8,128)(2,1)} %bitcast.234, bf16[8,1,256,256]{3,2,1,0:T(8,128)(2,1)S(1)} %all-to-all-done.6), kind=kOutput, calls=%fused_computation.146 | convolution fusion | flops 2148007936 | bytes 10485760 | tf_op jit(solution)/shard_map/qkyi,qix->kyx/dot_general | solution.py:113
  423.8 5.7 %fusion.75 = bf16[1,2048,256]{1,2,0:T(8,128)(2,1)S(1)} fusion(bf16[2048,2048]{1,0:T(8,128)(2,1)} %param.11, bf16[1,2048,256]{1,2,0:T(8,128)(2,1)S(1)} %copy-done.15), kind=kOutput, calls=%fused_computation.145 | convolution fusion | flops 2148007936 | bytes 10485760 | tf_op jit(solution)/shard_map/yj,kji->kyi/dot_general | solution.py:108
  439.2 7.1 %collective-permute-done.30 = bf16[1,256,512]{2,1,0:T(8,128)(2,1)S(1)} collective-permute-done((bf16[1,256,512]{2,1,0:T(8,128)(2,1)S(1)}, bf16[1,256,512]{2,1,0:T(8,128)(2,1)S(1)}, u32[]{:S(2)}, u32[]{:S(2)}) %collective-permute-start.30) | collective-permute-done | bytes 262176 | tf_op jit(solution)/shard_map/ppermute | solution.py:76
  449.8 5.7 %fusion.71 = bf16[256,2048]{1,0:T(8,128)(2,1)S(1)} fusion(bf16[8,256,2048]{2,1,0:T(8,128)(2,1)} %bitcast.235, bf16[8,1,256,256]{3,2,1,0:T(8,128)(2,1)S(1)} %all-to-all-done.8), kind=kOutput, calls=%fused_computation.133 | convolution fusion | flops 2148007936 | bytes 10485760 | tf_op jit(solution)/shard_map/qkyi,qix->kyx/dot_general | solution.py:113
  455.7 17.0 %collective-permute-done.31 = bf16[1,256,512]{2,1,0:T(8,128)(2,1)S(1)} collective-permute-done((bf16[1,256,512]{2,1,0:T(8,128)(2,1)}, bf16[1,256,512]{2,1,0:T(8,128)(2,1)S(1)}, u32[]{:S(2)}, u32[]{:S(2)}) %collective-permute-start.31) | collective-permute-done | bytes 262176 | tf_op jit(solution)/shard_map/ppermute | solution.py:76
  473.0 9.9 %collective-permute-done.34 = bf16[1,256,512]{2,1,0:T(8,128)(2,1)S(1)} collective-permute-done((bf16[1,256,512]{2,1,0:T(8,128)(2,1)S(1)}, bf16[1,256,512]{2,1,0:T(8,128)(2,1)S(1)}, u32[]{:S(2)}, u32[]{:S(2)}) %collective-permute-start.34) | collective-permute-done | bytes 262176 | tf_op jit(solution)/shard_map/ppermute | solution.py:76
  494.1 8.9 %collective-permute-done.37 = bf16[8,256,1]{2,1,0:T(8,128)(2,1)S(1)} collective-permute-done((bf16[8,256,1]{2,1,0:T(8,128)(2,1)S(1)}, bf16[8,256,1]{2,1,0:T(8,128)(2,1)S(1)}, u32[]{:S(2)}, u32[]{:S(2)}) %collective-permute-start.37) | collective-permute-done | bytes 4128 | tf_op jit(solution)/shard_map/ppermute | solution.py:17
  503.0 4.9 collective-permute-done.38
  507.9 6.4 %fusion.67 = f32[8,258,514]{2,1,0:T(8,128)S(1)} fusion(bf16[8,1,512]{2,1,0:T(2,128)(2,1)S(1)} %collective-permute-done.39, bf16[8,1,512]{2,1,0:T(2,128)(2,1)S(1)} %collective-permute-done.36, bf16[8,256,1]{2,1,0:T(8,128)(2,1)S(1)} %collective-permute-done.38, bf16[4,256,512]{2,1,0:T(8,128)(2,1)S(1)} %constant_dynamic-update-slice_fusion.23, ...), kind=kLoop, calls=%fused_computation.129 | loop fusion | flops 16974336 | bytes 6365312 | tf_op jit(solution)/shard_map/convert_element_type | solution.py:144
  514.3 5.9 %fusion.48 = f32[7,256,512]{2,1,0:T(8,128)} fusion(f32[8,258,514]{2,1,0:T(8,128)S(1)} %fusion.67, f32[8,258,514]{2,1,0:T(8,128)S(1)} %bitcast.223), kind=kLoop, calls=%fused_computation.79 | loop fusion | flops 3670016 | bytes 18350080 | tf_op jit(solution)/shard_map/mul | solution.py:54
  520.2 14.2 %fusion.8 = (f32[]{:T(128)}, f32[]{:T(128)}, f32[]{:T(128)}, f32[]{:T(128)}, f32[8,256,512]{2,1,0:T(8,128)}) fusion(f32[8,256,512]{2,1,0:T(8,128)} %copy-done.5, bf16[4,256,512]{2,1,0:T(8,128)(2,1)} %copy-done.8, bf16[4,256,512]{2,1,0:T(8,128)(2,1)} %copy-done.7, f32[8,256,512]{2,1,0:T(8,128)} %get-tuple-element.34, bf16[4,256,512]{2,1,0:T(8,128)(2,1)} %copy-done.3, ...), kind=kLoop, calls=%fused_computation.19 | loop fusion | flops 34603004 | bytes 62390288 | tf_op jit(solution)/shard_map/reduce_sum | solution.py:171
  536.9 12.3 %all_to_all.53 = f32[32,1,4]{2,1,0:T(1,128)S(1)} all-to-all(f32[32,1,4]{2,1,0:T(1,128)S(1)} %broadcast_in_dim.94), channel_id=1, replica_groups=mesh['px'=4,'py'=8] {'px','py'}, dimensions={0} | all-to-all | bytes 1024 | tf_op jit(solution)/shard_map/all_to_all | solution.py:41
  554.3 7.2 %fusion.14 = (f32[8,256,512]{2,1,0:T(8,128)}, f32[8,256,512]{2,1,0:T(8,128)}) fusion(f32[8,256,512]{2,1,0:T(8,128)} %param.8, f32[]{:T(128)S(6)} %div.27, f32[]{:T(128)S(6)} %div.23, bf16[4,256,512]{2,1,0:T(8,128)(2,1)} %copy-done.3, bf16[4,256,512]{2,1,0:T(8,128)(2,1)} %copy-done.2, f32[]{:T(128)S(6)} %div.26, bf16[4,256,512]{2,1,0:T(8,128)(2,1)} %copy-done.8, ...), kind=kLoop, calls=%fused_computation.25 | loop fusion | flops 10485760 | bytes 16777228 | tf_op jit(solution)/shard_map/add | solution.py:184
  (201 shorter events, 162.3 us)
Async XLA Ops:
  18.7 28.5 %collective-permute-start = (bf16[8,1,512]{2,1,0:T(2,128)(2,1)S(1)}, bf16[8,1,512]{2,1,0:T(2,128)(2,1)S(1)}, u32[]{:S(2)}, u32[]{:S(2)}) collective-permute-start(bf16[8,1,512]{2,1,0:T(2,128)(2,1)S(1)} %get-tuple-element.45), channel_id=1, source_target_pairs={{0,1},{1,2},{2,3},{3,4},{4,5},{5,6},{6,7},{8,9},{9,10},{10,11},{11... | collective-permute-start | bytes 24584 | tf_op jit(solution)/shard_map/ppermute | solution.py:17
  21.0 27.7 %collective-permute-start.3 = (bf16[8,1,512]{2,1,0:T(2,128)(2,1)S(1)}, bf16[8,1,512]{2,1,0:T(2,128)(2,1)S(1)}, u32[]{:S(2)}, u32[]{:S(2)}) collective-permute-start(bf16[8,1,512]{2,1,0:T(2,128)(2,1)S(1)} %get-tuple-element.46), channel_id=1, source_target_pairs={{1,0},{2,1},{3,2},{4,3},{5,4},{6,5},{7,6},{9,8},{10,9},{11,10},{12... | collective-permute-start | bytes 24584 | tf_op jit(solution)/shard_map/ppermute | solution.py:17
  23.6 15.4 %collective-permute-start.1 = (bf16[8,256,1]{2,1,0:T(8,128)(2,1)}, bf16[8,256,1]{2,1,0:T(8,128)(2,1)S(1)}, u32[]{:S(2)}, u32[]{:S(2)}) collective-permute-start(bf16[8,256,1]{2,1,0:T(8,128)(2,1)} %get-tuple-element.43), channel_id=1, source_target_pairs={{0,8},{8,16},{16,24},{1,9},{9,17},{17,25},{2,10},{10,18},{18,26},{... | collective-permute-start | bytes 12296 | tf_op jit(solution)/shard_map/ppermute | solution.py:17
  27.9 15.7 %collective-permute-start.2 = (bf16[8,256,1]{2,1,0:T(8,128)(2,1)}, bf16[8,256,1]{2,1,0:T(8,128)(2,1)S(1)}, u32[]{:S(2)}, u32[]{:S(2)}) collective-permute-start(bf16[8,256,1]{2,1,0:T(8,128)(2,1)} %get-tuple-element.44), channel_id=1, source_target_pairs={{8,0},{16,8},{24,16},{9,1},{17,9},{25,17},{10,2},{18,10},{26,18},{... | collective-permute-start | bytes 12296 | tf_op jit(solution)/shard_map/ppermute | solution.py:17
  29.6 34.4 %collective-permute-start.4 = (bf16[8,1,512]{2,1,0:T(2,128)(2,1)S(1)}, bf16[8,1,512]{2,1,0:T(2,128)(2,1)S(1)}, u32[]{:S(2)}, u32[]{:S(2)}) collective-permute-start(bf16[8,1,512]{2,1,0:T(2,128)(2,1)S(1)} %get-tuple-element.49), channel_id=1, source_target_pairs={{0,1},{1,2},{2,3},{3,4},{4,5},{5,6},{6,7},{8,9},{9,10},{10,11},{11... | collective-permute-start | bytes 24584 | tf_op jit(solution)/shard_map/ppermute | solution.py:17
  39.0 24.9 %collective-permute-start.7 = (bf16[8,1,512]{2,1,0:T(2,128)(2,1)S(1)}, bf16[8,1,512]{2,1,0:T(2,128)(2,1)S(1)}, u32[]{:S(2)}, u32[]{:S(2)}) collective-permute-start(bf16[8,1,512]{2,1,0:T(2,128)(2,1)S(1)} %get-tuple-element.50), channel_id=1, source_target_pairs={{1,0},{2,1},{3,2},{4,3},{5,4},{6,5},{7,6},{9,8},{10,9},{11,10},{12... | collective-permute-start | bytes 24584 | tf_op jit(solution)/shard_map/ppermute | solution.py:17
  43.7 16.0 %collective-permute-start.5 = (bf16[8,256,1]{2,1,0:T(8,128)(2,1)}, bf16[8,256,1]{2,1,0:T(8,128)(2,1)S(1)}, u32[]{:S(2)}, u32[]{:S(2)}) collective-permute-start(bf16[8,256,1]{2,1,0:T(8,128)(2,1)} %get-tuple-element.47), channel_id=1, source_target_pairs={{0,8},{8,16},{16,24},{1,9},{9,17},{17,25},{2,10},{10,18},{18,26},{... | collective-permute-start | bytes 12296 | tf_op jit(solution)/shard_map/ppermute | solution.py:17
  47.2 16.8 %collective-permute-start.6 = (bf16[8,256,1]{2,1,0:T(8,128)(2,1)}, bf16[8,256,1]{2,1,0:T(8,128)(2,1)S(1)}, u32[]{:S(2)}, u32[]{:S(2)}) collective-permute-start(bf16[8,256,1]{2,1,0:T(8,128)(2,1)} %get-tuple-element.48), channel_id=1, source_target_pairs={{8,0},{16,8},{24,16},{9,1},{17,9},{25,17},{10,2},{18,10},{26,18},{... | collective-permute-start | bytes 12296 | tf_op jit(solution)/shard_map/ppermute | solution.py:17
  85.7 11.2 %collective-permute-start.8 = (bf16[1,256,512]{2,1,0:T(8,128)(2,1)S(1)}, bf16[1,256,512]{2,1,0:T(8,128)(2,1)S(1)}, u32[]{:S(2)}, u32[]{:S(2)}) collective-permute-start(bf16[1,256,512]{2,1,0:T(8,128)(2,1)S(1)} %get-tuple-element.79), channel_id=1, source_target_pairs={{0,8},{8,16},{16,24},{24,0},{1,9},{9,17},{17,25},{25,1},{2,10},{10... | collective-permute-start | bytes 786440 | tf_op jit(solution)/shard_map/ppermute | solution.py:76
  87.3 19.7 %collective-permute-start.9 = (bf16[1,256,512]{2,1,0:T(8,128)(2,1)S(1)}, bf16[1,256,512]{2,1,0:T(8,128)(2,1)S(1)}, u32[]{:S(2)}, u32[]{:S(2)}) collective-permute-start(bf16[1,256,512]{2,1,0:T(8,128)(2,1)S(1)} %get-tuple-element.78), channel_id=1, source_target_pairs={{0,16},{8,24},{16,0},{24,8},{1,17},{9,25},{17,1},{25,9},{2,18},{10... | collective-permute-start | bytes 786440 | tf_op jit(solution)/shard_map/ppermute | solution.py:76
  87.3 19.7 %collective-permute-start.10 = (bf16[1,256,512]{2,1,0:T(8,128)(2,1)S(1)}, bf16[1,256,512]{2,1,0:T(8,128)(2,1)S(1)}, u32[]{:S(2)}, u32[]{:S(2)}) collective-permute-start(bf16[1,256,512]{2,1,0:T(8,128)(2,1)S(1)} %get-tuple-element.77), channel_id=1, source_target_pairs={{0,24},{8,0},{16,8},{24,16},{1,25},{9,1},{17,9},{25,17},{2,26},{10... | collective-permute-start | bytes 786440 | tf_op jit(solution)/shard_map/ppermute | solution.py:76
  109.7 30.6 %collective-permute-start.13 = (bf16[1,256,512]{2,1,0:T(8,128)(2,1)S(1)}, bf16[1,256,512]{2,1,0:T(8,128)(2,1)S(1)}, u32[]{:S(2)}, u32[]{:S(2)}) collective-permute-start(bf16[1,256,512]{2,1,0:T(8,128)(2,1)S(1)} %get-tuple-element.73), channel_id=1, source_target_pairs={{0,24},{8,0},{16,8},{24,16},{1,25},{9,1},{17,9},{25,17},{2,26},{10... | collective-permute-start | bytes 786440 | tf_op jit(solution)/shard_map/ppermute | solution.py:76
  115.7 24.5 %collective-permute-start.12 = (bf16[1,256,512]{2,1,0:T(8,128)(2,1)S(1)}, bf16[1,256,512]{2,1,0:T(8,128)(2,1)S(1)}, u32[]{:S(2)}, u32[]{:S(2)}) collective-permute-start(bf16[1,256,512]{2,1,0:T(8,128)(2,1)S(1)} %get-tuple-element.74), channel_id=1, source_target_pairs={{0,16},{8,24},{16,0},{24,8},{1,17},{9,25},{17,1},{25,9},{2,18},{10... | collective-permute-start | bytes 786440 | tf_op jit(solution)/shard_map/ppermute | solution.py:76
  117.2 16.5 %collective-permute-start.11 = (bf16[1,256,512]{2,1,0:T(8,128)(2,1)}, bf16[1,256,512]{2,1,0:T(8,128)(2,1)S(1)}, u32[]{:S(2)}, u32[]{:S(2)}) collective-permute-start(bf16[1,256,512]{2,1,0:T(8,128)(2,1)} %get-tuple-element.75), channel_id=1, source_target_pairs={{0,8},{8,16},{16,24},{24,0},{1,9},{9,17},{17,25},{25,1},{2,10},{10... | collective-permute-start | bytes 786440 | tf_op jit(solution)/shard_map/ppermute | solution.py:76
  124.0 23.1 %all-to-all-start = ((bf16[8,256,256]{2,1,0:T(8,128)(2,1)}), bf16[8,256,256]{2,1,0:T(8,128)(2,1)S(1)}, u32[]{:S(2)}, u32[]{:S(2)}) async-start(bf16[8,256,256]{2,1,0:T(8,128)(2,1)} %bitcast.219), calls=%async_computation | async-start | bytes 2097152 | tf_op jit(solution)/shard_map/all_to_all | solution.py:91
  147.1 18.9 %all-to-all-start.2 = ((bf16[8,256,256]{2,1,0:T(8,128)(2,1)}), bf16[8,256,256]{2,1,0:T(8,128)(2,1)S(1)}, u32[]{:S(2)}, u32[]{:S(2)}) async-start(bf16[8,256,256]{2,1,0:T(8,128)(2,1)} %bitcast.217), calls=%async_computation.2 | async-start | bytes 2097152 | tf_op jit(solution)/shard_map/all_to_all | solution.py:91
  166.0 19.3 %all-to-all-start.1 = ((bf16[8,1,256,256]{3,2,1,0:T(8,128)(2,1)}), bf16[8,1,256,256]{3,2,1,0:T(8,128)(2,1)S(1)}, u32[]{:S(2)}, u32[]{:S(2)}) async-start(bf16[8,1,256,256]{3,2,1,0:T(8,128)(2,1)} %bitcast.25), calls=%async_computation.1 | async-start | bytes 2097152 | tf_op jit(solution)/shard_map/all_to_all | solution.py:112
  198.2 18.9 %all-to-all-start.3 = ((bf16[8,1,256,256]{3,2,1,0:T(8,128)(2,1)}), bf16[8,1,256,256]{3,2,1,0:T(8,128)(2,1)S(1)}, u32[]{:S(2)}, u32[]{:S(2)}) async-start(bf16[8,1,256,256]{3,2,1,0:T(8,128)(2,1)} %bitcast.39), calls=%async_computation.3 | async-start | bytes 2097152 | tf_op jit(solution)/shard_map/all_to_all | solution.py:112
  202.8 11.2 %collective-permute-start.14 = (bf16[1,256,512]{2,1,0:T(8,128)(2,1)}, bf16[1,256,512]{2,1,0:T(8,128)(2,1)S(1)}, u32[]{:S(2)}, u32[]{:S(2)}) collective-permute-start(bf16[1,256,512]{2,1,0:T(8,128)(2,1)} %get-tuple-element.68), channel_id=1, source_target_pairs={{0,8},{8,16},{16,24},{24,0},{1,9},{9,17},{17,25},{25,1},{2,10},{10... | collective-permute-start | bytes 786440 | tf_op jit(solution)/shard_map/ppermute | solution.py:76
  202.8 37.3 %collective-permute-start.16 = (bf16[1,256,512]{2,1,0:T(8,128)(2,1)S(1)}, bf16[1,256,512]{2,1,0:T(8,128)(2,1)S(1)}, u32[]{:S(2)}, u32[]{:S(2)}) collective-permute-start(bf16[1,256,512]{2,1,0:T(8,128)(2,1)S(1)} %get-tuple-element.66), channel_id=1, source_target_pairs={{0,24},{8,0},{16,8},{24,16},{1,25},{9,1},{17,9},{25,17},{2,26},{10... | collective-permute-start | bytes 786440 | tf_op jit(solution)/shard_map/ppermute | solution.py:76
  206.6 33.4 %collective-permute-start.15 = (bf16[1,256,512]{2,1,0:T(8,128)(2,1)}, bf16[1,256,512]{2,1,0:T(8,128)(2,1)S(1)}, u32[]{:S(2)}, u32[]{:S(2)}) collective-permute-start(bf16[1,256,512]{2,1,0:T(8,128)(2,1)} %get-tuple-element.67), channel_id=1, source_target_pairs={{0,16},{8,24},{16,0},{24,8},{1,17},{9,25},{17,1},{25,9},{2,18},{10... | collective-permute-start | bytes 786440 | tf_op jit(solution)/shard_map/ppermute | solution.py:76
  222.9 17.4 %collective-permute-start.17 = (bf16[1,256,512]{2,1,0:T(8,128)(2,1)S(1)}, bf16[1,256,512]{2,1,0:T(8,128)(2,1)S(1)}, u32[]{:S(2)}, u32[]{:S(2)}) collective-permute-start(bf16[1,256,512]{2,1,0:T(8,128)(2,1)S(1)} %get-tuple-element.72), channel_id=1, source_target_pairs={{0,8},{8,16},{16,24},{24,0},{1,9},{9,17},{17,25},{25,1},{2,10},{10... | collective-permute-start | bytes 786440 | tf_op jit(solution)/shard_map/ppermute | solution.py:76
  240.0 10.2 %collective-permute-start.18 = (bf16[1,256,512]{2,1,0:T(8,128)(2,1)S(1)}, bf16[1,256,512]{2,1,0:T(8,128)(2,1)S(1)}, u32[]{:S(2)}, u32[]{:S(2)}) collective-permute-start(bf16[1,256,512]{2,1,0:T(8,128)(2,1)S(1)} %get-tuple-element.71), channel_id=1, source_target_pairs={{0,16},{8,24},{16,0},{24,8},{1,17},{9,25},{17,1},{25,9},{2,18},{10... | collective-permute-start | bytes 786440 | tf_op jit(solution)/shard_map/ppermute | solution.py:76
  240.1 13.1 %collective-permute-start.19 = (bf16[1,256,512]{2,1,0:T(8,128)(2,1)S(1)}, bf16[1,256,512]{2,1,0:T(8,128)(2,1)S(1)}, u32[]{:S(2)}, u32[]{:S(2)}) collective-permute-start(bf16[1,256,512]{2,1,0:T(8,128)(2,1)S(1)} %get-tuple-element.70), channel_id=1, source_target_pairs={{0,24},{8,0},{16,8},{24,16},{1,25},{9,1},{17,9},{25,17},{2,26},{10... | collective-permute-start | bytes 786440 | tf_op jit(solution)/shard_map/ppermute | solution.py:76
  253.4 21.7 %collective-permute-start.20 = (bf16[8,1,512]{2,1,0:T(2,128)(2,1)S(1)}, bf16[8,1,512]{2,1,0:T(2,128)(2,1)S(1)}, u32[]{:S(2)}, u32[]{:S(2)}) collective-permute-start(bf16[8,1,512]{2,1,0:T(2,128)(2,1)S(1)} %get-tuple-element.41), channel_id=1, source_target_pairs={{0,1},{1,2},{2,3},{3,4},{4,5},{5,6},{6,7},{8,9},{9,10},{10,11},{11... | collective-permute-start | bytes 24584 | tf_op jit(solution)/shard_map/ppermute | solution.py:17
  254.7 20.4 %collective-permute-start.23 = (bf16[8,1,512]{2,1,0:T(2,128)(2,1)S(1)}, bf16[8,1,512]{2,1,0:T(2,128)(2,1)S(1)}, u32[]{:S(2)}, u32[]{:S(2)}) collective-permute-start(bf16[8,1,512]{2,1,0:T(2,128)(2,1)S(1)} %get-tuple-element.42), channel_id=1, source_target_pairs={{1,0},{2,1},{3,2},{4,3},{5,4},{6,5},{7,6},{9,8},{10,9},{11,10},{12... | collective-permute-start | bytes 24584 | tf_op jit(solution)/shard_map/ppermute | solution.py:17
  256.2 14.0 %collective-permute-start.21 = (bf16[8,256,1]{2,1,0:T(8,128)(2,1)S(1)}, bf16[8,256,1]{2,1,0:T(8,128)(2,1)S(1)}, u32[]{:S(2)}, u32[]{:S(2)}) collective-permute-start(bf16[8,256,1]{2,1,0:T(8,128)(2,1)S(1)} %get-tuple-element.39), channel_id=1, source_target_pairs={{0,8},{8,16},{16,24},{1,9},{9,17},{17,25},{2,10},{10,18},{18,26},{... | collective-permute-start | bytes 12296 | tf_op jit(solution)/shard_map/ppermute | solution.py:17
  259.8 15.2 %collective-permute-start.22 = (bf16[8,256,1]{2,1,0:T(8,128)(2,1)S(1)}, bf16[8,256,1]{2,1,0:T(8,128)(2,1)S(1)}, u32[]{:S(2)}, u32[]{:S(2)}) collective-permute-start(bf16[8,256,1]{2,1,0:T(8,128)(2,1)S(1)} %get-tuple-element.40), channel_id=1, source_target_pairs={{8,0},{16,8},{24,16},{9,1},{17,9},{25,17},{10,2},{18,10},{26,18},{... | collective-permute-start | bytes 12296 | tf_op jit(solution)/shard_map/ppermute | solution.py:17
  321.6 11.1 %collective-permute-start.24 = (bf16[1,256,512]{2,1,0:T(8,128)(2,1)S(1)}, bf16[1,256,512]{2,1,0:T(8,128)(2,1)S(1)}, u32[]{:S(2)}, u32[]{:S(2)}) collective-permute-start(bf16[1,256,512]{2,1,0:T(8,128)(2,1)S(1)} %get-tuple-element.64), channel_id=1, source_target_pairs={{0,8},{8,16},{16,24},{24,0},{1,9},{9,17},{17,25},{25,1},{2,10},{10... | collective-permute-start | bytes 786440 | tf_op jit(solution)/shard_map/ppermute | solution.py:76
  322.2 20.7 %collective-permute-start.25 = (bf16[1,256,512]{2,1,0:T(8,128)(2,1)S(1)}, bf16[1,256,512]{2,1,0:T(8,128)(2,1)S(1)}, u32[]{:S(2)}, u32[]{:S(2)}) collective-permute-start(bf16[1,256,512]{2,1,0:T(8,128)(2,1)S(1)} %get-tuple-element.63), channel_id=1, source_target_pairs={{0,16},{8,24},{16,0},{24,8},{1,17},{9,25},{17,1},{25,9},{2,18},{10... | collective-permute-start | bytes 786440 | tf_op jit(solution)/shard_map/ppermute | solution.py:76
  322.8 20.2 %collective-permute-start.26 = (bf16[1,256,512]{2,1,0:T(8,128)(2,1)S(1)}, bf16[1,256,512]{2,1,0:T(8,128)(2,1)S(1)}, u32[]{:S(2)}, u32[]{:S(2)}) collective-permute-start(bf16[1,256,512]{2,1,0:T(8,128)(2,1)S(1)} %get-tuple-element.62), channel_id=1, source_target_pairs={{0,24},{8,0},{16,8},{24,16},{1,25},{9,1},{17,9},{25,17},{2,26},{10... | collective-permute-start | bytes 786440 | tf_op jit(solution)/shard_map/ppermute | solution.py:76
  344.1 29.0 %collective-permute-start.29 = (bf16[1,256,512]{2,1,0:T(8,128)(2,1)S(1)}, bf16[1,256,512]{2,1,0:T(8,128)(2,1)S(1)}, u32[]{:S(2)}, u32[]{:S(2)}) collective-permute-start(bf16[1,256,512]{2,1,0:T(8,128)(2,1)S(1)} %get-tuple-element.58), channel_id=1, source_target_pairs={{0,24},{8,0},{16,8},{24,16},{1,25},{9,1},{17,9},{25,17},{2,26},{10... | collective-permute-start | bytes 786440 | tf_op jit(solution)/shard_map/ppermute | solution.py:76
  349.1 24.0 %collective-permute-start.28 = (bf16[1,256,512]{2,1,0:T(8,128)(2,1)S(1)}, bf16[1,256,512]{2,1,0:T(8,128)(2,1)S(1)}, u32[]{:S(2)}, u32[]{:S(2)}) collective-permute-start(bf16[1,256,512]{2,1,0:T(8,128)(2,1)S(1)} %get-tuple-element.59), channel_id=1, source_target_pairs={{0,16},{8,24},{16,0},{24,8},{1,17},{9,25},{17,1},{25,9},{2,18},{10... | collective-permute-start | bytes 786440 | tf_op jit(solution)/shard_map/ppermute | solution.py:76
  350.8 15.7 %collective-permute-start.27 = (bf16[1,256,512]{2,1,0:T(8,128)(2,1)}, bf16[1,256,512]{2,1,0:T(8,128)(2,1)S(1)}, u32[]{:S(2)}, u32[]{:S(2)}) collective-permute-start(bf16[1,256,512]{2,1,0:T(8,128)(2,1)} %get-tuple-element.60), channel_id=1, source_target_pairs={{0,8},{8,16},{16,24},{24,0},{1,9},{9,17},{17,25},{25,1},{2,10},{10... | collective-permute-start | bytes 786440 | tf_op jit(solution)/shard_map/ppermute | solution.py:76
  354.5 25.4 %all-to-all-start.5 = ((bf16[8,256,256]{2,1,0:T(8,128)(2,1)}), bf16[8,256,256]{2,1,0:T(8,128)(2,1)S(1)}, u32[]{:S(2)}, u32[]{:S(2)}) async-start(bf16[8,256,256]{2,1,0:T(8,128)(2,1)} %bitcast.215), calls=%async_computation.5 | async-start | bytes 2097152 | tf_op jit(solution)/shard_map/all_to_all | solution.py:91
  379.9 18.9 %all-to-all-start.7 = ((bf16[8,256,256]{2,1,0:T(8,128)(2,1)}), bf16[8,256,256]{2,1,0:T(8,128)(2,1)S(1)}, u32[]{:S(2)}, u32[]{:S(2)}) async-start(bf16[8,256,256]{2,1,0:T(8,128)(2,1)} %bitcast.213), calls=%async_computation.7 | async-start | bytes 2097152 | tf_op jit(solution)/shard_map/all_to_all | solution.py:91
  398.8 19.3 %all-to-all-start.6 = ((bf16[8,1,256,256]{3,2,1,0:T(8,128)(2,1)}), bf16[8,1,256,256]{3,2,1,0:T(8,128)(2,1)S(1)}, u32[]{:S(2)}, u32[]{:S(2)}) async-start(bf16[8,1,256,256]{3,2,1,0:T(8,128)(2,1)} %bitcast.58), calls=%async_computation.6 | async-start | bytes 2097152 | tf_op jit(solution)/shard_map/all_to_all | solution.py:112
  430.9 18.9 %all-to-all-start.8 = ((bf16[8,1,256,256]{3,2,1,0:T(8,128)(2,1)}), bf16[8,1,256,256]{3,2,1,0:T(8,128)(2,1)S(1)}, u32[]{:S(2)}, u32[]{:S(2)}) async-start(bf16[8,1,256,256]{3,2,1,0:T(8,128)(2,1)} %bitcast.70), calls=%async_computation.8 | async-start | bytes 2097152 | tf_op jit(solution)/shard_map/all_to_all | solution.py:112
  435.4 11.0 %collective-permute-start.30 = (bf16[1,256,512]{2,1,0:T(8,128)(2,1)S(1)}, bf16[1,256,512]{2,1,0:T(8,128)(2,1)S(1)}, u32[]{:S(2)}, u32[]{:S(2)}) collective-permute-start(bf16[1,256,512]{2,1,0:T(8,128)(2,1)S(1)} %get-tuple-element.53), channel_id=1, source_target_pairs={{0,8},{8,16},{16,24},{24,0},{1,9},{9,17},{17,25},{25,1},{2,10},{10... | collective-permute-start | bytes 786440 | tf_op jit(solution)/shard_map/ppermute | solution.py:76
  435.4 37.4 %collective-permute-start.32 = (bf16[1,256,512]{2,1,0:T(8,128)(2,1)S(1)}, bf16[1,256,512]{2,1,0:T(8,128)(2,1)S(1)}, u32[]{:S(2)}, u32[]{:S(2)}) collective-permute-start(bf16[1,256,512]{2,1,0:T(8,128)(2,1)S(1)} %get-tuple-element.51), channel_id=1, source_target_pairs={{0,24},{8,0},{16,8},{24,16},{1,25},{9,1},{17,9},{25,17},{2,26},{10... | collective-permute-start | bytes 786440 | tf_op jit(solution)/shard_map/ppermute | solution.py:76
  439.2 33.4 %collective-permute-start.31 = (bf16[1,256,512]{2,1,0:T(8,128)(2,1)}, bf16[1,256,512]{2,1,0:T(8,128)(2,1)S(1)}, u32[]{:S(2)}, u32[]{:S(2)}) collective-permute-start(bf16[1,256,512]{2,1,0:T(8,128)(2,1)} %get-tuple-element.52), channel_id=1, source_target_pairs={{0,16},{8,24},{16,0},{24,8},{1,17},{9,25},{17,1},{25,9},{2,18},{10... | collective-permute-start | bytes 786440 | tf_op jit(solution)/shard_map/ppermute | solution.py:76
  455.6 17.4 %collective-permute-start.33 = (bf16[1,256,512]{2,1,0:T(8,128)(2,1)S(1)}, bf16[1,256,512]{2,1,0:T(8,128)(2,1)S(1)}, u32[]{:S(2)}, u32[]{:S(2)}) collective-permute-start(bf16[1,256,512]{2,1,0:T(8,128)(2,1)S(1)} %get-tuple-element.57), channel_id=1, source_target_pairs={{0,8},{8,16},{16,24},{24,0},{1,9},{9,17},{17,25},{25,1},{2,10},{10... | collective-permute-start | bytes 786440 | tf_op jit(solution)/shard_map/ppermute | solution.py:76
  472.7 10.2 %collective-permute-start.34 = (bf16[1,256,512]{2,1,0:T(8,128)(2,1)S(1)}, bf16[1,256,512]{2,1,0:T(8,128)(2,1)S(1)}, u32[]{:S(2)}, u32[]{:S(2)}) collective-permute-start(bf16[1,256,512]{2,1,0:T(8,128)(2,1)S(1)} %get-tuple-element.56), channel_id=1, source_target_pairs={{0,16},{8,24},{16,0},{24,8},{1,17},{9,25},{17,1},{25,9},{2,18},{10... | collective-permute-start | bytes 786440 | tf_op jit(solution)/shard_map/ppermute | solution.py:76
  472.8 13.2 %collective-permute-start.35 = (bf16[1,256,512]{2,1,0:T(8,128)(2,1)S(1)}, bf16[1,256,512]{2,1,0:T(8,128)(2,1)S(1)}, u32[]{:S(2)}, u32[]{:S(2)}) collective-permute-start(bf16[1,256,512]{2,1,0:T(8,128)(2,1)S(1)} %get-tuple-element.55), channel_id=1, source_target_pairs={{0,24},{8,0},{16,8},{24,16},{1,25},{9,1},{17,9},{25,17},{2,26},{10... | collective-permute-start | bytes 786440 | tf_op jit(solution)/shard_map/ppermute | solution.py:76
  486.1 21.8 %collective-permute-start.36 = (bf16[8,1,512]{2,1,0:T(2,128)(2,1)S(1)}, bf16[8,1,512]{2,1,0:T(2,128)(2,1)S(1)}, u32[]{:S(2)}, u32[]{:S(2)}) collective-permute-start(bf16[8,1,512]{2,1,0:T(2,128)(2,1)S(1)} %get-tuple-element.37), channel_id=1, source_target_pairs={{0,1},{1,2},{2,3},{3,4},{4,5},{5,6},{6,7},{8,9},{9,10},{10,11},{11... | collective-permute-start | bytes 24584 | tf_op jit(solution)/shard_map/ppermute | solution.py:17
  487.4 20.5 %collective-permute-start.39 = (bf16[8,1,512]{2,1,0:T(2,128)(2,1)S(1)}, bf16[8,1,512]{2,1,0:T(2,128)(2,1)S(1)}, u32[]{:S(2)}, u32[]{:S(2)}) collective-permute-start(bf16[8,1,512]{2,1,0:T(2,128)(2,1)S(1)} %get-tuple-element.38), channel_id=1, source_target_pairs={{1,0},{2,1},{3,2},{4,3},{5,4},{6,5},{7,6},{9,8},{10,9},{11,10},{12... | collective-permute-start | bytes 24584 | tf_op jit(solution)/shard_map/ppermute | solution.py:17
  488.9 14.1 %collective-permute-start.37 = (bf16[8,256,1]{2,1,0:T(8,128)(2,1)S(1)}, bf16[8,256,1]{2,1,0:T(8,128)(2,1)S(1)}, u32[]{:S(2)}, u32[]{:S(2)}) collective-permute-start(bf16[8,256,1]{2,1,0:T(8,128)(2,1)S(1)} %get-tuple-element.35), channel_id=1, source_target_pairs={{0,8},{8,16},{16,24},{1,9},{9,17},{17,25},{2,10},{10,18},{18,26},{... | collective-permute-start | bytes 12296 | tf_op jit(solution)/shard_map/ppermute | solution.py:17
  492.5 15.3 %collective-permute-start.38 = (bf16[8,256,1]{2,1,0:T(8,128)(2,1)S(1)}, bf16[8,256,1]{2,1,0:T(8,128)(2,1)S(1)}, u32[]{:S(2)}, u32[]{:S(2)}) collective-permute-start(bf16[8,256,1]{2,1,0:T(8,128)(2,1)S(1)} %get-tuple-element.36), channel_id=1, source_target_pairs={{8,0},{16,8},{24,16},{9,1},{17,9},{25,17},{10,2},{18,10},{26,18},{... | collective-permute-start | bytes 12296 | tf_op jit(solution)/shard_map/ppermute | solution.py:17
  (23 other events, 386.3 us)

commit v8 on v6

--- a/solution.py
+++ b/solution.py
@@ -51,14 +51,11 @@
         neighbour = padded[:, shift_y : shift_y + height, shift_x : shift_x + width]
         other = coeff_pad[:, shift_y : shift_y + height, shift_x : shift_x + width]
         result = result + 0.5 * (coeff + other) * (values - neighbour)
-    vertical = 0.5 * (coeff[:-1] + coeff[1:]) * (values[:-1] - values[1:])
-    zero_layer = jnp.zeros_like(values[:1])
-    result = (
-        result
-        + jnp.concatenate((vertical, zero_layer), 0)
-        - jnp.concatenate((zero_layer, vertical), 0)
-    )
-    return result
+    coeff_next = jnp.concatenate((coeff[1:], coeff[-1:]), 0)
+    values_next = jnp.concatenate((values[1:], values[-1:]), 0)
+    downward = 0.5 * (coeff + coeff_next) * (values - values_next)
+    upward = jnp.concatenate((jnp.zeros_like(downward[:1]), downward[:-1]), 0)
+    return result + downward - upward
 
 
 def exchange(block, axis, split_axis, concat_axis):
@@ -132,9 +129,11 @@
 
 
 def shards(right_side, solution_in, classes, coeff_table, eigenvectors, eigenvalues, level_shift):
-    coeff = jnp.zeros(classes.shape, jnp.float32)
+    labels = classes.astype(jnp.bfloat16)
+    table = coeff_table.astype(jnp.bfloat16)
+    coeff = jnp.zeros(classes.shape, jnp.bfloat16)
     for label in range(coeff_table.shape[0]):
-        coeff = jnp.where(classes == label, coeff_table[label], coeff)
+        coeff = jnp.where(labels == label, table[label], coeff)
     stacked = padded_2(
         jnp.stack((solution_in, coeff)).astype(jnp.bfloat16), (("px", 3), ("py", 2)), 1
     ).astype(jnp.float32)

time: 546 us -> 554 us (1.015)
  local copies, waits for them, and re-layouts: 37.2 us -> 57.7 us
  other arithmetic: 121 us -> 108 us
  waiting for transfers between devices: 151 us -> 143 us
  blocking collectives: 26.3 us -> 32.5 us
    mul x3, other arithmetic: 17.8 us -> 9.2 us  [face_sum(): downward = 0.5 * (coeff + coeff_next) * (values - values_next)]
    slice x1 -> x12, local copies, waits for them, and re-layouts: 1.95 us -> 10.1 us  [the longest x6 4.57 us: face_sum(): values_next = jnp.concatenate((values[1:], values[-1:]), 0)]
    all_to_all x2, blocking collectives: 26.3 us -> 32.5 us  [all_sum(): return jnp.sum(lax.all_to_all(spread, axes, 0, 0, tiled=True), 0)]
  transfers between devices with their start and end apart: 44 -> 44, of which waited for: 25 -> 25; matrix products, arithmetic and copies ran while one was open for 20% -> 22% of each run, Pallas kernels for 0% -> 0%
where the time goes in v8:
time: 554 us; the launch traced here: 549 us
  waiting for transfers between devices  143 us (26%)
  starting transfers between devices  111 us (20%)
  other arithmetic  108 us (19%)
  matrix products  89 us (16%)
  local copies, waits for them, and re-layouts  57.7 us (10%)
  blocking collectives  32.5 us (6%)
  between operations  7.79 us (1%)
    ppermute x24, waiting for transfers between devices, exchange(): lax.ppermute(part, axis, [(i, (i + shift) % size) for i in range(size)])  102 us
    ppermute x24, starting transfers between devices, exchange(): lax.ppermute(part, axis, [(i, (i + shift) % size) for i in range(size)])  57.5 us
    dot_general x4, matrix products, precondition_lines(): jnp.einsum('yj,kji->kyi', eigenvectors, scaled, preferred_element_type=jn...  46.3 us
    all_to_all x2, blocking collectives, all_sum(): return jnp.sum(lax.all_to_all(spread, axes, 0, 0, tiled=True), 0)  32.5 us
    reduce_sum x2, other arithmetic, shards(): jnp.sum(residual * precond)  25.6 us
    dot_general x4, matrix products, precondition_lines(): jnp.einsum('qkyi,qix->kyx', returned, eigenvectors.reshape(across, cols,...  23.2 us
    dot_general x4, matrix products, precondition_lines(): jnp.dot(lines.reshape(levels_here * rows, width), eigenvectors, preferred...  19.6 us
    ppermute x6, starting transfers between devices, padded_2(): lax.ppermute(last, axis, up)  15.6 us
  transfers between devices with their start and end apart: 44, of which 25 were waited for; matrix products, arithmetic and copies ran while one was open for 22% of the time, Pallas kernels for 0%

profile of v8, /device:TPU:0, one launch (start us, length us, event | category | flops | bytes accessed | tf_op | source)
XLA Modules:
  0.0 549.1 jit_solution(6182897886131484958)
XLA Ops:
  4.6 12.3 %fusion.79 = bf16[1,8,256,512]{3,2,1,0:T(8,128)(2,1)S(1)} fusion(s32[8,256,512]{2,1,0:T(8,128)S(1)} %copy-done.17, bf16[]{:T(256)} %bitcast.16, bf16[]{:T(256)} %bitcast.15, bf16[]{:T(256)} %bitcast.14, bf16[]{:T(256)} %bitcast.13, bf16[]{:T(256)} %bitcast.12, bf16[]{:T(256)} %bitcast.11, bf16[]{:T(256)} %bitcast.10, bf16[]{:T(256)} %bitcast.9, ...), kind=kLoop, calls=%fused_computation.168 | loop fusion | flops 34603008 | bytes 6291488 | tf_op jit(solution)/shard_map/stack | solution.py:138
  23.8 4.3 collective-permute-start.1
  35.4 13.7 %fusion.3 = f32[2,8,258,514]{3,2,1,0:T(8,128)} fusion(bf16[2,8,1,512]{3,2,1,0:T(2,128)(2,1)S(1)} %collective-permute-done.3, bf16[2,8,1,512]{3,2,1,0:T(2,128)(2,1)S(1)} %collective-permute-done, bf16[2,8,256,1]{3,2,1,0:T(8,128)(2,1)} %copy.64, bf16[1,8,256,512]{3,2,1,0:T(8,128)(2,1)} %copy-done.12, bf16[1,8,256,512]{3,2,1,0:T(8,128)(2,1)S(1)} %convert_bitcast_fusion, ...), kind=kLoop, calls=%fused_computation.14 | loop fusion | flops 33948672 | bytes 12730624 | tf_op jit(solution)/shard_map/convert_element_type | solution.py:139
  49.1 4.8 slice_bitcast_fusion.1
  61.4 11.6 %fusion.39 = f32[8,256,512]{2,1,0:T(8,128)} fusion(f32[8,256,512]{2,1,0:T(8,128)} %param.7, f32[8,256,512]{2,1,0:T(8,128)S(1)} %fusion.50, f32[8,258,514]{2,1,0:T(8,128)S(1)} %get-tuple-element.31, f32[7,256,512]{2,1,0:T(8,128)S(1)} %slice.326, f32[8,258,514]{2,1,0:T(8,128)S(1)} %get-tuple-element.30), kind=kLoop, calls=%fused_computation.63 | loop fusion | flops 23068672 | bytes 58195968 | tf_op jit(solution)/shard_map/sub | solution.py:142
  81.3 4.9 collective-permute-done.4
  86.3 11.1 %collective-permute-done.5 = bf16[1,256,512]{2,1,0:T(8,128)(2,1)S(1)} collective-permute-done((bf16[1,256,512]{2,1,0:T(8,128)(2,1)S(1)}, bf16[1,256,512]{2,1,0:T(8,128)(2,1)S(1)}, u32[]{:S(2)}, u32[]{:S(2)}) %collective-permute-start.5) | collective-permute-done | bytes 262176 | tf_op jit(solution)/shard_map/ppermute | solution.py:73
  100.1 7.2 %collective-permute-start.12 = (bf16[1,256,512]{2,1,0:T(8,128)(2,1)S(1)}, bf16[1,256,512]{2,1,0:T(8,128)(2,1)S(1)}, u32[]{:S(2)}, u32[]{:S(2)}) collective-permute-start(bf16[1,256,512]{2,1,0:T(8,128)(2,1)S(1)} %get-tuple-element.64), channel_id=1, source_target_pairs={{0,24},{8,0},{16,8},{24,16},{1,25},{9,1},{17,9},{25,17},{2,26},{10... | collective-permute-start | bytes 786440 | tf_op jit(solution)/shard_map/ppermute | solution.py:73
  107.9 5.7 %convolution_convert_fusion.7 = bf16[256,2048]{1,0:T(8,128)(2,1)S(1)} fusion(bf16[2048,2048]{1,0:T(8,128)(2,1)} %param.11, bf16[1,256,2048]{2,1,0:T(8,128)(2,1)S(1)} %constant_dynamic-update-slice_fusion.20), kind=kOutput, calls=%fused_computation.155 | convolution fusion | flops 2148007936 | bytes 10485760 | tf_op jit(solution)/shard_map/dot_general | solution.py:84
  118.2 7.0 %collective-permute-done.10 = bf16[1,256,512]{2,1,0:T(8,128)(2,1)S(1)} collective-permute-done((bf16[1,256,512]{2,1,0:T(8,128)(2,1)}, bf16[1,256,512]{2,1,0:T(8,128)(2,1)S(1)}, u32[]{:S(2)}, u32[]{:S(2)}) %collective-permute-start.10) | collective-permute-done | bytes 262176 | tf_op jit(solution)/shard_map/ppermute | solution.py:73
  125.3 5.5 %collective-permute-done.11 = bf16[1,256,512]{2,1,0:T(8,128)(2,1)S(1)} collective-permute-done((bf16[1,256,512]{2,1,0:T(8,128)(2,1)S(1)}, bf16[1,256,512]{2,1,0:T(8,128)(2,1)S(1)}, u32[]{:S(2)}, u32[]{:S(2)}) %collective-permute-start.11) | collective-permute-done | bytes 262176 | tf_op jit(solution)/shard_map/ppermute | solution.py:73
  130.9 5.7 %convolution_convert_fusion.5 = bf16[256,2048]{1,0:T(8,128)(2,1)S(1)} fusion(bf16[2048,2048]{1,0:T(8,128)(2,1)} %param.11, bf16[1,256,2048]{2,1,0:T(8,128)(2,1)S(1)} %constant_dynamic-update-slice_fusion.14), kind=kOutput, calls=%fused_computation.153 | convolution fusion | flops 2148007936 | bytes 10485760 | tf_op jit(solution)/shard_map/dot_general | solution.py:84
  141.2 11.0 %fusion.67 = bf16[1,2048,256]{1,2,0:T(8,128)(2,1)S(1)} fusion(bf16[2048,2048]{1,0:T(8,128)(2,1)} %param.11, bf16[2048,256]{1,0:T(8,128)(2,1)S(1)} %bitcast.251, f32[]{:T(128)} %bitcast.25, f32[256]{0:T(256)S(1)} %dynamic_slice.114, f32[2048]{0:T(1024)S(1)} %copy-done.19), kind=kOutput, calls=%fused_computation.156 | convolution fusion | flops 4297588736 | bytes 10494980 | tf_op jit(solution)/shard_map/yj,kji->kyi/dot_general | solution.py:98
  160.3 11.1 %fusion.68 = bf16[1,2048,256]{1,2,0:T(8,128)(2,1)S(1)} fusion(bf16[2048,2048]{1,0:T(8,128)(2,1)} %param.11, bf16[2048,256]{1,0:T(8,128)(2,1)S(1)} %bitcast.253, f32[]{:T(128)} %bitcast.42, f32[256]{0:T(256)S(1)} %dynamic_slice.114, f32[2048]{0:T(1024)S(1)} %copy-done.19), kind=kOutput, calls=%fused_computation.157 | convolution fusion | flops 4297588736 | bytes 10494980 | tf_op jit(solution)/shard_map/yj,kji->kyi/dot_general | solution.py:98
  179.2 5.7 %fusion.63 = bf16[256,2048]{1,0:T(8,128)(2,1)S(1)} fusion(bf16[8,256,2048]{2,1,0:T(8,128)(2,1)} %bitcast.258, bf16[8,1,256,256]{3,2,1,0:T(8,128)(2,1)S(1)} %all-to-all-done.1), kind=kOutput, calls=%fused_computation.144 | convolution fusion | flops 2148007936 | bytes 10485760 | tf_op jit(solution)/shard_map/qkyi,qix->kyx/dot_general | solution.py:103
  189.9 7.3 %collective-permute-done.7 = bf16[1,256,512]{2,1,0:T(8,128)(2,1)} collective-permute-done((bf16[1,256,512]{2,1,0:T(8,128)(2,1)}, bf16[1,256,512]{2,1,0:T(8,128)(2,1)}, u32[]{:S(2)}, u32[]{:S(2)}) %collective-permute-start.7) | collective-permute-done | bytes 262176 | tf_op jit(solution)/shard_map/ppermute | solution.py:73
  198.2 5.7 %fusion.64 = bf16[256,2048]{1,0:T(8,128)(2,1)S(1)} fusion(bf16[8,256,2048]{2,1,0:T(8,128)(2,1)} %bitcast.259, bf16[8,1,256,256]{3,2,1,0:T(8,128)(2,1)S(1)} %all-to-all-done.3), kind=kOutput, calls=%fused_computation.145 | convolution fusion | flops 2148007936 | bytes 10485760 | tf_op jit(solution)/shard_map/qkyi,qix->kyx/dot_general | solution.py:103
  204.0 9.3 %collective-permute-start.13 = (bf16[1,256,512]{2,1,0:T(8,128)(2,1)S(1)}, bf16[1,256,512]{2,1,0:T(8,128)(2,1)S(1)}, u32[]{:S(2)}, u32[]{:S(2)}) collective-permute-start(bf16[1,256,512]{2,1,0:T(8,128)(2,1)S(1)} %get-tuple-element.63), channel_id=1, source_target_pairs={{0,8},{8,16},{16,24},{24,0},{1,9},{9,17},{17,25},{25,1},{2,10},{10... | collective-permute-start | bytes 786440 | tf_op jit(solution)/shard_map/ppermute | solution.py:73
  213.3 11.3 %collective-permute-done.8 = bf16[1,256,512]{2,1,0:T(8,128)(2,1)} collective-permute-done((bf16[1,256,512]{2,1,0:T(8,128)(2,1)}, bf16[1,256,512]{2,1,0:T(8,128)(2,1)}, u32[]{:S(2)}, u32[]{:S(2)}) %collective-permute-start.8) | collective-permute-done | bytes 262176 | tf_op jit(solution)/shard_map/ppermute | solution.py:73
  226.8 6.1 %collective-permute-done.14 = bf16[1,256,512]{2,1,0:T(8,128)(2,1)S(1)} collective-permute-done((bf16[1,256,512]{2,1,0:T(8,128)(2,1)S(1)}, bf16[1,256,512]{2,1,0:T(8,128)(2,1)S(1)}, u32[]{:S(2)}, u32[]{:S(2)}) %collective-permute-start.14) | collective-permute-done | bytes 262176 | tf_op jit(solution)/shard_map/ppermute | solution.py:73
  238.6 4.1 collective-permute-start.17
  244.1 5.7 %collective-permute-done.17 = bf16[8,256,1]{2,1,0:T(8,128)(2,1)S(1)} collective-permute-done((bf16[8,256,1]{2,1,0:T(8,128)(2,1)S(1)}, bf16[8,256,1]{2,1,0:T(8,128)(2,1)S(1)}, u32[]{:S(2)}, u32[]{:S(2)}) %collective-permute-start.17) | collective-permute-done | bytes 4128 | tf_op jit(solution)/shard_map/ppermute | solution.py:17
  249.8 4.8 collective-permute-done.18
  254.7 5.8 %fusion.59 = f32[8,258,514]{2,1,0:T(8,128)S(1)} fusion(bf16[8,1,512]{2,1,0:T(2,128)(2,1)S(1)} %collective-permute-done.19, bf16[8,1,512]{2,1,0:T(2,128)(2,1)S(1)} %collective-permute-done.16, bf16[8,256,1]{2,1,0:T(8,128)(2,1)S(1)} %collective-permute-done.18, bf16[4,256,512]{2,1,0:T(8,128)(2,1)S(1)} %constant_dynamic-update-slice_fusion.10, ...), kind=kLoop, calls=%fused_computation.140 | loop fusion | flops 16974336 | bytes 6365312 | tf_op jit(solution)/shard_map/convert_element_type | solution.py:127
  266.2 12.2 %fusion.12 = (f32[]{:T(128)}, f32[]{:T(128)}, f32[8,256,512]{2,1,0:T(8,128)}) fusion(f32[8,256,512]{2,1,0:T(8,128)} %fusion.39, bf16[4,256,512]{2,1,0:T(8,128)(2,1)S(1)} %constant_dynamic-update-slice_fusion.10, bf16[4,256,512]{2,1,0:T(8,128)(2,1)S(1)} %constant_dynamic-update-slice_fusion.17, f32[7,256,512]{2,1,0:T(8,128)S(1)} %slice.344, ...), kind=kLoop, calls=%fused_computation.27 | loop fusion | flops 28311552 | bytes 60293128 | tf_op jit(solution)/shard_map/reduce_sum | solution.py:149
  279.9 19.0 %all_to_all.52 = f32[32,1,2]{2,1,0:T(1,128)S(1)} all-to-all(f32[32,1,2]{2,1,0:T(1,128)S(1)} %broadcast_in_dim.89), channel_id=1, replica_groups=mesh['px'=4,'py'=8] {'px','py'}, dimensions={0} | all-to-all | bytes 512 | tf_op jit(solution)/shard_map/all_to_all | solution.py:41
  300.7 4.7 multiply_subtract_fusion.1
  309.7 7.3 %collective-permute-done.20 = bf16[1,256,512]{2,1,0:T(8,128)(2,1)S(1)} collective-permute-done((bf16[1,256,512]{2,1,0:T(8,128)(2,1)S(1)}, bf16[1,256,512]{2,1,0:T(8,128)(2,1)S(1)}, u32[]{:S(2)}, u32[]{:S(2)}) %collective-permute-start.20) | collective-permute-done | bytes 262176 | tf_op jit(solution)/shard_map/ppermute | solution.py:73
  317.0 10.2 %collective-permute-done.21 = bf16[1,256,512]{2,1,0:T(8,128)(2,1)S(1)} collective-permute-done((bf16[1,256,512]{2,1,0:T(8,128)(2,1)S(1)}, bf16[1,256,512]{2,1,0:T(8,128)(2,1)S(1)}, u32[]{:S(2)}, u32[]{:S(2)}) %collective-permute-start.21) | collective-permute-done | bytes 262176 | tf_op jit(solution)/shard_map/ppermute | solution.py:73
  328.4 5.0 collective-permute-start.28
  342.4 8.8 %collective-permute-done.26 = bf16[1,256,512]{2,1,0:T(8,128)(2,1)} collective-permute-done((bf16[1,256,512]{2,1,0:T(8,128)(2,1)}, bf16[1,256,512]{2,1,0:T(8,128)(2,1)}, u32[]{:S(2)}, u32[]{:S(2)}) %collective-permute-start.26) | collective-permute-done | bytes 262176 | tf_op jit(solution)/shard_map/ppermute | solution.py:73
  352.1 5.6 %collective-permute-done.27 = bf16[1,256,512]{2,1,0:T(8,128)(2,1)} collective-permute-done((bf16[1,256,512]{2,1,0:T(8,128)(2,1)}, bf16[1,256,512]{2,1,0:T(8,128)(2,1)}, u32[]{:S(2)}, u32[]{:S(2)}) %collective-permute-start.27) | collective-permute-done | bytes 262176 | tf_op jit(solution)/shard_map/ppermute | solution.py:73
  359.7 5.7 %convolution_convert_fusion.1 = bf16[256,2048]{1,0:T(8,128)(2,1)S(1)} fusion(bf16[2048,2048]{1,0:T(8,128)(2,1)} %param.11, bf16[1,256,2048]{2,1,0:T(8,128)(2,1)S(1)} %constant_dynamic-update-slice_fusion), kind=kOutput, calls=%fused_computation.149 | convolution fusion | flops 2148007936 | bytes 10485760 | tf_op jit(solution)/shard_map/dot_general | solution.py:84
  370.0 12.0 %fusion.69 = bf16[1,2048,256]{1,2,0:T(8,128)(2,1)} fusion(bf16[2048,2048]{1,0:T(8,128)(2,1)} %param.11, bf16[2048,256]{1,0:T(8,128)(2,1)S(1)} %bitcast.250, f32[]{:T(128)} %bitcast.25, f32[256]{0:T(256)S(1)} %dynamic_slice.114, f32[2048]{0:T(1024)S(1)} %copy-done.19), kind=kOutput, calls=%fused_computation.158 | convolution fusion | flops 4297588736 | bytes 10494980 | tf_op jit(solution)/shard_map/yj,kji->kyi/dot_general | solution.py:98
  389.1 12.1 %fusion.70 = bf16[1,2048,256]{1,2,0:T(8,128)(2,1)} fusion(bf16[2048,2048]{1,0:T(8,128)(2,1)} %param.11, bf16[2048,256]{1,0:T(8,128)(2,1)S(1)} %bitcast.252, f32[]{:T(128)} %bitcast.42, f32[256]{0:T(256)S(1)} %dynamic_slice.114, f32[2048]{0:T(1024)S(1)} %copy-done.19), kind=kOutput, calls=%fused_computation.159 | convolution fusion | flops 4297588736 | bytes 10494980 | tf_op jit(solution)/shard_map/yj,kji->kyi/dot_general | solution.py:98
  404.4 4.3 all-to-all-start.8
  408.7 5.7 %fusion.65 = bf16[256,2048]{1,0:T(8,128)(2,1)S(1)} fusion(bf16[8,256,2048]{2,1,0:T(8,128)(2,1)} %bitcast.260, bf16[8,1,256,256]{3,2,1,0:T(8,128)(2,1)S(1)} %all-to-all-done.6), kind=kOutput, calls=%fused_computation.146 | convolution fusion | flops 2148007936 | bytes 10485760 | tf_op jit(solution)/shard_map/qkyi,qix->kyx/dot_general | solution.py:103
  419.3 4.9 all-to-all-done.8
  424.1 6.0 %fusion.66 = bf16[256,2048]{1,0:T(8,128)(2,1)S(1)} fusion(bf16[8,256,2048]{2,1,0:T(8,128)(2,1)} %bitcast.261, bf16[8,1,256,256]{3,2,1,0:T(8,128)(2,1)} %all-to-all-done.8), kind=kOutput, calls=%fused_computation.147 | convolution fusion | flops 2148007936 | bytes 10485760 | tf_op jit(solution)/shard_map/qkyi,qix->kyx/dot_general | solution.py:103
  432.3 5.1 collective-permute-done.23
  437.4 14.3 %collective-permute-start.29 = (bf16[1,256,512]{2,1,0:T(8,128)(2,1)S(1)}, bf16[1,256,512]{2,1,0:T(8,128)(2,1)S(1)}, u32[]{:S(2)}, u32[]{:S(2)}) collective-permute-start(bf16[1,256,512]{2,1,0:T(8,128)(2,1)S(1)} %get-tuple-element.49), channel_id=1, source_target_pairs={{0,8},{8,16},{16,24},{24,0},{1,9},{9,17},{17,25},{25,1},{2,10},{10... | collective-permute-start | bytes 786440 | tf_op jit(solution)/shard_map/ppermute | solution.py:73
  457.4 6.1 %collective-permute-done.30 = bf16[1,256,512]{2,1,0:T(8,128)(2,1)S(1)} collective-permute-done((bf16[1,256,512]{2,1,0:T(8,128)(2,1)S(1)}, bf16[1,256,512]{2,1,0:T(8,128)(2,1)S(1)}, u32[]{:S(2)}, u32[]{:S(2)}) %collective-permute-start.30) | collective-permute-done | bytes 262176 | tf_op jit(solution)/shard_map/ppermute | solution.py:73
  470.5 8.9 %collective-permute-done.33 = bf16[8,256,1]{2,1,0:T(8,128)(2,1)S(1)} collective-permute-done((bf16[8,256,1]{2,1,0:T(8,128)(2,1)S(1)}, bf16[8,256,1]{2,1,0:T(8,128)(2,1)S(1)}, u32[]{:S(2)}, u32[]{:S(2)}) %collective-permute-start.33) | collective-permute-done | bytes 4128 | tf_op jit(solution)/shard_map/ppermute | solution.py:17
  479.3 5.4 collective-permute-done.34
  484.7 5.4 fusion.62
  500.9 13.4 %fusion.9 = (f32[]{:T(128)}, f32[]{:T(128)}, f32[]{:T(128)}, f32[]{:T(128)}, f32[8,256,512]{2,1,0:T(8,128)}) fusion(f32[8,256,512]{2,1,0:T(8,128)} %copy-done.7, bf16[4,256,512]{2,1,0:T(8,128)(2,1)} %copy-done.9, bf16[4,256,512]{2,1,0:T(8,128)(2,1)} %copy-done.10, f32[8,256,512]{2,1,0:T(8,128)S(1)} %copy-done.1, bf16[4,256,512]{2,1,0:T(8,128)(2,1)} %copy-done.6, ...), kind=kLoop, calls=%fused_computation.24 | loop fusion | flops 34603004 | bytes 66584592 | tf_op jit(solution)/shard_map/reduce_sum | solution.py:156
  516.9 13.5 %all_to_all.53 = f32[32,1,4]{2,1,0:T(1,128)S(1)} all-to-all(f32[32,1,4]{2,1,0:T(1,128)S(1)} %broadcast_in_dim.90), channel_id=1, replica_groups=mesh['px'=4,'py'=8] {'px','py'}, dimensions={0} | all-to-all | bytes 1024 | tf_op jit(solution)/shard_map/all_to_all | solution.py:41
  535.6 7.0 %fusion.15 = (f32[8,256,512]{2,1,0:T(8,128)}, f32[8,256,512]{2,1,0:T(8,128)}) fusion(f32[8,256,512]{2,1,0:T(8,128)} %param.8, f32[]{:T(128)S(6)} %div.27, f32[]{:T(128)S(6)} %div.23, bf16[4,256,512]{2,1,0:T(8,128)(2,1)} %copy-done.6, bf16[4,256,512]{2,1,0:T(8,128)(2,1)S(1)} %constant_dynamic-update-slice_fusion.17, f32[]{:T(128)S(6)} %div.26, ...), kind=kLoop, calls=%fused_computation.30 | loop fusion | flops 10485760 | bytes 16777228 | tf_op jit(solution)/shard_map/add | solution.py:169
  (213 shorter events, 156.9 us)
Async XLA Ops:
  17.0 18.4 %collective-permute-start = (bf16[2,8,1,512]{3,2,1,0:T(2,128)(2,1)S(1)}, bf16[2,8,1,512]{3,2,1,0:T(2,128)(2,1)S(1)}, u32[]{:S(2)}, u32[]{:S(2)}) collective-permute-start(bf16[2,8,1,512]{3,2,1,0:T(2,128)(2,1)S(1)} %get-tuple-element.34), channel_id=1, source_target_pairs={{0,1},{1,2},{2,3},{3,4},{4,5},{5,6},{6,7},{8,9},{9,10},{10,11},{11... | collective-permute-start | bytes 49160 | tf_op jit(solution)/shard_map/ppermute | solution.py:17
  19.4 16.0 %collective-permute-start.3 = (bf16[2,8,1,512]{3,2,1,0:T(2,128)(2,1)S(1)}, bf16[2,8,1,512]{3,2,1,0:T(2,128)(2,1)S(1)}, u32[]{:S(2)}, u32[]{:S(2)}) collective-permute-start(bf16[2,8,1,512]{3,2,1,0:T(2,128)(2,1)S(1)} %get-tuple-element.35), channel_id=1, source_target_pairs={{1,0},{2,1},{3,2},{4,3},{5,4},{6,5},{7,6},{9,8},{10,9},{11,10},{12... | collective-permute-start | bytes 49160 | tf_op jit(solution)/shard_map/ppermute | solution.py:17
  23.8 6.1 %collective-permute-start.1 = (bf16[2,8,256,1]{2,1,3,0:T(8,128)(2,1)S(1)}, bf16[2,8,256,1]{2,1,3,0:T(8,128)(2,1)S(1)}, u32[]{:S(2)}, u32[]{:S(2)}) collective-permute-start(bf16[2,8,256,1]{2,1,3,0:T(8,128)(2,1)S(1)} %copy.61), channel_id=1, source_target_pairs={{0,8},{8,16},{16,24},{1,9},{9,17},{17,25},{2,10},{10,18},{18,26},{... | collective-permute-start | bytes 24584 | tf_op jit(solution)/shard_map/ppermute | solution.py:17
  28.5 5.5 %collective-permute-start.2 = (bf16[2,8,256,1]{2,1,3,0:T(8,128)(2,1)S(1)}, bf16[2,8,256,1]{2,1,3,0:T(8,128)(2,1)S(1)}, u32[]{:S(2)}, u32[]{:S(2)}) collective-permute-start(bf16[2,8,256,1]{2,1,3,0:T(8,128)(2,1)S(1)} %copy.62), channel_id=1, source_target_pairs={{8,0},{16,8},{24,16},{9,1},{17,9},{25,17},{10,2},{18,10},{26,18},{... | collective-permute-start | bytes 24584 | tf_op jit(solution)/shard_map/ppermute | solution.py:17
  75.0 11.2 %collective-permute-start.4 = (bf16[1,256,512]{2,1,0:T(8,128)(2,1)S(1)}, bf16[1,256,512]{2,1,0:T(8,128)(2,1)S(1)}, u32[]{:S(2)}, u32[]{:S(2)}) collective-permute-start(bf16[1,256,512]{2,1,0:T(8,128)(2,1)S(1)} %get-tuple-element.70), channel_id=1, source_target_pairs={{0,8},{8,16},{16,24},{24,0},{1,9},{9,17},{17,25},{25,1},{2,10},{10... | collective-permute-start | bytes 786440 | tf_op jit(solution)/shard_map/ppermute | solution.py:73
  76.7 20.7 %collective-permute-start.5 = (bf16[1,256,512]{2,1,0:T(8,128)(2,1)S(1)}, bf16[1,256,512]{2,1,0:T(8,128)(2,1)S(1)}, u32[]{:S(2)}, u32[]{:S(2)}) collective-permute-start(bf16[1,256,512]{2,1,0:T(8,128)(2,1)S(1)} %get-tuple-element.69), channel_id=1, source_target_pairs={{0,16},{8,24},{16,0},{24,8},{1,17},{9,25},{17,1},{25,9},{2,18},{10... | collective-permute-start | bytes 786440 | tf_op jit(solution)/shard_map/ppermute | solution.py:73
  77.8 19.6 %collective-permute-start.6 = (bf16[1,256,512]{2,1,0:T(8,128)(2,1)S(1)}, bf16[1,256,512]{2,1,0:T(8,128)(2,1)S(1)}, u32[]{:S(2)}, u32[]{:S(2)}) collective-permute-start(bf16[1,256,512]{2,1,0:T(8,128)(2,1)S(1)} %get-tuple-element.68), channel_id=1, source_target_pairs={{0,24},{8,0},{16,8},{24,16},{1,25},{9,1},{17,9},{25,17},{2,26},{10... | collective-permute-start | bytes 786440 | tf_op jit(solution)/shard_map/ppermute | solution.py:73
  100.1 30.7 %collective-permute-start.12 = (bf16[1,256,512]{2,1,0:T(8,128)(2,1)S(1)}, bf16[1,256,512]{2,1,0:T(8,128)(2,1)S(1)}, u32[]{:S(2)}, u32[]{:S(2)}) collective-permute-start(bf16[1,256,512]{2,1,0:T(8,128)(2,1)S(1)} %get-tuple-element.64), channel_id=1, source_target_pairs={{0,24},{8,0},{16,8},{24,16},{1,25},{9,1},{17,9},{25,17},{2,26},{10... | collective-permute-start | bytes 786440 | tf_op jit(solution)/shard_map/ppermute | solution.py:73
  107.3 23.5 %collective-permute-start.11 = (bf16[1,256,512]{2,1,0:T(8,128)(2,1)S(1)}, bf16[1,256,512]{2,1,0:T(8,128)(2,1)S(1)}, u32[]{:S(2)}, u32[]{:S(2)}) collective-permute-start(bf16[1,256,512]{2,1,0:T(8,128)(2,1)S(1)} %get-tuple-element.65), channel_id=1, source_target_pairs={{0,16},{8,24},{16,0},{24,8},{1,17},{9,25},{17,1},{25,9},{2,18},{10... | collective-permute-start | bytes 786440 | tf_op jit(solution)/shard_map/ppermute | solution.py:73
  107.7 17.6 %collective-permute-start.10 = (bf16[1,256,512]{2,1,0:T(8,128)(2,1)}, bf16[1,256,512]{2,1,0:T(8,128)(2,1)S(1)}, u32[]{:S(2)}, u32[]{:S(2)}) collective-permute-start(bf16[1,256,512]{2,1,0:T(8,128)(2,1)} %get-tuple-element.66), channel_id=1, source_target_pairs={{0,8},{8,16},{16,24},{24,0},{1,9},{9,17},{17,25},{25,1},{2,10},{10... | collective-permute-start | bytes 786440 | tf_op jit(solution)/shard_map/ppermute | solution.py:73
  114.7 23.0 %all-to-all-start = ((bf16[8,256,256]{2,1,0:T(8,128)(2,1)}), bf16[8,256,256]{2,1,0:T(8,128)(2,1)S(1)}, u32[]{:S(2)}, u32[]{:S(2)}) async-start(bf16[8,256,256]{2,1,0:T(8,128)(2,1)} %bitcast.245), calls=%async_computation | async-start | bytes 2097152 | tf_op jit(solution)/shard_map/all_to_all | solution.py:88
  137.6 18.9 %all-to-all-start.2 = ((bf16[8,256,256]{2,1,0:T(8,128)(2,1)}), bf16[8,256,256]{2,1,0:T(8,128)(2,1)S(1)}, u32[]{:S(2)}, u32[]{:S(2)}) async-start(bf16[8,256,256]{2,1,0:T(8,128)(2,1)} %bitcast.243), calls=%async_computation.2 | async-start | bytes 2097152 | tf_op jit(solution)/shard_map/all_to_all | solution.py:88
  156.5 19.1 %all-to-all-start.1 = ((bf16[8,1,256,256]{3,2,1,0:T(8,128)(2,1)}), bf16[8,1,256,256]{3,2,1,0:T(8,128)(2,1)S(1)}, u32[]{:S(2)}, u32[]{:S(2)}) async-start(bf16[8,1,256,256]{3,2,1,0:T(8,128)(2,1)} %bitcast.29), calls=%async_computation.1 | async-start | bytes 2097152 | tf_op jit(solution)/shard_map/all_to_all | solution.py:102
  175.7 22.5 %all-to-all-start.3 = ((bf16[8,1,256,256]{3,2,1,0:T(8,128)(2,1)}), bf16[8,1,256,256]{3,2,1,0:T(8,128)(2,1)S(1)}, u32[]{:S(2)}, u32[]{:S(2)}) async-start(bf16[8,1,256,256]{3,2,1,0:T(8,128)(2,1)} %bitcast.46), calls=%async_computation.3 | async-start | bytes 2097152 | tf_op jit(solution)/shard_map/all_to_all | solution.py:102
  185.9 11.3 %collective-permute-start.7 = (bf16[1,256,512]{2,1,0:T(8,128)(2,1)}, bf16[1,256,512]{2,1,0:T(8,128)(2,1)}, u32[]{:S(2)}, u32[]{:S(2)}) collective-permute-start(bf16[1,256,512]{2,1,0:T(8,128)(2,1)} %get-tuple-element.60), channel_id=1, source_target_pairs={{0,8},{8,16},{16,24},{24,0},{1,9},{9,17},{17,25},{25,1},{2,10},{10... | collective-permute-start | bytes 786440 | tf_op jit(solution)/shard_map/ppermute | solution.py:73
  185.9 39.7 %collective-permute-start.9 = (bf16[1,256,512]{2,1,0:T(8,128)(2,1)}, bf16[1,256,512]{2,1,0:T(8,128)(2,1)}, u32[]{:S(2)}, u32[]{:S(2)}) collective-permute-start(bf16[1,256,512]{2,1,0:T(8,128)(2,1)} %get-tuple-element.58), channel_id=1, source_target_pairs={{0,24},{8,0},{16,8},{24,16},{1,25},{9,1},{17,9},{25,17},{2,26},{10... | collective-permute-start | bytes 786440 | tf_op jit(solution)/shard_map/ppermute | solution.py:73
  189.7 34.9 %collective-permute-start.8 = (bf16[1,256,512]{2,1,0:T(8,128)(2,1)}, bf16[1,256,512]{2,1,0:T(8,128)(2,1)}, u32[]{:S(2)}, u32[]{:S(2)}) collective-permute-start(bf16[1,256,512]{2,1,0:T(8,128)(2,1)} %get-tuple-element.59), channel_id=1, source_target_pairs={{0,16},{8,24},{16,0},{24,8},{1,17},{9,25},{17,1},{25,9},{2,18},{10... | collective-permute-start | bytes 786440 | tf_op jit(solution)/shard_map/ppermute | solution.py:73
  204.0 22.8 %collective-permute-start.13 = (bf16[1,256,512]{2,1,0:T(8,128)(2,1)S(1)}, bf16[1,256,512]{2,1,0:T(8,128)(2,1)S(1)}, u32[]{:S(2)}, u32[]{:S(2)}) collective-permute-start(bf16[1,256,512]{2,1,0:T(8,128)(2,1)S(1)} %get-tuple-element.63), channel_id=1, source_target_pairs={{0,8},{8,16},{16,24},{24,0},{1,9},{9,17},{17,25},{25,1},{2,10},{10... | collective-permute-start | bytes 786440 | tf_op jit(solution)/shard_map/ppermute | solution.py:73
  225.5 7.4 %collective-permute-start.14 = (bf16[1,256,512]{2,1,0:T(8,128)(2,1)S(1)}, bf16[1,256,512]{2,1,0:T(8,128)(2,1)S(1)}, u32[]{:S(2)}, u32[]{:S(2)}) collective-permute-start(bf16[1,256,512]{2,1,0:T(8,128)(2,1)S(1)} %get-tuple-element.62), channel_id=1, source_target_pairs={{0,16},{8,24},{16,0},{24,8},{1,17},{9,25},{17,1},{25,9},{2,18},{10... | collective-permute-start | bytes 786440 | tf_op jit(solution)/shard_map/ppermute | solution.py:73
  226.6 9.1 %collective-permute-start.15 = (bf16[1,256,512]{2,1,0:T(8,128)(2,1)S(1)}, bf16[1,256,512]{2,1,0:T(8,128)(2,1)S(1)}, u32[]{:S(2)}, u32[]{:S(2)}) collective-permute-start(bf16[1,256,512]{2,1,0:T(8,128)(2,1)S(1)} %get-tuple-element.61), channel_id=1, source_target_pairs={{0,24},{8,0},{16,8},{24,16},{1,25},{9,1},{17,9},{25,17},{2,26},{10... | collective-permute-start | bytes 786440 | tf_op jit(solution)/shard_map/ppermute | solution.py:73
  235.8 18.9 %collective-permute-start.16 = (bf16[8,1,512]{2,1,0:T(2,128)(2,1)S(1)}, bf16[8,1,512]{2,1,0:T(2,128)(2,1)S(1)}, u32[]{:S(2)}, u32[]{:S(2)}) collective-permute-start(bf16[8,1,512]{2,1,0:T(2,128)(2,1)S(1)} %get-tuple-element.42), channel_id=1, source_target_pairs={{0,1},{1,2},{2,3},{3,4},{4,5},{5,6},{6,7},{8,9},{9,10},{10,11},{11... | collective-permute-start | bytes 24584 | tf_op jit(solution)/shard_map/ppermute | solution.py:17
  237.1 17.6 %collective-permute-start.19 = (bf16[8,1,512]{2,1,0:T(2,128)(2,1)S(1)}, bf16[8,1,512]{2,1,0:T(2,128)(2,1)S(1)}, u32[]{:S(2)}, u32[]{:S(2)}) collective-permute-start(bf16[8,1,512]{2,1,0:T(2,128)(2,1)S(1)} %get-tuple-element.43), channel_id=1, source_target_pairs={{1,0},{2,1},{3,2},{4,3},{5,4},{6,5},{7,6},{9,8},{10,9},{11,10},{12... | collective-permute-start | bytes 24584 | tf_op jit(solution)/shard_map/ppermute | solution.py:17
  238.6 11.2 %collective-permute-start.17 = (bf16[8,256,1]{2,1,0:T(8,128)(2,1)S(1)}, bf16[8,256,1]{2,1,0:T(8,128)(2,1)S(1)}, u32[]{:S(2)}, u32[]{:S(2)}) collective-permute-start(bf16[8,256,1]{2,1,0:T(8,128)(2,1)S(1)} %get-tuple-element.40), channel_id=1, source_target_pairs={{0,8},{8,16},{16,24},{1,9},{9,17},{17,25},{2,10},{10,18},{18,26},{... | collective-permute-start | bytes 12296 | tf_op jit(solution)/shard_map/ppermute | solution.py:17
  242.7 12.0 %collective-permute-start.18 = (bf16[8,256,1]{2,1,0:T(8,128)(2,1)S(1)}, bf16[8,256,1]{2,1,0:T(8,128)(2,1)S(1)}, u32[]{:S(2)}, u32[]{:S(2)}) collective-permute-start(bf16[8,256,1]{2,1,0:T(8,128)(2,1)S(1)} %get-tuple-element.41), channel_id=1, source_target_pairs={{8,0},{16,8},{24,16},{9,1},{17,9},{25,17},{10,2},{18,10},{26,18},{... | collective-permute-start | bytes 12296 | tf_op jit(solution)/shard_map/ppermute | solution.py:17
  300.7 34.6 %slice-start.4 = ((s8[8388608]{0:T(1024)(128)(4,1)}), s8[4194304]{0:T(1024)(128)(4,1)S(1)}, s32[]{:S(2)}) async-start(s8[8388608]{0:T(1024)(128)(4,1)} %bitcast.262), calls=%async_computation.14 | async-start | bytes 8388608
  300.7 34.6 %slice-start.5 = ((s8[8388608]{0:T(1024)(128)(4,1)}), s8[4194304]{0:T(1024)(128)(4,1)S(1)}, s32[]{:S(2)}) async-start(s8[8388608]{0:T(1024)(128)(4,1)} %bitcast.262), calls=%async_computation.15 | async-start | bytes 8388608
  305.4 32.3 %copy-start.7 = (f32[8,256,512]{2,1,0:T(8,128)}, f32[8,256,512]{2,1,0:T(8,128)S(1)}, u32[]{:S(2)}) copy-start(f32[8,256,512]{2,1,0:T(8,128)S(1)} %multiply_subtract_fusion.1) | copy-start | bytes 12582916
  305.8 11.1 %collective-permute-start.20 = (bf16[1,256,512]{2,1,0:T(8,128)(2,1)S(1)}, bf16[1,256,512]{2,1,0:T(8,128)(2,1)S(1)}, u32[]{:S(2)}, u32[]{:S(2)}) collective-permute-start(bf16[1,256,512]{2,1,0:T(8,128)(2,1)S(1)} %get-tuple-element.56), channel_id=1, source_target_pairs={{0,8},{8,16},{16,24},{24,0},{1,9},{9,17},{17,25},{25,1},{2,10},{10... | collective-permute-start | bytes 786440 | tf_op jit(solution)/shard_map/ppermute | solution.py:73
  306.4 20.7 %collective-permute-start.21 = (bf16[1,256,512]{2,1,0:T(8,128)(2,1)S(1)}, bf16[1,256,512]{2,1,0:T(8,128)(2,1)S(1)}, u32[]{:S(2)}, u32[]{:S(2)}) collective-permute-start(bf16[1,256,512]{2,1,0:T(8,128)(2,1)S(1)} %get-tuple-element.55), channel_id=1, source_target_pairs={{0,16},{8,24},{16,0},{24,8},{1,17},{9,25},{17,1},{25,9},{2,18},{10... | collective-permute-start | bytes 786440 | tf_op jit(solution)/shard_map/ppermute | solution.py:73
  307.0 20.2 %collective-permute-start.22 = (bf16[1,256,512]{2,1,0:T(8,128)(2,1)S(1)}, bf16[1,256,512]{2,1,0:T(8,128)(2,1)S(1)}, u32[]{:S(2)}, u32[]{:S(2)}) collective-permute-start(bf16[1,256,512]{2,1,0:T(8,128)(2,1)S(1)} %get-tuple-element.54), channel_id=1, source_target_pairs={{0,24},{8,0},{16,8},{24,16},{1,25},{9,1},{17,9},{25,17},{2,26},{10... | collective-permute-start | bytes 786440 | tf_op jit(solution)/shard_map/ppermute | solution.py:73
  328.4 30.2 %collective-permute-start.28 = (bf16[1,256,512]{2,1,0:T(8,128)(2,1)}, bf16[1,256,512]{2,1,0:T(8,128)(2,1)}, u32[]{:S(2)}, u32[]{:S(2)}) collective-permute-start(bf16[1,256,512]{2,1,0:T(8,128)(2,1)} %get-tuple-element.50), channel_id=1, source_target_pairs={{0,24},{8,0},{16,8},{24,16},{1,25},{9,1},{17,9},{25,17},{2,26},{10... | collective-permute-start | bytes 786440 | tf_op jit(solution)/shard_map/ppermute | solution.py:73
  333.4 24.3 %collective-permute-start.27 = (bf16[1,256,512]{2,1,0:T(8,128)(2,1)}, bf16[1,256,512]{2,1,0:T(8,128)(2,1)}, u32[]{:S(2)}, u32[]{:S(2)}) collective-permute-start(bf16[1,256,512]{2,1,0:T(8,128)(2,1)} %get-tuple-element.51), channel_id=1, source_target_pairs={{0,16},{8,24},{16,0},{24,8},{1,17},{9,25},{17,1},{25,9},{2,18},{10... | collective-permute-start | bytes 786440 | tf_op jit(solution)/shard_map/ppermute | solution.py:73
  335.1 16.0 %collective-permute-start.26 = (bf16[1,256,512]{2,1,0:T(8,128)(2,1)}, bf16[1,256,512]{2,1,0:T(8,128)(2,1)}, u32[]{:S(2)}, u32[]{:S(2)}) collective-permute-start(bf16[1,256,512]{2,1,0:T(8,128)(2,1)} %get-tuple-element.52), channel_id=1, source_target_pairs={{0,8},{8,16},{16,24},{24,0},{1,9},{9,17},{17,25},{25,1},{2,10},{10... | collective-permute-start | bytes 786440 | tf_op jit(solution)/shard_map/ppermute | solution.py:73
  338.8 27.6 %all-to-all-start.5 = ((bf16[8,256,256]{2,1,0:T(8,128)(2,1)}), bf16[8,256,256]{2,1,0:T(8,128)(2,1)S(1)}, u32[]{:S(2)}, u32[]{:S(2)}) async-start(bf16[8,256,256]{2,1,0:T(8,128)(2,1)} %bitcast.241), calls=%async_computation.5 | async-start | bytes 2097152 | tf_op jit(solution)/shard_map/all_to_all | solution.py:88
  366.4 18.9 %all-to-all-start.7 = ((bf16[8,256,256]{2,1,0:T(8,128)(2,1)}), bf16[8,256,256]{2,1,0:T(8,128)(2,1)S(1)}, u32[]{:S(2)}, u32[]{:S(2)}) async-start(bf16[8,256,256]{2,1,0:T(8,128)(2,1)} %bitcast.239), calls=%async_computation.7 | async-start | bytes 2097152 | tf_op jit(solution)/shard_map/all_to_all | solution.py:88
  385.3 19.1 %all-to-all-start.6 = ((bf16[8,1,256,256]{3,2,1,0:T(8,128)(2,1)}), bf16[8,1,256,256]{3,2,1,0:T(8,128)(2,1)S(1)}, u32[]{:S(2)}, u32[]{:S(2)}) async-start(bf16[8,1,256,256]{3,2,1,0:T(8,128)(2,1)} %bitcast.65), calls=%async_computation.6 | async-start | bytes 2097152 | tf_op jit(solution)/shard_map/all_to_all | solution.py:102
  404.4 19.7 %all-to-all-start.8 = ((bf16[8,1,256,256]{3,2,1,0:T(8,128)(2,1)}), bf16[8,1,256,256]{3,2,1,0:T(8,128)(2,1)}, u32[]{:S(2)}, u32[]{:S(2)}) async-start(bf16[8,1,256,256]{3,2,1,0:T(8,128)(2,1)} %bitcast.80), calls=%async_computation.8 | async-start | bytes 2097152 | tf_op jit(solution)/shard_map/all_to_all | solution.py:102
  415.3 38.3 %collective-permute-start.25 = (bf16[1,256,512]{2,1,0:T(8,128)(2,1)}, bf16[1,256,512]{2,1,0:T(8,128)(2,1)}, u32[]{:S(2)}, u32[]{:S(2)}) collective-permute-start(bf16[1,256,512]{2,1,0:T(8,128)(2,1)} %get-tuple-element.44), channel_id=1, source_target_pairs={{0,24},{8,0},{16,8},{24,16},{1,25},{9,1},{17,9},{25,17},{2,26},{10... | collective-permute-start | bytes 786440 | tf_op jit(solution)/shard_map/ppermute | solution.py:73
  415.3 37.3 %collective-permute-start.24 = (bf16[1,256,512]{2,1,0:T(8,128)(2,1)}, bf16[1,256,512]{2,1,0:T(8,128)(2,1)}, u32[]{:S(2)}, u32[]{:S(2)}) collective-permute-start(bf16[1,256,512]{2,1,0:T(8,128)(2,1)} %get-tuple-element.45), channel_id=1, source_target_pairs={{0,16},{8,24},{16,0},{24,8},{1,17},{9,25},{17,1},{25,9},{2,18},{10... | collective-permute-start | bytes 786440 | tf_op jit(solution)/shard_map/ppermute | solution.py:73
  417.1 20.3 %collective-permute-start.23 = (bf16[1,256,512]{2,1,0:T(8,128)(2,1)}, bf16[1,256,512]{2,1,0:T(8,128)(2,1)}, u32[]{:S(2)}, u32[]{:S(2)}) collective-permute-start(bf16[1,256,512]{2,1,0:T(8,128)(2,1)} %get-tuple-element.46), channel_id=1, source_target_pairs={{0,8},{8,16},{16,24},{24,0},{1,9},{9,17},{17,25},{25,1},{2,10},{10... | collective-permute-start | bytes 786440 | tf_op jit(solution)/shard_map/ppermute | solution.py:73
  430.4 33.2 %collective-permute-start.31 = (bf16[1,256,512]{2,1,0:T(8,128)(2,1)S(1)}, bf16[1,256,512]{2,1,0:T(8,128)(2,1)S(1)}, u32[]{:S(2)}, u32[]{:S(2)}) collective-permute-start(bf16[1,256,512]{2,1,0:T(8,128)(2,1)S(1)} %get-tuple-element.47), channel_id=1, source_target_pairs={{0,24},{8,0},{16,8},{24,16},{1,25},{9,1},{17,9},{25,17},{2,26},{10... | collective-permute-start | bytes 786440 | tf_op jit(solution)/shard_map/ppermute | solution.py:73
  430.4 33.1 %collective-permute-start.30 = (bf16[1,256,512]{2,1,0:T(8,128)(2,1)S(1)}, bf16[1,256,512]{2,1,0:T(8,128)(2,1)S(1)}, u32[]{:S(2)}, u32[]{:S(2)}) collective-permute-start(bf16[1,256,512]{2,1,0:T(8,128)(2,1)S(1)} %get-tuple-element.48), channel_id=1, source_target_pairs={{0,16},{8,24},{16,0},{24,8},{1,17},{9,25},{17,1},{25,9},{2,18},{10... | collective-permute-start | bytes 786440 | tf_op jit(solution)/shard_map/ppermute | solution.py:73
  437.4 20.0 %collective-permute-start.29 = (bf16[1,256,512]{2,1,0:T(8,128)(2,1)S(1)}, bf16[1,256,512]{2,1,0:T(8,128)(2,1)S(1)}, u32[]{:S(2)}, u32[]{:S(2)}) collective-permute-start(bf16[1,256,512]{2,1,0:T(8,128)(2,1)S(1)} %get-tuple-element.49), channel_id=1, source_target_pairs={{0,8},{8,16},{16,24},{24,0},{1,9},{9,17},{17,25},{25,1},{2,10},{10... | collective-permute-start | bytes 786440 | tf_op jit(solution)/shard_map/ppermute | solution.py:73
  454.7 35.5 %copy-start.10 = (bf16[4,256,512]{2,1,0:T(8,128)(2,1)}, bf16[4,256,512]{2,1,0:T(8,128)(2,1)S(1)}, u32[]{:S(2)}) copy-start(bf16[4,256,512]{2,1,0:T(8,128)(2,1)S(1)} %constant_dynamic-update-slice_fusion.3) | copy-start | bytes 3145732
  463.7 21.1 %collective-permute-start.32 = (bf16[8,1,512]{2,1,0:T(2,128)(2,1)S(1)}, bf16[8,1,512]{2,1,0:T(2,128)(2,1)S(1)}, u32[]{:S(2)}, u32[]{:S(2)}) collective-permute-start(bf16[8,1,512]{2,1,0:T(2,128)(2,1)S(1)} %get-tuple-element.38), channel_id=1, source_target_pairs={{0,1},{1,2},{2,3},{3,4},{4,5},{5,6},{6,7},{8,9},{9,10},{10,11},{11... | collective-permute-start | bytes 24584 | tf_op jit(solution)/shard_map/ppermute | solution.py:17
  465.8 19.0 %collective-permute-start.35 = (bf16[8,1,512]{2,1,0:T(2,128)(2,1)S(1)}, bf16[8,1,512]{2,1,0:T(2,128)(2,1)S(1)}, u32[]{:S(2)}, u32[]{:S(2)}) collective-permute-start(bf16[8,1,512]{2,1,0:T(2,128)(2,1)S(1)} %get-tuple-element.39), channel_id=1, source_target_pairs={{1,0},{2,1},{3,2},{4,3},{5,4},{6,5},{7,6},{9,8},{10,9},{11,10},{12... | collective-permute-start | bytes 24584 | tf_op jit(solution)/shard_map/ppermute | solution.py:17
  467.3 12.1 %collective-permute-start.33 = (bf16[8,256,1]{2,1,0:T(8,128)(2,1)S(1)}, bf16[8,256,1]{2,1,0:T(8,128)(2,1)S(1)}, u32[]{:S(2)}, u32[]{:S(2)}) collective-permute-start(bf16[8,256,1]{2,1,0:T(8,128)(2,1)S(1)} %get-tuple-element.36), channel_id=1, source_target_pairs={{0,8},{8,16},{16,24},{1,9},{9,17},{17,25},{2,10},{10,18},{18,26},{... | collective-permute-start | bytes 12296 | tf_op jit(solution)/shard_map/ppermute | solution.py:17
  468.8 15.9 %collective-permute-start.34 = (bf16[8,256,1]{2,1,0:T(8,128)(2,1)S(1)}, bf16[8,256,1]{2,1,0:T(8,128)(2,1)S(1)}, u32[]{:S(2)}, u32[]{:S(2)}) collective-permute-start(bf16[8,256,1]{2,1,0:T(8,128)(2,1)S(1)} %get-tuple-element.37), channel_id=1, source_target_pairs={{8,0},{16,8},{24,16},{9,1},{17,9},{25,17},{10,2},{18,10},{26,18},{... | collective-permute-start | bytes 12296 | tf_op jit(solution)/shard_map/ppermute | solution.py:17
  (22 other events, 227.3 us)

commit v9 on v6

--- a/solution.py
+++ b/solution.py
@@ -6,24 +6,29 @@
 ITERS = 2
 
 
-def padded_2(array, sides, width):
-    slabs = {}
+def padded_2(array, sides, width, interior=None, edge_map=None):
+    result = array if interior is None else interior
     for axis, dim in sides:
         size, length = (lax.axis_size(axis), array.shape[dim])
         up = [(i, (i + 1) % size) for i in range(size - 1)]
         down = [(j, i) for i, j in up]
         last = lax.slice_in_dim(array, length - width, length, axis=dim)
         initial = lax.slice_in_dim(array, 0, width, axis=dim)
-        slabs[dim] = (lax.ppermute(last, axis, up), lax.ppermute(initial, axis, down))
-    for position, (axis, dim) in enumerate(sides):
-        before, after = slabs[dim]
-        for _, other in sides[:position]:
-            pad = [(0, 0)] * array.ndim
-            pad[other] = (width, width)
-            before = jnp.pad(before, pad)
-            after = jnp.pad(after, pad)
+        before = lax.ppermute(last, axis, up)
+        after = lax.ppermute(initial, axis, down)
         array = jnp.concatenate([before, array, after], axis=dim)
-    return array
+        if edge_map is None:
+            result = array
+        else:
+            result = jnp.concatenate([edge_map(before), result, edge_map(after)], axis=dim)
+    return result
+
+
+def lookup(labels, table):
+    values = jnp.zeros(labels.shape, table.dtype)
+    for label in range(table.shape[0]):
+        values = jnp.where(labels == label, table[label], values)
+    return values
 
 
 def for_sending(array):
@@ -132,11 +137,15 @@
 
 
 def shards(right_side, solution_in, classes, coeff_table, eigenvectors, eigenvalues, level_shift):
-    coeff = jnp.zeros(classes.shape, jnp.float32)
-    for label in range(coeff_table.shape[0]):
-        coeff = jnp.where(classes == label, coeff_table[label], coeff)
+    table = coeff_table.astype(jnp.bfloat16)
+    rounded = solution_in.astype(jnp.bfloat16)
+    labels = classes.astype(jnp.bfloat16)
     stacked = padded_2(
-        jnp.stack((solution_in, coeff)).astype(jnp.bfloat16), (("px", 3), ("py", 2)), 1
+        jnp.stack((rounded, labels)),
+        (("px", 3), ("py", 2)),
+        1,
+        interior=jnp.stack((rounded, lookup(labels, table))),
+        edge_map=lambda slab: jnp.stack((slab[0], lookup(slab[1], table))),
     ).astype(jnp.float32)
     coeff_pad = stacked[1]
     solution = solution_in

time: 546 us -> 588 us (1.077)
  other arithmetic: 121 us -> 157 us
  starting transfers between devices: 113 us -> 103 us
  waiting for transfers between devices: 151 us -> 161 us
    slice x0 -> x4, other arithmetic: none -> 39.6 us  [shards(): slab[0]]
    ppermute x24, starting transfers between devices: 56.7 us -> 47.5 us  [exchange(): lax.ppermute(part, axis, [(i, (i + shift) % size) for i in range(size)])]
    ppermute x24, waiting for transfers between devices: 101 us -> 110 us  [exchange(): lax.ppermute(part, axis, [(i, (i + shift) % size) for i in range(size)])]
    convert_element_type x1 -> x2, other arithmetic: 13.2 us -> 8.61 us  [the longest x1 8.61 us: shards(): stacked = padded_2(jnp.stack((rounded, labels)), (('px', 3), ('py', 2)),...]
    another operation x2 -> x5, other arithmetic: 17.1 us -> 18 us  [the longest x1 14.8 us: shards(): jnp.stack((rounded, lookup(labels, table)))]
  transfers between devices with their start and end apart: 44 -> 44, of which waited for: 25 -> 26; matrix products, arithmetic and copies ran while one was open for 20% -> 26% of each run, Pallas kernels for 0% -> 0%
where the time goes in v9:
time: 588 us; the launch traced here: 582 us
  waiting for transfers between devices  161 us (27%)
  other arithmetic  157 us (27%)
  starting transfers between devices  103 us (18%)
  matrix products  86.5 us (15%)
  local copies, waits for them, and re-layouts  40 us (7%)
  blocking collectives  25.7 us (4%)
  between operations  7.84 us (1%)
    ppermute x24, waiting for transfers between devices, exchange(): lax.ppermute(part, axis, [(i, (i + shift) % size) for i in range(size)])  110 us
    ppermute x24, starting transfers between devices, exchange(): lax.ppermute(part, axis, [(i, (i + shift) % size) for i in range(size)])  47.5 us
    dot_general x4, matrix products, precondition_lines(): jnp.einsum('yj,kji->kyi', eigenvectors, scaled, preferred_element_type=jn...  44.1 us
    slice x4, other arithmetic, shards(): slab[0]  39.6 us
    reduce_sum x2, other arithmetic, shards(): jnp.sum(residual * precond)  27.5 us
    all_to_all x2, blocking collectives, all_sum(): return jnp.sum(lax.all_to_all(spread, axes, 0, 0, tiled=True), 0)  25.7 us
    dot_general x4, matrix products, precondition_lines(): jnp.einsum('qkyi,qix->kyx', returned, eigenvectors.reshape(across, cols,...  22.8 us
    dot_general x4, matrix products, precondition_lines(): jnp.dot(lines.reshape(levels_here * rows, width), eigenvectors, preferred...  19.6 us
  transfers between devices with their start and end apart: 44, of which 26 were waited for; matrix products, arithmetic and copies ran while one was open for 26% of the time, Pallas kernels for 0%

profile of v9, /device:TPU:0, one launch (start us, length us, event | category | flops | bytes accessed | tf_op | source)
XLA Modules:
  0.0 581.5 jit_solution(3900743385713446987)
XLA Ops:
  10.7 5.6 collective-permute-start
  17.0 14.8 %fusion.64 = bf16[1,8,256,512]{3,2,1,0:T(8,128)(2,1)} fusion(bf16[]{:T(256)} %bitcast.17, bf16[]{:T(256)} %bitcast.16, bf16[]{:T(256)} %bitcast.15, bf16[]{:T(256)} %bitcast.14, bf16[]{:T(256)} %bitcast.13, bf16[]{:T(256)} %bitcast.12, bf16[]{:T(256)} %bitcast.11, bf16[]{:T(256)} %bitcast.10, bf16[]{:T(256)} %bitcast.9, bf16[]{:T(256)} %bitcast.8, ...), kind=kLoop, calls=%fused_computation.144 | loop fusion | flops 34603008 | bytes 6291488 | tf_op jit(solution)/shard_map/stack | solution.py:147
  36.3 9.9 %fusion.82 = (bf16[1,8,256,1]{2,1,3,0:T(8,128)(2,1)S(1)}, bf16[1,8,256,1]{2,1,3,0:T(8,128)(2,1)S(1)}) fusion(bf16[2,8,256,1]{2,1,3,0:T(8,128)(2,1)S(1)} %collective-permute-done.1, bf16[]{:T(256)} %bitcast.17, bf16[]{:T(256)} %bitcast.16, bf16[]{:T(256)} %bitcast.15, bf16[]{:T(256)} %bitcast.14, bf16[]{:T(256)} %bitcast.13, bf16[]{:T(256)} %bitcast.12, ...), kind=kLoop, calls=%fused_computation.308 | loop fusion | flops 65536 | bytes 16416 | tf_op jit(solution)/shard_map/slice | solution.py:148
  46.2 9.9 %fusion.81 = (bf16[1,8,256,1]{2,1,3,0:T(8,128)(2,1)S(1)}, bf16[1,8,256,1]{2,1,3,0:T(8,128)(2,1)S(1)}) fusion(bf16[2,8,256,1]{2,1,3,0:T(8,128)(2,1)S(1)} %collective-permute-done, bf16[]{:T(256)} %bitcast.17, bf16[]{:T(256)} %bitcast.16, bf16[]{:T(256)} %bitcast.15, bf16[]{:T(256)} %bitcast.14, bf16[]{:T(256)} %bitcast.13, bf16[]{:T(256)} %bitcast.12, ...), kind=kLoop, calls=%fused_computation.307 | loop fusion | flops 65536 | bytes 16416 | tf_op jit(solution)/shard_map/slice | solution.py:148
  59.5 10.0 %fusion.79 = (bf16[1,8,1,514]{3,2,1,0:T(2,128)(2,1)S(1)}, bf16[1,8,1,514]{3,2,1,0:T(2,128)(2,1)S(1)}) fusion(bf16[2,8,1,514]{3,2,1,0:T(2,128)(2,1)S(1)} %collective-permute-done.2, bf16[]{:T(256)} %bitcast.17, bf16[]{:T(256)} %bitcast.16, bf16[]{:T(256)} %bitcast.15, bf16[]{:T(256)} %bitcast.14, bf16[]{:T(256)} %bitcast.13, bf16[]{:T(256)} %bitcast.12, ...), kind=kLoop, calls=%fused_computation.305 | loop fusion | flops 131584 | bytes 32928 | tf_op jit(solution)/shard_map/slice | solution.py:148
  69.5 10.0 %fusion.80 = (bf16[1,8,1,514]{3,2,1,0:T(2,128)(2,1)S(1)}, bf16[1,8,1,514]{3,2,1,0:T(2,128)(2,1)S(1)}) fusion(bf16[2,8,1,514]{3,2,1,0:T(2,128)(2,1)S(1)} %collective-permute-done.3, bf16[]{:T(256)} %bitcast.17, bf16[]{:T(256)} %bitcast.16, bf16[]{:T(256)} %bitcast.15, bf16[]{:T(256)} %bitcast.14, bf16[]{:T(256)} %bitcast.13, bf16[]{:T(256)} %bitcast.12, ...), kind=kLoop, calls=%fused_computation.306 | loop fusion | flops 131584 | bytes 32928 | tf_op jit(solution)/shard_map/slice | solution.py:148
  79.4 8.6 %maximum_convert_fusion = f32[2,8,258,514]{3,2,1,0:T(8,128)} fusion(bf16[1,8,1,514]{3,2,1,0:T(2,128)(2,1)S(1)} %get-tuple-element.75, bf16[1,8,1,514]{3,2,1,0:T(2,128)(2,1)S(1)} %get-tuple-element.74, bf16[2,8,256,1]{3,2,1,0:T(8,128)(2,1)} %copy.70, bf16[1,8,256,512]{3,2,1,0:T(8,128)(2,1)} %fusion.64, bf16[1,8,256,512]{3,2,1,0:T(8,128)(2,1)S(1)} %convert_bitcast_fusion, ...), kind=kLoop, calls=%fused_computation.11 | loop fusion | flops 33948672 | bytes 12730752 | tf_op jit(solution)/shard_map/convert_element_type | solution.py:149
  92.9 5.9 %fusion.42 = f32[7,256,512]{2,1,0:T(8,128)} fusion(f32[8,258,514]{2,1,0:T(8,128)S(1)} %get-tuple-element.31, f32[8,258,514]{2,1,0:T(8,128)S(1)} %get-tuple-element.30), kind=kLoop, calls=%fused_computation.91 | loop fusion | flops 3670016 | bytes 18350080 | tf_op jit(solution)/shard_map/mul | solution.py:59
  98.8 11.3 %fusion.30 = f32[8,256,512]{2,1,0:T(8,128)S(1)} fusion(f32[8,256,512]{2,1,0:T(8,128)} %param.7, f32[8,258,514]{2,1,0:T(8,128)S(1)} %get-tuple-element.31, f32[7,256,512]{2,1,0:T(8,128)} %fusion.42, f32[8,258,514]{2,1,0:T(8,128)S(1)} %get-tuple-element.30), kind=kLoop, calls=%fused_computation.51 | loop fusion | flops 23068672 | bytes 54001664 | tf_op jit(solution)/shard_map/sub | solution.py:152
  121.6 13.2 %collective-permute-done.5 = bf16[1,256,512]{2,1,0:T(8,128)(2,1)S(1)} collective-permute-done((bf16[1,256,512]{2,1,0:T(8,128)(2,1)S(1)}, bf16[1,256,512]{2,1,0:T(8,128)(2,1)S(1)}, u32[]{:S(2)}, u32[]{:S(2)}) %collective-permute-start.5) | collective-permute-done | bytes 262176 | tf_op jit(solution)/shard_map/ppermute | solution.py:81
  137.5 5.7 collective-permute-start.12
  145.3 5.7 convolution_convert_fusion.7
  152.1 5.3 all-to-all-start
  157.3 5.0 collective-permute-done.10
  162.4 5.8 %collective-permute-done.11 = bf16[1,256,512]{2,1,0:T(8,128)(2,1)S(1)} collective-permute-done((bf16[1,256,512]{2,1,0:T(8,128)(2,1)S(1)}, bf16[1,256,512]{2,1,0:T(8,128)(2,1)S(1)}, u32[]{:S(2)}, u32[]{:S(2)}) %collective-permute-start.11) | collective-permute-done | bytes 262176 | tf_op jit(solution)/shard_map/ppermute | solution.py:81
  168.3 5.7 convolution_convert_fusion.5
  175.1 4.9 all-to-all-start.2
  180.0 11.0 %fusion.52 = bf16[1,2048,256]{1,2,0:T(8,128)(2,1)S(1)} fusion(bf16[2048,2048]{1,0:T(8,128)(2,1)} %param.11, bf16[2048,256]{1,0:T(8,128)(2,1)S(1)} %bitcast.253, f32[]{:T(128)} %bitcast.26, f32[256]{0:T(256)S(1)} %dynamic_slice.114, f32[2048]{0:T(1024)S(1)} %copy-done.13), kind=kOutput, calls=%fused_computation.132 | convolution fusion | flops 4297588736 | bytes 10494980 | tf_op jit(solution)/shard_map/yj,kji->kyi/dot_general | solution.py:106
  199.5 11.1 %fusion.53 = bf16[1,2048,256]{1,2,0:T(8,128)(2,1)S(1)} fusion(bf16[2048,2048]{1,0:T(8,128)(2,1)} %param.11, bf16[2048,256]{1,0:T(8,128)(2,1)S(1)} %bitcast.255, f32[]{:T(128)} %bitcast.43, f32[256]{0:T(256)S(1)} %dynamic_slice.114, f32[2048]{0:T(1024)S(1)} %copy-done.13), kind=kOutput, calls=%fused_computation.133 | convolution fusion | flops 4297588736 | bytes 10494980 | tf_op jit(solution)/shard_map/yj,kji->kyi/dot_general | solution.py:106
  218.4 5.7 fusion.48
  228.9 7.3 %collective-permute-done.7 = bf16[1,256,512]{2,1,0:T(8,128)(2,1)} collective-permute-done((bf16[1,256,512]{2,1,0:T(8,128)(2,1)}, bf16[1,256,512]{2,1,0:T(8,128)(2,1)}, u32[]{:S(2)}, u32[]{:S(2)}) %collective-permute-start.7) | collective-permute-done | bytes 262176 | tf_op jit(solution)/shard_map/ppermute | solution.py:81
  237.2 5.7 fusion.49
  243.1 19.2 %collective-permute-done.8 = bf16[1,256,512]{2,1,0:T(8,128)(2,1)} collective-permute-done((bf16[1,256,512]{2,1,0:T(8,128)(2,1)}, bf16[1,256,512]{2,1,0:T(8,128)(2,1)}, u32[]{:S(2)}, u32[]{:S(2)}) %collective-permute-start.8) | collective-permute-done | bytes 262176 | tf_op jit(solution)/shard_map/ppermute | solution.py:81
  264.6 7.3 %collective-permute-done.14 = bf16[1,256,512]{2,1,0:T(8,128)(2,1)S(1)} collective-permute-done((bf16[1,256,512]{2,1,0:T(8,128)(2,1)S(1)}, bf16[1,256,512]{2,1,0:T(8,128)(2,1)S(1)}, u32[]{:S(2)}, u32[]{:S(2)}) %collective-permute-start.14) | collective-permute-done | bytes 262176 | tf_op jit(solution)/shard_map/ppermute | solution.py:81
  278.7 7.3 %collective-permute-done.16 = bf16[8,256,1]{2,1,0:T(8,128)(2,1)S(1)} collective-permute-done((bf16[8,256,1]{2,1,0:T(8,128)(2,1)S(1)}, bf16[8,256,1]{2,1,0:T(8,128)(2,1)S(1)}, u32[]{:S(2)}, u32[]{:S(2)}) %collective-permute-start.16) | collective-permute-done | bytes 4128 | tf_op jit(solution)/shard_map/ppermute | solution.py:17
  296.3 5.7 maximum_convert_fusion.1
  302.1 5.9 %fusion.41 = f32[7,256,512]{2,1,0:T(8,128)} fusion(f32[8,258,514]{2,1,0:T(8,128)S(1)} %maximum_convert_fusion.1, f32[8,258,514]{2,1,0:T(8,128)S(1)} %bitcast.249), kind=kLoop, calls=%fused_computation.89 | loop fusion | flops 3670016 | bytes 18350080 | tf_op jit(solution)/shard_map/mul | solution.py:59
  308.0 13.3 %fusion.3 = (f32[]{:T(128)}, f32[]{:T(128)}, f32[8,256,512]{2,1,0:T(8,128)}) fusion(f32[8,256,512]{2,1,0:T(8,128)} %copy-done.4, bf16[4,256,512]{2,1,0:T(8,128)(2,1)} %copy-done.3, bf16[4,256,512]{2,1,0:T(8,128)(2,1)} %copy-done.2, f32[7,256,512]{2,1,0:T(8,128)} %fusion.41, f32[8,258,514]{2,1,0:T(8,128)S(1)} %maximum_convert_fusion.1, ...), kind=kLoop, calls=%fused_computation.15 | loop fusion | flops 28311552 | bytes 56098824 | tf_op jit(solution)/shard_map/reduce_sum | solution.py:159
  322.6 11.8 %all_to_all.52 = f32[32,1,2]{2,1,0:T(1,128)S(1)} all-to-all(f32[32,1,2]{2,1,0:T(1,128)S(1)} %broadcast_in_dim.251), channel_id=1, replica_groups=mesh['px'=4,'py'=8] {'px','py'}, dimensions={0} | all-to-all | bytes 512 | tf_op jit(solution)/shard_map/all_to_all | solution.py:46
  345.5 7.3 %collective-permute-done.20 = bf16[1,256,512]{2,1,0:T(8,128)(2,1)S(1)} collective-permute-done((bf16[1,256,512]{2,1,0:T(8,128)(2,1)S(1)}, bf16[1,256,512]{2,1,0:T(8,128)(2,1)S(1)}, u32[]{:S(2)}, u32[]{:S(2)}) %collective-permute-start.20) | collective-permute-done | bytes 262176 | tf_op jit(solution)/shard_map/ppermute | solution.py:81
  352.8 10.2 %collective-permute-done.21 = bf16[1,256,512]{2,1,0:T(8,128)(2,1)S(1)} collective-permute-done((bf16[1,256,512]{2,1,0:T(8,128)(2,1)S(1)}, bf16[1,256,512]{2,1,0:T(8,128)(2,1)S(1)}, u32[]{:S(2)}, u32[]{:S(2)}) %collective-permute-start.21) | collective-permute-done | bytes 262176 | tf_op jit(solution)/shard_map/ppermute | solution.py:81
  364.1 5.0 collective-permute-start.28
  378.1 8.4 %collective-permute-done.26 = bf16[1,256,512]{2,1,0:T(8,128)(2,1)S(1)} collective-permute-done((bf16[1,256,512]{2,1,0:T(8,128)(2,1)}, bf16[1,256,512]{2,1,0:T(8,128)(2,1)S(1)}, u32[]{:S(2)}, u32[]{:S(2)}) %collective-permute-start.26) | collective-permute-done | bytes 262176 | tf_op jit(solution)/shard_map/ppermute | solution.py:81
  386.6 6.5 %collective-permute-done.27 = bf16[1,256,512]{2,1,0:T(8,128)(2,1)S(1)} collective-permute-done((bf16[1,256,512]{2,1,0:T(8,128)(2,1)S(1)}, bf16[1,256,512]{2,1,0:T(8,128)(2,1)S(1)}, u32[]{:S(2)}, u32[]{:S(2)}) %collective-permute-start.27) | collective-permute-done | bytes 262176 | tf_op jit(solution)/shard_map/ppermute | solution.py:81
  393.2 5.7 convolution_convert_fusion.1
  403.5 11.0 %fusion.54 = bf16[1,2048,256]{1,2,0:T(8,128)(2,1)S(1)} fusion(bf16[2048,2048]{1,0:T(8,128)(2,1)} %param.11, bf16[2048,256]{1,0:T(8,128)(2,1)S(1)} %bitcast.252, f32[]{:T(128)} %bitcast.26, f32[256]{0:T(256)S(1)} %dynamic_slice.114, f32[2048]{0:T(1024)S(1)} %copy-done.13), kind=kOutput, calls=%fused_computation.134 | convolution fusion | flops 4297588736 | bytes 10494980 | tf_op jit(solution)/shard_map/yj,kji->kyi/dot_general | solution.py:106
  422.8 11.1 %fusion.55 = bf16[1,2048,256]{1,2,0:T(8,128)(2,1)S(1)} fusion(bf16[2048,2048]{1,0:T(8,128)(2,1)} %param.11, bf16[2048,256]{1,0:T(8,128)(2,1)S(1)} %bitcast.254, f32[]{:T(128)} %bitcast.43, f32[256]{0:T(256)S(1)} %dynamic_slice.114, f32[2048]{0:T(1024)S(1)} %copy-done.13), kind=kOutput, calls=%fused_computation.135 | convolution fusion | flops 4297588736 | bytes 10494980 | tf_op jit(solution)/shard_map/yj,kji->kyi/dot_general | solution.py:106
  441.7 5.7 fusion.50
  450.5 6.5 %all-to-all-done.8 = bf16[8,1,256,256]{3,2,1,0:T(8,128)(2,1)S(1)} async-done(((bf16[8,1,256,256]{3,2,1,0:T(8,128)(2,1)}), bf16[8,1,256,256]{3,2,1,0:T(8,128)(2,1)S(1)}, u32[]{:S(2)}, u32[]{:S(2)}) %all-to-all-start.8) | async-done | bytes 1048608 | tf_op jit(solution)/shard_map/all_to_all | solution.py:110
  457.0 5.7 fusion.51
  468.4 15.2 %collective-permute-start.29 = (bf16[1,256,512]{2,1,0:T(8,128)(2,1)S(1)}, bf16[1,256,512]{2,1,0:T(8,128)(2,1)S(1)}, u32[]{:S(2)}, u32[]{:S(2)}) collective-permute-start(bf16[1,256,512]{2,1,0:T(8,128)(2,1)S(1)} %get-tuple-element.49), channel_id=1, source_target_pairs={{0,8},{8,16},{16,24},{24,0},{1,9},{9,17},{17,25},{25,1},{2,10},{10... | collective-permute-start | bytes 786440 | tf_op jit(solution)/shard_map/ppermute | solution.py:81
  489.4 5.3 collective-permute-done.30
  498.4 10.0 %collective-permute-done.32 = bf16[8,256,1]{2,1,0:T(8,128)(2,1)S(1)} collective-permute-done((bf16[8,256,1]{2,1,0:T(8,128)(2,1)S(1)}, bf16[8,256,1]{2,1,0:T(8,128)(2,1)S(1)}, u32[]{:S(2)}, u32[]{:S(2)}) %collective-permute-start.32) | collective-permute-done | bytes 4128 | tf_op jit(solution)/shard_map/ppermute | solution.py:17
  520.1 5.7 maximum_convert_fusion.2
  525.9 5.9 %fusion.40 = f32[7,256,512]{2,1,0:T(8,128)} fusion(f32[8,258,514]{2,1,0:T(8,128)S(1)} %maximum_convert_fusion.2, f32[8,258,514]{2,1,0:T(8,128)S(1)} %bitcast.251), kind=kLoop, calls=%fused_computation.87 | loop fusion | flops 3670016 | bytes 18350080 | tf_op jit(solution)/shard_map/mul | solution.py:59
  531.8 14.2 %fusion = (f32[]{:T(128)}, f32[]{:T(128)}, f32[]{:T(128)}, f32[]{:T(128)}, f32[8,256,512]{2,1,0:T(8,128)}) fusion(f32[8,256,512]{2,1,0:T(8,128)} %copy-done.5, bf16[4,256,512]{2,1,0:T(8,128)(2,1)} %copy-done.7, bf16[4,256,512]{2,1,0:T(8,128)(2,1)} %copy-done.8, f32[8,256,512]{2,1,0:T(8,128)} %get-tuple-element.29, bf16[4,256,512]{2,1,0:T(8,128)(2,1)} %copy-done.3, ...), kind=kLoop, calls=%fused_computation.12 | loop fusion | flops 34603004 | bytes 62390288 | tf_op jit(solution)/shard_map/reduce_sum | solution.py:166
  548.6 13.9 %all_to_all.53 = f32[32,1,4]{2,1,0:T(1,128)S(1)} all-to-all(f32[32,1,4]{2,1,0:T(1,128)S(1)} %broadcast_in_dim.252), channel_id=1, replica_groups=mesh['px'=4,'py'=8] {'px','py'}, dimensions={0} | all-to-all | bytes 1024 | tf_op jit(solution)/shard_map/all_to_all | solution.py:46
  567.7 7.2 %fusion.6 = (f32[8,256,512]{2,1,0:T(8,128)}, f32[8,256,512]{2,1,0:T(8,128)}) fusion(f32[8,256,512]{2,1,0:T(8,128)} %param.8, f32[]{:T(128)S(6)} %div.27, f32[]{:T(128)S(6)} %div.23, bf16[4,256,512]{2,1,0:T(8,128)(2,1)} %copy-done.3, bf16[4,256,512]{2,1,0:T(8,128)(2,1)} %copy-done.2, f32[]{:T(128)S(6)} %div.26, bf16[4,256,512]{2,1,0:T(8,128)(2,1)} %copy-done.7, ...), kind=kLoop, calls=%fused_computation.18 | loop fusion | flops 10485760 | bytes 16777228 | tf_op jit(solution)/shard_map/add | solution.py:179
  (201 shorter events, 164.6 us)
Async XLA Ops:
  9.1 23.3 %collective-permute-start.1 = (bf16[2,8,256,1]{2,1,3,0:T(8,128)(2,1)S(1)}, bf16[2,8,256,1]{2,1,3,0:T(8,128)(2,1)S(1)}, u32[]{:S(2)}, u32[]{:S(2)}) collective-permute-start(bf16[2,8,256,1]{2,1,3,0:T(8,128)(2,1)S(1)} %copy.66), channel_id=1, source_target_pairs={{8,0},{16,8},{24,16},{9,1},{17,9},{25,17},{10,2},{18,10},{26,18},{... | collective-permute-start | bytes 24584 | tf_op jit(solution)/shard_map/ppermute | solution.py:18
  10.7 21.1 %collective-permute-start = (bf16[2,8,256,1]{2,1,3,0:T(8,128)(2,1)S(1)}, bf16[2,8,256,1]{2,1,3,0:T(8,128)(2,1)S(1)}, u32[]{:S(2)}, u32[]{:S(2)}) collective-permute-start(bf16[2,8,256,1]{2,1,3,0:T(8,128)(2,1)S(1)} %copy.65), channel_id=1, source_target_pairs={{0,8},{8,16},{16,24},{1,9},{9,17},{17,25},{2,10},{10,18},{18,26},{... | collective-permute-start | bytes 24584 | tf_op jit(solution)/shard_map/ppermute | solution.py:17
  34.9 24.6 %collective-permute-start.2 = (bf16[2,8,1,514]{3,2,1,0:T(2,128)(2,1)S(1)}, bf16[2,8,1,514]{3,2,1,0:T(2,128)(2,1)S(1)}, u32[]{:S(2)}, u32[]{:S(2)}) collective-permute-start(bf16[2,8,1,514]{3,2,1,0:T(2,128)(2,1)S(1)} %get-tuple-element.32), channel_id=1, source_target_pairs={{0,1},{1,2},{2,3},{3,4},{4,5},{5,6},{6,7},{8,9},{9,10},{10,11},{11... | collective-permute-start | bytes 49352 | tf_op jit(solution)/shard_map/ppermute | solution.py:17
  58.0 11.5 %collective-permute-start.3 = (bf16[2,8,1,514]{3,2,1,0:T(2,128)(2,1)S(1)}, bf16[2,8,1,514]{3,2,1,0:T(2,128)(2,1)S(1)}, u32[]{:S(2)}, u32[]{:S(2)}) collective-permute-start(bf16[2,8,1,514]{3,2,1,0:T(2,128)(2,1)S(1)} %get-tuple-element.33), channel_id=1, source_target_pairs={{1,0},{2,1},{3,2},{4,3},{5,4},{6,5},{7,6},{9,8},{10,9},{11,10},{12... | collective-permute-start | bytes 49352 | tf_op jit(solution)/shard_map/ppermute | solution.py:18
  112.5 9.0 %collective-permute-start.4 = (bf16[1,256,512]{2,1,0:T(8,128)(2,1)S(1)}, bf16[1,256,512]{2,1,0:T(8,128)(2,1)S(1)}, u32[]{:S(2)}, u32[]{:S(2)}) collective-permute-start(bf16[1,256,512]{2,1,0:T(8,128)(2,1)S(1)} %get-tuple-element.70), channel_id=1, source_target_pairs={{0,8},{8,16},{16,24},{24,0},{1,9},{9,17},{17,25},{25,1},{2,10},{10... | collective-permute-start | bytes 786440 | tf_op jit(solution)/shard_map/ppermute | solution.py:81
  114.4 20.3 %collective-permute-start.5 = (bf16[1,256,512]{2,1,0:T(8,128)(2,1)S(1)}, bf16[1,256,512]{2,1,0:T(8,128)(2,1)S(1)}, u32[]{:S(2)}, u32[]{:S(2)}) collective-permute-start(bf16[1,256,512]{2,1,0:T(8,128)(2,1)S(1)} %get-tuple-element.69), channel_id=1, source_target_pairs={{0,16},{8,24},{16,0},{24,8},{1,17},{9,25},{17,1},{25,9},{2,18},{10... | collective-permute-start | bytes 786440 | tf_op jit(solution)/shard_map/ppermute | solution.py:81
  115.5 19.3 %collective-permute-start.6 = (bf16[1,256,512]{2,1,0:T(8,128)(2,1)S(1)}, bf16[1,256,512]{2,1,0:T(8,128)(2,1)S(1)}, u32[]{:S(2)}, u32[]{:S(2)}) collective-permute-start(bf16[1,256,512]{2,1,0:T(8,128)(2,1)S(1)} %get-tuple-element.68), channel_id=1, source_target_pairs={{0,24},{8,0},{16,8},{24,16},{1,25},{9,1},{17,9},{25,17},{2,26},{10... | collective-permute-start | bytes 786440 | tf_op jit(solution)/shard_map/ppermute | solution.py:81
  137.5 30.8 %collective-permute-start.12 = (bf16[1,256,512]{2,1,0:T(8,128)(2,1)S(1)}, bf16[1,256,512]{2,1,0:T(8,128)(2,1)S(1)}, u32[]{:S(2)}, u32[]{:S(2)}) collective-permute-start(bf16[1,256,512]{2,1,0:T(8,128)(2,1)S(1)} %get-tuple-element.64), channel_id=1, source_target_pairs={{0,24},{8,0},{16,8},{24,16},{1,25},{9,1},{17,9},{25,17},{2,26},{10... | collective-permute-start | bytes 786440 | tf_op jit(solution)/shard_map/ppermute | solution.py:81
  143.2 25.1 %collective-permute-start.11 = (bf16[1,256,512]{2,1,0:T(8,128)(2,1)S(1)}, bf16[1,256,512]{2,1,0:T(8,128)(2,1)S(1)}, u32[]{:S(2)}, u32[]{:S(2)}) collective-permute-start(bf16[1,256,512]{2,1,0:T(8,128)(2,1)S(1)} %get-tuple-element.65), channel_id=1, source_target_pairs={{0,16},{8,24},{16,0},{24,8},{1,17},{9,25},{17,1},{25,9},{2,18},{10... | collective-permute-start | bytes 786440 | tf_op jit(solution)/shard_map/ppermute | solution.py:81
  145.1 17.3 %collective-permute-start.10 = (bf16[1,256,512]{2,1,0:T(8,128)(2,1)}, bf16[1,256,512]{2,1,0:T(8,128)(2,1)S(1)}, u32[]{:S(2)}, u32[]{:S(2)}) collective-permute-start(bf16[1,256,512]{2,1,0:T(8,128)(2,1)} %get-tuple-element.66), channel_id=1, source_target_pairs={{0,8},{8,16},{16,24},{24,0},{1,9},{9,17},{17,25},{25,1},{2,10},{10... | collective-permute-start | bytes 786440 | tf_op jit(solution)/shard_map/ppermute | solution.py:81
  152.1 23.0 %all-to-all-start = ((bf16[8,256,256]{2,1,0:T(8,128)(2,1)}), bf16[8,256,256]{2,1,0:T(8,128)(2,1)S(1)}, u32[]{:S(2)}, u32[]{:S(2)}) async-start(bf16[8,256,256]{2,1,0:T(8,128)(2,1)} %bitcast.247), calls=%async_computation | async-start | bytes 2097152 | tf_op jit(solution)/shard_map/all_to_all | solution.py:96
  175.1 20.4 %all-to-all-start.2 = ((bf16[8,256,256]{2,1,0:T(8,128)(2,1)}), bf16[8,256,256]{2,1,0:T(8,128)(2,1)S(1)}, u32[]{:S(2)}, u32[]{:S(2)}) async-start(bf16[8,256,256]{2,1,0:T(8,128)(2,1)} %bitcast.245), calls=%async_computation.2 | async-start | bytes 2097152 | tf_op jit(solution)/shard_map/all_to_all | solution.py:96
  195.4 19.4 %all-to-all-start.1 = ((bf16[8,1,256,256]{3,2,1,0:T(8,128)(2,1)}), bf16[8,1,256,256]{3,2,1,0:T(8,128)(2,1)S(1)}, u32[]{:S(2)}, u32[]{:S(2)}) async-start(bf16[8,1,256,256]{3,2,1,0:T(8,128)(2,1)} %bitcast.30), calls=%async_computation.1 | async-start | bytes 2097152 | tf_op jit(solution)/shard_map/all_to_all | solution.py:110
  214.8 22.4 %all-to-all-start.3 = ((bf16[8,1,256,256]{3,2,1,0:T(8,128)(2,1)}), bf16[8,1,256,256]{3,2,1,0:T(8,128)(2,1)S(1)}, u32[]{:S(2)}, u32[]{:S(2)}) async-start(bf16[8,1,256,256]{3,2,1,0:T(8,128)(2,1)} %bitcast.47), calls=%async_computation.3 | async-start | bytes 2097152 | tf_op jit(solution)/shard_map/all_to_all | solution.py:110
  225.0 11.3 %collective-permute-start.7 = (bf16[1,256,512]{2,1,0:T(8,128)(2,1)}, bf16[1,256,512]{2,1,0:T(8,128)(2,1)}, u32[]{:S(2)}, u32[]{:S(2)}) collective-permute-start(bf16[1,256,512]{2,1,0:T(8,128)(2,1)} %get-tuple-element.60), channel_id=1, source_target_pairs={{0,8},{8,16},{16,24},{24,0},{1,9},{9,17},{17,25},{25,1},{2,10},{10... | collective-permute-start | bytes 786440 | tf_op jit(solution)/shard_map/ppermute | solution.py:81
  225.0 38.4 %collective-permute-start.9 = (bf16[1,256,512]{2,1,0:T(8,128)(2,1)S(1)}, bf16[1,256,512]{2,1,0:T(8,128)(2,1)}, u32[]{:S(2)}, u32[]{:S(2)}) collective-permute-start(bf16[1,256,512]{2,1,0:T(8,128)(2,1)S(1)} %get-tuple-element.58), channel_id=1, source_target_pairs={{0,24},{8,0},{16,8},{24,16},{1,25},{9,1},{17,9},{25,17},{2,26},{10... | collective-permute-start | bytes 786440 | tf_op jit(solution)/shard_map/ppermute | solution.py:81
  228.8 33.5 %collective-permute-start.8 = (bf16[1,256,512]{2,1,0:T(8,128)(2,1)}, bf16[1,256,512]{2,1,0:T(8,128)(2,1)}, u32[]{:S(2)}, u32[]{:S(2)}) collective-permute-start(bf16[1,256,512]{2,1,0:T(8,128)(2,1)} %get-tuple-element.59), channel_id=1, source_target_pairs={{0,16},{8,24},{16,0},{24,8},{1,17},{9,25},{17,1},{25,9},{2,18},{10... | collective-permute-start | bytes 786440 | tf_op jit(solution)/shard_map/ppermute | solution.py:81
  243.0 21.5 %collective-permute-start.13 = (bf16[1,256,512]{2,1,0:T(8,128)(2,1)S(1)}, bf16[1,256,512]{2,1,0:T(8,128)(2,1)S(1)}, u32[]{:S(2)}, u32[]{:S(2)}) collective-permute-start(bf16[1,256,512]{2,1,0:T(8,128)(2,1)S(1)} %get-tuple-element.63), channel_id=1, source_target_pairs={{0,8},{8,16},{16,24},{24,0},{1,9},{9,17},{17,25},{25,1},{2,10},{10... | collective-permute-start | bytes 786440 | tf_op jit(solution)/shard_map/ppermute | solution.py:81
  263.3 8.6 %collective-permute-start.14 = (bf16[1,256,512]{2,1,0:T(8,128)(2,1)S(1)}, bf16[1,256,512]{2,1,0:T(8,128)(2,1)S(1)}, u32[]{:S(2)}, u32[]{:S(2)}) collective-permute-start(bf16[1,256,512]{2,1,0:T(8,128)(2,1)S(1)} %get-tuple-element.62), channel_id=1, source_target_pairs={{0,16},{8,24},{16,0},{24,8},{1,17},{9,25},{17,1},{25,9},{2,18},{10... | collective-permute-start | bytes 786440 | tf_op jit(solution)/shard_map/ppermute | solution.py:81
  264.3 26.0 %copy-start.2 = (bf16[4,256,512]{2,1,0:T(8,128)(2,1)}, bf16[4,256,512]{2,1,0:T(8,128)(2,1)S(1)}, u32[]{:S(2)}) copy-start(bf16[4,256,512]{2,1,0:T(8,128)(2,1)S(1)} %constant_dynamic-update-slice_fusion.17) | copy-start | bytes 3145732
  264.4 10.2 %collective-permute-start.15 = (bf16[1,256,512]{2,1,0:T(8,128)(2,1)S(1)}, bf16[1,256,512]{2,1,0:T(8,128)(2,1)S(1)}, u32[]{:S(2)}, u32[]{:S(2)}) collective-permute-start(bf16[1,256,512]{2,1,0:T(8,128)(2,1)S(1)} %get-tuple-element.61), channel_id=1, source_target_pairs={{0,24},{8,0},{16,8},{24,16},{1,25},{9,1},{17,9},{25,17},{2,26},{10... | collective-permute-start | bytes 786440 | tf_op jit(solution)/shard_map/ppermute | solution.py:81
  274.8 11.2 %collective-permute-start.16 = (bf16[8,256,1]{2,1,0:T(8,128)(2,1)S(1)}, bf16[8,256,1]{2,1,0:T(8,128)(2,1)S(1)}, u32[]{:S(2)}, u32[]{:S(2)}) collective-permute-start(bf16[8,256,1]{2,1,0:T(8,128)(2,1)S(1)} %get-tuple-element.42), channel_id=1, source_target_pairs={{0,8},{8,16},{16,24},{1,9},{9,17},{17,25},{2,10},{10,18},{18,26},{... | collective-permute-start | bytes 12296 | tf_op jit(solution)/shard_map/ppermute | solution.py:17
  277.4 12.7 %collective-permute-start.17 = (bf16[8,256,1]{2,1,0:T(8,128)(2,1)S(1)}, bf16[8,256,1]{2,1,0:T(8,128)(2,1)S(1)}, u32[]{:S(2)}, u32[]{:S(2)}) collective-permute-start(bf16[8,256,1]{2,1,0:T(8,128)(2,1)S(1)} %get-tuple-element.43), channel_id=1, source_target_pairs={{8,0},{16,8},{24,16},{9,1},{17,9},{25,17},{10,2},{18,10},{26,18},{... | collective-permute-start | bytes 12296 | tf_op jit(solution)/shard_map/ppermute | solution.py:18
  290.3 3.2 collective-permute-start.18
  291.9 4.5 collective-permute-start.19
  336.5 34.5 %slice-start.4 = ((s8[8388608]{0:T(1024)(128)(4,1)}), s8[4194304]{0:T(1024)(128)(4,1)S(1)}, s32[]{:S(2)}) async-start(s8[8388608]{0:T(1024)(128)(4,1)} %bitcast.264), calls=%async_computation.14 | async-start | bytes 8388608
  336.5 34.5 %slice-start.5 = ((s8[8388608]{0:T(1024)(128)(4,1)}), s8[4194304]{0:T(1024)(128)(4,1)S(1)}, s32[]{:S(2)}) async-start(s8[8388608]{0:T(1024)(128)(4,1)} %bitcast.264), calls=%async_computation.15 | async-start | bytes 8388608
  341.6 11.1 %collective-permute-start.20 = (bf16[1,256,512]{2,1,0:T(8,128)(2,1)S(1)}, bf16[1,256,512]{2,1,0:T(8,128)(2,1)S(1)}, u32[]{:S(2)}, u32[]{:S(2)}) collective-permute-start(bf16[1,256,512]{2,1,0:T(8,128)(2,1)S(1)} %get-tuple-element.56), channel_id=1, source_target_pairs={{0,8},{8,16},{16,24},{24,0},{1,9},{9,17},{17,25},{25,1},{2,10},{10... | collective-permute-start | bytes 786440 | tf_op jit(solution)/shard_map/ppermute | solution.py:81
  342.2 20.7 %collective-permute-start.21 = (bf16[1,256,512]{2,1,0:T(8,128)(2,1)S(1)}, bf16[1,256,512]{2,1,0:T(8,128)(2,1)S(1)}, u32[]{:S(2)}, u32[]{:S(2)}) collective-permute-start(bf16[1,256,512]{2,1,0:T(8,128)(2,1)S(1)} %get-tuple-element.55), channel_id=1, source_target_pairs={{0,16},{8,24},{16,0},{24,8},{1,17},{9,25},{17,1},{25,9},{2,18},{10... | collective-permute-start | bytes 786440 | tf_op jit(solution)/shard_map/ppermute | solution.py:81
  342.8 20.2 %collective-permute-start.22 = (bf16[1,256,512]{2,1,0:T(8,128)(2,1)S(1)}, bf16[1,256,512]{2,1,0:T(8,128)(2,1)S(1)}, u32[]{:S(2)}, u32[]{:S(2)}) collective-permute-start(bf16[1,256,512]{2,1,0:T(8,128)(2,1)S(1)} %get-tuple-element.54), channel_id=1, source_target_pairs={{0,24},{8,0},{16,8},{24,16},{1,25},{9,1},{17,9},{25,17},{2,26},{10... | collective-permute-start | bytes 786440 | tf_op jit(solution)/shard_map/ppermute | solution.py:81
  364.1 29.0 %collective-permute-start.28 = (bf16[1,256,512]{2,1,0:T(8,128)(2,1)S(1)}, bf16[1,256,512]{2,1,0:T(8,128)(2,1)S(1)}, u32[]{:S(2)}, u32[]{:S(2)}) collective-permute-start(bf16[1,256,512]{2,1,0:T(8,128)(2,1)S(1)} %get-tuple-element.50), channel_id=1, source_target_pairs={{0,24},{8,0},{16,8},{24,16},{1,25},{9,1},{17,9},{25,17},{2,26},{10... | collective-permute-start | bytes 786440 | tf_op jit(solution)/shard_map/ppermute | solution.py:81
  369.1 24.0 %collective-permute-start.27 = (bf16[1,256,512]{2,1,0:T(8,128)(2,1)S(1)}, bf16[1,256,512]{2,1,0:T(8,128)(2,1)S(1)}, u32[]{:S(2)}, u32[]{:S(2)}) collective-permute-start(bf16[1,256,512]{2,1,0:T(8,128)(2,1)S(1)} %get-tuple-element.51), channel_id=1, source_target_pairs={{0,16},{8,24},{16,0},{24,8},{1,17},{9,25},{17,1},{25,9},{2,18},{10... | collective-permute-start | bytes 786440 | tf_op jit(solution)/shard_map/ppermute | solution.py:81
  370.8 15.7 %collective-permute-start.26 = (bf16[1,256,512]{2,1,0:T(8,128)(2,1)}, bf16[1,256,512]{2,1,0:T(8,128)(2,1)S(1)}, u32[]{:S(2)}, u32[]{:S(2)}) collective-permute-start(bf16[1,256,512]{2,1,0:T(8,128)(2,1)} %get-tuple-element.52), channel_id=1, source_target_pairs={{0,8},{8,16},{16,24},{24,0},{1,9},{9,17},{17,25},{25,1},{2,10},{10... | collective-permute-start | bytes 786440 | tf_op jit(solution)/shard_map/ppermute | solution.py:81
  374.5 25.4 %all-to-all-start.5 = ((bf16[8,256,256]{2,1,0:T(8,128)(2,1)}), bf16[8,256,256]{2,1,0:T(8,128)(2,1)S(1)}, u32[]{:S(2)}, u32[]{:S(2)}) async-start(bf16[8,256,256]{2,1,0:T(8,128)(2,1)} %bitcast.243), calls=%async_computation.5 | async-start | bytes 2097152 | tf_op jit(solution)/shard_map/all_to_all | solution.py:96
  399.9 18.9 %all-to-all-start.7 = ((bf16[8,256,256]{2,1,0:T(8,128)(2,1)}), bf16[8,256,256]{2,1,0:T(8,128)(2,1)S(1)}, u32[]{:S(2)}, u32[]{:S(2)}) async-start(bf16[8,256,256]{2,1,0:T(8,128)(2,1)} %bitcast.241), calls=%async_computation.7 | async-start | bytes 2097152 | tf_op jit(solution)/shard_map/all_to_all | solution.py:96
  418.8 19.3 %all-to-all-start.6 = ((bf16[8,1,256,256]{3,2,1,0:T(8,128)(2,1)}), bf16[8,1,256,256]{3,2,1,0:T(8,128)(2,1)S(1)}, u32[]{:S(2)}, u32[]{:S(2)}) async-start(bf16[8,1,256,256]{3,2,1,0:T(8,128)(2,1)} %bitcast.66), calls=%async_computation.6 | async-start | bytes 2097152 | tf_op jit(solution)/shard_map/all_to_all | solution.py:110
  438.1 18.9 %all-to-all-start.8 = ((bf16[8,1,256,256]{3,2,1,0:T(8,128)(2,1)}), bf16[8,1,256,256]{3,2,1,0:T(8,128)(2,1)S(1)}, u32[]{:S(2)}, u32[]{:S(2)}) async-start(bf16[8,1,256,256]{3,2,1,0:T(8,128)(2,1)} %bitcast.81), calls=%async_computation.8 | async-start | bytes 2097152 | tf_op jit(solution)/shard_map/all_to_all | solution.py:110
  447.5 37.2 %collective-permute-start.25 = (bf16[1,256,512]{2,1,0:T(8,128)(2,1)S(1)}, bf16[1,256,512]{2,1,0:T(8,128)(2,1)S(1)}, u32[]{:S(2)}, u32[]{:S(2)}) collective-permute-start(bf16[1,256,512]{2,1,0:T(8,128)(2,1)S(1)} %get-tuple-element.44), channel_id=1, source_target_pairs={{0,24},{8,0},{16,8},{24,16},{1,25},{9,1},{17,9},{25,17},{2,26},{10... | collective-permute-start | bytes 786440 | tf_op jit(solution)/shard_map/ppermute | solution.py:81
  447.6 37.0 %collective-permute-start.24 = (bf16[1,256,512]{2,1,0:T(8,128)(2,1)S(1)}, bf16[1,256,512]{2,1,0:T(8,128)(2,1)S(1)}, u32[]{:S(2)}, u32[]{:S(2)}) collective-permute-start(bf16[1,256,512]{2,1,0:T(8,128)(2,1)S(1)} %get-tuple-element.45), channel_id=1, source_target_pairs={{0,16},{8,24},{16,0},{24,8},{1,17},{9,25},{17,1},{25,9},{2,18},{10... | collective-permute-start | bytes 786440 | tf_op jit(solution)/shard_map/ppermute | solution.py:81
  448.5 20.0 %collective-permute-start.23 = (bf16[1,256,512]{2,1,0:T(8,128)(2,1)S(1)}, bf16[1,256,512]{2,1,0:T(8,128)(2,1)}, u32[]{:S(2)}, u32[]{:S(2)}) collective-permute-start(bf16[1,256,512]{2,1,0:T(8,128)(2,1)S(1)} %get-tuple-element.46), channel_id=1, source_target_pairs={{0,8},{8,16},{16,24},{24,0},{1,9},{9,17},{17,25},{25,1},{2,10},{10... | collective-permute-start | bytes 786440 | tf_op jit(solution)/shard_map/ppermute | solution.py:81
  463.0 31.7 %collective-permute-start.31 = (bf16[1,256,512]{2,1,0:T(8,128)(2,1)S(1)}, bf16[1,256,512]{2,1,0:T(8,128)(2,1)S(1)}, u32[]{:S(2)}, u32[]{:S(2)}) collective-permute-start(bf16[1,256,512]{2,1,0:T(8,128)(2,1)S(1)} %get-tuple-element.47), channel_id=1, source_target_pairs={{0,24},{8,0},{16,8},{24,16},{1,25},{9,1},{17,9},{25,17},{2,26},{10... | collective-permute-start | bytes 786440 | tf_op jit(solution)/shard_map/ppermute | solution.py:81
  463.0 31.6 %collective-permute-start.30 = (bf16[1,256,512]{2,1,0:T(8,128)(2,1)S(1)}, bf16[1,256,512]{2,1,0:T(8,128)(2,1)S(1)}, u32[]{:S(2)}, u32[]{:S(2)}) collective-permute-start(bf16[1,256,512]{2,1,0:T(8,128)(2,1)S(1)} %get-tuple-element.48), channel_id=1, source_target_pairs={{0,16},{8,24},{16,0},{24,8},{1,17},{9,25},{17,1},{25,9},{2,18},{10... | collective-permute-start | bytes 786440 | tf_op jit(solution)/shard_map/ppermute | solution.py:81
  468.4 20.9 %collective-permute-start.29 = (bf16[1,256,512]{2,1,0:T(8,128)(2,1)S(1)}, bf16[1,256,512]{2,1,0:T(8,128)(2,1)S(1)}, u32[]{:S(2)}, u32[]{:S(2)}) collective-permute-start(bf16[1,256,512]{2,1,0:T(8,128)(2,1)S(1)} %get-tuple-element.49), channel_id=1, source_target_pairs={{0,8},{8,16},{16,24},{24,0},{1,9},{9,17},{17,25},{25,1},{2,10},{10... | collective-permute-start | bytes 786440 | tf_op jit(solution)/shard_map/ppermute | solution.py:81
  484.7 32.0 %copy-start.8 = (bf16[4,256,512]{2,1,0:T(8,128)(2,1)}, bf16[4,256,512]{2,1,0:T(8,128)(2,1)S(1)}, u32[]{:S(2)}) copy-start(bf16[4,256,512]{2,1,0:T(8,128)(2,1)S(1)} %constant_dynamic-update-slice_fusion.3) | copy-start | bytes 3145732
  494.9 13.6 %collective-permute-start.32 = (bf16[8,256,1]{2,1,0:T(8,128)(2,1)S(1)}, bf16[8,256,1]{2,1,0:T(8,128)(2,1)S(1)}, u32[]{:S(2)}, u32[]{:S(2)}) collective-permute-start(bf16[8,256,1]{2,1,0:T(8,128)(2,1)S(1)} %get-tuple-element.40), channel_id=1, source_target_pairs={{0,8},{8,16},{16,24},{1,9},{9,17},{17,25},{2,10},{10,18},{18,26},{... | collective-permute-start | bytes 12296 | tf_op jit(solution)/shard_map/ppermute | solution.py:17
  497.1 16.2 %collective-permute-start.33 = (bf16[8,256,1]{2,1,0:T(8,128)(2,1)S(1)}, bf16[8,256,1]{2,1,0:T(8,128)(2,1)S(1)}, u32[]{:S(2)}, u32[]{:S(2)}) collective-permute-start(bf16[8,256,1]{2,1,0:T(8,128)(2,1)S(1)} %get-tuple-element.41), channel_id=1, source_target_pairs={{8,0},{16,8},{24,16},{9,1},{17,9},{25,17},{10,2},{18,10},{26,18},{... | collective-permute-start | bytes 12296 | tf_op jit(solution)/shard_map/ppermute | solution.py:18
  513.5 3.2 collective-permute-start.34
  515.0 5.1 collective-permute-start.35
  (17 other events, 176.1 us)

commit v10 on v6

--- a/solution.py
+++ b/solution.py
@@ -140,7 +140,16 @@
     ).astype(jnp.float32)
     coeff_pad = stacked[1]
     solution = solution_in
-    residual = right_side - face_sum(stacked[0], coeff_pad)
+    levels = right_side.shape[0]
+    chunk = lax.axis_size("px")
+    if levels % chunk or levels == chunk:
+        chunk = levels
+    pieces = []
+    for start in range(0, levels, chunk):
+        low, high = max(start - 1, 0), min(start + chunk + 1, levels)
+        image = face_sum(stacked[0, low:high], coeff_pad[low:high])
+        pieces.append(right_side[start : start + chunk] - image[start - low : start - low + chunk])
+    residual = jnp.concatenate(pieces, 0)
     direction = image = None
     gamma_prev = curvature_prev = None
     for iteration in range(ITERS):

time: 546 us -> 580 us (1.062)
  other arithmetic: 121 us -> 167 us
  waiting for transfers between devices: 151 us -> 139 us
    sub x1 -> x3, other arithmetic: 11.2 us -> 42.3 us  [the longest x2 36.4 us: face_sum(): result = result + 0.5 * (coeff + other) * (values - neighbour)]
    ppermute x24, waiting for transfers between devices: 101 us -> 87 us  [exchange(): lax.ppermute(part, axis, [(i, (i + shift) % size) for i in range(size)])]
    convert_element_type x0 -> x1, other arithmetic: none -> 10.6 us  [precondition(): waiting[start:start + chunk].astype(jnp.bfloat16)]
    slice x0 -> x1, local copies, waits for them, and re-layouts: none -> 9.23 us  [shards(): image = face_sum(stacked[0, low:high], coeff_pad[low:high])]
    ppermute x24, starting transfers between devices: 56.7 us -> 49.1 us  [exchange(): lax.ppermute(part, axis, [(i, (i + shift) % size) for i in range(size)])]
    all_to_all x4, waiting for transfers between devices: 6 us -> 13.2 us  [precondition_lines(): incoming = lax.all_to_all(outgoing, 'py', 0, 0, tiled=True)]
  transfers between devices with their start and end apart: 44 -> 44, of which waited for: 25 -> 24; matrix products, arithmetic and copies ran while one was open for 20% -> 21% of each run, Pallas kernels for 0% -> 0%
where the time goes in v10:
time: 580 us; the launch traced here: 575 us
  other arithmetic  167 us (29%)
  waiting for transfers between devices  139 us (24%)
  starting transfers between devices  108 us (19%)
  matrix products  90.1 us (16%)
  local copies, waits for them, and re-layouts  40.9 us (7%)
  blocking collectives  21.6 us (4%)
  between operations  7.94 us (1%)
    ppermute x24, waiting for transfers between devices, exchange(): lax.ppermute(part, axis, [(i, (i + shift) % size) for i in range(size)])  87 us
    ppermute x24, starting transfers between devices, exchange(): lax.ppermute(part, axis, [(i, (i + shift) % size) for i in range(size)])  49.1 us
    dot_general x4, matrix products, precondition_lines(): jnp.einsum('yj,kji->kyi', eigenvectors, scaled, preferred_element_type=jn...  44.3 us
    sub x2, other arithmetic, face_sum(): result = result + 0.5 * (coeff + other) * (values - neighbour)  36.4 us
    reduce_sum x2, other arithmetic, shards(): jnp.sum(residual * precond)  27.6 us
    dot_general x4, matrix products, precondition_lines(): jnp.einsum('qkyi,qix->kyx', returned, eigenvectors.reshape(across, cols,...  23 us
    dot_general x4, matrix products, precondition_lines(): jnp.dot(lines.reshape(levels_here * rows, width), eigenvectors, preferred...  22.9 us
    mul x3, other arithmetic, face_sum(): vertical = 0.5 * (coeff[:-1] + coeff[1:]) * (values[:-1] - values[1:])  22.8 us
  transfers between devices with their start and end apart: 44, of which 24 were waited for; matrix products, arithmetic and copies ran while one was open for 21% of the time, Pallas kernels for 0%

profile of v10, /device:TPU:0, one launch (start us, length us, event | category | flops | bytes accessed | tf_op | source)
XLA Modules:
  0.0 574.6 jit_solution(3943647368762973436)
XLA Ops:
  6.1 14.4 %fusion.90 = bf16[1,8,256,512]{3,2,1,0:T(8,128)(2,1)S(1)} fusion(bf16[]{:T(256)} %bitcast.16, s32[8,256,512]{2,1,0:T(8,128)S(1)} %copy-done.21, bf16[]{:T(256)} %bitcast.15, bf16[]{:T(256)} %bitcast.14, bf16[]{:T(256)} %bitcast.13, bf16[]{:T(256)} %bitcast.12, bf16[]{:T(256)} %bitcast.11, bf16[]{:T(256)} %bitcast.10, bf16[]{:T(256)} %bitcast.9, ...), kind=kLoop, calls=%fused_computation.197 | loop fusion | flops 33554432 | bytes 6291488 | tf_op jit(solution)/shard_map/stack | solution.py:139
  39.0 13.4 %fusion.3 = f32[2,8,258,514]{3,2,1,0:T(8,128)} fusion(bf16[2,8,1,512]{3,2,1,0:T(2,128)(2,1)S(1)} %collective-permute-done.3, bf16[2,8,1,512]{3,2,1,0:T(2,128)(2,1)S(1)} %collective-permute-done, bf16[2,8,256,1]{3,2,1,0:T(8,128)(2,1)} %copy.80, bf16[1,8,256,512]{3,2,1,0:T(8,128)(2,1)} %copy-done.11, bf16[1,8,256,512]{3,2,1,0:T(8,128)(2,1)S(1)} %convert_bitcast_fusion, ...), kind=kLoop, calls=%fused_computation.14 | loop fusion | flops 33948672 | bytes 12730624 | tf_op jit(solution)/shard_map/convert_element_type | solution.py:140
  52.4 9.2 %slice_bitcast_fusion.2 = (f32[5,258,514]{2,1,0:T(8,128)}, f32[5,258,514]{2,1,0:T(8,128)}, f32[5,258,514]{2,1,0:T(8,128)S(1)}, f32[5,258,514]{2,1,0:T(8,128)}) fusion(f32[2,8,258,514]{3,2,1,0:T(8,128)} %fusion.3), kind=kLoop, calls=%fused_computation.76 | loop fusion | bytes 21217920 | tf_op jit(solution)/shard_map/slice | solution.py:150
  61.6 20.5 %slice_subtract_fusion.11 = (f32[5,256,512]{2,1,0:T(8,128)}, f32[5,256,512]{2,1,0:T(8,128)}, f32[5,256,512]{2,1,0:T(8,128)}, f32[5,256,512]{2,1,0:T(8,128)}, f32...) fusion(f32[5,258,514]{2,1,0:T(8,128)} %get-tuple-element.33, ...), kind=kLoop, calls=%fused_computation.121 | loop fusion | flops 4587520 | bytes 52428800 | tf_op jit(solution)/shard_map/sub | solution.py:53
  82.1 11.0 %fusion.79 = (f32[4,256,512]{2,1,0:T(8,128)}, f32[4,256,512]{2,1,0:T(8,128)}) fusion(f32[5,258,514]{2,1,0:T(8,128)} %get-tuple-element.33, f32[5,258,514]{2,1,0:T(8,128)} %get-tuple-element.32, f32[5,258,514]{2,1,0:T(8,128)S(1)} %get-tuple-element.34, f32[5,258,514]{2,1,0:T(8,128)} %get-tuple-element.35), kind=kLoop, calls=%fused_computation.174 | loop fusion | flops 4194304 | bytes 20971520 | tf_op jit(solution)/shard_map/mul | solution.py:54
  93.1 15.9 %slice_subtract_fusion.13 = (f32[5,256,512]{2,1,0:T(8,128)}, f32[5,256,512]{2,1,0:T(8,128)}, f32[5,256,512]{2,1,0:T(8,128)}, f32[5,256,512]{2,1,0:T(8,128)}, f32...) fusion(f32[5,258,514]{2,1,0:T(8,128)S(1)} %get-tuple-element.34, ...), kind=kLoop, calls=%fused_computation.128 | loop fusion | flops 4587520 | bytes 52428800 | tf_op jit(solution)/shard_map/sub | solution.py:53
  109.1 10.6 %fusion.109 = (bf16[4,256,512]{2,1,0:T(8,128)(2,1)S(1)}, f32[4,256,512]{2,1,0:T(8,128)S(1)}) fusion(f32[4,256,512]{2,1,0:T(8,128)} %get-tuple-element.131, f32[5,256,512]{2,1,0:T(8,128)} %get-tuple-element.56, f32[5,256,512]{2,1,0:T(8,128)} %get-tuple-element.128, f32[5,256,512]{2,1,0:T(8,128)} %get-tuple-element.125, f32[5,256,512]{2,1,0:T(8,128)} %get-tuple-element.57, ...), kind=kLoop, calls=%fused_computation.280 | loop fusion | flops 8388608 | bytes 28311552 | tf_op jit(solution)/shard_map/convert_element_type | solution.py:123
  126.3 5.9 %fusion.72 = f32[4,256,512]{2,1,0:T(8,128)S(1)} fusion(f32[4,256,512]{2,1,0:T(8,128)} %get-tuple-element.130, f32[5,256,512]{2,1,0:T(8,128)S(1)} %copy-done.14, f32[5,256,512]{2,1,0:T(8,128)} %get-tuple-element.123, f32[5,256,512]{2,1,0:T(8,128)S(1)} %copy-done.18, f32[5,256,512]{2,1,0:T(8,128)S(1)} %copy-done.15, f32[5,256,512]{2,1,0:T(8,128)S(1)} %copy-done.17, ...), kind=kLoop, calls=%fused_computation.159 | loop fusion | flops 7864320 | bytes 27262976 | tf_op jit(solution)/shard_map/sub | solution.py:151
  133.6 9.7 %collective-permute-done.5 = bf16[1,256,512]{2,1,0:T(8,128)(2,1)S(1)} collective-permute-done((bf16[1,256,512]{2,1,0:T(8,128)(2,1)}, bf16[1,256,512]{2,1,0:T(8,128)(2,1)S(1)}, u32[]{:S(2)}, u32[]{:S(2)}) %collective-permute-start.5) | collective-permute-done | bytes 262176 | tf_op jit(solution)/shard_map/ppermute | solution.py:76
  144.3 6.1 %collective-permute-start.10 = (bf16[1,256,512]{2,1,0:T(8,128)(2,1)}, bf16[1,256,512]{2,1,0:T(8,128)(2,1)S(1)}, u32[]{:S(2)}, u32[]{:S(2)}) collective-permute-start(bf16[1,256,512]{2,1,0:T(8,128)(2,1)} %get-tuple-element.90), channel_id=1, source_target_pairs={{0,8},{8,16},{16,24},{24,0},{1,9},{9,17},{17,25},{25,1},{2,10},{10... | collective-permute-start | bytes 786440 | tf_op jit(solution)/shard_map/ppermute | solution.py:76
  152.8 5.7 convolution_convert_fusion.7
  163.6 6.1 %collective-permute-done.11 = bf16[1,256,512]{2,1,0:T(8,128)(2,1)S(1)} collective-permute-done((bf16[1,256,512]{2,1,0:T(8,128)(2,1)S(1)}, bf16[1,256,512]{2,1,0:T(8,128)(2,1)S(1)}, u32[]{:S(2)}, u32[]{:S(2)}) %collective-permute-start.11) | collective-permute-done | bytes 262176 | tf_op jit(solution)/shard_map/ppermute | solution.py:76
  169.8 5.7 convolution_convert_fusion.5
  182.5 11.1 %fusion.60 = bf16[1,2048,256]{1,2,0:T(8,128)(2,1)S(1)} fusion(bf16[2048,2048]{1,0:T(8,128)(2,1)} %param.11, bf16[2048,256]{1,0:T(8,128)(2,1)S(1)} %bitcast.257, f32[]{:T(128)} %bitcast.27, f32[256]{0:T(256)S(1)} %dynamic_slice.114, f32[2048]{0:T(1024)S(1)} %copy-done.23), kind=kOutput, calls=%fused_computation.143 | convolution fusion | flops 4297588736 | bytes 10494980 | tf_op jit(solution)/shard_map/yj,kji->kyi/dot_general | solution.py:101
  201.4 11.0 %fusion.61 = bf16[1,2048,256]{1,2,0:T(8,128)(2,1)S(1)} fusion(bf16[2048,2048]{1,0:T(8,128)(2,1)} %param.11, bf16[2048,256]{1,0:T(8,128)(2,1)S(1)} %bitcast.259, f32[]{:T(128)} %bitcast.44, f32[256]{0:T(256)S(1)} %dynamic_slice.114, f32[2048]{0:T(1024)S(1)} %copy-done.23), kind=kOutput, calls=%fused_computation.144 | convolution fusion | flops 4297588736 | bytes 10494980 | tf_op jit(solution)/shard_map/yj,kji->kyi/dot_general | solution.py:101
  220.5 5.7 fusion.56
  233.3 5.8 %collective-permute-done.7 = bf16[1,256,512]{2,1,0:T(8,128)(2,1)} collective-permute-done((bf16[1,256,512]{2,1,0:T(8,128)(2,1)}, bf16[1,256,512]{2,1,0:T(8,128)(2,1)}, u32[]{:S(2)}, u32[]{:S(2)}) %collective-permute-start.7) | collective-permute-done | bytes 262176 | tf_op jit(solution)/shard_map/ppermute | solution.py:76
  240.0 5.9 %fusion.57 = bf16[256,2048]{1,0:T(8,128)(2,1)S(1)} fusion(bf16[8,256,2048]{2,1,0:T(8,128)(2,1)} %bitcast.265, bf16[8,1,256,256]{3,2,1,0:T(8,128)(2,1)S(1)} %all-to-all-done.3), kind=kOutput, calls=%fused_computation.132 | convolution fusion | flops 2148007936 | bytes 10485760 | tf_op jit(solution)/shard_map/qkyi,qix->kyx/dot_general | solution.py:106
  252.1 7.6 %collective-permute-start.15 = (bf16[1,256,512]{2,1,0:T(8,128)(2,1)S(1)}, bf16[1,256,512]{2,1,0:T(8,128)(2,1)S(1)}, u32[]{:S(2)}, u32[]{:S(2)}) collective-permute-start(bf16[1,256,512]{2,1,0:T(8,128)(2,1)S(1)} %get-tuple-element.85), channel_id=1, source_target_pairs={{0,24},{8,0},{16,8},{24,16},{1,25},{9,1},{17,9},{25,17},{2,26},{10... | collective-permute-start | bytes 786440 | tf_op jit(solution)/shard_map/ppermute | solution.py:76
  259.8 12.6 %collective-permute-done.14 = bf16[1,256,512]{2,1,0:T(8,128)(2,1)S(1)} collective-permute-done((bf16[1,256,512]{2,1,0:T(8,128)(2,1)S(1)}, bf16[1,256,512]{2,1,0:T(8,128)(2,1)S(1)}, u32[]{:S(2)}, u32[]{:S(2)}) %collective-permute-start.14) | collective-permute-done | bytes 262176 | tf_op jit(solution)/shard_map/ppermute | solution.py:76
  272.4 5.5 collective-permute-done.15
  285.6 6.5 %collective-permute-done.17 = bf16[8,256,1]{2,1,0:T(8,128)(2,1)S(1)} collective-permute-done((bf16[8,256,1]{2,1,0:T(8,128)(2,1)S(1)}, bf16[8,256,1]{2,1,0:T(8,128)(2,1)S(1)}, u32[]{:S(2)}, u32[]{:S(2)}) %collective-permute-start.17) | collective-permute-done | bytes 4128 | tf_op jit(solution)/shard_map/ppermute | solution.py:17
  296.3 5.4 fusion.48
  301.7 5.9 %fusion.40 = f32[7,256,512]{2,1,0:T(8,128)} fusion(f32[8,258,514]{2,1,0:T(8,128)S(1)} %fusion.48, f32[8,258,514]{2,1,0:T(8,128)S(1)} %slice_bitcast_fusion), kind=kLoop, calls=%fused_computation.72 | loop fusion | flops 3670016 | bytes 18350080 | tf_op jit(solution)/shard_map/mul | solution.py:54
  307.6 13.3 %fusion.12 = (f32[]{:T(128)}, f32[]{:T(128)}, f32[8,256,512]{2,1,0:T(8,128)}) fusion(bf16[4,256,512]{2,1,0:T(8,128)(2,1)} %copy-done.4, bf16[4,256,512]{2,1,0:T(8,128)(2,1)} %copy-done.2, f32[4,256,512]{2,1,0:T(8,128)} %copy-done.10, f32[4,256,512]{2,1,0:T(8,128)} %copy-done.9, f32[7,256,512]{2,1,0:T(8,128)} %fusion.40, f32[8,258,514]{2,1,0:T(8,128)S(1)} %fusion.48, ...), kind=kLoop, calls=%fused_computation.26 | loop fusion | flops 29360128 | bytes 56098824 | tf_op jit(solution)/shard_map/reduce_sum | solution.py:159
  322.3 10.6 %all_to_all.52 = f32[32,1,2]{2,1,0:T(1,128)S(1)} all-to-all(f32[32,1,2]{2,1,0:T(1,128)S(1)} %broadcast_in_dim.93), channel_id=1, replica_groups=mesh['px'=4,'py'=8] {'px','py'}, dimensions={0} | all-to-all | bytes 512 | tf_op jit(solution)/shard_map/all_to_all | solution.py:41
  334.8 4.5 multiply_subtract_fusion.1
  343.5 7.3 %collective-permute-done.20 = bf16[1,256,512]{2,1,0:T(8,128)(2,1)S(1)} collective-permute-done((bf16[1,256,512]{2,1,0:T(8,128)(2,1)S(1)}, bf16[1,256,512]{2,1,0:T(8,128)(2,1)S(1)}, u32[]{:S(2)}, u32[]{:S(2)}) %collective-permute-start.20) | collective-permute-done | bytes 262176 | tf_op jit(solution)/shard_map/ppermute | solution.py:76
  350.8 10.2 %collective-permute-done.21 = bf16[1,256,512]{2,1,0:T(8,128)(2,1)S(1)} collective-permute-done((bf16[1,256,512]{2,1,0:T(8,128)(2,1)S(1)}, bf16[1,256,512]{2,1,0:T(8,128)(2,1)S(1)}, u32[]{:S(2)}, u32[]{:S(2)}) %collective-permute-start.21) | collective-permute-done | bytes 262176 | tf_op jit(solution)/shard_map/ppermute | solution.py:76
  362.2 5.2 collective-permute-start.26
  370.2 5.7 convolution_convert_fusion.3
  384.1 5.7 convolution_convert_fusion.1
  390.9 5.0 all-to-all-done.5
  399.4 11.1 %fusion.62 = bf16[1,2048,256]{1,2,0:T(8,128)(2,1)S(1)} fusion(bf16[2048,2048]{1,0:T(8,128)(2,1)} %param.11, bf16[2048,256]{1,0:T(8,128)(2,1)S(1)} %bitcast.256, f32[]{:T(128)} %bitcast.27, f32[256]{0:T(256)S(1)} %dynamic_slice.114, f32[2048]{0:T(1024)S(1)} %copy-done.23), kind=kOutput, calls=%fused_computation.145 | convolution fusion | flops 4297588736 | bytes 10494980 | tf_op jit(solution)/shard_map/yj,kji->kyi/dot_general | solution.py:101
  418.5 11.0 %fusion.63 = bf16[1,2048,256]{1,2,0:T(8,128)(2,1)S(1)} fusion(bf16[2048,2048]{1,0:T(8,128)(2,1)} %param.11, bf16[2048,256]{1,0:T(8,128)(2,1)S(1)} %bitcast.258, f32[]{:T(128)} %bitcast.44, f32[256]{0:T(256)S(1)} %dynamic_slice.114, f32[2048]{0:T(1024)S(1)} %copy-done.23), kind=kOutput, calls=%fused_computation.146 | convolution fusion | flops 4297588736 | bytes 10494980 | tf_op jit(solution)/shard_map/yj,kji->kyi/dot_general | solution.py:101
  437.4 5.7 fusion.58
  447.5 5.3 all-to-all-done.8
  452.7 5.7 fusion.59
  465.7 5.6 collective-permute-done.29
  471.2 16.3 %collective-permute-done.30 = bf16[1,256,512]{2,1,0:T(8,128)(2,1)S(1)} collective-permute-done((bf16[1,256,512]{2,1,0:T(8,128)(2,1)S(1)}, bf16[1,256,512]{2,1,0:T(8,128)(2,1)S(1)}, u32[]{:S(2)}, u32[]{:S(2)}) %collective-permute-start.30) | collective-permute-done | bytes 262176 | tf_op jit(solution)/shard_map/ppermute | solution.py:76
  491.1 8.3 %collective-permute-start.33 = (bf16[8,256,1]{2,1,0:T(8,128)(2,1)S(1)}, bf16[8,256,1]{2,1,0:T(8,128)(2,1)S(1)}, u32[]{:S(2)}, u32[]{:S(2)}) collective-permute-start(bf16[8,256,1]{2,1,0:T(8,128)(2,1)S(1)} %get-tuple-element.60), channel_id=1, source_target_pairs={{0,8},{8,16},{16,24},{1,9},{9,17},{17,25},{2,10},{10,18},{18,26},{... | collective-permute-start | bytes 12296 | tf_op jit(solution)/shard_map/ppermute | solution.py:17
  501.1 9.2 %collective-permute-done.33 = bf16[8,256,1]{2,1,0:T(8,128)(2,1)S(1)} collective-permute-done((bf16[8,256,1]{2,1,0:T(8,128)(2,1)S(1)}, bf16[8,256,1]{2,1,0:T(8,128)(2,1)S(1)}, u32[]{:S(2)}, u32[]{:S(2)}) %collective-permute-start.33) | collective-permute-done | bytes 4128 | tf_op jit(solution)/shard_map/ppermute | solution.py:17
  510.4 4.9 collective-permute-done.34
  515.3 6.4 %fusion.51 = f32[8,258,514]{2,1,0:T(8,128)S(1)} fusion(bf16[8,1,512]{2,1,0:T(2,128)(2,1)S(1)} %collective-permute-done.35, bf16[8,1,512]{2,1,0:T(2,128)(2,1)S(1)} %collective-permute-done.32, bf16[8,256,1]{2,1,0:T(8,128)(2,1)S(1)} %collective-permute-done.34, bf16[4,256,512]{2,1,0:T(8,128)(2,1)S(1)} %constant_dynamic-update-slice_fusion.23, ...), kind=kLoop, calls=%fused_computation.116 | loop fusion | flops 16974336 | bytes 6365312 | tf_op jit(solution)/shard_map/convert_element_type | solution.py:130
  521.7 5.9 %fusion.39 = f32[7,256,512]{2,1,0:T(8,128)} fusion(f32[8,258,514]{2,1,0:T(8,128)S(1)} %fusion.51, f32[8,258,514]{2,1,0:T(8,128)S(1)} %bitcast.253), kind=kLoop, calls=%fused_computation.70 | loop fusion | flops 3670016 | bytes 18350080 | tf_op jit(solution)/shard_map/mul | solution.py:54
  527.6 14.3 %fusion.9 = (f32[]{:T(128)}, f32[]{:T(128)}, f32[]{:T(128)}, f32[]{:T(128)}, f32[8,256,512]{2,1,0:T(8,128)}) fusion(f32[8,256,512]{2,1,0:T(8,128)} %copy-done.5, bf16[4,256,512]{2,1,0:T(8,128)(2,1)} %copy-done.7, bf16[4,256,512]{2,1,0:T(8,128)(2,1)} %copy-done.8, f32[8,256,512]{2,1,0:T(8,128)} %get-tuple-element.29, bf16[4,256,512]{2,1,0:T(8,128)(2,1)} %copy-done.4, ...), kind=kLoop, calls=%fused_computation.23 | loop fusion | flops 34603004 | bytes 62390288 | tf_op jit(solution)/shard_map/reduce_sum | solution.py:166
  544.6 10.9 %all_to_all.53 = f32[32,1,4]{2,1,0:T(1,128)S(1)} all-to-all(f32[32,1,4]{2,1,0:T(1,128)S(1)} %broadcast_in_dim.94), channel_id=1, replica_groups=mesh['px'=4,'py'=8] {'px','py'}, dimensions={0} | all-to-all | bytes 1024 | tf_op jit(solution)/shard_map/all_to_all | solution.py:41
  560.7 7.2 %fusion.15 = (f32[8,256,512]{2,1,0:T(8,128)}, f32[8,256,512]{2,1,0:T(8,128)}) fusion(f32[8,256,512]{2,1,0:T(8,128)} %param.8, f32[]{:T(128)S(6)} %div.27, f32[]{:T(128)S(6)} %div.23, bf16[4,256,512]{2,1,0:T(8,128)(2,1)} %copy-done.4, bf16[4,256,512]{2,1,0:T(8,128)(2,1)} %copy-done.2, f32[]{:T(128)S(6)} %div.26, bf16[4,256,512]{2,1,0:T(8,128)(2,1)} %copy-done.7, ...), kind=kLoop, calls=%fused_computation.29 | loop fusion | flops 10485760 | bytes 16777228 | tf_op jit(solution)/shard_map/add | solution.py:179
  (210 shorter events, 153.9 us)
Async XLA Ops:
  20.5 18.4 %collective-permute-start = (bf16[2,8,1,512]{3,2,1,0:T(2,128)(2,1)S(1)}, bf16[2,8,1,512]{3,2,1,0:T(2,128)(2,1)S(1)}, u32[]{:S(2)}, u32[]{:S(2)}) collective-permute-start(bf16[2,8,1,512]{3,2,1,0:T(2,128)(2,1)S(1)} %get-tuple-element.38), channel_id=1, source_target_pairs={{0,1},{1,2},{2,3},{3,4},{4,5},{5,6},{6,7},{8,9},{9,10},{10,11},{11... | collective-permute-start | bytes 49160 | tf_op jit(solution)/shard_map/ppermute | solution.py:17
  22.9 16.0 %collective-permute-start.3 = (bf16[2,8,1,512]{3,2,1,0:T(2,128)(2,1)S(1)}, bf16[2,8,1,512]{3,2,1,0:T(2,128)(2,1)S(1)}, u32[]{:S(2)}, u32[]{:S(2)}) collective-permute-start(bf16[2,8,1,512]{3,2,1,0:T(2,128)(2,1)S(1)} %get-tuple-element.39), channel_id=1, source_target_pairs={{1,0},{2,1},{3,2},{4,3},{5,4},{6,5},{7,6},{9,8},{10,9},{11,10},{12... | collective-permute-start | bytes 49160 | tf_op jit(solution)/shard_map/ppermute | solution.py:17
  27.3 6.9 %collective-permute-start.1 = (bf16[2,8,256,1]{2,1,3,0:T(8,128)(2,1)S(1)}, bf16[2,8,256,1]{2,1,3,0:T(8,128)(2,1)S(1)}, u32[]{:S(2)}, u32[]{:S(2)}) collective-permute-start(bf16[2,8,256,1]{2,1,3,0:T(8,128)(2,1)S(1)} %copy.77), channel_id=1, source_target_pairs={{0,8},{8,16},{16,24},{1,9},{9,17},{17,25},{2,10},{10,18},{18,26},{... | collective-permute-start | bytes 24584 | tf_op jit(solution)/shard_map/ppermute | solution.py:17
  32.0 5.5 collective-permute-start.2
  120.7 12.8 %collective-permute-start.4 = (bf16[1,256,512]{2,1,0:T(8,128)(2,1)}, bf16[1,256,512]{2,1,0:T(8,128)(2,1)S(1)}, u32[]{:S(2)}, u32[]{:S(2)}) collective-permute-start(bf16[1,256,512]{2,1,0:T(8,128)(2,1)} %get-tuple-element.94), channel_id=1, source_target_pairs={{0,8},{8,16},{16,24},{24,0},{1,9},{9,17},{17,25},{25,1},{2,10},{10... | collective-permute-start | bytes 786440 | tf_op jit(solution)/shard_map/ppermute | solution.py:76
  122.3 20.9 %collective-permute-start.5 = (bf16[1,256,512]{2,1,0:T(8,128)(2,1)}, bf16[1,256,512]{2,1,0:T(8,128)(2,1)S(1)}, u32[]{:S(2)}, u32[]{:S(2)}) collective-permute-start(bf16[1,256,512]{2,1,0:T(8,128)(2,1)} %get-tuple-element.93), channel_id=1, source_target_pairs={{0,16},{8,24},{16,0},{24,8},{1,17},{9,25},{17,1},{25,9},{2,18},{10... | collective-permute-start | bytes 786440 | tf_op jit(solution)/shard_map/ppermute | solution.py:76
  123.3 19.9 %collective-permute-start.6 = (bf16[1,256,512]{2,1,0:T(8,128)(2,1)S(1)}, bf16[1,256,512]{2,1,0:T(8,128)(2,1)S(1)}, u32[]{:S(2)}, u32[]{:S(2)}) collective-permute-start(bf16[1,256,512]{2,1,0:T(8,128)(2,1)S(1)} %get-tuple-element.92), channel_id=1, source_target_pairs={{0,24},{8,0},{16,8},{24,16},{1,25},{9,1},{17,9},{25,17},{2,26},{10... | collective-permute-start | bytes 786440 | tf_op jit(solution)/shard_map/ppermute | solution.py:76
  144.3 19.3 %collective-permute-start.10 = (bf16[1,256,512]{2,1,0:T(8,128)(2,1)}, bf16[1,256,512]{2,1,0:T(8,128)(2,1)S(1)}, u32[]{:S(2)}, u32[]{:S(2)}) collective-permute-start(bf16[1,256,512]{2,1,0:T(8,128)(2,1)} %get-tuple-element.90), channel_id=1, source_target_pairs={{0,8},{8,16},{16,24},{24,0},{1,9},{9,17},{17,25},{25,1},{2,10},{10... | collective-permute-start | bytes 786440 | tf_op jit(solution)/shard_map/ppermute | solution.py:76
  150.4 19.3 %collective-permute-start.11 = (bf16[1,256,512]{2,1,0:T(8,128)(2,1)S(1)}, bf16[1,256,512]{2,1,0:T(8,128)(2,1)S(1)}, u32[]{:S(2)}, u32[]{:S(2)}) collective-permute-start(bf16[1,256,512]{2,1,0:T(8,128)(2,1)S(1)} %get-tuple-element.89), channel_id=1, source_target_pairs={{0,16},{8,24},{16,0},{24,8},{1,17},{9,25},{17,1},{25,9},{2,18},{10... | collective-permute-start | bytes 786440 | tf_op jit(solution)/shard_map/ppermute | solution.py:76
  152.1 17.6 %collective-permute-start.12 = (bf16[1,256,512]{2,1,0:T(8,128)(2,1)S(1)}, bf16[1,256,512]{2,1,0:T(8,128)(2,1)S(1)}, u32[]{:S(2)}, u32[]{:S(2)}) collective-permute-start(bf16[1,256,512]{2,1,0:T(8,128)(2,1)S(1)} %get-tuple-element.88), channel_id=1, source_target_pairs={{0,24},{8,0},{16,8},{24,16},{1,25},{9,1},{17,9},{25,17},{2,26},{10... | collective-permute-start | bytes 786440 | tf_op jit(solution)/shard_map/ppermute | solution.py:76
  159.6 19.4 %all-to-all-start = ((bf16[8,256,256]{2,1,0:T(8,128)(2,1)}), bf16[8,256,256]{2,1,0:T(8,128)(2,1)S(1)}, u32[]{:S(2)}, u32[]{:S(2)}) async-start(bf16[8,256,256]{2,1,0:T(8,128)(2,1)} %bitcast.251), calls=%async_computation | async-start | bytes 2097152 | tf_op jit(solution)/shard_map/all_to_all | solution.py:91
  178.9 18.9 %all-to-all-start.2 = ((bf16[8,256,256]{2,1,0:T(8,128)(2,1)}), bf16[8,256,256]{2,1,0:T(8,128)(2,1)S(1)}, u32[]{:S(2)}, u32[]{:S(2)}) async-start(bf16[8,256,256]{2,1,0:T(8,128)(2,1)} %bitcast.249), calls=%async_computation.2 | async-start | bytes 2097152 | tf_op jit(solution)/shard_map/all_to_all | solution.py:91
  197.8 18.9 %all-to-all-start.1 = ((bf16[8,1,256,256]{3,2,1,0:T(8,128)(2,1)}), bf16[8,1,256,256]{3,2,1,0:T(8,128)(2,1)S(1)}, u32[]{:S(2)}, u32[]{:S(2)}) async-start(bf16[8,1,256,256]{3,2,1,0:T(8,128)(2,1)} %bitcast.31), calls=%async_computation.1 | async-start | bytes 2097152 | tf_op jit(solution)/shard_map/all_to_all | solution.py:105
  216.7 23.3 %all-to-all-start.3 = ((bf16[8,1,256,256]{3,2,1,0:T(8,128)(2,1)}), bf16[8,1,256,256]{3,2,1,0:T(8,128)(2,1)S(1)}, u32[]{:S(2)}, u32[]{:S(2)}) async-start(bf16[8,1,256,256]{3,2,1,0:T(8,128)(2,1)} %bitcast.48), calls=%async_computation.3 | async-start | bytes 2097152 | tf_op jit(solution)/shard_map/all_to_all | solution.py:105
  227.1 12.0 %collective-permute-start.7 = (bf16[1,256,512]{2,1,0:T(8,128)(2,1)}, bf16[1,256,512]{2,1,0:T(8,128)(2,1)}, u32[]{:S(2)}, u32[]{:S(2)}) collective-permute-start(bf16[1,256,512]{2,1,0:T(8,128)(2,1)} %get-tuple-element.84), channel_id=1, source_target_pairs={{0,8},{8,16},{16,24},{24,0},{1,9},{9,17},{17,25},{25,1},{2,10},{10... | collective-permute-start | bytes 786440 | tf_op jit(solution)/shard_map/ppermute | solution.py:76
  230.8 19.2 %collective-permute-start.8 = (bf16[1,256,512]{2,1,0:T(8,128)(2,1)}, bf16[1,256,512]{2,1,0:T(8,128)(2,1)}, u32[]{:S(2)}, u32[]{:S(2)}) collective-permute-start(bf16[1,256,512]{2,1,0:T(8,128)(2,1)} %get-tuple-element.83), channel_id=1, source_target_pairs={{0,16},{8,24},{16,0},{24,8},{1,17},{9,25},{17,1},{25,9},{2,18},{10... | collective-permute-start | bytes 786440 | tf_op jit(solution)/shard_map/ppermute | solution.py:76
  232.0 19.1 %collective-permute-start.9 = (bf16[1,256,512]{2,1,0:T(8,128)(2,1)S(1)}, bf16[1,256,512]{2,1,0:T(8,128)(2,1)}, u32[]{:S(2)}, u32[]{:S(2)}) collective-permute-start(bf16[1,256,512]{2,1,0:T(8,128)(2,1)S(1)} %get-tuple-element.82), channel_id=1, source_target_pairs={{0,24},{8,0},{16,8},{24,16},{1,25},{9,1},{17,9},{25,17},{2,26},{10... | collective-permute-start | bytes 786440 | tf_op jit(solution)/shard_map/ppermute | solution.py:76
  240.0 45.2 %slice-start.2 = ((s8[10813440]{0:T(1024)(128)(4,1)}), s8[4194304]{0:T(1024)(128)(4,1)S(1)}, s32[]{:S(2)}) async-start(s8[10813440]{0:T(1024)(128)(4,1)} %bitcast.254), calls=%async_computation.12 | async-start | bytes 8388608
  240.0 45.2 %slice-start.3 = ((s8[10813440]{0:T(1024)(128)(4,1)}), s8[4194304]{0:T(1024)(128)(4,1)S(1)}, s32[]{:S(2)}) async-start(s8[10813440]{0:T(1024)(128)(4,1)} %bitcast.254), calls=%async_computation.13 | async-start | bytes 8388608
  246.0 13.7 %collective-permute-start.13 = (bf16[1,256,512]{2,1,0:T(8,128)(2,1)S(1)}, bf16[1,256,512]{2,1,0:T(8,128)(2,1)S(1)}, u32[]{:S(2)}, u32[]{:S(2)}) collective-permute-start(bf16[1,256,512]{2,1,0:T(8,128)(2,1)S(1)} %get-tuple-element.87), channel_id=1, source_target_pairs={{0,8},{8,16},{16,24},{24,0},{1,9},{9,17},{17,25},{25,1},{2,10},{10... | collective-permute-start | bytes 786440 | tf_op jit(solution)/shard_map/ppermute | solution.py:76
  251.0 21.4 %collective-permute-start.14 = (bf16[1,256,512]{2,1,0:T(8,128)(2,1)S(1)}, bf16[1,256,512]{2,1,0:T(8,128)(2,1)S(1)}, u32[]{:S(2)}, u32[]{:S(2)}) collective-permute-start(bf16[1,256,512]{2,1,0:T(8,128)(2,1)S(1)} %get-tuple-element.86), channel_id=1, source_target_pairs={{0,16},{8,24},{16,0},{24,8},{1,17},{9,25},{17,1},{25,9},{2,18},{10... | collective-permute-start | bytes 786440 | tf_op jit(solution)/shard_map/ppermute | solution.py:76
  252.0 33.2 %slice-start.4 = ((s8[10813440]{0:T(1024)(128)(4,1)}), s8[2424832]{0:T(1024)(128)(4,1)S(1)}, s32[]{:S(2)}) async-start(s8[10813440]{0:T(1024)(128)(4,1)} %bitcast.254), calls=%async_computation.14 | async-start | bytes 4849664
  252.1 25.9 %collective-permute-start.15 = (bf16[1,256,512]{2,1,0:T(8,128)(2,1)S(1)}, bf16[1,256,512]{2,1,0:T(8,128)(2,1)S(1)}, u32[]{:S(2)}, u32[]{:S(2)}) collective-permute-start(bf16[1,256,512]{2,1,0:T(8,128)(2,1)S(1)} %get-tuple-element.85), channel_id=1, source_target_pairs={{0,24},{8,0},{16,8},{24,16},{1,25},{9,1},{17,9},{25,17},{2,26},{10... | collective-permute-start | bytes 786440 | tf_op jit(solution)/shard_map/ppermute | solution.py:76
  278.2 13.9 %collective-permute-start.17 = (bf16[8,256,1]{2,1,0:T(8,128)(2,1)S(1)}, bf16[8,256,1]{2,1,0:T(8,128)(2,1)S(1)}, u32[]{:S(2)}, u32[]{:S(2)}) collective-permute-start(bf16[8,256,1]{2,1,0:T(8,128)(2,1)S(1)} %get-tuple-element.64), channel_id=1, source_target_pairs={{0,8},{8,16},{16,24},{1,9},{9,17},{17,25},{2,10},{10,18},{18,26},{... | collective-permute-start | bytes 12296 | tf_op jit(solution)/shard_map/ppermute | solution.py:17
  280.8 15.5 %collective-permute-start.18 = (bf16[8,256,1]{2,1,0:T(8,128)(2,1)S(1)}, bf16[8,256,1]{2,1,0:T(8,128)(2,1)S(1)}, u32[]{:S(2)}, u32[]{:S(2)}) collective-permute-start(bf16[8,256,1]{2,1,0:T(8,128)(2,1)S(1)} %get-tuple-element.65), channel_id=1, source_target_pairs={{8,0},{16,8},{24,16},{9,1},{17,9},{25,17},{10,2},{18,10},{26,18},{... | collective-permute-start | bytes 12296 | tf_op jit(solution)/shard_map/ppermute | solution.py:17
  282.1 14.2 %collective-permute-start.16 = (bf16[8,1,512]{2,1,0:T(2,128)(2,1)S(1)}, bf16[8,1,512]{2,1,0:T(2,128)(2,1)S(1)}, u32[]{:S(2)}, u32[]{:S(2)}) collective-permute-start(bf16[8,1,512]{2,1,0:T(2,128)(2,1)S(1)} %get-tuple-element.66), channel_id=1, source_target_pairs={{0,1},{1,2},{2,3},{3,4},{4,5},{5,6},{6,7},{8,9},{9,10},{10,11},{11... | collective-permute-start | bytes 24584 | tf_op jit(solution)/shard_map/ppermute | solution.py:17
  283.8 12.5 %collective-permute-start.19 = (bf16[8,1,512]{2,1,0:T(2,128)(2,1)S(1)}, bf16[8,1,512]{2,1,0:T(2,128)(2,1)S(1)}, u32[]{:S(2)}, u32[]{:S(2)}) collective-permute-start(bf16[8,1,512]{2,1,0:T(2,128)(2,1)S(1)} %get-tuple-element.67), channel_id=1, source_target_pairs={{1,0},{2,1},{3,2},{4,3},{5,4},{6,5},{7,6},{9,8},{10,9},{11,10},{12... | collective-permute-start | bytes 24584 | tf_op jit(solution)/shard_map/ppermute | solution.py:17
  339.7 11.1 %collective-permute-start.20 = (bf16[1,256,512]{2,1,0:T(8,128)(2,1)S(1)}, bf16[1,256,512]{2,1,0:T(8,128)(2,1)S(1)}, u32[]{:S(2)}, u32[]{:S(2)}) collective-permute-start(bf16[1,256,512]{2,1,0:T(8,128)(2,1)S(1)} %get-tuple-element.80), channel_id=1, source_target_pairs={{0,8},{8,16},{16,24},{24,0},{1,9},{9,17},{17,25},{25,1},{2,10},{10... | collective-permute-start | bytes 786440 | tf_op jit(solution)/shard_map/ppermute | solution.py:76
  340.3 20.7 %collective-permute-start.21 = (bf16[1,256,512]{2,1,0:T(8,128)(2,1)S(1)}, bf16[1,256,512]{2,1,0:T(8,128)(2,1)S(1)}, u32[]{:S(2)}, u32[]{:S(2)}) collective-permute-start(bf16[1,256,512]{2,1,0:T(8,128)(2,1)S(1)} %get-tuple-element.79), channel_id=1, source_target_pairs={{0,16},{8,24},{16,0},{24,8},{1,17},{9,25},{17,1},{25,9},{2,18},{10... | collective-permute-start | bytes 786440 | tf_op jit(solution)/shard_map/ppermute | solution.py:76
  340.8 20.2 %collective-permute-start.22 = (bf16[1,256,512]{2,1,0:T(8,128)(2,1)S(1)}, bf16[1,256,512]{2,1,0:T(8,128)(2,1)S(1)}, u32[]{:S(2)}, u32[]{:S(2)}) collective-permute-start(bf16[1,256,512]{2,1,0:T(8,128)(2,1)S(1)} %get-tuple-element.78), channel_id=1, source_target_pairs={{0,24},{8,0},{16,8},{24,16},{1,25},{9,1},{17,9},{25,17},{2,26},{10... | collective-permute-start | bytes 786440 | tf_op jit(solution)/shard_map/ppermute | solution.py:76
  362.2 18.3 %collective-permute-start.26 = (bf16[1,256,512]{2,1,0:T(8,128)(2,1)}, bf16[1,256,512]{2,1,0:T(8,128)(2,1)S(1)}, u32[]{:S(2)}, u32[]{:S(2)}) collective-permute-start(bf16[1,256,512]{2,1,0:T(8,128)(2,1)} %get-tuple-element.76), channel_id=1, source_target_pairs={{0,8},{8,16},{16,24},{24,0},{1,9},{9,17},{17,25},{25,1},{2,10},{10... | collective-permute-start | bytes 786440 | tf_op jit(solution)/shard_map/ppermute | solution.py:76
  367.4 16.6 %collective-permute-start.27 = (bf16[1,256,512]{2,1,0:T(8,128)(2,1)S(1)}, bf16[1,256,512]{2,1,0:T(8,128)(2,1)S(1)}, u32[]{:S(2)}, u32[]{:S(2)}) collective-permute-start(bf16[1,256,512]{2,1,0:T(8,128)(2,1)S(1)} %get-tuple-element.75), channel_id=1, source_target_pairs={{0,16},{8,24},{16,0},{24,8},{1,17},{9,25},{17,1},{25,9},{2,18},{10... | collective-permute-start | bytes 786440 | tf_op jit(solution)/shard_map/ppermute | solution.py:76
  367.7 16.3 %collective-permute-start.28 = (bf16[1,256,512]{2,1,0:T(8,128)(2,1)S(1)}, bf16[1,256,512]{2,1,0:T(8,128)(2,1)S(1)}, u32[]{:S(2)}, u32[]{:S(2)}) collective-permute-start(bf16[1,256,512]{2,1,0:T(8,128)(2,1)S(1)} %get-tuple-element.74), channel_id=1, source_target_pairs={{0,24},{8,0},{16,8},{24,16},{1,25},{9,1},{17,9},{25,17},{2,26},{10... | collective-permute-start | bytes 786440 | tf_op jit(solution)/shard_map/ppermute | solution.py:76
  377.0 18.9 %all-to-all-start.5 = ((bf16[8,256,256]{2,1,0:T(8,128)(2,1)}), bf16[8,256,256]{2,1,0:T(8,128)(2,1)S(1)}, u32[]{:S(2)}, u32[]{:S(2)}) async-start(bf16[8,256,256]{2,1,0:T(8,128)(2,1)} %bitcast.247), calls=%async_computation.5 | async-start | bytes 2097152 | tf_op jit(solution)/shard_map/all_to_all | solution.py:91
  395.9 18.9 %all-to-all-start.7 = ((bf16[8,256,256]{2,1,0:T(8,128)(2,1)}), bf16[8,256,256]{2,1,0:T(8,128)(2,1)S(1)}, u32[]{:S(2)}, u32[]{:S(2)}) async-start(bf16[8,256,256]{2,1,0:T(8,128)(2,1)} %bitcast.245), calls=%async_computation.7 | async-start | bytes 2097152 | tf_op jit(solution)/shard_map/all_to_all | solution.py:91
  414.8 19.1 %all-to-all-start.6 = ((bf16[8,1,256,256]{3,2,1,0:T(8,128)(2,1)}), bf16[8,1,256,256]{3,2,1,0:T(8,128)(2,1)S(1)}, u32[]{:S(2)}, u32[]{:S(2)}) async-start(bf16[8,1,256,256]{3,2,1,0:T(8,128)(2,1)} %bitcast.68), calls=%async_computation.6 | async-start | bytes 2097152 | tf_op jit(solution)/shard_map/all_to_all | solution.py:105
  433.8 18.9 %all-to-all-start.8 = ((bf16[8,1,256,256]{3,2,1,0:T(8,128)(2,1)}), bf16[8,1,256,256]{3,2,1,0:T(8,128)(2,1)S(1)}, u32[]{:S(2)}, u32[]{:S(2)}) async-start(bf16[8,1,256,256]{3,2,1,0:T(8,128)(2,1)} %bitcast.83), calls=%async_computation.8 | async-start | bytes 2097152 | tf_op jit(solution)/shard_map/all_to_all | solution.py:105
  443.2 19.6 %collective-permute-start.23 = (bf16[1,256,512]{2,1,0:T(8,128)(2,1)S(1)}, bf16[1,256,512]{2,1,0:T(8,128)(2,1)}, u32[]{:S(2)}, u32[]{:S(2)}) collective-permute-start(bf16[1,256,512]{2,1,0:T(8,128)(2,1)S(1)} %get-tuple-element.70), channel_id=1, source_target_pairs={{0,8},{8,16},{16,24},{24,0},{1,9},{9,17},{17,25},{25,1},{2,10},{10... | collective-permute-start | bytes 786440 | tf_op jit(solution)/shard_map/ppermute | solution.py:76
  444.3 21.3 %collective-permute-start.24 = (bf16[1,256,512]{2,1,0:T(8,128)(2,1)S(1)}, bf16[1,256,512]{2,1,0:T(8,128)(2,1)S(1)}, u32[]{:S(2)}, u32[]{:S(2)}) collective-permute-start(bf16[1,256,512]{2,1,0:T(8,128)(2,1)S(1)} %get-tuple-element.69), channel_id=1, source_target_pairs={{0,16},{8,24},{16,0},{24,8},{1,17},{9,25},{17,1},{25,9},{2,18},{10... | collective-permute-start | bytes 786440 | tf_op jit(solution)/shard_map/ppermute | solution.py:76
  447.3 18.3 %collective-permute-start.25 = (bf16[1,256,512]{2,1,0:T(8,128)(2,1)S(1)}, bf16[1,256,512]{2,1,0:T(8,128)(2,1)S(1)}, u32[]{:S(2)}, u32[]{:S(2)}) collective-permute-start(bf16[1,256,512]{2,1,0:T(8,128)(2,1)S(1)} %get-tuple-element.68), channel_id=1, source_target_pairs={{0,24},{8,0},{16,8},{24,16},{1,25},{9,1},{17,9},{25,17},{2,26},{10... | collective-permute-start | bytes 786440 | tf_op jit(solution)/shard_map/ppermute | solution.py:76
  458.6 12.7 %collective-permute-start.29 = (bf16[1,256,512]{2,1,0:T(8,128)(2,1)S(1)}, bf16[1,256,512]{2,1,0:T(8,128)(2,1)S(1)}, u32[]{:S(2)}, u32[]{:S(2)}) collective-permute-start(bf16[1,256,512]{2,1,0:T(8,128)(2,1)S(1)} %get-tuple-element.73), channel_id=1, source_target_pairs={{0,8},{8,16},{16,24},{24,0},{1,9},{9,17},{17,25},{25,1},{2,10},{10... | collective-permute-start | bytes 786440 | tf_op jit(solution)/shard_map/ppermute | solution.py:76
  459.8 27.8 %collective-permute-start.30 = (bf16[1,256,512]{2,1,0:T(8,128)(2,1)S(1)}, bf16[1,256,512]{2,1,0:T(8,128)(2,1)S(1)}, u32[]{:S(2)}, u32[]{:S(2)}) collective-permute-start(bf16[1,256,512]{2,1,0:T(8,128)(2,1)S(1)} %get-tuple-element.72), channel_id=1, source_target_pairs={{0,16},{8,24},{16,0},{24,8},{1,17},{9,25},{17,1},{25,9},{2,18},{10... | collective-permute-start | bytes 786440 | tf_op jit(solution)/shard_map/ppermute | solution.py:76
  462.9 24.7 %collective-permute-start.31 = (bf16[1,256,512]{2,1,0:T(8,128)(2,1)S(1)}, bf16[1,256,512]{2,1,0:T(8,128)(2,1)S(1)}, u32[]{:S(2)}, u32[]{:S(2)}) collective-permute-start(bf16[1,256,512]{2,1,0:T(8,128)(2,1)S(1)} %get-tuple-element.71), channel_id=1, source_target_pairs={{0,24},{8,0},{16,8},{24,16},{1,25},{9,1},{17,9},{25,17},{2,26},{10... | collective-permute-start | bytes 786440 | tf_op jit(solution)/shard_map/ppermute | solution.py:76
  487.7 27.6 %collective-permute-start.32 = (bf16[8,1,512]{2,1,0:T(2,128)(2,1)S(1)}, bf16[8,1,512]{2,1,0:T(2,128)(2,1)S(1)}, u32[]{:S(2)}, u32[]{:S(2)}) collective-permute-start(bf16[8,1,512]{2,1,0:T(2,128)(2,1)S(1)} %get-tuple-element.62), channel_id=1, source_target_pairs={{0,1},{1,2},{2,3},{3,4},{4,5},{5,6},{6,7},{8,9},{9,10},{10,11},{11... | collective-permute-start | bytes 24584 | tf_op jit(solution)/shard_map/ppermute | solution.py:17
  489.6 25.7 %collective-permute-start.35 = (bf16[8,1,512]{2,1,0:T(2,128)(2,1)S(1)}, bf16[8,1,512]{2,1,0:T(2,128)(2,1)S(1)}, u32[]{:S(2)}, u32[]{:S(2)}) collective-permute-start(bf16[8,1,512]{2,1,0:T(2,128)(2,1)S(1)} %get-tuple-element.63), channel_id=1, source_target_pairs={{1,0},{2,1},{3,2},{4,3},{5,4},{6,5},{7,6},{9,8},{10,9},{11,10},{12... | collective-permute-start | bytes 24584 | tf_op jit(solution)/shard_map/ppermute | solution.py:17
  490.9 30.8 %slice-start = ((s8[5406720]{0:T(1024)(128)(4,1)}), s8[4194304]{0:T(1024)(128)(4,1)S(1)}, s32[]{:S(2)}) async-start(s8[5406720]{0:T(1024)(128)(4,1)} %bitcast.252), calls=%async_computation.10 | async-start | bytes 8388608
  491.1 19.2 %collective-permute-start.33 = (bf16[8,256,1]{2,1,0:T(8,128)(2,1)S(1)}, bf16[8,256,1]{2,1,0:T(8,128)(2,1)S(1)}, u32[]{:S(2)}, u32[]{:S(2)}) collective-permute-start(bf16[8,256,1]{2,1,0:T(8,128)(2,1)S(1)} %get-tuple-element.60), channel_id=1, source_target_pairs={{0,8},{8,16},{16,24},{1,9},{9,17},{17,25},{2,10},{10,18},{18,26},{... | collective-permute-start | bytes 12296 | tf_op jit(solution)/shard_map/ppermute | solution.py:17
  499.5 15.8 %collective-permute-start.34 = (bf16[8,256,1]{2,1,0:T(8,128)(2,1)S(1)}, bf16[8,256,1]{2,1,0:T(8,128)(2,1)S(1)}, u32[]{:S(2)}, u32[]{:S(2)}) collective-permute-start(bf16[8,256,1]{2,1,0:T(8,128)(2,1)S(1)} %get-tuple-element.61), channel_id=1, source_target_pairs={{8,0},{16,8},{24,16},{9,1},{17,9},{25,17},{10,2},{18,10},{26,18},{... | collective-permute-start | bytes 12296 | tf_op jit(solution)/shard_map/ppermute | solution.py:17
  (25 other events, 373.4 us)

commit v11 on v6

--- a/solution.py
+++ b/solution.py
@@ -109,7 +109,7 @@
         eigenvectors.reshape(across, cols, width),
         preferred_element_type=jnp.float32,
     )
-    return exchange(pencil.astype(jnp.bfloat16), "px", 2, 0).astype(jnp.float32)
+    return return_lines(pencil.astype(jnp.bfloat16))
 
 
 def precondition(residual, eigenvectors, eigenvalues, level_shift):
@@ -126,8 +126,25 @@
     return jnp.concatenate(parts, 0)
 
 
-def operator(field, coeff_pad):
-    padded = padded_2(for_sending(field), (("px", 2), ("py", 1)), 1).astype(field.dtype)
+def return_lines(pencil):
+    size = lax.axis_size("px")
+    me = lax.axis_index("px")
+    levels_here, rows, width = pencil.shape
+    piece = width // size
+    padded = jnp.pad(pencil, ((0, 0), (0, 0), (1, 1)))
+    result = jnp.zeros((levels_here * size, rows, piece + 2), pencil.dtype)
+    for shift in range(size):
+        part = lax.dynamic_slice_in_dim(padded, ((me + shift) % size) * piece, piece + 2, 2)
+        if shift:
+            part = lax.ppermute(part, "px", [(i, (i + shift) % size) for i in range(size)])
+        result = lax.dynamic_update_slice_in_dim(
+            result, part, ((me - shift) % size) * levels_here, 0
+        )
+    return result
+
+
+def operator(wide, coeff_pad):
+    padded = padded_2(wide, (("py", 1),), 1).astype(jnp.float32)
     return face_sum(padded, coeff_pad)
 
 
@@ -144,8 +161,9 @@
     direction = image = None
     gamma_prev = curvature_prev = None
     for iteration in range(ITERS):
-        precond = precondition(residual, eigenvectors, eigenvalues, level_shift)
-        precond_image = operator(precond, coeff_pad)
+        wide = precondition(residual, eigenvectors, eigenvalues, level_shift)
+        precond = wide[:, :, 1:-1].astype(jnp.float32)
+        precond_image = operator(wide, coeff_pad)
         if iteration == 0:
             sums = all_sum(jnp.stack((jnp.sum(residual * precond), jnp.sum(precond * precond_image))))
             gamma, curvature = sums[0], sums[1]

time: 546 us -> 532 us (0.974)
  starting transfers between devices: 113 us -> 82.3 us
  waiting for transfers between devices: 151 us -> 168 us
    ppermute x0 -> x12, waiting for transfers between devices: none -> 75.8 us  [return_lines(): lax.ppermute(part, 'px', [(i, (i + shift) % size) for i in range(size)])]
    ppermute x24 -> x12, waiting for transfers between devices: 101 us -> 60.7 us  [exchange(): lax.ppermute(part, axis, [(i, (i + shift) % size) for i in range(size)])]
    ppermute x24 -> x12, starting transfers between devices: 56.7 us -> 24.4 us  [exchange(): lax.ppermute(part, axis, [(i, (i + shift) % size) for i in range(size)])]
    ppermute x6 -> x4, waiting for transfers between devices: 17.9 us -> 0.01 us  [padded_2(): lax.ppermute(last, axis, up)]
    reduce_sum x0 -> x1, other arithmetic: none -> 15.5 us  [shards(): jnp.sum(precond * precond_image)]
    reduce_sum x2 -> x1, other arithmetic: 27.5 us -> 14.7 us  [shards(): jnp.sum(residual * precond)]
    ppermute x0 -> x12, starting transfers between devices: none -> 11.7 us  [return_lines(): lax.ppermute(part, 'px', [(i, (i + shift) % size) for i in range(size)])]
    convert_element_type x2, other arithmetic: 12.7 us -> 3.83 us  [operator(): padded = padded_2(wide, (('py', 1),), 1).astype(jnp.float32)]
  transfers between devices with their start and end apart: 44 -> 40, of which waited for: 25 -> 25; matrix products, arithmetic and copies ran while one was open for 20% -> 21% of each run, Pallas kernels for 0% -> 0%
where the time goes in v11:
time: 532 us; the launch traced here: 528 us
  waiting for transfers between devices  168 us (32%)
  other arithmetic  117 us (22%)
  matrix products  86.6 us (16%)
  starting transfers between devices  82.3 us (15%)
  local copies, waits for them, and re-layouts  39 us (7%)
  blocking collectives  27.5 us (5%)
  between operations  7.7 us (1%)
    ppermute x12, waiting for transfers between devices, return_lines(): lax.ppermute(part, 'px', [(i, (i + shift) % size) for i in range(size)])  75.8 us
    ppermute x12, waiting for transfers between devices, exchange(): lax.ppermute(part, axis, [(i, (i + shift) % size) for i in range(size)])  60.7 us
    dot_general x4, matrix products, precondition_lines(): jnp.einsum('yj,kji->kyi', eigenvectors, scaled, preferred_element_type=jn...  44.2 us
    all_to_all x2, blocking collectives, all_sum(): return jnp.sum(lax.all_to_all(spread, axes, 0, 0, tiled=True), 0)  27.5 us
    ppermute x12, starting transfers between devices, exchange(): lax.ppermute(part, axis, [(i, (i + shift) % size) for i in range(size)])  24.4 us
    dot_general x4, matrix products, precondition_lines(): jnp.einsum('qkyi,qix->kyx', returned, eigenvectors.reshape(across, cols,...  22.8 us
    dot_general x4, matrix products, precondition_lines(): jnp.dot(lines.reshape(levels_here * rows, width), eigenvectors, preferred...  19.6 us
    mul x3, other arithmetic, face_sum(): vertical = 0.5 * (coeff[:-1] + coeff[1:]) * (values[:-1] - values[1:])  17.7 us
  transfers between devices with their start and end apart: 40, of which 25 were waited for; matrix products, arithmetic and copies ran while one was open for 21% of the time, Pallas kernels for 0%

profile of v11, /device:TPU:0, one launch (start us, length us, event | category | flops | bytes accessed | tf_op | source)
XLA Modules:
  0.0 527.8 jit_solution(1227830733601276956)
XLA Ops:
  5.1 14.5 %fusion.75 = bf16[1,8,256,512]{3,2,1,0:T(8,128)(2,1)S(1)} fusion(bf16[]{:T(256)} %bitcast.16, s32[8,256,512]{2,1,0:T(8,128)S(1)} %copy-done.8, bf16[]{:T(256)} %bitcast.15, bf16[]{:T(256)} %bitcast.14, bf16[]{:T(256)} %bitcast.13, bf16[]{:T(256)} %bitcast.12, bf16[]{:T(256)} %bitcast.11, bf16[]{:T(256)} %bitcast.10, bf16[]{:T(256)} %bitcast.9, bf16[]{:T(256)} %bitcast.8, ...), kind=kLoop, calls=%fused_computation.144 | loop fusion | flops 33554432 | bytes 6291488 | tf_op jit(solution)/shard_map/stack | solution.py:156
  26.5 4.3 collective-permute-start.1
  38.1 13.4 %fusion.3 = f32[2,8,258,514]{3,2,1,0:T(8,128)} fusion(bf16[2,8,1,512]{3,2,1,0:T(2,128)(2,1)S(1)} %collective-permute-done.3, bf16[2,8,1,512]{3,2,1,0:T(2,128)(2,1)S(1)} %collective-permute-done, bf16[2,8,256,1]{3,2,1,0:T(8,128)(2,1)} %copy.95, bf16[1,8,256,512]{3,2,1,0:T(8,128)(2,1)} %copy-done.3, bf16[1,8,256,512]{3,2,1,0:T(8,128)(2,1)S(1)} %convert_bitcast_fusion, ...), kind=kLoop, calls=%fused_computation.14 | loop fusion | flops 33948672 | bytes 12730624 | tf_op jit(solution)/shard_map/convert_element_type | solution.py:157
  51.4 4.8 slice_bitcast_fusion.1
  56.3 5.9 %fusion.47 = f32[7,256,512]{2,1,0:T(8,128)} fusion(f32[8,258,514]{2,1,0:T(8,128)S(1)} %get-tuple-element.31, f32[8,258,514]{2,1,0:T(8,128)S(1)} %get-tuple-element.30), kind=kLoop, calls=%fused_computation.82 | loop fusion | flops 3670016 | bytes 18350080 | tf_op jit(solution)/shard_map/mul | solution.py:54
  62.2 11.2 %fusion.35 = f32[8,256,512]{2,1,0:T(8,128)S(1)} fusion(f32[8,256,512]{2,1,0:T(8,128)} %param.7, f32[8,258,514]{2,1,0:T(8,128)S(1)} %get-tuple-element.31, f32[7,256,512]{2,1,0:T(8,128)} %fusion.47, f32[8,258,514]{2,1,0:T(8,128)S(1)} %get-tuple-element.30), kind=kLoop, calls=%fused_computation.57 | loop fusion | flops 23068672 | bytes 54001664 | tf_op jit(solution)/shard_map/sub | solution.py:160
  82.4 4.7 collective-permute-done.4
  87.1 11.1 %collective-permute-done.5 = bf16[1,256,512]{2,1,0:T(8,128)(2,1)S(1)} collective-permute-done((bf16[1,256,512]{2,1,0:T(8,128)(2,1)S(1)}, bf16[1,256,512]{2,1,0:T(8,128)(2,1)S(1)}, u32[]{:S(2)}, u32[]{:S(2)}) %collective-permute-start.5) | collective-permute-done | bytes 262176 | tf_op jit(solution)/shard_map/ppermute | solution.py:76
  100.9 7.2 %collective-permute-start.12 = (bf16[1,256,512]{2,1,0:T(8,128)(2,1)S(1)}, bf16[1,256,512]{2,1,0:T(8,128)(2,1)S(1)}, u32[]{:S(2)}, u32[]{:S(2)}) collective-permute-start(bf16[1,256,512]{2,1,0:T(8,128)(2,1)S(1)} %get-tuple-element.64), channel_id=1, source_target_pairs={{0,24},{8,0},{16,8},{24,16},{1,25},{9,1},{17,9},{25,17},{2,26},{10... | collective-permute-start | bytes 786440 | tf_op jit(solution)/shard_map/ppermute | solution.py:76
  108.7 5.7 %convolution_convert_fusion.7 = bf16[256,2048]{1,0:T(8,128)(2,1)S(1)} fusion(bf16[2048,2048]{1,0:T(8,128)(2,1)} %param.11, bf16[1,256,2048]{2,1,0:T(8,128)(2,1)S(1)} %constant_dynamic-update-slice_fusion.21), kind=kOutput, calls=%fused_computation.120 | convolution fusion | flops 2148007936 | bytes 10485760 | tf_op jit(solution)/shard_map/dot_general | solution.py:87
  115.5 3.6 all-to-all-start
  119.0 7.0 %collective-permute-done.10 = bf16[1,256,512]{2,1,0:T(8,128)(2,1)S(1)} collective-permute-done((bf16[1,256,512]{2,1,0:T(8,128)(2,1)}, bf16[1,256,512]{2,1,0:T(8,128)(2,1)S(1)}, u32[]{:S(2)}, u32[]{:S(2)}) %collective-permute-start.10) | collective-permute-done | bytes 262176 | tf_op jit(solution)/shard_map/ppermute | solution.py:76
  126.1 5.5 %collective-permute-done.11 = bf16[1,256,512]{2,1,0:T(8,128)(2,1)S(1)} collective-permute-done((bf16[1,256,512]{2,1,0:T(8,128)(2,1)S(1)}, bf16[1,256,512]{2,1,0:T(8,128)(2,1)S(1)}, u32[]{:S(2)}, u32[]{:S(2)}) %collective-permute-start.11) | collective-permute-done | bytes 262176 | tf_op jit(solution)/shard_map/ppermute | solution.py:76
  131.7 5.7 %convolution_convert_fusion.5 = bf16[256,2048]{1,0:T(8,128)(2,1)S(1)} fusion(bf16[2048,2048]{1,0:T(8,128)(2,1)} %param.11, bf16[1,256,2048]{2,1,0:T(8,128)(2,1)S(1)} %constant_dynamic-update-slice_fusion.14), kind=kOutput, calls=%fused_computation.118 | convolution fusion | flops 2148007936 | bytes 10485760 | tf_op jit(solution)/shard_map/dot_general | solution.py:87
  138.5 3.6 all-to-all-start.2
  142.0 11.1 %fusion.57 = bf16[1,2048,256]{1,2,0:T(8,128)(2,1)S(1)} fusion(bf16[2048,2048]{1,0:T(8,128)(2,1)} %param.11, bf16[2048,256]{1,0:T(8,128)(2,1)S(1)} %bitcast.235, f32[]{:T(128)} %bitcast.25, f32[256]{0:T(256)S(1)} %dynamic_slice.114, f32[2048]{0:T(1024)S(1)} %copy-done.10), kind=kOutput, calls=%fused_computation.121 | convolution fusion | flops 4297588736 | bytes 10494980 | tf_op jit(solution)/shard_map/yj,kji->kyi/dot_general | solution.py:101
  157.4 4.0 all-to-all-start.1
  161.3 11.0 %fusion.58 = bf16[1,2048,256]{1,2,0:T(8,128)(2,1)S(1)} fusion(bf16[2048,2048]{1,0:T(8,128)(2,1)} %param.11, bf16[2048,256]{1,0:T(8,128)(2,1)S(1)} %bitcast.237, f32[]{:T(128)} %bitcast.39, f32[256]{0:T(256)S(1)} %dynamic_slice.114, f32[2048]{0:T(1024)S(1)} %copy-done.10), kind=kOutput, calls=%fused_computation.122 | convolution fusion | flops 4297588736 | bytes 10494980 | tf_op jit(solution)/shard_map/yj,kji->kyi/dot_general | solution.py:101
  176.7 3.6 all-to-all-start.3
  180.3 5.7 %fusion.64 = bf16[1,256,2048]{2,1,0:T(8,128)(2,1)S(1)} fusion(bf16[8,256,2048]{2,1,0:T(8,128)(2,1)} %bitcast.242, bf16[8,1,256,256]{3,2,1,0:T(8,128)(2,1)S(1)} %all-to-all-done.1), kind=kOutput, calls=%fused_computation.128 | convolution fusion | flops 2148007936 | bytes 10485760 | tf_op jit(solution)/shard_map/qkyi,qix->kyx/dot_general | solution.py:106
  190.8 4.8 all-to-all-done.3
  195.6 5.7 %fusion.63 = bf16[1,256,2048]{2,1,0:T(8,128)(2,1)S(1)} fusion(bf16[8,256,2048]{2,1,0:T(8,128)(2,1)} %bitcast.243, bf16[8,1,256,256]{3,2,1,0:T(8,128)(2,1)S(1)} %all-to-all-done.3), kind=kOutput, calls=%fused_computation.127 | convolution fusion | flops 2148007936 | bytes 10485760 | tf_op jit(solution)/shard_map/qkyi,qix->kyx/dot_general | solution.py:106
  207.1 11.4 %collective-permute-done.8 = bf16[1,256,514]{2,1,0:T(8,128)(2,1)} collective-permute-done((bf16[1,256,514]{2,1,0:T(8,128)(2,1)S(1)}, bf16[1,256,514]{2,1,0:T(8,128)(2,1)}, u32[]{:S(2)}, u32[]{:S(2)}) %collective-permute-start.8) | collective-permute-done | bytes 263200 | tf_op jit(solution)/shard_map/ppermute | solution.py:139
  220.5 6.5 %collective-permute-done.13 = bf16[1,256,514]{2,1,0:T(8,128)(2,1)S(1)} collective-permute-done((bf16[1,256,514]{2,1,0:T(8,128)(2,1)S(1)}, bf16[1,256,514]{2,1,0:T(8,128)(2,1)S(1)}, u32[]{:S(2)}, u32[]{:S(2)}) %collective-permute-start.13) | collective-permute-done | bytes 263200 | tf_op jit(solution)/shard_map/ppermute | solution.py:139
  227.1 19.1 %collective-permute-done.14 = bf16[1,256,514]{2,1,0:T(8,128)(2,1)S(1)} collective-permute-done((bf16[1,256,514]{2,1,0:T(8,128)(2,1)S(1)}, bf16[1,256,514]{2,1,0:T(8,128)(2,1)S(1)}, u32[]{:S(2)}, u32[]{:S(2)}) %collective-permute-start.14) | collective-permute-done | bytes 263200 | tf_op jit(solution)/shard_map/ppermute | solution.py:139
  255.0 5.9 %fusion.46 = f32[7,256,512]{2,1,0:T(8,128)} fusion(f32[8,258,514]{2,1,0:T(8,128)S(1)} %maximum_convert_fusion, f32[8,258,514]{2,1,0:T(8,128)S(1)} %bitcast.231), kind=kLoop, calls=%fused_computation.80 | loop fusion | flops 3670016 | bytes 18350080 | tf_op jit(solution)/shard_map/mul | solution.py:54
  260.9 14.7 %fusion.8 = (f32[]{:T(128)}, f32[]{:T(128)}, f32[8,256,512]{2,1,0:T(8,128)}, bf16[8,256,512]{2,1,0:T(8,128)(2,1)}) fusion(f32[8,256,512]{2,1,0:T(8,128)} %copy-done.1, f32[7,256,512]{2,1,0:T(8,128)} %fusion.46, f32[8,258,514]{2,1,0:T(8,128)S(1)} %maximum_convert_fusion, f32[8,258,514]{2,1,0:T(8,128)S(1)} %bitcast.231, bf16[4,256,514]{2,1,0:T(8,128)(2,1)} %copy-done.6, ...), kind=kLoop, calls=%fused_computation.21 | loop fusion | flops 28311552 | bytes 58204168 | tf_op jit(solution)/shard_map/reduce_sum | solution.py:168
  277.0 13.3 %all_to_all.52 = f32[32,1,2]{2,1,0:T(1,128)S(1)} all-to-all(f32[32,1,2]{2,1,0:T(1,128)S(1)} %broadcast_in_dim.93), channel_id=1, replica_groups=mesh['px'=4,'py'=8] {'px','py'}, dimensions={0} | all-to-all | bytes 512 | tf_op jit(solution)/shard_map/all_to_all | solution.py:41
  292.3 4.7 multiply_subtract_fusion.1
  301.3 7.3 %collective-permute-done.18 = bf16[1,256,512]{2,1,0:T(8,128)(2,1)S(1)} collective-permute-done((bf16[1,256,512]{2,1,0:T(8,128)(2,1)S(1)}, bf16[1,256,512]{2,1,0:T(8,128)(2,1)S(1)}, u32[]{:S(2)}, u32[]{:S(2)}) %collective-permute-start.18) | collective-permute-done | bytes 262176 | tf_op jit(solution)/shard_map/ppermute | solution.py:76
  308.6 10.2 %collective-permute-done.19 = bf16[1,256,512]{2,1,0:T(8,128)(2,1)S(1)} collective-permute-done((bf16[1,256,512]{2,1,0:T(8,128)(2,1)S(1)}, bf16[1,256,512]{2,1,0:T(8,128)(2,1)S(1)}, u32[]{:S(2)}, u32[]{:S(2)}) %collective-permute-start.19) | collective-permute-done | bytes 262176 | tf_op jit(solution)/shard_map/ppermute | solution.py:76
  320.0 5.0 collective-permute-start.26
  333.9 8.4 %collective-permute-done.24 = bf16[1,256,512]{2,1,0:T(8,128)(2,1)S(1)} collective-permute-done((bf16[1,256,512]{2,1,0:T(8,128)(2,1)}, bf16[1,256,512]{2,1,0:T(8,128)(2,1)S(1)}, u32[]{:S(2)}, u32[]{:S(2)}) %collective-permute-start.24) | collective-permute-done | bytes 262176 | tf_op jit(solution)/shard_map/ppermute | solution.py:76
  342.4 6.5 %collective-permute-done.25 = bf16[1,256,512]{2,1,0:T(8,128)(2,1)S(1)} collective-permute-done((bf16[1,256,512]{2,1,0:T(8,128)(2,1)S(1)}, bf16[1,256,512]{2,1,0:T(8,128)(2,1)S(1)}, u32[]{:S(2)}, u32[]{:S(2)}) %collective-permute-start.25) | collective-permute-done | bytes 262176 | tf_op jit(solution)/shard_map/ppermute | solution.py:76
  349.0 5.7 %convolution_convert_fusion.1 = bf16[256,2048]{1,0:T(8,128)(2,1)S(1)} fusion(bf16[2048,2048]{1,0:T(8,128)(2,1)} %param.11, bf16[1,256,2048]{2,1,0:T(8,128)(2,1)S(1)} %constant_dynamic-update-slice_fusion), kind=kOutput, calls=%fused_computation.114 | convolution fusion | flops 2148007936 | bytes 10485760 | tf_op jit(solution)/shard_map/dot_general | solution.py:87
  359.4 11.1 %fusion.59 = bf16[1,2048,256]{1,2,0:T(8,128)(2,1)S(1)} fusion(bf16[2048,2048]{1,0:T(8,128)(2,1)} %param.11, bf16[2048,256]{1,0:T(8,128)(2,1)S(1)} %bitcast.234, f32[]{:T(128)} %bitcast.25, f32[256]{0:T(256)S(1)} %dynamic_slice.114, f32[2048]{0:T(1024)S(1)} %copy-done.10), kind=kOutput, calls=%fused_computation.123 | convolution fusion | flops 4297588736 | bytes 10494980 | tf_op jit(solution)/shard_map/yj,kji->kyi/dot_general | solution.py:101
  374.7 4.0 all-to-all-start.6
  378.7 11.0 %fusion.60 = bf16[1,2048,256]{1,2,0:T(8,128)(2,1)S(1)} fusion(bf16[2048,2048]{1,0:T(8,128)(2,1)} %param.11, bf16[2048,256]{1,0:T(8,128)(2,1)S(1)} %bitcast.236, f32[]{:T(128)} %bitcast.39, f32[256]{0:T(256)S(1)} %dynamic_slice.114, f32[2048]{0:T(1024)S(1)} %copy-done.10), kind=kOutput, calls=%fused_computation.124 | convolution fusion | flops 4297588736 | bytes 10494980 | tf_op jit(solution)/shard_map/yj,kji->kyi/dot_general | solution.py:101
  397.6 5.7 %fusion.62 = bf16[1,256,2048]{2,1,0:T(8,128)(2,1)S(1)} fusion(bf16[8,256,2048]{2,1,0:T(8,128)(2,1)} %bitcast.244, bf16[8,1,256,256]{3,2,1,0:T(8,128)(2,1)S(1)} %all-to-all-done.6), kind=kOutput, calls=%fused_computation.126 | convolution fusion | flops 2148007936 | bytes 10485760 | tf_op jit(solution)/shard_map/qkyi,qix->kyx/dot_general | solution.py:106
  407.1 5.8 %all-to-all-done.8 = bf16[8,1,256,256]{3,2,1,0:T(8,128)(2,1)S(1)} async-done(((bf16[8,1,256,256]{3,2,1,0:T(8,128)(2,1)}), bf16[8,1,256,256]{3,2,1,0:T(8,128)(2,1)S(1)}, u32[]{:S(2)}, u32[]{:S(2)}) %all-to-all-start.8) | async-done | bytes 1048608 | tf_op jit(solution)/shard_map/all_to_all | solution.py:105
  413.0 5.7 %fusion.61 = bf16[1,256,2048]{2,1,0:T(8,128)(2,1)S(1)} fusion(bf16[8,256,2048]{2,1,0:T(8,128)(2,1)} %bitcast.245, bf16[8,1,256,256]{3,2,1,0:T(8,128)(2,1)S(1)} %all-to-all-done.8), kind=kOutput, calls=%fused_computation.125 | convolution fusion | flops 2148007936 | bytes 10485760 | tf_op jit(solution)/shard_map/qkyi,qix->kyx/dot_general | solution.py:106
  424.0 11.0 %collective-permute-done.22 = bf16[1,256,514]{2,1,0:T(8,128)(2,1)} collective-permute-done((bf16[1,256,514]{2,1,0:T(8,128)(2,1)S(1)}, bf16[1,256,514]{2,1,0:T(8,128)(2,1)}, u32[]{:S(2)}, u32[]{:S(2)}) %collective-permute-start.22) | collective-permute-done | bytes 263200 | tf_op jit(solution)/shard_map/ppermute | solution.py:139
  437.0 6.3 %collective-permute-done.27 = bf16[1,256,514]{2,1,0:T(8,128)(2,1)S(1)} collective-permute-done((bf16[1,256,514]{2,1,0:T(8,128)(2,1)S(1)}, bf16[1,256,514]{2,1,0:T(8,128)(2,1)S(1)}, u32[]{:S(2)}, u32[]{:S(2)}) %collective-permute-start.27) | collective-permute-done | bytes 263200 | tf_op jit(solution)/shard_map/ppermute | solution.py:139
  443.3 19.3 %collective-permute-done.28 = bf16[1,256,514]{2,1,0:T(8,128)(2,1)S(1)} collective-permute-done((bf16[1,256,514]{2,1,0:T(8,128)(2,1)S(1)}, bf16[1,256,514]{2,1,0:T(8,128)(2,1)S(1)}, u32[]{:S(2)}, u32[]{:S(2)}) %collective-permute-start.28) | collective-permute-done | bytes 263200 | tf_op jit(solution)/shard_map/ppermute | solution.py:139
  471.4 5.9 %fusion.45 = f32[7,256,512]{2,1,0:T(8,128)} fusion(f32[8,258,514]{2,1,0:T(8,128)S(1)} %maximum_convert_fusion.1, f32[8,258,514]{2,1,0:T(8,128)S(1)} %bitcast.233), kind=kLoop, calls=%fused_computation.78 | loop fusion | flops 3670016 | bytes 18350080 | tf_op jit(solution)/shard_map/mul | solution.py:54
  477.3 15.5 %fusion.6 = (f32[]{:T(128)}, f32[]{:T(128)}, f32[]{:T(128)}, f32[]{:T(128)}, f32[8,256,512]{2,1,0:T(8,128)}, /*index=5*/bf16[8,256,512]{2,1,0:T(8,128)(2,1)}) fusion(bf16[8,256,512]{2,1,0:T(8,128)(2,1)} %get-tuple-element.29, f32[8,256,512]{2,1,0:T(8,128)} %copy-done.2, f32[8,256,512]{2,1,0:T(8,128)} %get-tuple-element.28, f32[7,256,512]{2,1,0:T(8,128)} %fusion.45, ...), kind=kLoop, calls=%fused_computation.19 | loop fusion | flops 33554432 | bytes 64495632 | tf_op jit(solution)/shard_map/reduce_sum | solution.py:176
  495.4 14.2 %all_to_all.53 = f32[32,1,4]{2,1,0:T(1,128)S(1)} all-to-all(f32[32,1,4]{2,1,0:T(1,128)S(1)} %broadcast_in_dim.94), channel_id=1, replica_groups=mesh['px'=4,'py'=8] {'px','py'}, dimensions={0} | all-to-all | bytes 1024 | tf_op jit(solution)/shard_map/all_to_all | solution.py:41
  514.8 12.8 %fusion.11 = (f32[8,256,512]{2,1,0:T(8,128)}, f32[8,256,512]{2,1,0:T(8,128)}, f32[8,256,512]{2,1,0:T(8,128)}) fusion(f32[8,256,512]{2,1,0:T(8,128)} %param.8, bf16[8,256,512]{2,1,0:T(8,128)(2,1)} %get-tuple-element.29, f32[]{:T(128)S(6)} %div.27, f32[]{:T(128)S(6)} %div.23, f32[]{:T(128)S(6)} %div.26, bf16[8,256,512]{2,1,0:T(8,128)(2,1)} %get-tuple-element.27, ...), kind=kLoop, calls=%fused_computation.24 | loop fusion | flops 12582912 | bytes 33554444 | tf_op jit(solution)/shard_map/add | solution.py:188
  (168 shorter events, 119.0 us)
Async XLA Ops:
  19.7 18.4 %collective-permute-start = (bf16[2,8,1,512]{3,2,1,0:T(2,128)(2,1)S(1)}, bf16[2,8,1,512]{3,2,1,0:T(2,128)(2,1)S(1)}, u32[]{:S(2)}, u32[]{:S(2)}) collective-permute-start(bf16[2,8,1,512]{3,2,1,0:T(2,128)(2,1)S(1)} %get-tuple-element.34), channel_id=1, source_target_pairs={{0,1},{1,2},{2,3},{3,4},{4,5},{5,6},{6,7},{8,9},{9,10},{10,11},{11... | collective-permute-start | bytes 49160 | tf_op jit(solution)/shard_map/ppermute | solution.py:17
  22.0 16.0 %collective-permute-start.3 = (bf16[2,8,1,512]{3,2,1,0:T(2,128)(2,1)S(1)}, bf16[2,8,1,512]{3,2,1,0:T(2,128)(2,1)S(1)}, u32[]{:S(2)}, u32[]{:S(2)}) collective-permute-start(bf16[2,8,1,512]{3,2,1,0:T(2,128)(2,1)S(1)} %get-tuple-element.35), channel_id=1, source_target_pairs={{1,0},{2,1},{3,2},{4,3},{5,4},{6,5},{7,6},{9,8},{10,9},{11,10},{12... | collective-permute-start | bytes 49160 | tf_op jit(solution)/shard_map/ppermute | solution.py:17
  26.5 6.2 %collective-permute-start.1 = (bf16[2,8,256,1]{2,1,3,0:T(8,128)(2,1)S(1)}, bf16[2,8,256,1]{2,1,3,0:T(8,128)(2,1)S(1)}, u32[]{:S(2)}, u32[]{:S(2)}) collective-permute-start(bf16[2,8,256,1]{2,1,3,0:T(8,128)(2,1)S(1)} %copy.92), channel_id=1, source_target_pairs={{0,8},{8,16},{16,24},{1,9},{9,17},{17,25},{2,10},{10,18},{18,26},{... | collective-permute-start | bytes 24584 | tf_op jit(solution)/shard_map/ppermute | solution.py:17
  31.1 5.5 %collective-permute-start.2 = (bf16[2,8,256,1]{2,1,3,0:T(8,128)(2,1)S(1)}, bf16[2,8,256,1]{2,1,3,0:T(8,128)(2,1)S(1)}, u32[]{:S(2)}, u32[]{:S(2)}) collective-permute-start(bf16[2,8,256,1]{2,1,3,0:T(8,128)(2,1)S(1)} %copy.93), channel_id=1, source_target_pairs={{8,0},{16,8},{24,16},{9,1},{17,9},{25,17},{10,2},{18,10},{26,18},{... | collective-permute-start | bytes 24584 | tf_op jit(solution)/shard_map/ppermute | solution.py:17
  75.8 11.2 %collective-permute-start.4 = (bf16[1,256,512]{2,1,0:T(8,128)(2,1)S(1)}, bf16[1,256,512]{2,1,0:T(8,128)(2,1)S(1)}, u32[]{:S(2)}, u32[]{:S(2)}) collective-permute-start(bf16[1,256,512]{2,1,0:T(8,128)(2,1)S(1)} %get-tuple-element.70), channel_id=1, source_target_pairs={{0,8},{8,16},{16,24},{24,0},{1,9},{9,17},{17,25},{25,1},{2,10},{10... | collective-permute-start | bytes 786440 | tf_op jit(solution)/shard_map/ppermute | solution.py:76
  77.5 20.7 %collective-permute-start.5 = (bf16[1,256,512]{2,1,0:T(8,128)(2,1)S(1)}, bf16[1,256,512]{2,1,0:T(8,128)(2,1)S(1)}, u32[]{:S(2)}, u32[]{:S(2)}) collective-permute-start(bf16[1,256,512]{2,1,0:T(8,128)(2,1)S(1)} %get-tuple-element.69), channel_id=1, source_target_pairs={{0,16},{8,24},{16,0},{24,8},{1,17},{9,25},{17,1},{25,9},{2,18},{10... | collective-permute-start | bytes 786440 | tf_op jit(solution)/shard_map/ppermute | solution.py:76
  78.6 19.6 %collective-permute-start.6 = (bf16[1,256,512]{2,1,0:T(8,128)(2,1)S(1)}, bf16[1,256,512]{2,1,0:T(8,128)(2,1)S(1)}, u32[]{:S(2)}, u32[]{:S(2)}) collective-permute-start(bf16[1,256,512]{2,1,0:T(8,128)(2,1)S(1)} %get-tuple-element.68), channel_id=1, source_target_pairs={{0,24},{8,0},{16,8},{24,16},{1,25},{9,1},{17,9},{25,17},{2,26},{10... | collective-permute-start | bytes 786440 | tf_op jit(solution)/shard_map/ppermute | solution.py:76
  100.9 30.7 %collective-permute-start.12 = (bf16[1,256,512]{2,1,0:T(8,128)(2,1)S(1)}, bf16[1,256,512]{2,1,0:T(8,128)(2,1)S(1)}, u32[]{:S(2)}, u32[]{:S(2)}) collective-permute-start(bf16[1,256,512]{2,1,0:T(8,128)(2,1)S(1)} %get-tuple-element.64), channel_id=1, source_target_pairs={{0,24},{8,0},{16,8},{24,16},{1,25},{9,1},{17,9},{25,17},{2,26},{10... | collective-permute-start | bytes 786440 | tf_op jit(solution)/shard_map/ppermute | solution.py:76
  108.2 23.5 %collective-permute-start.11 = (bf16[1,256,512]{2,1,0:T(8,128)(2,1)S(1)}, bf16[1,256,512]{2,1,0:T(8,128)(2,1)S(1)}, u32[]{:S(2)}, u32[]{:S(2)}) collective-permute-start(bf16[1,256,512]{2,1,0:T(8,128)(2,1)S(1)} %get-tuple-element.65), channel_id=1, source_target_pairs={{0,16},{8,24},{16,0},{24,8},{1,17},{9,25},{17,1},{25,9},{2,18},{10... | collective-permute-start | bytes 786440 | tf_op jit(solution)/shard_map/ppermute | solution.py:76
  108.5 17.6 %collective-permute-start.10 = (bf16[1,256,512]{2,1,0:T(8,128)(2,1)}, bf16[1,256,512]{2,1,0:T(8,128)(2,1)S(1)}, u32[]{:S(2)}, u32[]{:S(2)}) collective-permute-start(bf16[1,256,512]{2,1,0:T(8,128)(2,1)} %get-tuple-element.66), channel_id=1, source_target_pairs={{0,8},{8,16},{16,24},{24,0},{1,9},{9,17},{17,25},{25,1},{2,10},{10... | collective-permute-start | bytes 786440 | tf_op jit(solution)/shard_map/ppermute | solution.py:76
  115.5 23.0 %all-to-all-start = ((bf16[8,256,256]{2,1,0:T(8,128)(2,1)}), bf16[8,256,256]{2,1,0:T(8,128)(2,1)S(1)}, u32[]{:S(2)}, u32[]{:S(2)}) async-start(bf16[8,256,256]{2,1,0:T(8,128)(2,1)} %bitcast.229), calls=%async_computation | async-start | bytes 2097152 | tf_op jit(solution)/shard_map/all_to_all | solution.py:91
  138.5 18.9 %all-to-all-start.2 = ((bf16[8,256,256]{2,1,0:T(8,128)(2,1)}), bf16[8,256,256]{2,1,0:T(8,128)(2,1)S(1)}, u32[]{:S(2)}, u32[]{:S(2)}) async-start(bf16[8,256,256]{2,1,0:T(8,128)(2,1)} %bitcast.227), calls=%async_computation.2 | async-start | bytes 2097152 | tf_op jit(solution)/shard_map/all_to_all | solution.py:91
  157.4 19.3 %all-to-all-start.1 = ((bf16[8,1,256,256]{3,2,1,0:T(8,128)(2,1)}), bf16[8,1,256,256]{3,2,1,0:T(8,128)(2,1)S(1)}, u32[]{:S(2)}, u32[]{:S(2)}) async-start(bf16[8,1,256,256]{3,2,1,0:T(8,128)(2,1)} %bitcast.29), calls=%async_computation.1 | async-start | bytes 2097152 | tf_op jit(solution)/shard_map/all_to_all | solution.py:105
  176.7 18.9 %all-to-all-start.3 = ((bf16[8,1,256,256]{3,2,1,0:T(8,128)(2,1)}), bf16[8,1,256,256]{3,2,1,0:T(8,128)(2,1)S(1)}, u32[]{:S(2)}, u32[]{:S(2)}) async-start(bf16[8,1,256,256]{3,2,1,0:T(8,128)(2,1)} %bitcast.43), calls=%async_computation.3 | async-start | bytes 2097152 | tf_op jit(solution)/shard_map/all_to_all | solution.py:105
  186.9 32.6 %collective-permute-start.9 = (bf16[1,256,514]{2,1,0:T(8,128)(2,1)S(1)}, bf16[1,256,514]{2,1,0:T(8,128)(2,1)}, u32[]{:S(2)}, u32[]{:S(2)}) collective-permute-start(bf16[1,256,514]{2,1,0:T(8,128)(2,1)S(1)} %get-tuple-element.56), channel_id=1, source_target_pairs={{0,24},{8,0},{16,8},{24,16},{1,25},{9,1},{17,9},{25,17},{2,26},{10... | collective-permute-start | bytes 789512 | tf_op jit(solution)/shard_map/ppermute | solution.py:139
  187.0 19.0 %collective-permute-start.7 = (bf16[1,256,514]{2,1,0:T(8,128)(2,1)S(1)}, bf16[1,256,514]{2,1,0:T(8,128)(2,1)}, u32[]{:S(2)}, u32[]{:S(2)}) collective-permute-start(bf16[1,256,514]{2,1,0:T(8,128)(2,1)S(1)} %get-tuple-element.57), channel_id=1, source_target_pairs={{0,8},{8,16},{16,24},{24,0},{1,9},{9,17},{17,25},{25,1},{2,10},{10... | collective-permute-start | bytes 789512 | tf_op jit(solution)/shard_map/ppermute | solution.py:139
  189.0 29.5 %collective-permute-start.8 = (bf16[1,256,514]{2,1,0:T(8,128)(2,1)S(1)}, bf16[1,256,514]{2,1,0:T(8,128)(2,1)}, u32[]{:S(2)}, u32[]{:S(2)}) collective-permute-start(bf16[1,256,514]{2,1,0:T(8,128)(2,1)S(1)} %get-tuple-element.58), channel_id=1, source_target_pairs={{0,16},{8,24},{16,0},{24,8},{1,17},{9,25},{17,1},{25,9},{2,18},{10... | collective-permute-start | bytes 789512 | tf_op jit(solution)/shard_map/ppermute | solution.py:139
  202.2 44.0 %collective-permute-start.15 = (bf16[1,256,514]{2,1,0:T(8,128)(2,1)S(1)}, bf16[1,256,514]{2,1,0:T(8,128)(2,1)S(1)}, u32[]{:S(2)}, u32[]{:S(2)}) collective-permute-start(bf16[1,256,514]{2,1,0:T(8,128)(2,1)S(1)} %get-tuple-element.60), channel_id=1, source_target_pairs={{0,24},{8,0},{16,8},{24,16},{1,25},{9,1},{17,9},{25,17},{2,26},{10... | collective-permute-start | bytes 789512 | tf_op jit(solution)/shard_map/ppermute | solution.py:139
  202.3 24.8 %collective-permute-start.13 = (bf16[1,256,514]{2,1,0:T(8,128)(2,1)S(1)}, bf16[1,256,514]{2,1,0:T(8,128)(2,1)S(1)}, u32[]{:S(2)}, u32[]{:S(2)}) collective-permute-start(bf16[1,256,514]{2,1,0:T(8,128)(2,1)S(1)} %get-tuple-element.61), channel_id=1, source_target_pairs={{0,8},{8,16},{16,24},{24,0},{1,9},{9,17},{17,25},{25,1},{2,10},{10... | collective-permute-start | bytes 789512 | tf_op jit(solution)/shard_map/ppermute | solution.py:139
  206.0 40.2 %collective-permute-start.14 = (bf16[1,256,514]{2,1,0:T(8,128)(2,1)S(1)}, bf16[1,256,514]{2,1,0:T(8,128)(2,1)S(1)}, u32[]{:S(2)}, u32[]{:S(2)}) collective-permute-start(bf16[1,256,514]{2,1,0:T(8,128)(2,1)S(1)} %get-tuple-element.62), channel_id=1, source_target_pairs={{0,16},{8,24},{16,0},{24,8},{1,17},{9,25},{17,1},{25,9},{2,18},{10... | collective-permute-start | bytes 789512 | tf_op jit(solution)/shard_map/ppermute | solution.py:139
  220.5 29.6 %copy-start.5 = (bf16[4,256,514]{2,1,0:T(8,128)(2,1)}, bf16[4,256,514]{2,1,0:T(8,128)(2,1)S(1)}, u32[]{:S(2)}) copy-start(bf16[4,256,514]{2,1,0:T(8,128)(2,1)S(1)} %constant_dynamic-update-slice_fusion.17) | copy-start | bytes 3158020
  246.3 8.6 %slice-start = ((s8[5406720]{0:T(1024)(128)(4,1)}), s8[4194304]{0:T(1024)(128)(4,1)S(1)}, s32[]{:S(2)}) async-start(s8[5406720]{0:T(1024)(128)(4,1)} %bitcast.230), calls=%async_computation.10 | async-start | bytes 8388608
  246.4 3.8 collective-permute-start.16
  248.6 4.5 collective-permute-start.17
  292.3 34.6 %slice-start.4 = ((s8[8388608]{0:T(1024)(128)(4,1)}), s8[4194304]{0:T(1024)(128)(4,1)S(1)}, s32[]{:S(2)}) async-start(s8[8388608]{0:T(1024)(128)(4,1)} %bitcast.246), calls=%async_computation.14 | async-start | bytes 8388608
  292.3 34.5 %slice-start.5 = ((s8[8388608]{0:T(1024)(128)(4,1)}), s8[4194304]{0:T(1024)(128)(4,1)S(1)}, s32[]{:S(2)}) async-start(s8[8388608]{0:T(1024)(128)(4,1)} %bitcast.246), calls=%async_computation.15 | async-start | bytes 8388608
  297.0 22.0 %copy-start.2 = (f32[8,256,512]{2,1,0:T(8,128)}, f32[8,256,512]{2,1,0:T(8,128)S(1)}, u32[]{:S(2)}) copy-start(f32[8,256,512]{2,1,0:T(8,128)S(1)} %multiply_subtract_fusion.1) | copy-start | bytes 12582916
  297.4 11.1 %collective-permute-start.18 = (bf16[1,256,512]{2,1,0:T(8,128)(2,1)S(1)}, bf16[1,256,512]{2,1,0:T(8,128)(2,1)S(1)}, u32[]{:S(2)}, u32[]{:S(2)}) collective-permute-start(bf16[1,256,512]{2,1,0:T(8,128)(2,1)S(1)} %get-tuple-element.54), channel_id=1, source_target_pairs={{0,8},{8,16},{16,24},{24,0},{1,9},{9,17},{17,25},{25,1},{2,10},{10... | collective-permute-start | bytes 786440 | tf_op jit(solution)/shard_map/ppermute | solution.py:76
  298.0 20.7 %collective-permute-start.19 = (bf16[1,256,512]{2,1,0:T(8,128)(2,1)S(1)}, bf16[1,256,512]{2,1,0:T(8,128)(2,1)S(1)}, u32[]{:S(2)}, u32[]{:S(2)}) collective-permute-start(bf16[1,256,512]{2,1,0:T(8,128)(2,1)S(1)} %get-tuple-element.53), channel_id=1, source_target_pairs={{0,16},{8,24},{16,0},{24,8},{1,17},{9,25},{17,1},{25,9},{2,18},{10... | collective-permute-start | bytes 786440 | tf_op jit(solution)/shard_map/ppermute | solution.py:76
  298.6 20.2 %collective-permute-start.20 = (bf16[1,256,512]{2,1,0:T(8,128)(2,1)S(1)}, bf16[1,256,512]{2,1,0:T(8,128)(2,1)S(1)}, u32[]{:S(2)}, u32[]{:S(2)}) collective-permute-start(bf16[1,256,512]{2,1,0:T(8,128)(2,1)S(1)} %get-tuple-element.52), channel_id=1, source_target_pairs={{0,24},{8,0},{16,8},{24,16},{1,25},{9,1},{17,9},{25,17},{2,26},{10... | collective-permute-start | bytes 786440 | tf_op jit(solution)/shard_map/ppermute | solution.py:76
  320.0 29.0 %collective-permute-start.26 = (bf16[1,256,512]{2,1,0:T(8,128)(2,1)S(1)}, bf16[1,256,512]{2,1,0:T(8,128)(2,1)S(1)}, u32[]{:S(2)}, u32[]{:S(2)}) collective-permute-start(bf16[1,256,512]{2,1,0:T(8,128)(2,1)S(1)} %get-tuple-element.48), channel_id=1, source_target_pairs={{0,24},{8,0},{16,8},{24,16},{1,25},{9,1},{17,9},{25,17},{2,26},{10... | collective-permute-start | bytes 786440 | tf_op jit(solution)/shard_map/ppermute | solution.py:76
  324.9 24.0 %collective-permute-start.25 = (bf16[1,256,512]{2,1,0:T(8,128)(2,1)S(1)}, bf16[1,256,512]{2,1,0:T(8,128)(2,1)S(1)}, u32[]{:S(2)}, u32[]{:S(2)}) collective-permute-start(bf16[1,256,512]{2,1,0:T(8,128)(2,1)S(1)} %get-tuple-element.49), channel_id=1, source_target_pairs={{0,16},{8,24},{16,0},{24,8},{1,17},{9,25},{17,1},{25,9},{2,18},{10... | collective-permute-start | bytes 786440 | tf_op jit(solution)/shard_map/ppermute | solution.py:76
  326.7 15.7 %collective-permute-start.24 = (bf16[1,256,512]{2,1,0:T(8,128)(2,1)}, bf16[1,256,512]{2,1,0:T(8,128)(2,1)S(1)}, u32[]{:S(2)}, u32[]{:S(2)}) collective-permute-start(bf16[1,256,512]{2,1,0:T(8,128)(2,1)} %get-tuple-element.50), channel_id=1, source_target_pairs={{0,8},{8,16},{16,24},{24,0},{1,9},{9,17},{17,25},{25,1},{2,10},{10... | collective-permute-start | bytes 786440 | tf_op jit(solution)/shard_map/ppermute | solution.py:76
  330.4 25.5 %all-to-all-start.5 = ((bf16[8,256,256]{2,1,0:T(8,128)(2,1)}), bf16[8,256,256]{2,1,0:T(8,128)(2,1)S(1)}, u32[]{:S(2)}, u32[]{:S(2)}) async-start(bf16[8,256,256]{2,1,0:T(8,128)(2,1)} %bitcast.225), calls=%async_computation.5 | async-start | bytes 2097152 | tf_op jit(solution)/shard_map/all_to_all | solution.py:91
  355.8 18.9 %all-to-all-start.7 = ((bf16[8,256,256]{2,1,0:T(8,128)(2,1)}), bf16[8,256,256]{2,1,0:T(8,128)(2,1)S(1)}, u32[]{:S(2)}, u32[]{:S(2)}) async-start(bf16[8,256,256]{2,1,0:T(8,128)(2,1)} %bitcast.223), calls=%async_computation.7 | async-start | bytes 2097152 | tf_op jit(solution)/shard_map/all_to_all | solution.py:91
  374.7 19.3 %all-to-all-start.6 = ((bf16[8,1,256,256]{3,2,1,0:T(8,128)(2,1)}), bf16[8,1,256,256]{3,2,1,0:T(8,128)(2,1)S(1)}, u32[]{:S(2)}, u32[]{:S(2)}) async-start(bf16[8,1,256,256]{3,2,1,0:T(8,128)(2,1)} %bitcast.59), calls=%async_computation.6 | async-start | bytes 2097152 | tf_op jit(solution)/shard_map/all_to_all | solution.py:105
  394.1 18.9 %all-to-all-start.8 = ((bf16[8,1,256,256]{3,2,1,0:T(8,128)(2,1)}), bf16[8,1,256,256]{3,2,1,0:T(8,128)(2,1)S(1)}, u32[]{:S(2)}, u32[]{:S(2)}) async-start(bf16[8,1,256,256]{3,2,1,0:T(8,128)(2,1)} %bitcast.71), calls=%async_computation.8 | async-start | bytes 2097152 | tf_op jit(solution)/shard_map/all_to_all | solution.py:105
  404.2 31.7 %collective-permute-start.23 = (bf16[1,256,514]{2,1,0:T(8,128)(2,1)S(1)}, bf16[1,256,514]{2,1,0:T(8,128)(2,1)}, u32[]{:S(2)}, u32[]{:S(2)}) collective-permute-start(bf16[1,256,514]{2,1,0:T(8,128)(2,1)S(1)} %get-tuple-element.40), channel_id=1, source_target_pairs={{0,24},{8,0},{16,8},{24,16},{1,25},{9,1},{17,9},{25,17},{2,26},{10... | collective-permute-start | bytes 789512 | tf_op jit(solution)/shard_map/ppermute | solution.py:139
  404.3 17.9 %collective-permute-start.21 = (bf16[1,256,514]{2,1,0:T(8,128)(2,1)S(1)}, bf16[1,256,514]{2,1,0:T(8,128)(2,1)}, u32[]{:S(2)}, u32[]{:S(2)}) collective-permute-start(bf16[1,256,514]{2,1,0:T(8,128)(2,1)S(1)} %get-tuple-element.41), channel_id=1, source_target_pairs={{0,8},{8,16},{16,24},{24,0},{1,9},{9,17},{17,25},{25,1},{2,10},{10... | collective-permute-start | bytes 789512 | tf_op jit(solution)/shard_map/ppermute | solution.py:139
  406.3 28.6 %collective-permute-start.22 = (bf16[1,256,514]{2,1,0:T(8,128)(2,1)S(1)}, bf16[1,256,514]{2,1,0:T(8,128)(2,1)}, u32[]{:S(2)}, u32[]{:S(2)}) collective-permute-start(bf16[1,256,514]{2,1,0:T(8,128)(2,1)S(1)} %get-tuple-element.42), channel_id=1, source_target_pairs={{0,16},{8,24},{16,0},{24,8},{1,17},{9,25},{17,1},{25,9},{2,18},{10... | collective-permute-start | bytes 789512 | tf_op jit(solution)/shard_map/ppermute | solution.py:139
  419.6 43.1 %collective-permute-start.29 = (bf16[1,256,514]{2,1,0:T(8,128)(2,1)S(1)}, bf16[1,256,514]{2,1,0:T(8,128)(2,1)S(1)}, u32[]{:S(2)}, u32[]{:S(2)}) collective-permute-start(bf16[1,256,514]{2,1,0:T(8,128)(2,1)S(1)} %get-tuple-element.44), channel_id=1, source_target_pairs={{0,24},{8,0},{16,8},{24,16},{1,25},{9,1},{17,9},{25,17},{2,26},{10... | collective-permute-start | bytes 789512 | tf_op jit(solution)/shard_map/ppermute | solution.py:139
  419.6 23.6 %collective-permute-start.27 = (bf16[1,256,514]{2,1,0:T(8,128)(2,1)S(1)}, bf16[1,256,514]{2,1,0:T(8,128)(2,1)S(1)}, u32[]{:S(2)}, u32[]{:S(2)}) collective-permute-start(bf16[1,256,514]{2,1,0:T(8,128)(2,1)S(1)} %get-tuple-element.45), channel_id=1, source_target_pairs={{0,8},{8,16},{16,24},{24,0},{1,9},{9,17},{17,25},{25,1},{2,10},{10... | collective-permute-start | bytes 789512 | tf_op jit(solution)/shard_map/ppermute | solution.py:139
  422.2 40.4 %collective-permute-start.28 = (bf16[1,256,514]{2,1,0:T(8,128)(2,1)S(1)}, bf16[1,256,514]{2,1,0:T(8,128)(2,1)S(1)}, u32[]{:S(2)}, u32[]{:S(2)}) collective-permute-start(bf16[1,256,514]{2,1,0:T(8,128)(2,1)S(1)} %get-tuple-element.46), channel_id=1, source_target_pairs={{0,16},{8,24},{16,0},{24,8},{1,17},{9,25},{17,1},{25,9},{2,18},{10... | collective-permute-start | bytes 789512 | tf_op jit(solution)/shard_map/ppermute | solution.py:139
  437.0 29.6 %copy-start.7 = (bf16[4,256,514]{2,1,0:T(8,128)(2,1)}, bf16[4,256,514]{2,1,0:T(8,128)(2,1)S(1)}, u32[]{:S(2)}) copy-start(bf16[4,256,514]{2,1,0:T(8,128)(2,1)S(1)} %constant_dynamic-update-slice_fusion.4) | copy-start | bytes 3158020
  462.7 6.7 %copy-start.4 = (bf16[4,256,514]{2,1,0:T(8,128)(2,1)}, bf16[4,256,514]{2,1,0:T(8,128)(2,1)S(1)}, u32[]{:S(2)}) copy-start(bf16[4,256,514]{2,1,0:T(8,128)(2,1)S(1)} %constant_dynamic-update-slice_fusion.20) | copy-start | bytes 3158020
  462.8 8.6 %slice-start.2 = ((s8[5406720]{0:T(1024)(128)(4,1)}), s8[4194304]{0:T(1024)(128)(4,1)S(1)}, s32[]{:S(2)}) async-start(s8[5406720]{0:T(1024)(128)(4,1)} %bitcast.232), calls=%async_computation.12 | async-start | bytes 8388608
  462.8 3.7 collective-permute-start.30
  465.0 4.5 collective-permute-start.31
  (9 other events, 49.7 us)

commit v12 on v11

--- a/solution.py
+++ b/solution.py
@@ -101,7 +101,10 @@
     fourth = jnp.einsum(
         "yj,kji->kyi", eigenvectors, scaled, preferred_element_type=jnp.float32
     ).astype(jnp.bfloat16)
-    outgoing = fourth.reshape(levels_here, across, rows, cols).transpose(1, 0, 2, 3)
+    edged = jnp.pad(fourth, ((0, 0), (1, 1), (0, 0)))
+    outgoing = jnp.stack(
+        [edged[:, target * rows : target * rows + rows + 2] for target in range(across)], 0
+    )
     returned = lax.all_to_all(outgoing, "py", 0, 0, tiled=True)
     pencil = jnp.einsum(
         "qkyi,qix->kyx",
@@ -144,8 +147,7 @@
 
 
 def operator(wide, coeff_pad):
-    padded = padded_2(wide, (("py", 1),), 1).astype(jnp.float32)
-    return face_sum(padded, coeff_pad)
+    return face_sum(wide.astype(jnp.float32), coeff_pad)
 
 
 def shards(right_side, solution_in, classes, coeff_table, eigenvectors, eigenvalues, level_shift):
@@ -162,7 +164,7 @@
     gamma_prev = curvature_prev = None
     for iteration in range(ITERS):
         wide = precondition(residual, eigenvectors, eigenvalues, level_shift)
-        precond = wide[:, :, 1:-1].astype(jnp.float32)
+        precond = wide[:, 1:-1, 1:-1].astype(jnp.float32)
         precond_image = operator(wide, coeff_pad)
         if iteration == 0:
             sums = all_sum(jnp.stack((jnp.sum(residual * precond), jnp.sum(precond * precond_image))))

time: 532 us -> 527 us (level)
  waiting for transfers between devices: 168 us -> 155 us
  local copies, waits for them, and re-layouts: 39 us -> 49.4 us
    unnamed x34 -> x58, local copies, waits for them, and re-layouts: 2.08 us -> 8.83 us
    ppermute x4 -> x2, waiting for transfers between devices: 9.22 us -> 3.36 us  [padded_2(): lax.ppermute(initial, axis, down)]
    ppermute x4 -> x2, starting transfers between devices: 10.9 us -> 6.67 us  [padded_2(): lax.ppermute(last, axis, up)]
  transfers between devices with their start and end apart: 40 -> 36, of which waited for: 25 -> 23; matrix products, arithmetic and copies ran while one was open for 21% -> 24% of each run, Pallas kernels for 0% -> 0%
where the time goes in v12:
time: 527 us; the launch traced here: 522 us
  waiting for transfers between devices  155 us (29%)
  other arithmetic  116 us (22%)
  matrix products  91.7 us (17%)
  starting transfers between devices  79.8 us (15%)
  local copies, waits for them, and re-layouts  49.4 us (9%)
  blocking collectives  23 us (4%)
  between operations  7.42 us (1%)
    ppermute x12, waiting for transfers between devices, return_lines(): lax.ppermute(part, 'px', [(i, (i + shift) % size) for i in range(size)])  78.7 us
    ppermute x12, waiting for transfers between devices, exchange(): lax.ppermute(part, axis, [(i, (i + shift) % size) for i in range(size)])  56.2 us
    dot_general x4, matrix products, precondition_lines(): jnp.einsum('yj,kji->kyi', eigenvectors, scaled, preferred_element_type=jn...  44.9 us
    ppermute x12, starting transfers between devices, exchange(): lax.ppermute(part, axis, [(i, (i + shift) % size) for i in range(size)])  24.9 us
    dot_general x4, matrix products, precondition_lines(): jnp.einsum('qkyi,qix->kyx', returned, eigenvectors.reshape(across, cols,...  23.9 us
    all_to_all x2, blocking collectives, all_sum(): return jnp.sum(lax.all_to_all(spread, axes, 0, 0, tiled=True), 0)  23 us
    dot_general x4, matrix products, precondition_lines(): jnp.dot(lines.reshape(levels_here * rows, width), eigenvectors, preferred...  22.9 us
    mul x3, other arithmetic, face_sum(): vertical = 0.5 * (coeff[:-1] + coeff[1:]) * (values[:-1] - values[1:])  17.7 us
  transfers between devices with their start and end apart: 36, of which 23 were waited for; matrix products, arithmetic and copies ran while one was open for 24% of the time, Pallas kernels for 0%

profile of v12, /device:TPU:0, one launch (start us, length us, event | category | flops | bytes accessed | tf_op | source)
XLA Modules:
  0.0 522.0 jit_solution(9269923721539747537)
XLA Ops:
  6.0 14.5 %fusion.77 = bf16[1,8,256,512]{3,2,1,0:T(8,128)(2,1)S(1)} fusion(bf16[]{:T(256)} %bitcast.16, s32[8,256,512]{2,1,0:T(8,128)S(1)} %copy-done.8, bf16[]{:T(256)} %bitcast.15, bf16[]{:T(256)} %bitcast.14, bf16[]{:T(256)} %bitcast.13, bf16[]{:T(256)} %bitcast.12, bf16[]{:T(256)} %bitcast.11, bf16[]{:T(256)} %bitcast.10, bf16[]{:T(256)} %bitcast.9, bf16[]{:T(256)} %bitcast.8, ...), kind=kLoop, calls=%fused_computation.142 | loop fusion | flops 33554432 | bytes 6291488 | tf_op jit(solution)/shard_map/stack | solution.py:158
  27.4 4.3 collective-permute-start.1
  39.0 13.3 %fusion.3 = f32[2,8,258,514]{3,2,1,0:T(8,128)} fusion(bf16[2,8,1,512]{3,2,1,0:T(2,128)(2,1)S(1)} %collective-permute-done.3, bf16[2,8,1,512]{3,2,1,0:T(2,128)(2,1)S(1)} %collective-permute-done, bf16[2,8,256,1]{3,2,1,0:T(8,128)(2,1)} %copy.95, bf16[1,8,256,512]{3,2,1,0:T(8,128)(2,1)} %copy-done.3, bf16[1,8,256,512]{3,2,1,0:T(8,128)(2,1)S(1)} %convert_bitcast_fusion, ...), kind=kLoop, calls=%fused_computation.14 | loop fusion | flops 33948672 | bytes 12730624 | tf_op jit(solution)/shard_map/convert_element_type | solution.py:159
  52.3 4.8 slice_bitcast_fusion.1
  57.2 5.9 %fusion.47 = f32[7,256,512]{2,1,0:T(8,128)} fusion(f32[8,258,514]{2,1,0:T(8,128)S(1)} %get-tuple-element.31, f32[8,258,514]{2,1,0:T(8,128)S(1)} %get-tuple-element.30), kind=kLoop, calls=%fused_computation.82 | loop fusion | flops 3670016 | bytes 18350080 | tf_op jit(solution)/shard_map/mul | solution.py:54
  63.1 11.2 %fusion.35 = f32[8,256,512]{2,1,0:T(8,128)S(1)} fusion(f32[8,256,512]{2,1,0:T(8,128)} %param.7, f32[8,258,514]{2,1,0:T(8,128)S(1)} %get-tuple-element.31, f32[7,256,512]{2,1,0:T(8,128)} %fusion.47, f32[8,258,514]{2,1,0:T(8,128)S(1)} %get-tuple-element.30), kind=kLoop, calls=%fused_computation.57 | loop fusion | flops 23068672 | bytes 54001664 | tf_op jit(solution)/shard_map/sub | solution.py:162
  83.6 4.4 collective-permute-done.4
  88.0 11.1 %collective-permute-done.5 = bf16[1,256,512]{2,1,0:T(8,128)(2,1)S(1)} collective-permute-done((bf16[1,256,512]{2,1,0:T(8,128)(2,1)S(1)}, bf16[1,256,512]{2,1,0:T(8,128)(2,1)S(1)}, u32[]{:S(2)}, u32[]{:S(2)}) %collective-permute-start.5) | collective-permute-done | bytes 262176 | tf_op jit(solution)/shard_map/ppermute | solution.py:76
  101.9 7.2 %collective-permute-start.12 = (bf16[1,256,512]{2,1,0:T(8,128)(2,1)}, bf16[1,256,512]{2,1,0:T(8,128)(2,1)S(1)}, u32[]{:S(2)}, u32[]{:S(2)}) collective-permute-start(bf16[1,256,512]{2,1,0:T(8,128)(2,1)} %get-tuple-element.60), channel_id=1, source_target_pairs={{0,24},{8,0},{16,8},{24,16},{1,25},{9,1},{17,9},{25,17},{2,26},{10... | collective-permute-start | bytes 786440 | tf_op jit(solution)/shard_map/ppermute | solution.py:76
  109.7 5.7 %convolution_convert_fusion.7 = bf16[256,2048]{1,0:T(8,128)(2,1)S(1)} fusion(bf16[2048,2048]{1,0:T(8,128)(2,1)} %param.11, bf16[1,256,2048]{2,1,0:T(8,128)(2,1)S(1)} %constant_dynamic-update-slice_fusion.21), kind=kOutput, calls=%fused_computation.118 | convolution fusion | flops 2148007936 | bytes 10485760 | tf_op jit(solution)/shard_map/dot_general | solution.py:87
  120.0 7.3 %collective-permute-done.10 = bf16[1,256,512]{2,1,0:T(8,128)(2,1)} collective-permute-done((bf16[1,256,512]{2,1,0:T(8,128)(2,1)}, bf16[1,256,512]{2,1,0:T(8,128)(2,1)}, u32[]{:S(2)}, u32[]{:S(2)}) %collective-permute-start.10) | collective-permute-done | bytes 262176 | tf_op jit(solution)/shard_map/ppermute | solution.py:76
  128.4 4.6 collective-permute-done.11
  134.0 5.7 %convolution_convert_fusion.5 = bf16[256,2048]{1,0:T(8,128)(2,1)S(1)} fusion(bf16[2048,2048]{1,0:T(8,128)(2,1)} %param.11, bf16[1,256,2048]{2,1,0:T(8,128)(2,1)S(1)} %constant_dynamic-update-slice_fusion.14), kind=kOutput, calls=%fused_computation.116 | convolution fusion | flops 2148007936 | bytes 10485760 | tf_op jit(solution)/shard_map/dot_general | solution.py:87
  140.7 4.2 all-to-all-start.2
  145.0 11.1 %fusion.63 = bf16[1,2048,256]{1,2,0:T(8,128)(2,1)S(1)} fusion(bf16[2048,2048]{1,0:T(8,128)(2,1)} %param.11, bf16[2048,256]{1,0:T(8,128)(2,1)S(1)} %bitcast.359, f32[]{:T(128)} %bitcast.25, f32[256]{0:T(256)S(1)} %dynamic_slice.114, f32[2048]{0:T(1024)S(1)} %copy-done.10), kind=kOutput, calls=%fused_computation.123 | convolution fusion | flops 4297588736 | bytes 10494980 | tf_op jit(solution)/shard_map/yj,kji->kyi/dot_general | solution.py:101
  160.4 4.4 all-to-all-start.1
  164.8 11.3 %fusion.64 = bf16[1,2048,256]{1,2,0:T(8,128)(2,1)S(1)} fusion(bf16[2048,2048]{1,0:T(8,128)(2,1)} %param.11, bf16[2048,256]{1,0:T(8,128)(2,1)} %bitcast.44, f32[]{:T(128)} %bitcast.47, f32[256]{0:T(256)S(1)} %dynamic_slice.114, f32[2048]{0:T(1024)S(1)} %copy-done.10), kind=kOutput, calls=%fused_computation.124 | convolution fusion | flops 4297588736 | bytes 10494980 | tf_op jit(solution)/shard_map/yj,kji->kyi/dot_general | solution.py:101
  184.2 6.1 %fusion.62 = bf16[1,258,2048]{2,1,0:T(8,128)(2,1)S(1)} fusion(bf16[8,256,2048]{2,1,0:T(8,128)(2,1)} %bitcast.364, bf16[8,1,258,256]{3,2,1,0:T(8,128)(2,1)} %all-to-all-done.1), kind=kOutput, calls=%fused_computation.122 | convolution fusion | flops 2164789248 | bytes 10502144 | tf_op jit(solution)/shard_map/qkyi,qix->kyx/dot_general | solution.py:109
  196.1 3.7 all-to-all-done.3
  199.8 5.8 %fusion.61 = bf16[1,258,2048]{2,1,0:T(8,128)(2,1)S(1)} fusion(bf16[8,256,2048]{2,1,0:T(8,128)(2,1)} %bitcast.365, bf16[8,1,258,256]{3,2,1,0:T(8,128)(2,1)S(1)} %all-to-all-done.3), kind=kOutput, calls=%fused_computation.121 | convolution fusion | flops 2164789248 | bytes 10502144 | tf_op jit(solution)/shard_map/qkyi,qix->kyx/dot_general | solution.py:109
  212.8 11.9 %collective-permute-done.8 = bf16[1,258,514]{2,1,0:T(8,128)(2,1)} collective-permute-done((bf16[1,258,514]{2,1,0:T(8,128)(2,1)S(1)}, bf16[1,258,514]{2,1,0:T(8,128)(2,1)}, u32[]{:S(2)}, u32[]{:S(2)}) %collective-permute-start.8) | collective-permute-done | bytes 265256 | tf_op jit(solution)/shard_map/ppermute | solution.py:142
  227.1 6.4 %collective-permute-done.13 = bf16[1,258,514]{2,1,0:T(8,128)(2,1)S(1)} collective-permute-done((bf16[1,258,514]{2,1,0:T(8,128)(2,1)S(1)}, bf16[1,258,514]{2,1,0:T(8,128)(2,1)S(1)}, u32[]{:S(2)}, u32[]{:S(2)}) %collective-permute-start.13) | collective-permute-done | bytes 265256 | tf_op jit(solution)/shard_map/ppermute | solution.py:142
  233.5 19.8 %collective-permute-done.14 = bf16[1,258,514]{2,1,0:T(8,128)(2,1)S(1)} collective-permute-done((bf16[1,258,514]{2,1,0:T(8,128)(2,1)S(1)}, bf16[1,258,514]{2,1,0:T(8,128)(2,1)S(1)}, u32[]{:S(2)}, u32[]{:S(2)}) %collective-permute-start.14) | collective-permute-done | bytes 265256 | tf_op jit(solution)/shard_map/ppermute | solution.py:142
  256.4 5.9 %fusion.46 = f32[7,256,512]{2,1,0:T(8,128)} fusion(f32[8,258,514]{2,1,0:T(8,128)S(1)} %fusion.54, f32[8,258,514]{2,1,0:T(8,128)S(1)} %bitcast.355), kind=kLoop, calls=%fused_computation.80 | loop fusion | flops 3670016 | bytes 18350080 | tf_op jit(solution)/shard_map/mul | solution.py:54
  262.3 14.5 %fusion.8 = (f32[]{:T(128)}, f32[]{:T(128)}, f32[8,256,512]{2,1,0:T(8,128)}, bf16[8,256,512]{2,1,0:T(8,128)(2,1)}) fusion(f32[8,256,512]{2,1,0:T(8,128)} %copy-done.1, f32[7,256,512]{2,1,0:T(8,128)} %fusion.46, f32[8,258,514]{2,1,0:T(8,128)S(1)} %fusion.54, f32[8,258,514]{2,1,0:T(8,128)S(1)} %bitcast.355, bf16[4,258,514]{2,1,0:T(8,128)(2,1)} %copy-done.6, ...), kind=kLoop, calls=%fused_computation.21 | loop fusion | flops 28311552 | bytes 58220616 | tf_op jit(solution)/shard_map/reduce_sum | solution.py:170
  278.1 10.4 %all_to_all.52 = f32[32,1,2]{2,1,0:T(1,128)S(1)} all-to-all(f32[32,1,2]{2,1,0:T(1,128)S(1)} %broadcast_in_dim.93), channel_id=1, replica_groups=mesh['px'=4,'py'=8] {'px','py'}, dimensions={0} | all-to-all | bytes 512 | tf_op jit(solution)/shard_map/all_to_all | solution.py:41
  290.5 4.5 multiply_subtract_fusion.1
  299.2 7.3 %collective-permute-done.16 = bf16[1,256,512]{2,1,0:T(8,128)(2,1)S(1)} collective-permute-done((bf16[1,256,512]{2,1,0:T(8,128)(2,1)S(1)}, bf16[1,256,512]{2,1,0:T(8,128)(2,1)S(1)}, u32[]{:S(2)}, u32[]{:S(2)}) %collective-permute-start.16) | collective-permute-done | bytes 262176 | tf_op jit(solution)/shard_map/ppermute | solution.py:76
  306.5 10.2 %collective-permute-done.17 = bf16[1,256,512]{2,1,0:T(8,128)(2,1)S(1)} collective-permute-done((bf16[1,256,512]{2,1,0:T(8,128)(2,1)S(1)}, bf16[1,256,512]{2,1,0:T(8,128)(2,1)S(1)}, u32[]{:S(2)}, u32[]{:S(2)}) %collective-permute-start.17) | collective-permute-done | bytes 262176 | tf_op jit(solution)/shard_map/ppermute | solution.py:76
  317.9 5.0 collective-permute-start.24
  325.0 5.7 %convolution_convert_fusion.3 = bf16[256,2048]{1,0:T(8,128)(2,1)S(1)} fusion(bf16[2048,2048]{1,0:T(8,128)(2,1)} %param.11, bf16[1,256,2048]{2,1,0:T(8,128)(2,1)S(1)} %constant_dynamic-update-slice_fusion.8), kind=kOutput, calls=%fused_computation.114 | convolution fusion | flops 2148007936 | bytes 10485760 | tf_op jit(solution)/shard_map/dot_general | solution.py:87
  335.4 4.9 collective-permute-done.22
  340.3 6.5 %collective-permute-done.23 = bf16[1,256,512]{2,1,0:T(8,128)(2,1)S(1)} collective-permute-done((bf16[1,256,512]{2,1,0:T(8,128)(2,1)S(1)}, bf16[1,256,512]{2,1,0:T(8,128)(2,1)S(1)}, u32[]{:S(2)}, u32[]{:S(2)}) %collective-permute-start.23) | collective-permute-done | bytes 262176 | tf_op jit(solution)/shard_map/ppermute | solution.py:76
  346.9 5.7 %convolution_convert_fusion.1 = bf16[256,2048]{1,0:T(8,128)(2,1)S(1)} fusion(bf16[2048,2048]{1,0:T(8,128)(2,1)} %param.11, bf16[1,256,2048]{2,1,0:T(8,128)(2,1)S(1)} %constant_dynamic-update-slice_fusion), kind=kOutput, calls=%fused_computation.112 | convolution fusion | flops 2148007936 | bytes 10485760 | tf_op jit(solution)/shard_map/dot_general | solution.py:87
  353.7 4.2 all-to-all-start.7
  357.9 11.1 %fusion.65 = bf16[1,2048,256]{1,2,0:T(8,128)(2,1)S(1)} fusion(bf16[2048,2048]{1,0:T(8,128)(2,1)} %param.11, bf16[2048,256]{1,0:T(8,128)(2,1)S(1)} %bitcast.358, f32[]{:T(128)} %bitcast.25, f32[256]{0:T(256)S(1)} %dynamic_slice.114, f32[2048]{0:T(1024)S(1)} %copy-done.10), kind=kOutput, calls=%fused_computation.125 | convolution fusion | flops 4297588736 | bytes 10494980 | tf_op jit(solution)/shard_map/yj,kji->kyi/dot_general | solution.py:101
  373.3 4.4 all-to-all-start.6
  377.8 11.3 %fusion.66 = bf16[1,2048,256]{1,2,0:T(8,128)(2,1)S(1)} fusion(bf16[2048,2048]{1,0:T(8,128)(2,1)} %param.11, bf16[2048,256]{1,0:T(8,128)(2,1)} %bitcast.89, f32[]{:T(128)} %bitcast.47, f32[256]{0:T(256)S(1)} %dynamic_slice.114, f32[2048]{0:T(1024)S(1)} %copy-done.10), kind=kOutput, calls=%fused_computation.126 | convolution fusion | flops 4297588736 | bytes 10494980 | tf_op jit(solution)/shard_map/yj,kji->kyi/dot_general | solution.py:101
  397.1 6.1 %fusion.60 = bf16[1,258,2048]{2,1,0:T(8,128)(2,1)S(1)} fusion(bf16[8,256,2048]{2,1,0:T(8,128)(2,1)} %bitcast.366, bf16[8,1,258,256]{3,2,1,0:T(8,128)(2,1)} %all-to-all-done.6), kind=kOutput, calls=%fused_computation.120 | convolution fusion | flops 2164789248 | bytes 10502144 | tf_op jit(solution)/shard_map/qkyi,qix->kyx/dot_general | solution.py:109
  407.1 5.7 %all-to-all-done.8 = bf16[8,1,258,256]{3,2,1,0:T(8,128)(2,1)S(1)} async-done(((bf16[8,1,258,256]{3,2,1,0:T(8,128)(2,1)}), bf16[8,1,258,256]{3,2,1,0:T(8,128)(2,1)S(1)}, u32[]{:S(2)}, u32[]{:S(2)}) %all-to-all-start.8) | async-done | bytes 1056800 | tf_op jit(solution)/shard_map/all_to_all | solution.py:108
  412.8 5.8 %fusion.59 = bf16[1,258,2048]{2,1,0:T(8,128)(2,1)S(1)} fusion(bf16[8,256,2048]{2,1,0:T(8,128)(2,1)} %bitcast.367, bf16[8,1,258,256]{3,2,1,0:T(8,128)(2,1)S(1)} %all-to-all-done.8), kind=kOutput, calls=%fused_computation.119 | convolution fusion | flops 2164789248 | bytes 10502144 | tf_op jit(solution)/shard_map/qkyi,qix->kyx/dot_general | solution.py:109
  425.1 10.6 %collective-permute-done.20 = bf16[1,258,514]{2,1,0:T(8,128)(2,1)} collective-permute-done((bf16[1,258,514]{2,1,0:T(8,128)(2,1)S(1)}, bf16[1,258,514]{2,1,0:T(8,128)(2,1)}, u32[]{:S(2)}, u32[]{:S(2)}) %collective-permute-start.20) | collective-permute-done | bytes 265256 | tf_op jit(solution)/shard_map/ppermute | solution.py:142
  437.8 6.5 %collective-permute-done.25 = bf16[1,258,514]{2,1,0:T(8,128)(2,1)S(1)} collective-permute-done((bf16[1,258,514]{2,1,0:T(8,128)(2,1)S(1)}, bf16[1,258,514]{2,1,0:T(8,128)(2,1)S(1)}, u32[]{:S(2)}, u32[]{:S(2)}) %collective-permute-start.25) | collective-permute-done | bytes 265256 | tf_op jit(solution)/shard_map/ppermute | solution.py:142
  444.3 20.0 %collective-permute-done.26 = bf16[1,258,514]{2,1,0:T(8,128)(2,1)S(1)} collective-permute-done((bf16[1,258,514]{2,1,0:T(8,128)(2,1)S(1)}, bf16[1,258,514]{2,1,0:T(8,128)(2,1)S(1)}, u32[]{:S(2)}, u32[]{:S(2)}) %collective-permute-start.26) | collective-permute-done | bytes 265256 | tf_op jit(solution)/shard_map/ppermute | solution.py:142
  467.5 5.9 %fusion.45 = f32[7,256,512]{2,1,0:T(8,128)} fusion(f32[8,258,514]{2,1,0:T(8,128)S(1)} %fusion.53, f32[8,258,514]{2,1,0:T(8,128)S(1)} %bitcast.357), kind=kLoop, calls=%fused_computation.78 | loop fusion | flops 3670016 | bytes 18350080 | tf_op jit(solution)/shard_map/mul | solution.py:54
  473.3 15.5 %fusion.6 = (f32[]{:T(128)}, f32[]{:T(128)}, f32[]{:T(128)}, f32[]{:T(128)}, f32[8,256,512]{2,1,0:T(8,128)}, /*index=5*/bf16[8,256,512]{2,1,0:T(8,128)(2,1)}) fusion(bf16[8,256,512]{2,1,0:T(8,128)(2,1)} %get-tuple-element.29, f32[8,256,512]{2,1,0:T(8,128)} %copy-done.2, f32[8,256,512]{2,1,0:T(8,128)} %get-tuple-element.28, f32[7,256,512]{2,1,0:T(8,128)} %fusion.45, ...), kind=kLoop, calls=%fused_computation.19 | loop fusion | flops 33554432 | bytes 64512080 | tf_op jit(solution)/shard_map/reduce_sum | solution.py:178
  491.5 12.6 %all_to_all.53 = f32[32,1,4]{2,1,0:T(1,128)S(1)} all-to-all(f32[32,1,4]{2,1,0:T(1,128)S(1)} %broadcast_in_dim.94), channel_id=1, replica_groups=mesh['px'=4,'py'=8] {'px','py'}, dimensions={0} | all-to-all | bytes 1024 | tf_op jit(solution)/shard_map/all_to_all | solution.py:41
  508.9 12.8 %fusion.11 = (f32[8,256,512]{2,1,0:T(8,128)}, f32[8,256,512]{2,1,0:T(8,128)}, f32[8,256,512]{2,1,0:T(8,128)}) fusion(f32[8,256,512]{2,1,0:T(8,128)} %param.8, bf16[8,256,512]{2,1,0:T(8,128)(2,1)} %get-tuple-element.29, f32[]{:T(128)S(6)} %div.27, f32[]{:T(128)S(6)} %div.23, f32[]{:T(128)S(6)} %div.26, bf16[8,256,512]{2,1,0:T(8,128)(2,1)} %get-tuple-element.27, ...), kind=kLoop, calls=%fused_computation.24 | loop fusion | flops 12582912 | bytes 33554444 | tf_op jit(solution)/shard_map/add | solution.py:190
  (185 shorter events, 116.3 us)
Async XLA Ops:
  2.6 3.5 copy-start.8
  20.6 5.3 %copy-start.3 = (bf16[1,8,256,512]{3,2,1,0:T(8,128)(2,1)}, bf16[1,8,256,512]{3,2,1,0:T(8,128)(2,1)S(1)}, u32[]{:S(2)}) copy-start(bf16[1,8,256,512]{3,2,1,0:T(8,128)(2,1)S(1)} %fusion.77) | copy-start | bytes 6291460
  20.6 18.4 %collective-permute-start = (bf16[2,8,1,512]{3,2,1,0:T(2,128)(2,1)S(1)}, bf16[2,8,1,512]{3,2,1,0:T(2,128)(2,1)S(1)}, u32[]{:S(2)}, u32[]{:S(2)}) collective-permute-start(bf16[2,8,1,512]{3,2,1,0:T(2,128)(2,1)S(1)} %get-tuple-element.34), channel_id=1, source_target_pairs={{0,1},{1,2},{2,3},{3,4},{4,5},{5,6},{6,7},{8,9},{9,10},{10,11},{11... | collective-permute-start | bytes 49160 | tf_op jit(solution)/shard_map/ppermute | solution.py:17
  23.0 16.0 %collective-permute-start.3 = (bf16[2,8,1,512]{3,2,1,0:T(2,128)(2,1)S(1)}, bf16[2,8,1,512]{3,2,1,0:T(2,128)(2,1)S(1)}, u32[]{:S(2)}, u32[]{:S(2)}) collective-permute-start(bf16[2,8,1,512]{3,2,1,0:T(2,128)(2,1)S(1)} %get-tuple-element.35), channel_id=1, source_target_pairs={{1,0},{2,1},{3,2},{4,3},{5,4},{6,5},{7,6},{9,8},{10,9},{11,10},{12... | collective-permute-start | bytes 49160 | tf_op jit(solution)/shard_map/ppermute | solution.py:17
  27.4 6.4 %collective-permute-start.1 = (bf16[2,8,256,1]{2,1,3,0:T(8,128)(2,1)S(1)}, bf16[2,8,256,1]{2,1,3,0:T(8,128)(2,1)S(1)}, u32[]{:S(2)}, u32[]{:S(2)}) collective-permute-start(bf16[2,8,256,1]{2,1,3,0:T(8,128)(2,1)S(1)} %copy.92), channel_id=1, source_target_pairs={{0,8},{8,16},{16,24},{1,9},{9,17},{17,25},{2,10},{10,18},{18,26},{... | collective-permute-start | bytes 24584 | tf_op jit(solution)/shard_map/ppermute | solution.py:17
  32.1 5.5 %collective-permute-start.2 = (bf16[2,8,256,1]{2,1,3,0:T(8,128)(2,1)S(1)}, bf16[2,8,256,1]{2,1,3,0:T(8,128)(2,1)S(1)}, u32[]{:S(2)}, u32[]{:S(2)}) collective-permute-start(bf16[2,8,256,1]{2,1,3,0:T(8,128)(2,1)S(1)} %copy.93), channel_id=1, source_target_pairs={{8,0},{16,8},{24,16},{9,1},{17,9},{25,17},{10,2},{18,10},{26,18},{... | collective-permute-start | bytes 24584 | tf_op jit(solution)/shard_map/ppermute | solution.py:17
  57.2 5.9 %copy-start = (f32[8,258,514]{2,1,0:T(8,128)}, f32[8,258,514]{2,1,0:T(8,128)S(1)}, u32[]{:S(2)}) copy-start(f32[8,258,514]{2,1,0:T(8,128)S(1)} %get-tuple-element.30) | copy-start | bytes 12730756
  74.4 2.0 copy-start.1
  76.4 6.5 %copy-start.10 = (f32[2048]{0:T(1024)S(1)}, f32[2048]{0:T(1024)}, u32[]{:S(2)}) copy-start(f32[2048]{0:T(1024)} %param.12) | copy-start | bytes 24580
  76.4 6.6 %copy-start.9 = (f32[8]{0:T(128)S(1)}, f32[8]{0:T(128)}, u32[]{:S(2)}) copy-start(f32[8]{0:T(128)} %param.13) | copy-start | bytes 100
  76.7 11.2 %collective-permute-start.4 = (bf16[1,256,512]{2,1,0:T(8,128)(2,1)S(1)}, bf16[1,256,512]{2,1,0:T(8,128)(2,1)S(1)}, u32[]{:S(2)}, u32[]{:S(2)}) collective-permute-start(bf16[1,256,512]{2,1,0:T(8,128)(2,1)S(1)} %get-tuple-element.66), channel_id=1, source_target_pairs={{0,8},{8,16},{16,24},{24,0},{1,9},{9,17},{17,25},{25,1},{2,10},{10... | collective-permute-start | bytes 786440 | tf_op jit(solution)/shard_map/ppermute | solution.py:76
  78.4 20.7 %collective-permute-start.5 = (bf16[1,256,512]{2,1,0:T(8,128)(2,1)S(1)}, bf16[1,256,512]{2,1,0:T(8,128)(2,1)S(1)}, u32[]{:S(2)}, u32[]{:S(2)}) collective-permute-start(bf16[1,256,512]{2,1,0:T(8,128)(2,1)S(1)} %get-tuple-element.65), channel_id=1, source_target_pairs={{0,16},{8,24},{16,0},{24,8},{1,17},{9,25},{17,1},{25,9},{2,18},{10... | collective-permute-start | bytes 786440 | tf_op jit(solution)/shard_map/ppermute | solution.py:76
  79.5 19.6 %collective-permute-start.6 = (bf16[1,256,512]{2,1,0:T(8,128)(2,1)S(1)}, bf16[1,256,512]{2,1,0:T(8,128)(2,1)S(1)}, u32[]{:S(2)}, u32[]{:S(2)}) collective-permute-start(bf16[1,256,512]{2,1,0:T(8,128)(2,1)S(1)} %get-tuple-element.64), channel_id=1, source_target_pairs={{0,24},{8,0},{16,8},{24,16},{1,25},{9,1},{17,9},{25,17},{2,26},{10... | collective-permute-start | bytes 786440 | tf_op jit(solution)/shard_map/ppermute | solution.py:76
  101.9 32.0 %collective-permute-start.12 = (bf16[1,256,512]{2,1,0:T(8,128)(2,1)}, bf16[1,256,512]{2,1,0:T(8,128)(2,1)S(1)}, u32[]{:S(2)}, u32[]{:S(2)}) collective-permute-start(bf16[1,256,512]{2,1,0:T(8,128)(2,1)} %get-tuple-element.60), channel_id=1, source_target_pairs={{0,24},{8,0},{16,8},{24,16},{1,25},{9,1},{17,9},{25,17},{2,26},{10... | collective-permute-start | bytes 786440 | tf_op jit(solution)/shard_map/ppermute | solution.py:76
  109.2 23.8 %collective-permute-start.11 = (bf16[1,256,512]{2,1,0:T(8,128)(2,1)}, bf16[1,256,512]{2,1,0:T(8,128)(2,1)}, u32[]{:S(2)}, u32[]{:S(2)}) collective-permute-start(bf16[1,256,512]{2,1,0:T(8,128)(2,1)} %get-tuple-element.61), channel_id=1, source_target_pairs={{0,16},{8,24},{16,0},{24,8},{1,17},{9,25},{17,1},{25,9},{2,18},{10... | collective-permute-start | bytes 786440 | tf_op jit(solution)/shard_map/ppermute | solution.py:76
  109.5 17.9 %collective-permute-start.10 = (bf16[1,256,512]{2,1,0:T(8,128)(2,1)}, bf16[1,256,512]{2,1,0:T(8,128)(2,1)}, u32[]{:S(2)}, u32[]{:S(2)}) collective-permute-start(bf16[1,256,512]{2,1,0:T(8,128)(2,1)} %get-tuple-element.62), channel_id=1, source_target_pairs={{0,8},{8,16},{16,24},{24,0},{1,9},{9,17},{17,25},{25,1},{2,10},{10... | collective-permute-start | bytes 786440 | tf_op jit(solution)/shard_map/ppermute | solution.py:76
  116.5 24.2 %all-to-all-start = ((bf16[8,256,256]{2,1,0:T(8,128)(2,1)}), bf16[8,256,256]{2,1,0:T(8,128)(2,1)S(1)}, u32[]{:S(2)}, u32[]{:S(2)}) async-start(bf16[8,256,256]{2,1,0:T(8,128)(2,1)} %bitcast.353), calls=%async_computation | async-start | bytes 2097152 | tf_op jit(solution)/shard_map/all_to_all | solution.py:91
  140.7 19.7 %all-to-all-start.2 = ((bf16[8,256,256]{2,1,0:T(8,128)(2,1)}), bf16[8,256,256]{2,1,0:T(8,128)(2,1)}, u32[]{:S(2)}, u32[]{:S(2)}) async-start(bf16[8,256,256]{2,1,0:T(8,128)(2,1)} %bitcast.351), calls=%async_computation.2 | async-start | bytes 2097152 | tf_op jit(solution)/shard_map/all_to_all | solution.py:91
  160.4 20.2 %all-to-all-start.1 = ((bf16[8,1,258,256]{3,2,1,0:T(8,128)(2,1)}), bf16[8,1,258,256]{3,2,1,0:T(8,128)(2,1)}, u32[]{:S(2)}, u32[]{:S(2)}) async-start(bf16[8,1,258,256]{3,2,1,0:T(8,128)(2,1)} %copy.97), calls=%async_computation.1 | async-start | bytes 2162688 | tf_op jit(solution)/shard_map/all_to_all | solution.py:108
  180.6 19.3 %all-to-all-start.3 = ((bf16[8,1,258,256]{3,2,1,0:T(8,128)(2,1)}), bf16[8,1,258,256]{3,2,1,0:T(8,128)(2,1)S(1)}, u32[]{:S(2)}, u32[]{:S(2)}) async-start(bf16[8,1,258,256]{3,2,1,0:T(8,128)(2,1)} %copy.99), calls=%async_computation.3 | async-start | bytes 2162688 | tf_op jit(solution)/shard_map/all_to_all | solution.py:108
  191.3 34.6 %collective-permute-start.9 = (bf16[1,258,514]{2,1,0:T(8,128)(2,1)S(1)}, bf16[1,258,514]{2,1,0:T(8,128)(2,1)}, u32[]{:S(2)}, u32[]{:S(2)}) collective-permute-start(bf16[1,258,514]{2,1,0:T(8,128)(2,1)S(1)} %get-tuple-element.44), channel_id=1, source_target_pairs={{0,24},{8,0},{16,8},{24,16},{1,25},{9,1},{17,9},{25,17},{2,26},{10... | collective-permute-start | bytes 795680 | tf_op jit(solution)/shard_map/ppermute | solution.py:142
  191.3 20.4 %collective-permute-start.7 = (bf16[1,258,514]{2,1,0:T(8,128)(2,1)S(1)}, bf16[1,258,514]{2,1,0:T(8,128)(2,1)}, u32[]{:S(2)}, u32[]{:S(2)}) collective-permute-start(bf16[1,258,514]{2,1,0:T(8,128)(2,1)S(1)} %get-tuple-element.45), channel_id=1, source_target_pairs={{0,8},{8,16},{16,24},{24,0},{1,9},{9,17},{17,25},{25,1},{2,10},{10... | collective-permute-start | bytes 795680 | tf_op jit(solution)/shard_map/ppermute | solution.py:142
  193.4 31.3 %collective-permute-start.8 = (bf16[1,258,514]{2,1,0:T(8,128)(2,1)S(1)}, bf16[1,258,514]{2,1,0:T(8,128)(2,1)}, u32[]{:S(2)}, u32[]{:S(2)}) collective-permute-start(bf16[1,258,514]{2,1,0:T(8,128)(2,1)S(1)} %get-tuple-element.46), channel_id=1, source_target_pairs={{0,16},{8,24},{16,0},{24,8},{1,17},{9,25},{17,1},{25,9},{2,18},{10... | collective-permute-start | bytes 795680 | tf_op jit(solution)/shard_map/ppermute | solution.py:142
  206.6 46.7 %collective-permute-start.15 = (bf16[1,258,514]{2,1,0:T(8,128)(2,1)S(1)}, bf16[1,258,514]{2,1,0:T(8,128)(2,1)S(1)}, u32[]{:S(2)}, u32[]{:S(2)}) collective-permute-start(bf16[1,258,514]{2,1,0:T(8,128)(2,1)S(1)} %get-tuple-element.48), channel_id=1, source_target_pairs={{0,24},{8,0},{16,8},{24,16},{1,25},{9,1},{17,9},{25,17},{2,26},{10... | collective-permute-start | bytes 795680 | tf_op jit(solution)/shard_map/ppermute | solution.py:142
  206.7 26.8 %collective-permute-start.13 = (bf16[1,258,514]{2,1,0:T(8,128)(2,1)S(1)}, bf16[1,258,514]{2,1,0:T(8,128)(2,1)S(1)}, u32[]{:S(2)}, u32[]{:S(2)}) collective-permute-start(bf16[1,258,514]{2,1,0:T(8,128)(2,1)S(1)} %get-tuple-element.49), channel_id=1, source_target_pairs={{0,8},{8,16},{16,24},{24,0},{1,9},{9,17},{17,25},{25,1},{2,10},{10... | collective-permute-start | bytes 795680 | tf_op jit(solution)/shard_map/ppermute | solution.py:142
  211.8 41.5 %collective-permute-start.14 = (bf16[1,258,514]{2,1,0:T(8,128)(2,1)S(1)}, bf16[1,258,514]{2,1,0:T(8,128)(2,1)S(1)}, u32[]{:S(2)}, u32[]{:S(2)}) collective-permute-start(bf16[1,258,514]{2,1,0:T(8,128)(2,1)S(1)} %get-tuple-element.50), channel_id=1, source_target_pairs={{0,16},{8,24},{16,0},{24,8},{1,17},{9,25},{17,1},{25,9},{2,18},{10... | collective-permute-start | bytes 795680 | tf_op jit(solution)/shard_map/ppermute | solution.py:142
  224.7 31.7 %slice-start = ((s8[5406720]{0:T(1024)(128)(4,1)}), s8[4194304]{0:T(1024)(128)(4,1)S(1)}, s32[]{:S(2)}) async-start(s8[5406720]{0:T(1024)(128)(4,1)} %bitcast.354), calls=%async_computation.10 | async-start | bytes 8388608
  227.0 26.3 %copy-start.5 = (bf16[4,258,514]{2,1,0:T(8,128)(2,1)}, bf16[4,258,514]{2,1,0:T(8,128)(2,1)S(1)}, u32[]{:S(2)}) copy-start(bf16[4,258,514]{2,1,0:T(8,128)(2,1)S(1)} %constant_dynamic-update-slice_fusion.17) | copy-start | bytes 3182692
  254.5 1.9 slice-start.1
  295.0 21.8 %copy-start.2 = (f32[8,256,512]{2,1,0:T(8,128)}, f32[8,256,512]{2,1,0:T(8,128)S(1)}, u32[]{:S(2)}) copy-start(f32[8,256,512]{2,1,0:T(8,128)S(1)} %multiply_subtract_fusion.1) | copy-start | bytes 12582916
  295.3 11.1 %collective-permute-start.16 = (bf16[1,256,512]{2,1,0:T(8,128)(2,1)S(1)}, bf16[1,256,512]{2,1,0:T(8,128)(2,1)S(1)}, u32[]{:S(2)}, u32[]{:S(2)}) collective-permute-start(bf16[1,256,512]{2,1,0:T(8,128)(2,1)S(1)} %get-tuple-element.58), channel_id=1, source_target_pairs={{0,8},{8,16},{16,24},{24,0},{1,9},{9,17},{17,25},{25,1},{2,10},{10... | collective-permute-start | bytes 786440 | tf_op jit(solution)/shard_map/ppermute | solution.py:76
  296.0 20.7 %collective-permute-start.17 = (bf16[1,256,512]{2,1,0:T(8,128)(2,1)S(1)}, bf16[1,256,512]{2,1,0:T(8,128)(2,1)S(1)}, u32[]{:S(2)}, u32[]{:S(2)}) collective-permute-start(bf16[1,256,512]{2,1,0:T(8,128)(2,1)S(1)} %get-tuple-element.57), channel_id=1, source_target_pairs={{0,16},{8,24},{16,0},{24,8},{1,17},{9,25},{17,1},{25,9},{2,18},{10... | collective-permute-start | bytes 786440 | tf_op jit(solution)/shard_map/ppermute | solution.py:76
  296.5 20.2 %collective-permute-start.18 = (bf16[1,256,512]{2,1,0:T(8,128)(2,1)S(1)}, bf16[1,256,512]{2,1,0:T(8,128)(2,1)S(1)}, u32[]{:S(2)}, u32[]{:S(2)}) collective-permute-start(bf16[1,256,512]{2,1,0:T(8,128)(2,1)S(1)} %get-tuple-element.56), channel_id=1, source_target_pairs={{0,24},{8,0},{16,8},{24,16},{1,25},{9,1},{17,9},{25,17},{2,26},{10... | collective-permute-start | bytes 786440 | tf_op jit(solution)/shard_map/ppermute | solution.py:76
  317.9 29.0 %collective-permute-start.24 = (bf16[1,256,512]{2,1,0:T(8,128)(2,1)S(1)}, bf16[1,256,512]{2,1,0:T(8,128)(2,1)S(1)}, u32[]{:S(2)}, u32[]{:S(2)}) collective-permute-start(bf16[1,256,512]{2,1,0:T(8,128)(2,1)S(1)} %get-tuple-element.52), channel_id=1, source_target_pairs={{0,24},{8,0},{16,8},{24,16},{1,25},{9,1},{17,9},{25,17},{2,26},{10... | collective-permute-start | bytes 786440 | tf_op jit(solution)/shard_map/ppermute | solution.py:76
  322.8 24.0 %collective-permute-start.23 = (bf16[1,256,512]{2,1,0:T(8,128)(2,1)S(1)}, bf16[1,256,512]{2,1,0:T(8,128)(2,1)S(1)}, u32[]{:S(2)}, u32[]{:S(2)}) collective-permute-start(bf16[1,256,512]{2,1,0:T(8,128)(2,1)S(1)} %get-tuple-element.53), channel_id=1, source_target_pairs={{0,16},{8,24},{16,0},{24,8},{1,17},{9,25},{17,1},{25,9},{2,18},{10... | collective-permute-start | bytes 786440 | tf_op jit(solution)/shard_map/ppermute | solution.py:76
  324.6 15.7 %collective-permute-start.22 = (bf16[1,256,512]{2,1,0:T(8,128)(2,1)}, bf16[1,256,512]{2,1,0:T(8,128)(2,1)S(1)}, u32[]{:S(2)}, u32[]{:S(2)}) collective-permute-start(bf16[1,256,512]{2,1,0:T(8,128)(2,1)} %get-tuple-element.54), channel_id=1, source_target_pairs={{0,8},{8,16},{16,24},{24,0},{1,9},{9,17},{17,25},{25,1},{2,10},{10... | collective-permute-start | bytes 786440 | tf_op jit(solution)/shard_map/ppermute | solution.py:76
  331.8 21.8 %all-to-all-start.5 = ((bf16[8,256,256]{2,1,0:T(8,128)(2,1)}), bf16[8,256,256]{2,1,0:T(8,128)(2,1)S(1)}, u32[]{:S(2)}, u32[]{:S(2)}) async-start(bf16[8,256,256]{2,1,0:T(8,128)(2,1)} %bitcast.349), calls=%async_computation.5 | async-start | bytes 2097152 | tf_op jit(solution)/shard_map/all_to_all | solution.py:91
  353.7 19.7 %all-to-all-start.7 = ((bf16[8,256,256]{2,1,0:T(8,128)(2,1)}), bf16[8,256,256]{2,1,0:T(8,128)(2,1)}, u32[]{:S(2)}, u32[]{:S(2)}) async-start(bf16[8,256,256]{2,1,0:T(8,128)(2,1)} %bitcast.347), calls=%async_computation.7 | async-start | bytes 2097152 | tf_op jit(solution)/shard_map/all_to_all | solution.py:91
  373.3 20.2 %all-to-all-start.6 = ((bf16[8,1,258,256]{3,2,1,0:T(8,128)(2,1)}), bf16[8,1,258,256]{3,2,1,0:T(8,128)(2,1)}, u32[]{:S(2)}, u32[]{:S(2)}) async-start(bf16[8,1,258,256]{3,2,1,0:T(8,128)(2,1)} %copy.102), calls=%async_computation.6 | async-start | bytes 2162688 | tf_op jit(solution)/shard_map/all_to_all | solution.py:108
  393.5 19.3 %all-to-all-start.8 = ((bf16[8,1,258,256]{3,2,1,0:T(8,128)(2,1)}), bf16[8,1,258,256]{3,2,1,0:T(8,128)(2,1)S(1)}, u32[]{:S(2)}, u32[]{:S(2)}) async-start(bf16[8,1,258,256]{3,2,1,0:T(8,128)(2,1)} %copy.104), calls=%async_computation.8 | async-start | bytes 2162688 | tf_op jit(solution)/shard_map/all_to_all | solution.py:108
  404.2 32.6 %collective-permute-start.21 = (bf16[1,258,514]{2,1,0:T(8,128)(2,1)S(1)}, bf16[1,258,514]{2,1,0:T(8,128)(2,1)}, u32[]{:S(2)}, u32[]{:S(2)}) collective-permute-start(bf16[1,258,514]{2,1,0:T(8,128)(2,1)S(1)} %get-tuple-element.36), channel_id=1, source_target_pairs={{0,24},{8,0},{16,8},{24,16},{1,25},{9,1},{17,9},{25,17},{2,26},{10... | collective-permute-start | bytes 795680 | tf_op jit(solution)/shard_map/ppermute | solution.py:142
  405.1 17.4 %collective-permute-start.19 = (bf16[1,258,514]{2,1,0:T(8,128)(2,1)S(1)}, bf16[1,258,514]{2,1,0:T(8,128)(2,1)}, u32[]{:S(2)}, u32[]{:S(2)}) collective-permute-start(bf16[1,258,514]{2,1,0:T(8,128)(2,1)S(1)} %get-tuple-element.37), channel_id=1, source_target_pairs={{0,8},{8,16},{16,24},{24,0},{1,9},{9,17},{17,25},{25,1},{2,10},{10... | collective-permute-start | bytes 795680 | tf_op jit(solution)/shard_map/ppermute | solution.py:142
  406.2 29.5 %collective-permute-start.20 = (bf16[1,258,514]{2,1,0:T(8,128)(2,1)S(1)}, bf16[1,258,514]{2,1,0:T(8,128)(2,1)}, u32[]{:S(2)}, u32[]{:S(2)}) collective-permute-start(bf16[1,258,514]{2,1,0:T(8,128)(2,1)S(1)} %get-tuple-element.38), channel_id=1, source_target_pairs={{0,16},{8,24},{16,0},{24,8},{1,17},{9,25},{17,1},{25,9},{2,18},{10... | collective-permute-start | bytes 795680 | tf_op jit(solution)/shard_map/ppermute | solution.py:142
  418.7 48.7 %slice-start.2 = ((s8[5406720]{0:T(1024)(128)(4,1)}), s8[4194304]{0:T(1024)(128)(4,1)S(1)}, s32[]{:S(2)}) async-start(s8[5406720]{0:T(1024)(128)(4,1)} %bitcast.356), calls=%async_computation.12 | async-start | bytes 8388608
  419.6 44.8 %collective-permute-start.27 = (bf16[1,258,514]{2,1,0:T(8,128)(2,1)S(1)}, bf16[1,258,514]{2,1,0:T(8,128)(2,1)S(1)}, u32[]{:S(2)}, u32[]{:S(2)}) collective-permute-start(bf16[1,258,514]{2,1,0:T(8,128)(2,1)S(1)} %get-tuple-element.40), channel_id=1, source_target_pairs={{0,24},{8,0},{16,8},{24,16},{1,25},{9,1},{17,9},{25,17},{2,26},{10... | collective-permute-start | bytes 795680 | tf_op jit(solution)/shard_map/ppermute | solution.py:142
  420.5 23.8 %collective-permute-start.25 = (bf16[1,258,514]{2,1,0:T(8,128)(2,1)S(1)}, bf16[1,258,514]{2,1,0:T(8,128)(2,1)S(1)}, u32[]{:S(2)}, u32[]{:S(2)}) collective-permute-start(bf16[1,258,514]{2,1,0:T(8,128)(2,1)S(1)} %get-tuple-element.41), channel_id=1, source_target_pairs={{0,8},{8,16},{16,24},{24,0},{1,9},{9,17},{17,25},{25,1},{2,10},{10... | collective-permute-start | bytes 795680 | tf_op jit(solution)/shard_map/ppermute | solution.py:142
  422.6 41.8 %collective-permute-start.26 = (bf16[1,258,514]{2,1,0:T(8,128)(2,1)S(1)}, bf16[1,258,514]{2,1,0:T(8,128)(2,1)S(1)}, u32[]{:S(2)}, u32[]{:S(2)}) collective-permute-start(bf16[1,258,514]{2,1,0:T(8,128)(2,1)S(1)} %get-tuple-element.42), channel_id=1, source_target_pairs={{0,16},{8,24},{16,0},{24,8},{1,17},{9,25},{17,1},{25,9},{2,18},{10... | collective-permute-start | bytes 795680 | tf_op jit(solution)/shard_map/ppermute | solution.py:142
  437.8 26.6 %copy-start.7 = (bf16[4,258,514]{2,1,0:T(8,128)(2,1)}, bf16[4,258,514]{2,1,0:T(8,128)(2,1)S(1)}, u32[]{:S(2)}) copy-start(bf16[4,258,514]{2,1,0:T(8,128)(2,1)S(1)} %constant_dynamic-update-slice_fusion.4) | copy-start | bytes 3182692
  (3 other events, 4.1 us)

commit v13 on v12

--- a/solution.py
+++ b/solution.py
@@ -151,9 +151,11 @@
 
 
 def shards(right_side, solution_in, classes, coeff_table, eigenvectors, eigenvalues, level_shift):
-    coeff = jnp.zeros(classes.shape, jnp.float32)
+    labels = classes.astype(jnp.bfloat16)
+    table = coeff_table.astype(jnp.bfloat16)
+    coeff = jnp.zeros(classes.shape, jnp.bfloat16)
     for label in range(coeff_table.shape[0]):
-        coeff = jnp.where(classes == label, coeff_table[label], coeff)
+        coeff = jnp.where(labels == label, table[label], coeff)
     stacked = padded_2(
         jnp.stack((solution_in, coeff)).astype(jnp.bfloat16), (("px", 3), ("py", 2)), 1
     ).astype(jnp.float32)

time: 527 us -> 524 us (level)
  no operation moved by 1% of the time
where the time goes in v13:
time: 524 us; the launch traced here: 519 us
  waiting for transfers between devices  155 us (30%)
  other arithmetic  115 us (22%)
  matrix products  91.7 us (18%)
  starting transfers between devices  79.8 us (15%)
  local copies, waits for them, and re-layouts  47.8 us (9%)
  blocking collectives  23 us (4%)
  between operations  7.45 us (1%)
    ppermute x12, waiting for transfers between devices, return_lines(): lax.ppermute(part, 'px', [(i, (i + shift) % size) for i in range(size)])  78.7 us
    ppermute x12, waiting for transfers between devices, exchange(): lax.ppermute(part, axis, [(i, (i + shift) % size) for i in range(size)])  56.2 us
    dot_general x4, matrix products, precondition_lines(): jnp.einsum('yj,kji->kyi', eigenvectors, scaled, preferred_element_type=jn...  44.9 us
    ppermute x12, starting transfers between devices, exchange(): lax.ppermute(part, axis, [(i, (i + shift) % size) for i in range(size)])  24.8 us
    dot_general x4, matrix products, precondition_lines(): jnp.einsum('qkyi,qix->kyx', returned, eigenvectors.reshape(across, cols,...  23.9 us
    all_to_all x2, blocking collectives, all_sum(): return jnp.sum(lax.all_to_all(spread, axes, 0, 0, tiled=True), 0)  23 us
    dot_general x4, matrix products, precondition_lines(): jnp.dot(lines.reshape(levels_here * rows, width), eigenvectors, preferred...  22.9 us
    mul x3, other arithmetic, face_sum(): vertical = 0.5 * (coeff[:-1] + coeff[1:]) * (values[:-1] - values[1:])  17.7 us
  transfers between devices with their start and end apart: 36, of which 23 were waited for; matrix products, arithmetic and copies ran while one was open for 24% of the time, Pallas kernels for 0%

profile of v13, /device:TPU:0, one launch (start us, length us, event | category | flops | bytes accessed | tf_op | source)
XLA Modules:
  0.0 518.9 jit_solution(15351653342805418762)
XLA Ops:
  5.5 12.5 %fusion.77 = bf16[1,8,256,512]{3,2,1,0:T(8,128)(2,1)S(1)} fusion(s32[8,256,512]{2,1,0:T(8,128)S(1)} %copy-done.8, bf16[]{:T(256)} %bitcast.16, bf16[]{:T(256)} %bitcast.15, bf16[]{:T(256)} %bitcast.14, bf16[]{:T(256)} %bitcast.13, bf16[]{:T(256)} %bitcast.12, bf16[]{:T(256)} %bitcast.11, bf16[]{:T(256)} %bitcast.10, bf16[]{:T(256)} %bitcast.9, bf16[]{:T(256)} %bitcast.8, ...), kind=kLoop, calls=%fused_computation.152 | loop fusion | flops 34603008 | bytes 6291488 | tf_op jit(solution)/shard_map/stack | solution.py:160
  24.8 4.3 collective-permute-start.1
  36.4 13.3 %fusion.3 = f32[2,8,258,514]{3,2,1,0:T(8,128)} fusion(bf16[2,8,1,512]{3,2,1,0:T(2,128)(2,1)S(1)} %collective-permute-done.3, bf16[2,8,1,512]{3,2,1,0:T(2,128)(2,1)S(1)} %collective-permute-done, bf16[2,8,256,1]{3,2,1,0:T(8,128)(2,1)} %copy.80, bf16[1,8,256,512]{3,2,1,0:T(8,128)(2,1)} %copy-done.3, bf16[1,8,256,512]{3,2,1,0:T(8,128)(2,1)S(1)} %convert_bitcast_fusion, ...), kind=kLoop, calls=%fused_computation.14 | loop fusion | flops 33948672 | bytes 12730624 | tf_op jit(solution)/shard_map/convert_element_type | solution.py:161
  49.7 4.8 slice_bitcast_fusion.1
  54.6 5.9 %fusion.47 = f32[7,256,512]{2,1,0:T(8,128)} fusion(f32[8,258,514]{2,1,0:T(8,128)S(1)} %get-tuple-element.31, f32[8,258,514]{2,1,0:T(8,128)S(1)} %get-tuple-element.30), kind=kLoop, calls=%fused_computation.97 | loop fusion | flops 3670016 | bytes 18350080 | tf_op jit(solution)/shard_map/mul | solution.py:54
  60.5 11.2 %fusion.35 = f32[8,256,512]{2,1,0:T(8,128)S(1)} fusion(f32[8,256,512]{2,1,0:T(8,128)} %param.7, f32[8,258,514]{2,1,0:T(8,128)S(1)} %get-tuple-element.31, f32[7,256,512]{2,1,0:T(8,128)} %fusion.47, f32[8,258,514]{2,1,0:T(8,128)S(1)} %get-tuple-element.30), kind=kLoop, calls=%fused_computation.57 | loop fusion | flops 23068672 | bytes 54001664 | tf_op jit(solution)/shard_map/sub | solution.py:164
  80.5 4.4 collective-permute-done.4
  84.9 11.1 %collective-permute-done.5 = bf16[1,256,512]{2,1,0:T(8,128)(2,1)S(1)} collective-permute-done((bf16[1,256,512]{2,1,0:T(8,128)(2,1)S(1)}, bf16[1,256,512]{2,1,0:T(8,128)(2,1)S(1)}, u32[]{:S(2)}, u32[]{:S(2)}) %collective-permute-start.5) | collective-permute-done | bytes 262176 | tf_op jit(solution)/shard_map/ppermute | solution.py:76
  98.9 7.2 %collective-permute-start.12 = (bf16[1,256,512]{2,1,0:T(8,128)(2,1)}, bf16[1,256,512]{2,1,0:T(8,128)(2,1)S(1)}, u32[]{:S(2)}, u32[]{:S(2)}) collective-permute-start(bf16[1,256,512]{2,1,0:T(8,128)(2,1)} %get-tuple-element.60), channel_id=1, source_target_pairs={{0,24},{8,0},{16,8},{24,16},{1,25},{9,1},{17,9},{25,17},{2,26},{10... | collective-permute-start | bytes 786440 | tf_op jit(solution)/shard_map/ppermute | solution.py:76
  106.7 5.7 %convolution_convert_fusion.7 = bf16[256,2048]{1,0:T(8,128)(2,1)S(1)} fusion(bf16[2048,2048]{1,0:T(8,128)(2,1)} %param.11, bf16[1,256,2048]{2,1,0:T(8,128)(2,1)S(1)} %constant_dynamic-update-slice_fusion.21), kind=kOutput, calls=%fused_computation.133 | convolution fusion | flops 2148007936 | bytes 10485760 | tf_op jit(solution)/shard_map/dot_general | solution.py:87
  117.0 7.3 %collective-permute-done.10 = bf16[1,256,512]{2,1,0:T(8,128)(2,1)} collective-permute-done((bf16[1,256,512]{2,1,0:T(8,128)(2,1)}, bf16[1,256,512]{2,1,0:T(8,128)(2,1)}, u32[]{:S(2)}, u32[]{:S(2)}) %collective-permute-start.10) | collective-permute-done | bytes 262176 | tf_op jit(solution)/shard_map/ppermute | solution.py:76
  125.3 4.6 collective-permute-done.11
  130.9 5.7 %convolution_convert_fusion.5 = bf16[256,2048]{1,0:T(8,128)(2,1)S(1)} fusion(bf16[2048,2048]{1,0:T(8,128)(2,1)} %param.11, bf16[1,256,2048]{2,1,0:T(8,128)(2,1)S(1)} %constant_dynamic-update-slice_fusion.14), kind=kOutput, calls=%fused_computation.131 | convolution fusion | flops 2148007936 | bytes 10485760 | tf_op jit(solution)/shard_map/dot_general | solution.py:87
  137.7 4.2 all-to-all-start.2
  141.9 11.1 %fusion.63 = bf16[1,2048,256]{1,2,0:T(8,128)(2,1)S(1)} fusion(bf16[2048,2048]{1,0:T(8,128)(2,1)} %param.11, bf16[2048,256]{1,0:T(8,128)(2,1)S(1)} %bitcast.359, f32[]{:T(128)} %bitcast.25, f32[256]{0:T(256)S(1)} %dynamic_slice.114, f32[2048]{0:T(1024)S(1)} %copy-done.10), kind=kOutput, calls=%fused_computation.138 | convolution fusion | flops 4297588736 | bytes 10494980 | tf_op jit(solution)/shard_map/yj,kji->kyi/dot_general | solution.py:101
  157.3 4.4 all-to-all-start.1
  161.8 11.3 %fusion.64 = bf16[1,2048,256]{1,2,0:T(8,128)(2,1)S(1)} fusion(bf16[2048,2048]{1,0:T(8,128)(2,1)} %param.11, bf16[2048,256]{1,0:T(8,128)(2,1)} %bitcast.44, f32[]{:T(128)} %bitcast.47, f32[256]{0:T(256)S(1)} %dynamic_slice.114, f32[2048]{0:T(1024)S(1)} %copy-done.10), kind=kOutput, calls=%fused_computation.139 | convolution fusion | flops 4297588736 | bytes 10494980 | tf_op jit(solution)/shard_map/yj,kji->kyi/dot_general | solution.py:101
  181.2 6.1 %fusion.62 = bf16[1,258,2048]{2,1,0:T(8,128)(2,1)S(1)} fusion(bf16[8,256,2048]{2,1,0:T(8,128)(2,1)} %bitcast.364, bf16[8,1,258,256]{3,2,1,0:T(8,128)(2,1)} %all-to-all-done.1), kind=kOutput, calls=%fused_computation.137 | convolution fusion | flops 2164789248 | bytes 10502144 | tf_op jit(solution)/shard_map/qkyi,qix->kyx/dot_general | solution.py:109
  193.1 3.7 all-to-all-done.3
  196.8 5.8 %fusion.61 = bf16[1,258,2048]{2,1,0:T(8,128)(2,1)S(1)} fusion(bf16[8,256,2048]{2,1,0:T(8,128)(2,1)} %bitcast.365, bf16[8,1,258,256]{3,2,1,0:T(8,128)(2,1)S(1)} %all-to-all-done.3), kind=kOutput, calls=%fused_computation.136 | convolution fusion | flops 2164789248 | bytes 10502144 | tf_op jit(solution)/shard_map/qkyi,qix->kyx/dot_general | solution.py:109
  209.7 11.9 %collective-permute-done.8 = bf16[1,258,514]{2,1,0:T(8,128)(2,1)} collective-permute-done((bf16[1,258,514]{2,1,0:T(8,128)(2,1)S(1)}, bf16[1,258,514]{2,1,0:T(8,128)(2,1)}, u32[]{:S(2)}, u32[]{:S(2)}) %collective-permute-start.8) | collective-permute-done | bytes 265256 | tf_op jit(solution)/shard_map/ppermute | solution.py:142
  224.0 6.4 %collective-permute-done.13 = bf16[1,258,514]{2,1,0:T(8,128)(2,1)S(1)} collective-permute-done((bf16[1,258,514]{2,1,0:T(8,128)(2,1)S(1)}, bf16[1,258,514]{2,1,0:T(8,128)(2,1)S(1)}, u32[]{:S(2)}, u32[]{:S(2)}) %collective-permute-start.13) | collective-permute-done | bytes 265256 | tf_op jit(solution)/shard_map/ppermute | solution.py:142
  230.4 19.8 %collective-permute-done.14 = bf16[1,258,514]{2,1,0:T(8,128)(2,1)S(1)} collective-permute-done((bf16[1,258,514]{2,1,0:T(8,128)(2,1)S(1)}, bf16[1,258,514]{2,1,0:T(8,128)(2,1)S(1)}, u32[]{:S(2)}, u32[]{:S(2)}) %collective-permute-start.14) | collective-permute-done | bytes 265256 | tf_op jit(solution)/shard_map/ppermute | solution.py:142
  253.3 5.9 %fusion.46 = f32[7,256,512]{2,1,0:T(8,128)} fusion(f32[8,258,514]{2,1,0:T(8,128)S(1)} %fusion.54, f32[8,258,514]{2,1,0:T(8,128)S(1)} %bitcast.355), kind=kLoop, calls=%fused_computation.95 | loop fusion | flops 3670016 | bytes 18350080 | tf_op jit(solution)/shard_map/mul | solution.py:54
  259.2 14.5 %fusion.8 = (f32[]{:T(128)}, f32[]{:T(128)}, f32[8,256,512]{2,1,0:T(8,128)}, bf16[8,256,512]{2,1,0:T(8,128)(2,1)}) fusion(f32[8,256,512]{2,1,0:T(8,128)} %copy-done.1, f32[7,256,512]{2,1,0:T(8,128)} %fusion.46, f32[8,258,514]{2,1,0:T(8,128)S(1)} %fusion.54, f32[8,258,514]{2,1,0:T(8,128)S(1)} %bitcast.355, bf16[4,258,514]{2,1,0:T(8,128)(2,1)} %copy-done.6, ...), kind=kLoop, calls=%fused_computation.21 | loop fusion | flops 28311552 | bytes 58220616 | tf_op jit(solution)/shard_map/reduce_sum | solution.py:172
  275.1 10.4 %all_to_all.52 = f32[32,1,2]{2,1,0:T(1,128)S(1)} all-to-all(f32[32,1,2]{2,1,0:T(1,128)S(1)} %broadcast_in_dim.89), channel_id=1, replica_groups=mesh['px'=4,'py'=8] {'px','py'}, dimensions={0} | all-to-all | bytes 512 | tf_op jit(solution)/shard_map/all_to_all | solution.py:41
  287.4 4.5 multiply_subtract_fusion.1
  296.2 7.3 %collective-permute-done.16 = bf16[1,256,512]{2,1,0:T(8,128)(2,1)S(1)} collective-permute-done((bf16[1,256,512]{2,1,0:T(8,128)(2,1)S(1)}, bf16[1,256,512]{2,1,0:T(8,128)(2,1)S(1)}, u32[]{:S(2)}, u32[]{:S(2)}) %collective-permute-start.16) | collective-permute-done | bytes 262176 | tf_op jit(solution)/shard_map/ppermute | solution.py:76
  303.5 10.2 %collective-permute-done.17 = bf16[1,256,512]{2,1,0:T(8,128)(2,1)S(1)} collective-permute-done((bf16[1,256,512]{2,1,0:T(8,128)(2,1)S(1)}, bf16[1,256,512]{2,1,0:T(8,128)(2,1)S(1)}, u32[]{:S(2)}, u32[]{:S(2)}) %collective-permute-start.17) | collective-permute-done | bytes 262176 | tf_op jit(solution)/shard_map/ppermute | solution.py:76
  314.8 5.0 collective-permute-start.24
  321.9 5.7 %convolution_convert_fusion.3 = bf16[256,2048]{1,0:T(8,128)(2,1)S(1)} fusion(bf16[2048,2048]{1,0:T(8,128)(2,1)} %param.11, bf16[1,256,2048]{2,1,0:T(8,128)(2,1)S(1)} %constant_dynamic-update-slice_fusion.8), kind=kOutput, calls=%fused_computation.129 | convolution fusion | flops 2148007936 | bytes 10485760 | tf_op jit(solution)/shard_map/dot_general | solution.py:87
  332.4 4.9 collective-permute-done.22
  337.3 6.5 %collective-permute-done.23 = bf16[1,256,512]{2,1,0:T(8,128)(2,1)S(1)} collective-permute-done((bf16[1,256,512]{2,1,0:T(8,128)(2,1)S(1)}, bf16[1,256,512]{2,1,0:T(8,128)(2,1)S(1)}, u32[]{:S(2)}, u32[]{:S(2)}) %collective-permute-start.23) | collective-permute-done | bytes 262176 | tf_op jit(solution)/shard_map/ppermute | solution.py:76
  343.9 5.7 %convolution_convert_fusion.1 = bf16[256,2048]{1,0:T(8,128)(2,1)S(1)} fusion(bf16[2048,2048]{1,0:T(8,128)(2,1)} %param.11, bf16[1,256,2048]{2,1,0:T(8,128)(2,1)S(1)} %constant_dynamic-update-slice_fusion), kind=kOutput, calls=%fused_computation.127 | convolution fusion | flops 2148007936 | bytes 10485760 | tf_op jit(solution)/shard_map/dot_general | solution.py:87
  350.6 4.2 all-to-all-start.7
  354.9 11.1 %fusion.65 = bf16[1,2048,256]{1,2,0:T(8,128)(2,1)S(1)} fusion(bf16[2048,2048]{1,0:T(8,128)(2,1)} %param.11, bf16[2048,256]{1,0:T(8,128)(2,1)S(1)} %bitcast.358, f32[]{:T(128)} %bitcast.25, f32[256]{0:T(256)S(1)} %dynamic_slice.114, f32[2048]{0:T(1024)S(1)} %copy-done.10), kind=kOutput, calls=%fused_computation.140 | convolution fusion | flops 4297588736 | bytes 10494980 | tf_op jit(solution)/shard_map/yj,kji->kyi/dot_general | solution.py:101
  370.3 4.4 all-to-all-start.6
  374.7 11.3 %fusion.66 = bf16[1,2048,256]{1,2,0:T(8,128)(2,1)S(1)} fusion(bf16[2048,2048]{1,0:T(8,128)(2,1)} %param.11, bf16[2048,256]{1,0:T(8,128)(2,1)} %bitcast.89, f32[]{:T(128)} %bitcast.47, f32[256]{0:T(256)S(1)} %dynamic_slice.114, f32[2048]{0:T(1024)S(1)} %copy-done.10), kind=kOutput, calls=%fused_computation.141 | convolution fusion | flops 4297588736 | bytes 10494980 | tf_op jit(solution)/shard_map/yj,kji->kyi/dot_general | solution.py:101
  394.1 6.1 %fusion.60 = bf16[1,258,2048]{2,1,0:T(8,128)(2,1)S(1)} fusion(bf16[8,256,2048]{2,1,0:T(8,128)(2,1)} %bitcast.366, bf16[8,1,258,256]{3,2,1,0:T(8,128)(2,1)} %all-to-all-done.6), kind=kOutput, calls=%fused_computation.135 | convolution fusion | flops 2164789248 | bytes 10502144 | tf_op jit(solution)/shard_map/qkyi,qix->kyx/dot_general | solution.py:109
  404.0 5.7 %all-to-all-done.8 = bf16[8,1,258,256]{3,2,1,0:T(8,128)(2,1)S(1)} async-done(((bf16[8,1,258,256]{3,2,1,0:T(8,128)(2,1)}), bf16[8,1,258,256]{3,2,1,0:T(8,128)(2,1)S(1)}, u32[]{:S(2)}, u32[]{:S(2)}) %all-to-all-start.8) | async-done | bytes 1056800 | tf_op jit(solution)/shard_map/all_to_all | solution.py:108
  409.7 5.8 %fusion.59 = bf16[1,258,2048]{2,1,0:T(8,128)(2,1)S(1)} fusion(bf16[8,256,2048]{2,1,0:T(8,128)(2,1)} %bitcast.367, bf16[8,1,258,256]{3,2,1,0:T(8,128)(2,1)S(1)} %all-to-all-done.8), kind=kOutput, calls=%fused_computation.134 | convolution fusion | flops 2164789248 | bytes 10502144 | tf_op jit(solution)/shard_map/qkyi,qix->kyx/dot_general | solution.py:109
  422.1 10.6 %collective-permute-done.20 = bf16[1,258,514]{2,1,0:T(8,128)(2,1)} collective-permute-done((bf16[1,258,514]{2,1,0:T(8,128)(2,1)S(1)}, bf16[1,258,514]{2,1,0:T(8,128)(2,1)}, u32[]{:S(2)}, u32[]{:S(2)}) %collective-permute-start.20) | collective-permute-done | bytes 265256 | tf_op jit(solution)/shard_map/ppermute | solution.py:142
  434.8 6.5 %collective-permute-done.25 = bf16[1,258,514]{2,1,0:T(8,128)(2,1)S(1)} collective-permute-done((bf16[1,258,514]{2,1,0:T(8,128)(2,1)S(1)}, bf16[1,258,514]{2,1,0:T(8,128)(2,1)S(1)}, u32[]{:S(2)}, u32[]{:S(2)}) %collective-permute-start.25) | collective-permute-done | bytes 265256 | tf_op jit(solution)/shard_map/ppermute | solution.py:142
  441.3 20.0 %collective-permute-done.26 = bf16[1,258,514]{2,1,0:T(8,128)(2,1)S(1)} collective-permute-done((bf16[1,258,514]{2,1,0:T(8,128)(2,1)S(1)}, bf16[1,258,514]{2,1,0:T(8,128)(2,1)S(1)}, u32[]{:S(2)}, u32[]{:S(2)}) %collective-permute-start.26) | collective-permute-done | bytes 265256 | tf_op jit(solution)/shard_map/ppermute | solution.py:142
  464.4 5.9 %fusion.45 = f32[7,256,512]{2,1,0:T(8,128)} fusion(f32[8,258,514]{2,1,0:T(8,128)S(1)} %fusion.53, f32[8,258,514]{2,1,0:T(8,128)S(1)} %bitcast.357), kind=kLoop, calls=%fused_computation.93 | loop fusion | flops 3670016 | bytes 18350080 | tf_op jit(solution)/shard_map/mul | solution.py:54
  470.3 15.5 %fusion.6 = (f32[]{:T(128)}, f32[]{:T(128)}, f32[]{:T(128)}, f32[]{:T(128)}, f32[8,256,512]{2,1,0:T(8,128)}, /*index=5*/bf16[8,256,512]{2,1,0:T(8,128)(2,1)}) fusion(bf16[8,256,512]{2,1,0:T(8,128)(2,1)} %get-tuple-element.29, f32[8,256,512]{2,1,0:T(8,128)} %copy-done.2, f32[8,256,512]{2,1,0:T(8,128)} %get-tuple-element.28, f32[7,256,512]{2,1,0:T(8,128)} %fusion.45, ...), kind=kLoop, calls=%fused_computation.19 | loop fusion | flops 33554432 | bytes 64512080 | tf_op jit(solution)/shard_map/reduce_sum | solution.py:180
  488.4 12.6 %all_to_all.53 = f32[32,1,4]{2,1,0:T(1,128)S(1)} all-to-all(f32[32,1,4]{2,1,0:T(1,128)S(1)} %broadcast_in_dim.90), channel_id=1, replica_groups=mesh['px'=4,'py'=8] {'px','py'}, dimensions={0} | all-to-all | bytes 1024 | tf_op jit(solution)/shard_map/all_to_all | solution.py:41
  505.9 12.8 %fusion.11 = (f32[8,256,512]{2,1,0:T(8,128)}, f32[8,256,512]{2,1,0:T(8,128)}, f32[8,256,512]{2,1,0:T(8,128)}) fusion(f32[8,256,512]{2,1,0:T(8,128)} %param.8, bf16[8,256,512]{2,1,0:T(8,128)(2,1)} %get-tuple-element.29, f32[]{:T(128)S(6)} %div.27, f32[]{:T(128)S(6)} %div.23, f32[]{:T(128)S(6)} %div.26, bf16[8,256,512]{2,1,0:T(8,128)(2,1)} %get-tuple-element.27, ...), kind=kLoop, calls=%fused_computation.24 | loop fusion | flops 12582912 | bytes 33554444 | tf_op jit(solution)/shard_map/add | solution.py:192
  (186 shorter events, 115.3 us)
Async XLA Ops:
  2.0 3.5 copy-start.8
  17.9 3.7 copy-start.3
  18.0 18.4 %collective-permute-start = (bf16[2,8,1,512]{3,2,1,0:T(2,128)(2,1)S(1)}, bf16[2,8,1,512]{3,2,1,0:T(2,128)(2,1)S(1)}, u32[]{:S(2)}, u32[]{:S(2)}) collective-permute-start(bf16[2,8,1,512]{3,2,1,0:T(2,128)(2,1)S(1)} %get-tuple-element.34), channel_id=1, source_target_pairs={{0,1},{1,2},{2,3},{3,4},{4,5},{5,6},{6,7},{8,9},{9,10},{10,11},{11... | collective-permute-start | bytes 49160 | tf_op jit(solution)/shard_map/ppermute | solution.py:17
  20.4 16.0 %collective-permute-start.3 = (bf16[2,8,1,512]{3,2,1,0:T(2,128)(2,1)S(1)}, bf16[2,8,1,512]{3,2,1,0:T(2,128)(2,1)S(1)}, u32[]{:S(2)}, u32[]{:S(2)}) collective-permute-start(bf16[2,8,1,512]{3,2,1,0:T(2,128)(2,1)S(1)} %get-tuple-element.35), channel_id=1, source_target_pairs={{1,0},{2,1},{3,2},{4,3},{5,4},{6,5},{7,6},{9,8},{10,9},{11,10},{12... | collective-permute-start | bytes 49160 | tf_op jit(solution)/shard_map/ppermute | solution.py:17
  24.8 6.4 %collective-permute-start.1 = (bf16[2,8,256,1]{2,1,3,0:T(8,128)(2,1)S(1)}, bf16[2,8,256,1]{2,1,3,0:T(8,128)(2,1)S(1)}, u32[]{:S(2)}, u32[]{:S(2)}) collective-permute-start(bf16[2,8,256,1]{2,1,3,0:T(8,128)(2,1)S(1)} %copy.77), channel_id=1, source_target_pairs={{0,8},{8,16},{16,24},{1,9},{9,17},{17,25},{2,10},{10,18},{18,26},{... | collective-permute-start | bytes 24584 | tf_op jit(solution)/shard_map/ppermute | solution.py:17
  29.5 5.5 %collective-permute-start.2 = (bf16[2,8,256,1]{2,1,3,0:T(8,128)(2,1)S(1)}, bf16[2,8,256,1]{2,1,3,0:T(8,128)(2,1)S(1)}, u32[]{:S(2)}, u32[]{:S(2)}) collective-permute-start(bf16[2,8,256,1]{2,1,3,0:T(8,128)(2,1)S(1)} %copy.78), channel_id=1, source_target_pairs={{8,0},{16,8},{24,16},{9,1},{17,9},{25,17},{10,2},{18,10},{26,18},{... | collective-permute-start | bytes 24584 | tf_op jit(solution)/shard_map/ppermute | solution.py:17
  54.5 5.9 %copy-start = (f32[8,258,514]{2,1,0:T(8,128)}, f32[8,258,514]{2,1,0:T(8,128)S(1)}, u32[]{:S(2)}) copy-start(f32[8,258,514]{2,1,0:T(8,128)S(1)} %get-tuple-element.30) | copy-start | bytes 12730756
  71.7 2.0 copy-start.1
  71.9 7.9 %copy-start.10 = (f32[2048]{0:T(1024)S(1)}, f32[2048]{0:T(1024)}, u32[]{:S(2)}) copy-start(f32[2048]{0:T(1024)} %param.12) | copy-start | bytes 24580
  71.9 8.0 %copy-start.9 = (f32[8]{0:T(128)S(1)}, f32[8]{0:T(128)}, u32[]{:S(2)}) copy-start(f32[8]{0:T(128)} %param.13) | copy-start | bytes 100
  73.7 11.2 %collective-permute-start.4 = (bf16[1,256,512]{2,1,0:T(8,128)(2,1)S(1)}, bf16[1,256,512]{2,1,0:T(8,128)(2,1)S(1)}, u32[]{:S(2)}, u32[]{:S(2)}) collective-permute-start(bf16[1,256,512]{2,1,0:T(8,128)(2,1)S(1)} %get-tuple-element.66), channel_id=1, source_target_pairs={{0,8},{8,16},{16,24},{24,0},{1,9},{9,17},{17,25},{25,1},{2,10},{10... | collective-permute-start | bytes 786440 | tf_op jit(solution)/shard_map/ppermute | solution.py:76
  75.3 20.7 %collective-permute-start.5 = (bf16[1,256,512]{2,1,0:T(8,128)(2,1)S(1)}, bf16[1,256,512]{2,1,0:T(8,128)(2,1)S(1)}, u32[]{:S(2)}, u32[]{:S(2)}) collective-permute-start(bf16[1,256,512]{2,1,0:T(8,128)(2,1)S(1)} %get-tuple-element.65), channel_id=1, source_target_pairs={{0,16},{8,24},{16,0},{24,8},{1,17},{9,25},{17,1},{25,9},{2,18},{10... | collective-permute-start | bytes 786440 | tf_op jit(solution)/shard_map/ppermute | solution.py:76
  76.3 19.7 %collective-permute-start.6 = (bf16[1,256,512]{2,1,0:T(8,128)(2,1)S(1)}, bf16[1,256,512]{2,1,0:T(8,128)(2,1)S(1)}, u32[]{:S(2)}, u32[]{:S(2)}) collective-permute-start(bf16[1,256,512]{2,1,0:T(8,128)(2,1)S(1)} %get-tuple-element.64), channel_id=1, source_target_pairs={{0,24},{8,0},{16,8},{24,16},{1,25},{9,1},{17,9},{25,17},{2,26},{10... | collective-permute-start | bytes 786440 | tf_op jit(solution)/shard_map/ppermute | solution.py:76
  98.9 32.0 %collective-permute-start.12 = (bf16[1,256,512]{2,1,0:T(8,128)(2,1)}, bf16[1,256,512]{2,1,0:T(8,128)(2,1)S(1)}, u32[]{:S(2)}, u32[]{:S(2)}) collective-permute-start(bf16[1,256,512]{2,1,0:T(8,128)(2,1)} %get-tuple-element.60), channel_id=1, source_target_pairs={{0,24},{8,0},{16,8},{24,16},{1,25},{9,1},{17,9},{25,17},{2,26},{10... | collective-permute-start | bytes 786440 | tf_op jit(solution)/shard_map/ppermute | solution.py:76
  106.1 23.8 %collective-permute-start.11 = (bf16[1,256,512]{2,1,0:T(8,128)(2,1)}, bf16[1,256,512]{2,1,0:T(8,128)(2,1)}, u32[]{:S(2)}, u32[]{:S(2)}) collective-permute-start(bf16[1,256,512]{2,1,0:T(8,128)(2,1)} %get-tuple-element.61), channel_id=1, source_target_pairs={{0,16},{8,24},{16,0},{24,8},{1,17},{9,25},{17,1},{25,9},{2,18},{10... | collective-permute-start | bytes 786440 | tf_op jit(solution)/shard_map/ppermute | solution.py:76
  106.4 17.9 %collective-permute-start.10 = (bf16[1,256,512]{2,1,0:T(8,128)(2,1)}, bf16[1,256,512]{2,1,0:T(8,128)(2,1)}, u32[]{:S(2)}, u32[]{:S(2)}) collective-permute-start(bf16[1,256,512]{2,1,0:T(8,128)(2,1)} %get-tuple-element.62), channel_id=1, source_target_pairs={{0,8},{8,16},{16,24},{24,0},{1,9},{9,17},{17,25},{25,1},{2,10},{10... | collective-permute-start | bytes 786440 | tf_op jit(solution)/shard_map/ppermute | solution.py:76
  113.4 24.2 %all-to-all-start = ((bf16[8,256,256]{2,1,0:T(8,128)(2,1)}), bf16[8,256,256]{2,1,0:T(8,128)(2,1)S(1)}, u32[]{:S(2)}, u32[]{:S(2)}) async-start(bf16[8,256,256]{2,1,0:T(8,128)(2,1)} %bitcast.353), calls=%async_computation | async-start | bytes 2097152 | tf_op jit(solution)/shard_map/all_to_all | solution.py:91
  137.7 19.7 %all-to-all-start.2 = ((bf16[8,256,256]{2,1,0:T(8,128)(2,1)}), bf16[8,256,256]{2,1,0:T(8,128)(2,1)}, u32[]{:S(2)}, u32[]{:S(2)}) async-start(bf16[8,256,256]{2,1,0:T(8,128)(2,1)} %bitcast.351), calls=%async_computation.2 | async-start | bytes 2097152 | tf_op jit(solution)/shard_map/all_to_all | solution.py:91
  157.3 20.2 %all-to-all-start.1 = ((bf16[8,1,258,256]{3,2,1,0:T(8,128)(2,1)}), bf16[8,1,258,256]{3,2,1,0:T(8,128)(2,1)}, u32[]{:S(2)}, u32[]{:S(2)}) async-start(bf16[8,1,258,256]{3,2,1,0:T(8,128)(2,1)} %copy.82), calls=%async_computation.1 | async-start | bytes 2162688 | tf_op jit(solution)/shard_map/all_to_all | solution.py:108
  177.5 19.3 %all-to-all-start.3 = ((bf16[8,1,258,256]{3,2,1,0:T(8,128)(2,1)}), bf16[8,1,258,256]{3,2,1,0:T(8,128)(2,1)S(1)}, u32[]{:S(2)}, u32[]{:S(2)}) async-start(bf16[8,1,258,256]{3,2,1,0:T(8,128)(2,1)} %copy.84), calls=%async_computation.3 | async-start | bytes 2162688 | tf_op jit(solution)/shard_map/all_to_all | solution.py:108
  188.2 34.6 %collective-permute-start.9 = (bf16[1,258,514]{2,1,0:T(8,128)(2,1)S(1)}, bf16[1,258,514]{2,1,0:T(8,128)(2,1)}, u32[]{:S(2)}, u32[]{:S(2)}) collective-permute-start(bf16[1,258,514]{2,1,0:T(8,128)(2,1)S(1)} %get-tuple-element.44), channel_id=1, source_target_pairs={{0,24},{8,0},{16,8},{24,16},{1,25},{9,1},{17,9},{25,17},{2,26},{10... | collective-permute-start | bytes 795680 | tf_op jit(solution)/shard_map/ppermute | solution.py:142
  188.3 20.4 %collective-permute-start.7 = (bf16[1,258,514]{2,1,0:T(8,128)(2,1)S(1)}, bf16[1,258,514]{2,1,0:T(8,128)(2,1)}, u32[]{:S(2)}, u32[]{:S(2)}) collective-permute-start(bf16[1,258,514]{2,1,0:T(8,128)(2,1)S(1)} %get-tuple-element.45), channel_id=1, source_target_pairs={{0,8},{8,16},{16,24},{24,0},{1,9},{9,17},{17,25},{25,1},{2,10},{10... | collective-permute-start | bytes 795680 | tf_op jit(solution)/shard_map/ppermute | solution.py:142
  190.3 31.3 %collective-permute-start.8 = (bf16[1,258,514]{2,1,0:T(8,128)(2,1)S(1)}, bf16[1,258,514]{2,1,0:T(8,128)(2,1)}, u32[]{:S(2)}, u32[]{:S(2)}) collective-permute-start(bf16[1,258,514]{2,1,0:T(8,128)(2,1)S(1)} %get-tuple-element.46), channel_id=1, source_target_pairs={{0,16},{8,24},{16,0},{24,8},{1,17},{9,25},{17,1},{25,9},{2,18},{10... | collective-permute-start | bytes 795680 | tf_op jit(solution)/shard_map/ppermute | solution.py:142
  203.6 46.7 %collective-permute-start.15 = (bf16[1,258,514]{2,1,0:T(8,128)(2,1)S(1)}, bf16[1,258,514]{2,1,0:T(8,128)(2,1)S(1)}, u32[]{:S(2)}, u32[]{:S(2)}) collective-permute-start(bf16[1,258,514]{2,1,0:T(8,128)(2,1)S(1)} %get-tuple-element.48), channel_id=1, source_target_pairs={{0,24},{8,0},{16,8},{24,16},{1,25},{9,1},{17,9},{25,17},{2,26},{10... | collective-permute-start | bytes 795680 | tf_op jit(solution)/shard_map/ppermute | solution.py:142
  203.6 26.8 %collective-permute-start.13 = (bf16[1,258,514]{2,1,0:T(8,128)(2,1)S(1)}, bf16[1,258,514]{2,1,0:T(8,128)(2,1)S(1)}, u32[]{:S(2)}, u32[]{:S(2)}) collective-permute-start(bf16[1,258,514]{2,1,0:T(8,128)(2,1)S(1)} %get-tuple-element.49), channel_id=1, source_target_pairs={{0,8},{8,16},{16,24},{24,0},{1,9},{9,17},{17,25},{25,1},{2,10},{10... | collective-permute-start | bytes 795680 | tf_op jit(solution)/shard_map/ppermute | solution.py:142
  208.7 41.5 %collective-permute-start.14 = (bf16[1,258,514]{2,1,0:T(8,128)(2,1)S(1)}, bf16[1,258,514]{2,1,0:T(8,128)(2,1)S(1)}, u32[]{:S(2)}, u32[]{:S(2)}) collective-permute-start(bf16[1,258,514]{2,1,0:T(8,128)(2,1)S(1)} %get-tuple-element.50), channel_id=1, source_target_pairs={{0,16},{8,24},{16,0},{24,8},{1,17},{9,25},{17,1},{25,9},{2,18},{10... | collective-permute-start | bytes 795680 | tf_op jit(solution)/shard_map/ppermute | solution.py:142
  221.6 31.7 %slice-start = ((s8[5406720]{0:T(1024)(128)(4,1)}), s8[4194304]{0:T(1024)(128)(4,1)S(1)}, s32[]{:S(2)}) async-start(s8[5406720]{0:T(1024)(128)(4,1)} %bitcast.354), calls=%async_computation.10 | async-start | bytes 8388608
  224.0 26.3 %copy-start.5 = (bf16[4,258,514]{2,1,0:T(8,128)(2,1)}, bf16[4,258,514]{2,1,0:T(8,128)(2,1)S(1)}, u32[]{:S(2)}) copy-start(bf16[4,258,514]{2,1,0:T(8,128)(2,1)S(1)} %constant_dynamic-update-slice_fusion.17) | copy-start | bytes 3182692
  251.4 1.9 slice-start.1
  291.9 21.8 %copy-start.2 = (f32[8,256,512]{2,1,0:T(8,128)}, f32[8,256,512]{2,1,0:T(8,128)S(1)}, u32[]{:S(2)}) copy-start(f32[8,256,512]{2,1,0:T(8,128)S(1)} %multiply_subtract_fusion.1) | copy-start | bytes 12582916
  292.3 11.1 %collective-permute-start.16 = (bf16[1,256,512]{2,1,0:T(8,128)(2,1)S(1)}, bf16[1,256,512]{2,1,0:T(8,128)(2,1)S(1)}, u32[]{:S(2)}, u32[]{:S(2)}) collective-permute-start(bf16[1,256,512]{2,1,0:T(8,128)(2,1)S(1)} %get-tuple-element.58), channel_id=1, source_target_pairs={{0,8},{8,16},{16,24},{24,0},{1,9},{9,17},{17,25},{25,1},{2,10},{10... | collective-permute-start | bytes 786440 | tf_op jit(solution)/shard_map/ppermute | solution.py:76
  292.9 20.7 %collective-permute-start.17 = (bf16[1,256,512]{2,1,0:T(8,128)(2,1)S(1)}, bf16[1,256,512]{2,1,0:T(8,128)(2,1)S(1)}, u32[]{:S(2)}, u32[]{:S(2)}) collective-permute-start(bf16[1,256,512]{2,1,0:T(8,128)(2,1)S(1)} %get-tuple-element.57), channel_id=1, source_target_pairs={{0,16},{8,24},{16,0},{24,8},{1,17},{9,25},{17,1},{25,9},{2,18},{10... | collective-permute-start | bytes 786440 | tf_op jit(solution)/shard_map/ppermute | solution.py:76
  293.5 20.2 %collective-permute-start.18 = (bf16[1,256,512]{2,1,0:T(8,128)(2,1)S(1)}, bf16[1,256,512]{2,1,0:T(8,128)(2,1)S(1)}, u32[]{:S(2)}, u32[]{:S(2)}) collective-permute-start(bf16[1,256,512]{2,1,0:T(8,128)(2,1)S(1)} %get-tuple-element.56), channel_id=1, source_target_pairs={{0,24},{8,0},{16,8},{24,16},{1,25},{9,1},{17,9},{25,17},{2,26},{10... | collective-permute-start | bytes 786440 | tf_op jit(solution)/shard_map/ppermute | solution.py:76
  314.8 29.0 %collective-permute-start.24 = (bf16[1,256,512]{2,1,0:T(8,128)(2,1)S(1)}, bf16[1,256,512]{2,1,0:T(8,128)(2,1)S(1)}, u32[]{:S(2)}, u32[]{:S(2)}) collective-permute-start(bf16[1,256,512]{2,1,0:T(8,128)(2,1)S(1)} %get-tuple-element.52), channel_id=1, source_target_pairs={{0,24},{8,0},{16,8},{24,16},{1,25},{9,1},{17,9},{25,17},{2,26},{10... | collective-permute-start | bytes 786440 | tf_op jit(solution)/shard_map/ppermute | solution.py:76
  319.8 24.0 %collective-permute-start.23 = (bf16[1,256,512]{2,1,0:T(8,128)(2,1)S(1)}, bf16[1,256,512]{2,1,0:T(8,128)(2,1)S(1)}, u32[]{:S(2)}, u32[]{:S(2)}) collective-permute-start(bf16[1,256,512]{2,1,0:T(8,128)(2,1)S(1)} %get-tuple-element.53), channel_id=1, source_target_pairs={{0,16},{8,24},{16,0},{24,8},{1,17},{9,25},{17,1},{25,9},{2,18},{10... | collective-permute-start | bytes 786440 | tf_op jit(solution)/shard_map/ppermute | solution.py:76
  321.5 15.7 %collective-permute-start.22 = (bf16[1,256,512]{2,1,0:T(8,128)(2,1)}, bf16[1,256,512]{2,1,0:T(8,128)(2,1)S(1)}, u32[]{:S(2)}, u32[]{:S(2)}) collective-permute-start(bf16[1,256,512]{2,1,0:T(8,128)(2,1)} %get-tuple-element.54), channel_id=1, source_target_pairs={{0,8},{8,16},{16,24},{24,0},{1,9},{9,17},{17,25},{25,1},{2,10},{10... | collective-permute-start | bytes 786440 | tf_op jit(solution)/shard_map/ppermute | solution.py:76
  328.8 21.8 %all-to-all-start.5 = ((bf16[8,256,256]{2,1,0:T(8,128)(2,1)}), bf16[8,256,256]{2,1,0:T(8,128)(2,1)S(1)}, u32[]{:S(2)}, u32[]{:S(2)}) async-start(bf16[8,256,256]{2,1,0:T(8,128)(2,1)} %bitcast.349), calls=%async_computation.5 | async-start | bytes 2097152 | tf_op jit(solution)/shard_map/all_to_all | solution.py:91
  350.6 19.7 %all-to-all-start.7 = ((bf16[8,256,256]{2,1,0:T(8,128)(2,1)}), bf16[8,256,256]{2,1,0:T(8,128)(2,1)}, u32[]{:S(2)}, u32[]{:S(2)}) async-start(bf16[8,256,256]{2,1,0:T(8,128)(2,1)} %bitcast.347), calls=%async_computation.7 | async-start | bytes 2097152 | tf_op jit(solution)/shard_map/all_to_all | solution.py:91
  370.3 20.2 %all-to-all-start.6 = ((bf16[8,1,258,256]{3,2,1,0:T(8,128)(2,1)}), bf16[8,1,258,256]{3,2,1,0:T(8,128)(2,1)}, u32[]{:S(2)}, u32[]{:S(2)}) async-start(bf16[8,1,258,256]{3,2,1,0:T(8,128)(2,1)} %copy.87), calls=%async_computation.6 | async-start | bytes 2162688 | tf_op jit(solution)/shard_map/all_to_all | solution.py:108
  390.5 19.3 %all-to-all-start.8 = ((bf16[8,1,258,256]{3,2,1,0:T(8,128)(2,1)}), bf16[8,1,258,256]{3,2,1,0:T(8,128)(2,1)S(1)}, u32[]{:S(2)}, u32[]{:S(2)}) async-start(bf16[8,1,258,256]{3,2,1,0:T(8,128)(2,1)} %copy.89), calls=%async_computation.8 | async-start | bytes 2162688 | tf_op jit(solution)/shard_map/all_to_all | solution.py:108
  401.1 32.6 %collective-permute-start.21 = (bf16[1,258,514]{2,1,0:T(8,128)(2,1)S(1)}, bf16[1,258,514]{2,1,0:T(8,128)(2,1)}, u32[]{:S(2)}, u32[]{:S(2)}) collective-permute-start(bf16[1,258,514]{2,1,0:T(8,128)(2,1)S(1)} %get-tuple-element.36), channel_id=1, source_target_pairs={{0,24},{8,0},{16,8},{24,16},{1,25},{9,1},{17,9},{25,17},{2,26},{10... | collective-permute-start | bytes 795680 | tf_op jit(solution)/shard_map/ppermute | solution.py:142
  402.1 17.4 %collective-permute-start.19 = (bf16[1,258,514]{2,1,0:T(8,128)(2,1)S(1)}, bf16[1,258,514]{2,1,0:T(8,128)(2,1)}, u32[]{:S(2)}, u32[]{:S(2)}) collective-permute-start(bf16[1,258,514]{2,1,0:T(8,128)(2,1)S(1)} %get-tuple-element.37), channel_id=1, source_target_pairs={{0,8},{8,16},{16,24},{24,0},{1,9},{9,17},{17,25},{25,1},{2,10},{10... | collective-permute-start | bytes 795680 | tf_op jit(solution)/shard_map/ppermute | solution.py:142
  403.2 29.5 %collective-permute-start.20 = (bf16[1,258,514]{2,1,0:T(8,128)(2,1)S(1)}, bf16[1,258,514]{2,1,0:T(8,128)(2,1)}, u32[]{:S(2)}, u32[]{:S(2)}) collective-permute-start(bf16[1,258,514]{2,1,0:T(8,128)(2,1)S(1)} %get-tuple-element.38), channel_id=1, source_target_pairs={{0,16},{8,24},{16,0},{24,8},{1,17},{9,25},{17,1},{25,9},{2,18},{10... | collective-permute-start | bytes 795680 | tf_op jit(solution)/shard_map/ppermute | solution.py:142
  415.7 48.7 %slice-start.2 = ((s8[5406720]{0:T(1024)(128)(4,1)}), s8[4194304]{0:T(1024)(128)(4,1)S(1)}, s32[]{:S(2)}) async-start(s8[5406720]{0:T(1024)(128)(4,1)} %bitcast.356), calls=%async_computation.12 | async-start | bytes 8388608
  416.5 44.8 %collective-permute-start.27 = (bf16[1,258,514]{2,1,0:T(8,128)(2,1)S(1)}, bf16[1,258,514]{2,1,0:T(8,128)(2,1)S(1)}, u32[]{:S(2)}, u32[]{:S(2)}) collective-permute-start(bf16[1,258,514]{2,1,0:T(8,128)(2,1)S(1)} %get-tuple-element.40), channel_id=1, source_target_pairs={{0,24},{8,0},{16,8},{24,16},{1,25},{9,1},{17,9},{25,17},{2,26},{10... | collective-permute-start | bytes 795680 | tf_op jit(solution)/shard_map/ppermute | solution.py:142
  417.5 23.8 %collective-permute-start.25 = (bf16[1,258,514]{2,1,0:T(8,128)(2,1)S(1)}, bf16[1,258,514]{2,1,0:T(8,128)(2,1)S(1)}, u32[]{:S(2)}, u32[]{:S(2)}) collective-permute-start(bf16[1,258,514]{2,1,0:T(8,128)(2,1)S(1)} %get-tuple-element.41), channel_id=1, source_target_pairs={{0,8},{8,16},{16,24},{24,0},{1,9},{9,17},{17,25},{25,1},{2,10},{10... | collective-permute-start | bytes 795680 | tf_op jit(solution)/shard_map/ppermute | solution.py:142
  419.5 41.8 %collective-permute-start.26 = (bf16[1,258,514]{2,1,0:T(8,128)(2,1)S(1)}, bf16[1,258,514]{2,1,0:T(8,128)(2,1)S(1)}, u32[]{:S(2)}, u32[]{:S(2)}) collective-permute-start(bf16[1,258,514]{2,1,0:T(8,128)(2,1)S(1)} %get-tuple-element.42), channel_id=1, source_target_pairs={{0,16},{8,24},{16,0},{24,8},{1,17},{9,25},{17,1},{25,9},{2,18},{10... | collective-permute-start | bytes 795680 | tf_op jit(solution)/shard_map/ppermute | solution.py:142
  434.8 26.6 %copy-start.7 = (bf16[4,258,514]{2,1,0:T(8,128)(2,1)}, bf16[4,258,514]{2,1,0:T(8,128)(2,1)S(1)}, u32[]{:S(2)}) copy-start(bf16[4,258,514]{2,1,0:T(8,128)(2,1)S(1)} %constant_dynamic-update-slice_fusion.4) | copy-start | bytes 3182692
  (3 other events, 4.1 us)

commit v14 on v13

--- a/solution.py
+++ b/solution.py
@@ -158,10 +158,10 @@
         coeff = jnp.where(labels == label, table[label], coeff)
     stacked = padded_2(
         jnp.stack((solution_in, coeff)).astype(jnp.bfloat16), (("px", 3), ("py", 2)), 1
-    ).astype(jnp.float32)
-    coeff_pad = stacked[1]
+    )
+    coeff_pad = stacked[1].astype(jnp.float32)
     solution = solution_in
-    residual = right_side - face_sum(stacked[0], coeff_pad)
+    residual = right_side - face_sum(stacked[0].astype(jnp.float32), coeff_pad)
     direction = image = None
     gamma_prev = curvature_prev = None
     for iteration in range(ITERS):

time: 524 us -> 513 us (0.979)
  other arithmetic: 115 us -> 109 us
    convert_element_type x1, other arithmetic: 13.3 us -> 0.7 us  [shards(): coeff_pad = stacked[1].astype(jnp.float32)]
    concatenate x0 -> x1, other arithmetic: none -> 6.79 us  [padded_2(): array = jnp.concatenate([before, array, after], axis=dim)]
  transfers between devices with their start and end apart: 36 -> 36, of which waited for: 23 -> 23; matrix products, arithmetic and copies ran while one was open for 24% -> 25% of each run, Pallas kernels for 0% -> 0%
where the time goes in v14:
time: 513 us; the launch traced here: 509 us
  waiting for transfers between devices  155 us (30%)
  other arithmetic  109 us (21%)
  matrix products  91.7 us (18%)
  starting transfers between devices  79.4 us (15%)
  local copies, waits for them, and re-layouts  43 us (8%)
  blocking collectives  23 us (4%)
  between operations  7.42 us (1%)
    ppermute x12, waiting for transfers between devices, return_lines(): lax.ppermute(part, 'px', [(i, (i + shift) % size) for i in range(size)])  78.9 us
    ppermute x12, waiting for transfers between devices, exchange(): lax.ppermute(part, axis, [(i, (i + shift) % size) for i in range(size)])  56.7 us
    dot_general x4, matrix products, precondition_lines(): jnp.einsum('yj,kji->kyi', eigenvectors, scaled, preferred_element_type=jn...  44.9 us
    ppermute x12, starting transfers between devices, exchange(): lax.ppermute(part, axis, [(i, (i + shift) % size) for i in range(size)])  24.3 us
    dot_general x4, matrix products, precondition_lines(): jnp.einsum('qkyi,qix->kyx', returned, eigenvectors.reshape(across, cols,...  23.9 us
    all_to_all x2, blocking collectives, all_sum(): return jnp.sum(lax.all_to_all(spread, axes, 0, 0, tiled=True), 0)  23 us
    dot_general x4, matrix products, precondition_lines(): jnp.dot(lines.reshape(levels_here * rows, width), eigenvectors, preferred...  22.9 us
    mul x3, other arithmetic, face_sum(): vertical = 0.5 * (coeff[:-1] + coeff[1:]) * (values[:-1] - values[1:])  17.7 us
  transfers between devices with their start and end apart: 36, of which 23 were waited for; matrix products, arithmetic and copies ran while one was open for 25% of the time, Pallas kernels for 0%

profile of v14, /device:TPU:0, one launch (start us, length us, event | category | flops | bytes accessed | tf_op | source)
XLA Modules:
  0.0 508.7 jit_solution(17016332229147383168)
XLA Ops:
  5.5 12.5 %fusion.78 = bf16[1,8,256,512]{3,2,1,0:T(8,128)(2,1)S(1)} fusion(s32[8,256,512]{2,1,0:T(8,128)S(1)} %copy-done.8, bf16[]{:T(256)} %bitcast.16, bf16[]{:T(256)} %bitcast.15, bf16[]{:T(256)} %bitcast.14, bf16[]{:T(256)} %bitcast.13, bf16[]{:T(256)} %bitcast.12, bf16[]{:T(256)} %bitcast.11, bf16[]{:T(256)} %bitcast.10, bf16[]{:T(256)} %bitcast.9, bf16[]{:T(256)} %bitcast.8, ...), kind=kLoop, calls=%fused_computation.153 | loop fusion | flops 34603008 | bytes 6291488 | tf_op jit(solution)/shard_map/stack | solution.py:160
  24.8 4.3 collective-permute-start.1
  36.4 6.8 %fusion.2 = bf16[2,8,258,514]{3,2,1,0:T(8,128)(2,1)S(1)} fusion(bf16[2,8,1,512]{3,2,1,0:T(2,128)(2,1)S(1)} %collective-permute-done.3, bf16[2,8,1,512]{3,2,1,0:T(2,128)(2,1)S(1)} %collective-permute-done, bf16[2,8,256,1]{3,2,1,0:T(8,128)(2,1)} %copy.80, bf16[1,8,256,512]{3,2,1,0:T(8,128)(2,1)} %copy-done.3, ...), kind=kLoop, calls=%fused_computation.13 | loop fusion | flops 33948672 | bytes 8487040 | tf_op jit(solution)/shard_map/concatenate | solution.py:25
  43.9 5.9 %fusion.46 = f32[7,256,512]{2,1,0:T(8,128)} fusion(f32[8,258,514]{2,1,0:T(8,128)S(1)} %get-tuple-element.31, f32[8,258,514]{2,1,0:T(8,128)S(1)} %get-tuple-element.30), kind=kLoop, calls=%fused_computation.94 | loop fusion | flops 3670016 | bytes 18350080 | tf_op jit(solution)/shard_map/mul | solution.py:54
  49.8 11.2 %fusion.34 = f32[8,256,512]{2,1,0:T(8,128)S(1)} fusion(f32[8,256,512]{2,1,0:T(8,128)} %param.7, f32[8,258,514]{2,1,0:T(8,128)S(1)} %get-tuple-element.31, f32[7,256,512]{2,1,0:T(8,128)} %fusion.46, f32[8,258,514]{2,1,0:T(8,128)S(1)} %get-tuple-element.30), kind=kLoop, calls=%fused_computation.54 | loop fusion | flops 23068672 | bytes 54001664 | tf_op jit(solution)/shard_map/sub | solution.py:164
  69.4 4.9 collective-permute-done.4
  74.3 11.1 %collective-permute-done.5 = bf16[1,256,512]{2,1,0:T(8,128)(2,1)S(1)} collective-permute-done((bf16[1,256,512]{2,1,0:T(8,128)(2,1)S(1)}, bf16[1,256,512]{2,1,0:T(8,128)(2,1)S(1)}, u32[]{:S(2)}, u32[]{:S(2)}) %collective-permute-start.5) | collective-permute-done | bytes 262176 | tf_op jit(solution)/shard_map/ppermute | solution.py:76
  88.2 7.2 %collective-permute-start.12 = (bf16[1,256,512]{2,1,0:T(8,128)(2,1)}, bf16[1,256,512]{2,1,0:T(8,128)(2,1)S(1)}, u32[]{:S(2)}, u32[]{:S(2)}) collective-permute-start(bf16[1,256,512]{2,1,0:T(8,128)(2,1)} %get-tuple-element.60), channel_id=1, source_target_pairs={{0,24},{8,0},{16,8},{24,16},{1,25},{9,1},{17,9},{25,17},{2,26},{10... | collective-permute-start | bytes 786440 | tf_op jit(solution)/shard_map/ppermute | solution.py:76
  96.2 5.7 %convolution_convert_fusion.7 = bf16[256,2048]{1,0:T(8,128)(2,1)S(1)} fusion(bf16[2048,2048]{1,0:T(8,128)(2,1)} %param.11, bf16[1,256,2048]{2,1,0:T(8,128)(2,1)S(1)} %constant_dynamic-update-slice_fusion.21), kind=kOutput, calls=%fused_computation.134 | convolution fusion | flops 2148007936 | bytes 10485760 | tf_op jit(solution)/shard_map/dot_general | solution.py:87
  106.5 7.2 %collective-permute-done.10 = bf16[1,256,512]{2,1,0:T(8,128)(2,1)} collective-permute-done((bf16[1,256,512]{2,1,0:T(8,128)(2,1)}, bf16[1,256,512]{2,1,0:T(8,128)(2,1)}, u32[]{:S(2)}, u32[]{:S(2)}) %collective-permute-start.10) | collective-permute-done | bytes 262176 | tf_op jit(solution)/shard_map/ppermute | solution.py:76
  114.7 4.6 collective-permute-done.11
  120.3 5.7 %convolution_convert_fusion.5 = bf16[256,2048]{1,0:T(8,128)(2,1)S(1)} fusion(bf16[2048,2048]{1,0:T(8,128)(2,1)} %param.11, bf16[1,256,2048]{2,1,0:T(8,128)(2,1)S(1)} %constant_dynamic-update-slice_fusion.14), kind=kOutput, calls=%fused_computation.132 | convolution fusion | flops 2148007936 | bytes 10485760 | tf_op jit(solution)/shard_map/dot_general | solution.py:87
  127.0 4.2 all-to-all-start.2
  131.3 11.1 %fusion.64 = bf16[1,2048,256]{1,2,0:T(8,128)(2,1)S(1)} fusion(bf16[2048,2048]{1,0:T(8,128)(2,1)} %param.11, bf16[2048,256]{1,0:T(8,128)(2,1)S(1)} %bitcast.365, f32[]{:T(128)} %bitcast.27, f32[256]{0:T(256)S(1)} %dynamic_slice.114, f32[2048]{0:T(1024)S(1)} %copy-done.10), kind=kOutput, calls=%fused_computation.139 | convolution fusion | flops 4297588736 | bytes 10494980 | tf_op jit(solution)/shard_map/yj,kji->kyi/dot_general | solution.py:101
  146.7 4.7 all-to-all-start.1
  151.4 11.3 %fusion.65 = bf16[1,2048,256]{1,2,0:T(8,128)(2,1)S(1)} fusion(bf16[2048,2048]{1,0:T(8,128)(2,1)} %param.11, bf16[2048,256]{1,0:T(8,128)(2,1)} %bitcast.46, f32[]{:T(128)} %bitcast.49, f32[256]{0:T(256)S(1)} %dynamic_slice.114, f32[2048]{0:T(1024)S(1)} %copy-done.10), kind=kOutput, calls=%fused_computation.140 | convolution fusion | flops 4297588736 | bytes 10494980 | tf_op jit(solution)/shard_map/yj,kji->kyi/dot_general | solution.py:101
  167.1 3.6 all-to-all-start.3
  170.8 6.1 %fusion.63 = bf16[1,258,2048]{2,1,0:T(8,128)(2,1)S(1)} fusion(bf16[8,256,2048]{2,1,0:T(8,128)(2,1)} %bitcast.370, bf16[8,1,258,256]{3,2,1,0:T(8,128)(2,1)} %all-to-all-done.1), kind=kOutput, calls=%fused_computation.138 | convolution fusion | flops 2164789248 | bytes 10502144 | tf_op jit(solution)/shard_map/qkyi,qix->kyx/dot_general | solution.py:109
  182.7 3.7 all-to-all-done.3
  186.4 5.8 %fusion.62 = bf16[1,258,2048]{2,1,0:T(8,128)(2,1)S(1)} fusion(bf16[8,256,2048]{2,1,0:T(8,128)(2,1)} %bitcast.371, bf16[8,1,258,256]{3,2,1,0:T(8,128)(2,1)S(1)} %all-to-all-done.3), kind=kOutput, calls=%fused_computation.137 | convolution fusion | flops 2164789248 | bytes 10502144 | tf_op jit(solution)/shard_map/qkyi,qix->kyx/dot_general | solution.py:109
  199.3 11.9 %collective-permute-done.8 = bf16[1,258,514]{2,1,0:T(8,128)(2,1)} collective-permute-done((bf16[1,258,514]{2,1,0:T(8,128)(2,1)S(1)}, bf16[1,258,514]{2,1,0:T(8,128)(2,1)}, u32[]{:S(2)}, u32[]{:S(2)}) %collective-permute-start.8) | collective-permute-done | bytes 265256 | tf_op jit(solution)/shard_map/ppermute | solution.py:142
  213.6 6.4 %collective-permute-done.13 = bf16[1,258,514]{2,1,0:T(8,128)(2,1)S(1)} collective-permute-done((bf16[1,258,514]{2,1,0:T(8,128)(2,1)S(1)}, bf16[1,258,514]{2,1,0:T(8,128)(2,1)S(1)}, u32[]{:S(2)}, u32[]{:S(2)}) %collective-permute-start.13) | collective-permute-done | bytes 265256 | tf_op jit(solution)/shard_map/ppermute | solution.py:142
  220.0 19.8 %collective-permute-done.14 = bf16[1,258,514]{2,1,0:T(8,128)(2,1)S(1)} collective-permute-done((bf16[1,258,514]{2,1,0:T(8,128)(2,1)S(1)}, bf16[1,258,514]{2,1,0:T(8,128)(2,1)S(1)}, u32[]{:S(2)}, u32[]{:S(2)}) %collective-permute-start.14) | collective-permute-done | bytes 265256 | tf_op jit(solution)/shard_map/ppermute | solution.py:142
  242.9 5.9 %fusion.45 = f32[7,256,512]{2,1,0:T(8,128)} fusion(f32[8,258,514]{2,1,0:T(8,128)S(1)} %fusion.53, f32[8,258,514]{2,1,0:T(8,128)S(1)} %bitcast.361), kind=kLoop, calls=%fused_computation.92 | loop fusion | flops 3670016 | bytes 18350080 | tf_op jit(solution)/shard_map/mul | solution.py:54
  248.8 14.5 %fusion.7 = (f32[]{:T(128)}, f32[]{:T(128)}, f32[8,256,512]{2,1,0:T(8,128)}, bf16[8,256,512]{2,1,0:T(8,128)(2,1)}) fusion(f32[8,256,512]{2,1,0:T(8,128)} %copy-done.1, f32[7,256,512]{2,1,0:T(8,128)} %fusion.45, f32[8,258,514]{2,1,0:T(8,128)S(1)} %fusion.53, f32[8,258,514]{2,1,0:T(8,128)S(1)} %bitcast.361, bf16[4,258,514]{2,1,0:T(8,128)(2,1)} %copy-done.6, ...), kind=kLoop, calls=%fused_computation.18 | loop fusion | flops 28311552 | bytes 58220616 | tf_op jit(solution)/shard_map/reduce_sum | solution.py:172
  264.7 10.4 %all_to_all.52 = f32[32,1,2]{2,1,0:T(1,128)S(1)} all-to-all(f32[32,1,2]{2,1,0:T(1,128)S(1)} %broadcast_in_dim.89), channel_id=1, replica_groups=mesh['px'=4,'py'=8] {'px','py'}, dimensions={0} | all-to-all | bytes 512 | tf_op jit(solution)/shard_map/all_to_all | solution.py:41
  277.0 4.5 multiply_subtract_fusion.1
  285.8 7.3 %collective-permute-done.16 = bf16[1,256,512]{2,1,0:T(8,128)(2,1)S(1)} collective-permute-done((bf16[1,256,512]{2,1,0:T(8,128)(2,1)S(1)}, bf16[1,256,512]{2,1,0:T(8,128)(2,1)S(1)}, u32[]{:S(2)}, u32[]{:S(2)}) %collective-permute-start.16) | collective-permute-done | bytes 262176 | tf_op jit(solution)/shard_map/ppermute | solution.py:76
  293.1 10.2 %collective-permute-done.17 = bf16[1,256,512]{2,1,0:T(8,128)(2,1)S(1)} collective-permute-done((bf16[1,256,512]{2,1,0:T(8,128)(2,1)S(1)}, bf16[1,256,512]{2,1,0:T(8,128)(2,1)S(1)}, u32[]{:S(2)}, u32[]{:S(2)}) %collective-permute-start.17) | collective-permute-done | bytes 262176 | tf_op jit(solution)/shard_map/ppermute | solution.py:76
  304.4 5.0 collective-permute-start.24
  311.3 5.7 %convolution_convert_fusion.3 = bf16[256,2048]{1,0:T(8,128)(2,1)S(1)} fusion(bf16[2048,2048]{1,0:T(8,128)(2,1)} %param.11, bf16[1,256,2048]{2,1,0:T(8,128)(2,1)S(1)} %constant_dynamic-update-slice_fusion.8), kind=kOutput, calls=%fused_computation.130 | convolution fusion | flops 2148007936 | bytes 10485760 | tf_op jit(solution)/shard_map/dot_general | solution.py:87
  321.8 5.1 collective-permute-done.22
  326.9 6.5 %collective-permute-done.23 = bf16[1,256,512]{2,1,0:T(8,128)(2,1)S(1)} collective-permute-done((bf16[1,256,512]{2,1,0:T(8,128)(2,1)S(1)}, bf16[1,256,512]{2,1,0:T(8,128)(2,1)S(1)}, u32[]{:S(2)}, u32[]{:S(2)}) %collective-permute-start.23) | collective-permute-done | bytes 262176 | tf_op jit(solution)/shard_map/ppermute | solution.py:76
  333.4 5.7 %convolution_convert_fusion.1 = bf16[256,2048]{1,0:T(8,128)(2,1)S(1)} fusion(bf16[2048,2048]{1,0:T(8,128)(2,1)} %param.11, bf16[1,256,2048]{2,1,0:T(8,128)(2,1)S(1)} %constant_dynamic-update-slice_fusion), kind=kOutput, calls=%fused_computation.128 | convolution fusion | flops 2148007936 | bytes 10485760 | tf_op jit(solution)/shard_map/dot_general | solution.py:87
  340.2 4.2 all-to-all-start.7
  344.5 11.1 %fusion.66 = bf16[1,2048,256]{1,2,0:T(8,128)(2,1)S(1)} fusion(bf16[2048,2048]{1,0:T(8,128)(2,1)} %param.11, bf16[2048,256]{1,0:T(8,128)(2,1)S(1)} %bitcast.364, f32[]{:T(128)} %bitcast.27, f32[256]{0:T(256)S(1)} %dynamic_slice.114, f32[2048]{0:T(1024)S(1)} %copy-done.10), kind=kOutput, calls=%fused_computation.141 | convolution fusion | flops 4297588736 | bytes 10494980 | tf_op jit(solution)/shard_map/yj,kji->kyi/dot_general | solution.py:101
  359.9 4.6 all-to-all-start.6
  364.5 11.3 %fusion.67 = bf16[1,2048,256]{1,2,0:T(8,128)(2,1)S(1)} fusion(bf16[2048,2048]{1,0:T(8,128)(2,1)} %param.11, bf16[2048,256]{1,0:T(8,128)(2,1)} %bitcast.91, f32[]{:T(128)} %bitcast.49, f32[256]{0:T(256)S(1)} %dynamic_slice.114, f32[2048]{0:T(1024)S(1)} %copy-done.10), kind=kOutput, calls=%fused_computation.142 | convolution fusion | flops 4297588736 | bytes 10494980 | tf_op jit(solution)/shard_map/yj,kji->kyi/dot_general | solution.py:101
  383.9 6.1 %fusion.61 = bf16[1,258,2048]{2,1,0:T(8,128)(2,1)S(1)} fusion(bf16[8,256,2048]{2,1,0:T(8,128)(2,1)} %bitcast.372, bf16[8,1,258,256]{3,2,1,0:T(8,128)(2,1)} %all-to-all-done.6), kind=kOutput, calls=%fused_computation.136 | convolution fusion | flops 2164789248 | bytes 10502144 | tf_op jit(solution)/shard_map/qkyi,qix->kyx/dot_general | solution.py:109
  393.8 5.7 %all-to-all-done.8 = bf16[8,1,258,256]{3,2,1,0:T(8,128)(2,1)S(1)} async-done(((bf16[8,1,258,256]{3,2,1,0:T(8,128)(2,1)}), bf16[8,1,258,256]{3,2,1,0:T(8,128)(2,1)S(1)}, u32[]{:S(2)}, u32[]{:S(2)}) %all-to-all-start.8) | async-done | bytes 1056800 | tf_op jit(solution)/shard_map/all_to_all | solution.py:108
  399.6 5.8 %fusion.60 = bf16[1,258,2048]{2,1,0:T(8,128)(2,1)S(1)} fusion(bf16[8,256,2048]{2,1,0:T(8,128)(2,1)} %bitcast.373, bf16[8,1,258,256]{3,2,1,0:T(8,128)(2,1)S(1)} %all-to-all-done.8), kind=kOutput, calls=%fused_computation.135 | convolution fusion | flops 2164789248 | bytes 10502144 | tf_op jit(solution)/shard_map/qkyi,qix->kyx/dot_general | solution.py:109
  411.8 10.7 %collective-permute-done.20 = bf16[1,258,514]{2,1,0:T(8,128)(2,1)} collective-permute-done((bf16[1,258,514]{2,1,0:T(8,128)(2,1)S(1)}, bf16[1,258,514]{2,1,0:T(8,128)(2,1)}, u32[]{:S(2)}, u32[]{:S(2)}) %collective-permute-start.20) | collective-permute-done | bytes 265256 | tf_op jit(solution)/shard_map/ppermute | solution.py:142
  424.6 6.5 %collective-permute-done.25 = bf16[1,258,514]{2,1,0:T(8,128)(2,1)S(1)} collective-permute-done((bf16[1,258,514]{2,1,0:T(8,128)(2,1)S(1)}, bf16[1,258,514]{2,1,0:T(8,128)(2,1)S(1)}, u32[]{:S(2)}, u32[]{:S(2)}) %collective-permute-start.25) | collective-permute-done | bytes 265256 | tf_op jit(solution)/shard_map/ppermute | solution.py:142
  431.1 20.0 %collective-permute-done.26 = bf16[1,258,514]{2,1,0:T(8,128)(2,1)S(1)} collective-permute-done((bf16[1,258,514]{2,1,0:T(8,128)(2,1)S(1)}, bf16[1,258,514]{2,1,0:T(8,128)(2,1)S(1)}, u32[]{:S(2)}, u32[]{:S(2)}) %collective-permute-start.26) | collective-permute-done | bytes 265256 | tf_op jit(solution)/shard_map/ppermute | solution.py:142
  454.2 5.9 %fusion.44 = f32[7,256,512]{2,1,0:T(8,128)} fusion(f32[8,258,514]{2,1,0:T(8,128)S(1)} %fusion.52, f32[8,258,514]{2,1,0:T(8,128)S(1)} %bitcast.363), kind=kLoop, calls=%fused_computation.90 | loop fusion | flops 3670016 | bytes 18350080 | tf_op jit(solution)/shard_map/mul | solution.py:54
  460.1 15.5 %fusion.5 = (f32[]{:T(128)}, f32[]{:T(128)}, f32[]{:T(128)}, f32[]{:T(128)}, f32[8,256,512]{2,1,0:T(8,128)}, /*index=5*/bf16[8,256,512]{2,1,0:T(8,128)(2,1)}) fusion(bf16[8,256,512]{2,1,0:T(8,128)(2,1)} %get-tuple-element.29, f32[8,256,512]{2,1,0:T(8,128)} %copy-done.2, f32[8,256,512]{2,1,0:T(8,128)} %get-tuple-element.28, f32[7,256,512]{2,1,0:T(8,128)} %fusion.44, ...), kind=kLoop, calls=%fused_computation.16 | loop fusion | flops 33554432 | bytes 64512080 | tf_op jit(solution)/shard_map/reduce_sum | solution.py:180
  478.3 12.6 %all_to_all.53 = f32[32,1,4]{2,1,0:T(1,128)S(1)} all-to-all(f32[32,1,4]{2,1,0:T(1,128)S(1)} %broadcast_in_dim.90), channel_id=1, replica_groups=mesh['px'=4,'py'=8] {'px','py'}, dimensions={0} | all-to-all | bytes 1024 | tf_op jit(solution)/shard_map/all_to_all | solution.py:41
  495.7 12.8 %fusion.10 = (f32[8,256,512]{2,1,0:T(8,128)}, f32[8,256,512]{2,1,0:T(8,128)}, f32[8,256,512]{2,1,0:T(8,128)}) fusion(f32[8,256,512]{2,1,0:T(8,128)} %param.8, bf16[8,256,512]{2,1,0:T(8,128)(2,1)} %get-tuple-element.29, f32[]{:T(128)S(6)} %div.27, f32[]{:T(128)S(6)} %div.23, f32[]{:T(128)S(6)} %div.26, bf16[8,256,512]{2,1,0:T(8,128)(2,1)} %get-tuple-element.27, ...), kind=kLoop, calls=%fused_computation.21 | loop fusion | flops 12582912 | bytes 33554444 | tf_op jit(solution)/shard_map/add | solution.py:192
  (186 shorter events, 111.8 us)
Async XLA Ops:
  2.0 3.5 copy-start.8
  17.9 3.7 copy-start.3
  18.0 18.4 %collective-permute-start = (bf16[2,8,1,512]{3,2,1,0:T(2,128)(2,1)S(1)}, bf16[2,8,1,512]{3,2,1,0:T(2,128)(2,1)S(1)}, u32[]{:S(2)}, u32[]{:S(2)}) collective-permute-start(bf16[2,8,1,512]{3,2,1,0:T(2,128)(2,1)S(1)} %get-tuple-element.34), channel_id=1, source_target_pairs={{0,1},{1,2},{2,3},{3,4},{4,5},{5,6},{6,7},{8,9},{9,10},{10,11},{11... | collective-permute-start | bytes 49160 | tf_op jit(solution)/shard_map/ppermute | solution.py:17
  20.4 16.0 %collective-permute-start.3 = (bf16[2,8,1,512]{3,2,1,0:T(2,128)(2,1)S(1)}, bf16[2,8,1,512]{3,2,1,0:T(2,128)(2,1)S(1)}, u32[]{:S(2)}, u32[]{:S(2)}) collective-permute-start(bf16[2,8,1,512]{3,2,1,0:T(2,128)(2,1)S(1)} %get-tuple-element.35), channel_id=1, source_target_pairs={{1,0},{2,1},{3,2},{4,3},{5,4},{6,5},{7,6},{9,8},{10,9},{11,10},{12... | collective-permute-start | bytes 49160 | tf_op jit(solution)/shard_map/ppermute | solution.py:17
  24.8 6.2 %collective-permute-start.1 = (bf16[2,8,256,1]{2,1,3,0:T(8,128)(2,1)S(1)}, bf16[2,8,256,1]{2,1,3,0:T(8,128)(2,1)S(1)}, u32[]{:S(2)}, u32[]{:S(2)}) collective-permute-start(bf16[2,8,256,1]{2,1,3,0:T(8,128)(2,1)S(1)} %copy.77), channel_id=1, source_target_pairs={{0,8},{8,16},{16,24},{1,9},{9,17},{17,25},{2,10},{10,18},{18,26},{... | collective-permute-start | bytes 24584 | tf_op jit(solution)/shard_map/ppermute | solution.py:17
  29.5 5.5 %collective-permute-start.2 = (bf16[2,8,256,1]{2,1,3,0:T(8,128)(2,1)S(1)}, bf16[2,8,256,1]{2,1,3,0:T(8,128)(2,1)S(1)}, u32[]{:S(2)}, u32[]{:S(2)}) collective-permute-start(bf16[2,8,256,1]{2,1,3,0:T(8,128)(2,1)S(1)} %copy.78), channel_id=1, source_target_pairs={{8,0},{16,8},{24,16},{9,1},{17,9},{25,17},{10,2},{18,10},{26,18},{... | collective-permute-start | bytes 24584 | tf_op jit(solution)/shard_map/ppermute | solution.py:17
  43.9 5.9 %copy-start = (f32[8,258,514]{2,1,0:T(8,128)}, f32[8,258,514]{2,1,0:T(8,128)S(1)}, u32[]{:S(2)}) copy-start(f32[8,258,514]{2,1,0:T(8,128)S(1)} %get-tuple-element.30) | copy-start | bytes 12730756
  61.1 2.0 copy-start.1
  61.2 7.4 %copy-start.10 = (f32[2048]{0:T(1024)S(1)}, f32[2048]{0:T(1024)}, u32[]{:S(2)}) copy-start(f32[2048]{0:T(1024)} %param.12) | copy-start | bytes 24580
  61.3 7.4 %copy-start.9 = (f32[8]{0:T(128)S(1)}, f32[8]{0:T(128)}, u32[]{:S(2)}) copy-start(f32[8]{0:T(128)} %param.13) | copy-start | bytes 100
  63.1 11.2 %collective-permute-start.4 = (bf16[1,256,512]{2,1,0:T(8,128)(2,1)S(1)}, bf16[1,256,512]{2,1,0:T(8,128)(2,1)S(1)}, u32[]{:S(2)}, u32[]{:S(2)}) collective-permute-start(bf16[1,256,512]{2,1,0:T(8,128)(2,1)S(1)} %get-tuple-element.66), channel_id=1, source_target_pairs={{0,8},{8,16},{16,24},{24,0},{1,9},{9,17},{17,25},{25,1},{2,10},{10... | collective-permute-start | bytes 786440 | tf_op jit(solution)/shard_map/ppermute | solution.py:76
  64.7 20.7 %collective-permute-start.5 = (bf16[1,256,512]{2,1,0:T(8,128)(2,1)S(1)}, bf16[1,256,512]{2,1,0:T(8,128)(2,1)S(1)}, u32[]{:S(2)}, u32[]{:S(2)}) collective-permute-start(bf16[1,256,512]{2,1,0:T(8,128)(2,1)S(1)} %get-tuple-element.65), channel_id=1, source_target_pairs={{0,16},{8,24},{16,0},{24,8},{1,17},{9,25},{17,1},{25,9},{2,18},{10... | collective-permute-start | bytes 786440 | tf_op jit(solution)/shard_map/ppermute | solution.py:76
  65.7 19.7 %collective-permute-start.6 = (bf16[1,256,512]{2,1,0:T(8,128)(2,1)S(1)}, bf16[1,256,512]{2,1,0:T(8,128)(2,1)S(1)}, u32[]{:S(2)}, u32[]{:S(2)}) collective-permute-start(bf16[1,256,512]{2,1,0:T(8,128)(2,1)S(1)} %get-tuple-element.64), channel_id=1, source_target_pairs={{0,24},{8,0},{16,8},{24,16},{1,25},{9,1},{17,9},{25,17},{2,26},{10... | collective-permute-start | bytes 786440 | tf_op jit(solution)/shard_map/ppermute | solution.py:76
  88.2 32.0 %collective-permute-start.12 = (bf16[1,256,512]{2,1,0:T(8,128)(2,1)}, bf16[1,256,512]{2,1,0:T(8,128)(2,1)S(1)}, u32[]{:S(2)}, u32[]{:S(2)}) collective-permute-start(bf16[1,256,512]{2,1,0:T(8,128)(2,1)} %get-tuple-element.60), channel_id=1, source_target_pairs={{0,24},{8,0},{16,8},{24,16},{1,25},{9,1},{17,9},{25,17},{2,26},{10... | collective-permute-start | bytes 786440 | tf_op jit(solution)/shard_map/ppermute | solution.py:76
  95.5 23.8 %collective-permute-start.11 = (bf16[1,256,512]{2,1,0:T(8,128)(2,1)}, bf16[1,256,512]{2,1,0:T(8,128)(2,1)}, u32[]{:S(2)}, u32[]{:S(2)}) collective-permute-start(bf16[1,256,512]{2,1,0:T(8,128)(2,1)} %get-tuple-element.61), channel_id=1, source_target_pairs={{0,16},{8,24},{16,0},{24,8},{1,17},{9,25},{17,1},{25,9},{2,18},{10... | collective-permute-start | bytes 786440 | tf_op jit(solution)/shard_map/ppermute | solution.py:76
  95.8 17.9 %collective-permute-start.10 = (bf16[1,256,512]{2,1,0:T(8,128)(2,1)}, bf16[1,256,512]{2,1,0:T(8,128)(2,1)}, u32[]{:S(2)}, u32[]{:S(2)}) collective-permute-start(bf16[1,256,512]{2,1,0:T(8,128)(2,1)} %get-tuple-element.62), channel_id=1, source_target_pairs={{0,8},{8,16},{16,24},{24,0},{1,9},{9,17},{17,25},{25,1},{2,10},{10... | collective-permute-start | bytes 786440 | tf_op jit(solution)/shard_map/ppermute | solution.py:76
  103.0 24.1 %all-to-all-start = ((bf16[8,256,256]{2,1,0:T(8,128)(2,1)}), bf16[8,256,256]{2,1,0:T(8,128)(2,1)S(1)}, u32[]{:S(2)}, u32[]{:S(2)}) async-start(bf16[8,256,256]{2,1,0:T(8,128)(2,1)} %bitcast.359), calls=%async_computation | async-start | bytes 2097152 | tf_op jit(solution)/shard_map/all_to_all | solution.py:91
  127.0 19.7 %all-to-all-start.2 = ((bf16[8,256,256]{2,1,0:T(8,128)(2,1)}), bf16[8,256,256]{2,1,0:T(8,128)(2,1)}, u32[]{:S(2)}, u32[]{:S(2)}) async-start(bf16[8,256,256]{2,1,0:T(8,128)(2,1)} %bitcast.357), calls=%async_computation.2 | async-start | bytes 2097152 | tf_op jit(solution)/shard_map/all_to_all | solution.py:91
  146.7 20.4 %all-to-all-start.1 = ((bf16[8,1,258,256]{3,2,1,0:T(8,128)(2,1)}), bf16[8,1,258,256]{3,2,1,0:T(8,128)(2,1)}, u32[]{:S(2)}, u32[]{:S(2)}) async-start(bf16[8,1,258,256]{3,2,1,0:T(8,128)(2,1)} %copy.82), calls=%async_computation.1 | async-start | bytes 2162688 | tf_op jit(solution)/shard_map/all_to_all | solution.py:108
  167.1 19.3 %all-to-all-start.3 = ((bf16[8,1,258,256]{3,2,1,0:T(8,128)(2,1)}), bf16[8,1,258,256]{3,2,1,0:T(8,128)(2,1)S(1)}, u32[]{:S(2)}, u32[]{:S(2)}) async-start(bf16[8,1,258,256]{3,2,1,0:T(8,128)(2,1)} %copy.84), calls=%async_computation.3 | async-start | bytes 2162688 | tf_op jit(solution)/shard_map/all_to_all | solution.py:108
  177.8 34.6 %collective-permute-start.9 = (bf16[1,258,514]{2,1,0:T(8,128)(2,1)S(1)}, bf16[1,258,514]{2,1,0:T(8,128)(2,1)}, u32[]{:S(2)}, u32[]{:S(2)}) collective-permute-start(bf16[1,258,514]{2,1,0:T(8,128)(2,1)S(1)} %get-tuple-element.44), channel_id=1, source_target_pairs={{0,24},{8,0},{16,8},{24,16},{1,25},{9,1},{17,9},{25,17},{2,26},{10... | collective-permute-start | bytes 795680 | tf_op jit(solution)/shard_map/ppermute | solution.py:142
  177.9 20.4 %collective-permute-start.7 = (bf16[1,258,514]{2,1,0:T(8,128)(2,1)S(1)}, bf16[1,258,514]{2,1,0:T(8,128)(2,1)}, u32[]{:S(2)}, u32[]{:S(2)}) collective-permute-start(bf16[1,258,514]{2,1,0:T(8,128)(2,1)S(1)} %get-tuple-element.45), channel_id=1, source_target_pairs={{0,8},{8,16},{16,24},{24,0},{1,9},{9,17},{17,25},{25,1},{2,10},{10... | collective-permute-start | bytes 795680 | tf_op jit(solution)/shard_map/ppermute | solution.py:142
  179.9 31.3 %collective-permute-start.8 = (bf16[1,258,514]{2,1,0:T(8,128)(2,1)S(1)}, bf16[1,258,514]{2,1,0:T(8,128)(2,1)}, u32[]{:S(2)}, u32[]{:S(2)}) collective-permute-start(bf16[1,258,514]{2,1,0:T(8,128)(2,1)S(1)} %get-tuple-element.46), channel_id=1, source_target_pairs={{0,16},{8,24},{16,0},{24,8},{1,17},{9,25},{17,1},{25,9},{2,18},{10... | collective-permute-start | bytes 795680 | tf_op jit(solution)/shard_map/ppermute | solution.py:142
  193.2 46.7 %collective-permute-start.15 = (bf16[1,258,514]{2,1,0:T(8,128)(2,1)S(1)}, bf16[1,258,514]{2,1,0:T(8,128)(2,1)S(1)}, u32[]{:S(2)}, u32[]{:S(2)}) collective-permute-start(bf16[1,258,514]{2,1,0:T(8,128)(2,1)S(1)} %get-tuple-element.48), channel_id=1, source_target_pairs={{0,24},{8,0},{16,8},{24,16},{1,25},{9,1},{17,9},{25,17},{2,26},{10... | collective-permute-start | bytes 795680 | tf_op jit(solution)/shard_map/ppermute | solution.py:142
  193.2 26.8 %collective-permute-start.13 = (bf16[1,258,514]{2,1,0:T(8,128)(2,1)S(1)}, bf16[1,258,514]{2,1,0:T(8,128)(2,1)S(1)}, u32[]{:S(2)}, u32[]{:S(2)}) collective-permute-start(bf16[1,258,514]{2,1,0:T(8,128)(2,1)S(1)} %get-tuple-element.49), channel_id=1, source_target_pairs={{0,8},{8,16},{16,24},{24,0},{1,9},{9,17},{17,25},{25,1},{2,10},{10... | collective-permute-start | bytes 795680 | tf_op jit(solution)/shard_map/ppermute | solution.py:142
  198.3 41.5 %collective-permute-start.14 = (bf16[1,258,514]{2,1,0:T(8,128)(2,1)S(1)}, bf16[1,258,514]{2,1,0:T(8,128)(2,1)S(1)}, u32[]{:S(2)}, u32[]{:S(2)}) collective-permute-start(bf16[1,258,514]{2,1,0:T(8,128)(2,1)S(1)} %get-tuple-element.50), channel_id=1, source_target_pairs={{0,16},{8,24},{16,0},{24,8},{1,17},{9,25},{17,1},{25,9},{2,18},{10... | collective-permute-start | bytes 795680 | tf_op jit(solution)/shard_map/ppermute | solution.py:142
  211.2 31.7 %slice-start = ((s8[5406720]{0:T(1024)(128)(4,1)}), s8[4194304]{0:T(1024)(128)(4,1)S(1)}, s32[]{:S(2)}) async-start(s8[5406720]{0:T(1024)(128)(4,1)} %bitcast.360), calls=%async_computation.10 | async-start | bytes 8388608
  213.6 26.3 %copy-start.5 = (bf16[4,258,514]{2,1,0:T(8,128)(2,1)}, bf16[4,258,514]{2,1,0:T(8,128)(2,1)S(1)}, u32[]{:S(2)}) copy-start(bf16[4,258,514]{2,1,0:T(8,128)(2,1)S(1)} %constant_dynamic-update-slice_fusion.17) | copy-start | bytes 3182692
  241.0 1.9 slice-start.1
  281.5 21.8 %copy-start.2 = (f32[8,256,512]{2,1,0:T(8,128)}, f32[8,256,512]{2,1,0:T(8,128)S(1)}, u32[]{:S(2)}) copy-start(f32[8,256,512]{2,1,0:T(8,128)S(1)} %multiply_subtract_fusion.1) | copy-start | bytes 12582916
  281.9 11.1 %collective-permute-start.16 = (bf16[1,256,512]{2,1,0:T(8,128)(2,1)S(1)}, bf16[1,256,512]{2,1,0:T(8,128)(2,1)S(1)}, u32[]{:S(2)}, u32[]{:S(2)}) collective-permute-start(bf16[1,256,512]{2,1,0:T(8,128)(2,1)S(1)} %get-tuple-element.58), channel_id=1, source_target_pairs={{0,8},{8,16},{16,24},{24,0},{1,9},{9,17},{17,25},{25,1},{2,10},{10... | collective-permute-start | bytes 786440 | tf_op jit(solution)/shard_map/ppermute | solution.py:76
  282.5 20.7 %collective-permute-start.17 = (bf16[1,256,512]{2,1,0:T(8,128)(2,1)S(1)}, bf16[1,256,512]{2,1,0:T(8,128)(2,1)S(1)}, u32[]{:S(2)}, u32[]{:S(2)}) collective-permute-start(bf16[1,256,512]{2,1,0:T(8,128)(2,1)S(1)} %get-tuple-element.57), channel_id=1, source_target_pairs={{0,16},{8,24},{16,0},{24,8},{1,17},{9,25},{17,1},{25,9},{2,18},{10... | collective-permute-start | bytes 786440 | tf_op jit(solution)/shard_map/ppermute | solution.py:76
  283.1 20.2 %collective-permute-start.18 = (bf16[1,256,512]{2,1,0:T(8,128)(2,1)S(1)}, bf16[1,256,512]{2,1,0:T(8,128)(2,1)S(1)}, u32[]{:S(2)}, u32[]{:S(2)}) collective-permute-start(bf16[1,256,512]{2,1,0:T(8,128)(2,1)S(1)} %get-tuple-element.56), channel_id=1, source_target_pairs={{0,24},{8,0},{16,8},{24,16},{1,25},{9,1},{17,9},{25,17},{2,26},{10... | collective-permute-start | bytes 786440 | tf_op jit(solution)/shard_map/ppermute | solution.py:76
  304.4 29.0 %collective-permute-start.24 = (bf16[1,256,512]{2,1,0:T(8,128)(2,1)S(1)}, bf16[1,256,512]{2,1,0:T(8,128)(2,1)S(1)}, u32[]{:S(2)}, u32[]{:S(2)}) collective-permute-start(bf16[1,256,512]{2,1,0:T(8,128)(2,1)S(1)} %get-tuple-element.52), channel_id=1, source_target_pairs={{0,24},{8,0},{16,8},{24,16},{1,25},{9,1},{17,9},{25,17},{2,26},{10... | collective-permute-start | bytes 786440 | tf_op jit(solution)/shard_map/ppermute | solution.py:76
  309.4 24.0 %collective-permute-start.23 = (bf16[1,256,512]{2,1,0:T(8,128)(2,1)S(1)}, bf16[1,256,512]{2,1,0:T(8,128)(2,1)S(1)}, u32[]{:S(2)}, u32[]{:S(2)}) collective-permute-start(bf16[1,256,512]{2,1,0:T(8,128)(2,1)S(1)} %get-tuple-element.53), channel_id=1, source_target_pairs={{0,16},{8,24},{16,0},{24,8},{1,17},{9,25},{17,1},{25,9},{2,18},{10... | collective-permute-start | bytes 786440 | tf_op jit(solution)/shard_map/ppermute | solution.py:76
  311.1 15.7 %collective-permute-start.22 = (bf16[1,256,512]{2,1,0:T(8,128)(2,1)}, bf16[1,256,512]{2,1,0:T(8,128)(2,1)S(1)}, u32[]{:S(2)}, u32[]{:S(2)}) collective-permute-start(bf16[1,256,512]{2,1,0:T(8,128)(2,1)} %get-tuple-element.54), channel_id=1, source_target_pairs={{0,8},{8,16},{16,24},{24,0},{1,9},{9,17},{17,25},{25,1},{2,10},{10... | collective-permute-start | bytes 786440 | tf_op jit(solution)/shard_map/ppermute | solution.py:76
  318.2 22.0 %all-to-all-start.5 = ((bf16[8,256,256]{2,1,0:T(8,128)(2,1)}), bf16[8,256,256]{2,1,0:T(8,128)(2,1)S(1)}, u32[]{:S(2)}, u32[]{:S(2)}) async-start(bf16[8,256,256]{2,1,0:T(8,128)(2,1)} %bitcast.355), calls=%async_computation.5 | async-start | bytes 2097152 | tf_op jit(solution)/shard_map/all_to_all | solution.py:91
  340.2 19.7 %all-to-all-start.7 = ((bf16[8,256,256]{2,1,0:T(8,128)(2,1)}), bf16[8,256,256]{2,1,0:T(8,128)(2,1)}, u32[]{:S(2)}, u32[]{:S(2)}) async-start(bf16[8,256,256]{2,1,0:T(8,128)(2,1)} %bitcast.353), calls=%async_computation.7 | async-start | bytes 2097152 | tf_op jit(solution)/shard_map/all_to_all | solution.py:91
  359.9 20.4 %all-to-all-start.6 = ((bf16[8,1,258,256]{3,2,1,0:T(8,128)(2,1)}), bf16[8,1,258,256]{3,2,1,0:T(8,128)(2,1)}, u32[]{:S(2)}, u32[]{:S(2)}) async-start(bf16[8,1,258,256]{3,2,1,0:T(8,128)(2,1)} %copy.87), calls=%async_computation.6 | async-start | bytes 2162688 | tf_op jit(solution)/shard_map/all_to_all | solution.py:108
  380.3 19.3 %all-to-all-start.8 = ((bf16[8,1,258,256]{3,2,1,0:T(8,128)(2,1)}), bf16[8,1,258,256]{3,2,1,0:T(8,128)(2,1)S(1)}, u32[]{:S(2)}, u32[]{:S(2)}) async-start(bf16[8,1,258,256]{3,2,1,0:T(8,128)(2,1)} %copy.89), calls=%async_computation.8 | async-start | bytes 2162688 | tf_op jit(solution)/shard_map/all_to_all | solution.py:108
  390.9 32.6 %collective-permute-start.21 = (bf16[1,258,514]{2,1,0:T(8,128)(2,1)S(1)}, bf16[1,258,514]{2,1,0:T(8,128)(2,1)}, u32[]{:S(2)}, u32[]{:S(2)}) collective-permute-start(bf16[1,258,514]{2,1,0:T(8,128)(2,1)S(1)} %get-tuple-element.36), channel_id=1, source_target_pairs={{0,24},{8,0},{16,8},{24,16},{1,25},{9,1},{17,9},{25,17},{2,26},{10... | collective-permute-start | bytes 795680 | tf_op jit(solution)/shard_map/ppermute | solution.py:142
  391.7 17.6 %collective-permute-start.19 = (bf16[1,258,514]{2,1,0:T(8,128)(2,1)S(1)}, bf16[1,258,514]{2,1,0:T(8,128)(2,1)}, u32[]{:S(2)}, u32[]{:S(2)}) collective-permute-start(bf16[1,258,514]{2,1,0:T(8,128)(2,1)S(1)} %get-tuple-element.37), channel_id=1, source_target_pairs={{0,8},{8,16},{16,24},{24,0},{1,9},{9,17},{17,25},{25,1},{2,10},{10... | collective-permute-start | bytes 795680 | tf_op jit(solution)/shard_map/ppermute | solution.py:142
  393.0 29.5 %collective-permute-start.20 = (bf16[1,258,514]{2,1,0:T(8,128)(2,1)S(1)}, bf16[1,258,514]{2,1,0:T(8,128)(2,1)}, u32[]{:S(2)}, u32[]{:S(2)}) collective-permute-start(bf16[1,258,514]{2,1,0:T(8,128)(2,1)S(1)} %get-tuple-element.38), channel_id=1, source_target_pairs={{0,16},{8,24},{16,0},{24,8},{1,17},{9,25},{17,1},{25,9},{2,18},{10... | collective-permute-start | bytes 795680 | tf_op jit(solution)/shard_map/ppermute | solution.py:142
  405.5 48.7 %slice-start.2 = ((s8[5406720]{0:T(1024)(128)(4,1)}), s8[4194304]{0:T(1024)(128)(4,1)S(1)}, s32[]{:S(2)}) async-start(s8[5406720]{0:T(1024)(128)(4,1)} %bitcast.362), calls=%async_computation.12 | async-start | bytes 8388608
  406.3 44.8 %collective-permute-start.27 = (bf16[1,258,514]{2,1,0:T(8,128)(2,1)S(1)}, bf16[1,258,514]{2,1,0:T(8,128)(2,1)S(1)}, u32[]{:S(2)}, u32[]{:S(2)}) collective-permute-start(bf16[1,258,514]{2,1,0:T(8,128)(2,1)S(1)} %get-tuple-element.40), channel_id=1, source_target_pairs={{0,24},{8,0},{16,8},{24,16},{1,25},{9,1},{17,9},{25,17},{2,26},{10... | collective-permute-start | bytes 795680 | tf_op jit(solution)/shard_map/ppermute | solution.py:142
  407.1 24.0 %collective-permute-start.25 = (bf16[1,258,514]{2,1,0:T(8,128)(2,1)S(1)}, bf16[1,258,514]{2,1,0:T(8,128)(2,1)S(1)}, u32[]{:S(2)}, u32[]{:S(2)}) collective-permute-start(bf16[1,258,514]{2,1,0:T(8,128)(2,1)S(1)} %get-tuple-element.41), channel_id=1, source_target_pairs={{0,8},{8,16},{16,24},{24,0},{1,9},{9,17},{17,25},{25,1},{2,10},{10... | collective-permute-start | bytes 795680 | tf_op jit(solution)/shard_map/ppermute | solution.py:142
  409.3 41.8 %collective-permute-start.26 = (bf16[1,258,514]{2,1,0:T(8,128)(2,1)S(1)}, bf16[1,258,514]{2,1,0:T(8,128)(2,1)S(1)}, u32[]{:S(2)}, u32[]{:S(2)}) collective-permute-start(bf16[1,258,514]{2,1,0:T(8,128)(2,1)S(1)} %get-tuple-element.42), channel_id=1, source_target_pairs={{0,16},{8,24},{16,0},{24,8},{1,17},{9,25},{17,1},{25,9},{2,18},{10... | collective-permute-start | bytes 795680 | tf_op jit(solution)/shard_map/ppermute | solution.py:142
  424.6 26.6 %copy-start.7 = (bf16[4,258,514]{2,1,0:T(8,128)(2,1)}, bf16[4,258,514]{2,1,0:T(8,128)(2,1)S(1)}, u32[]{:S(2)}) copy-start(bf16[4,258,514]{2,1,0:T(8,128)(2,1)S(1)} %constant_dynamic-update-slice_fusion.4) | copy-start | bytes 3182692
  (3 other events, 4.1 us)

commit v15 on v14

--- a/solution.py
+++ b/solution.py
@@ -151,11 +151,15 @@
 
 
 def shards(right_side, solution_in, classes, coeff_table, eigenvectors, eigenvalues, level_shift):
-    labels = classes.astype(jnp.bfloat16)
     table = coeff_table.astype(jnp.bfloat16)
-    coeff = jnp.zeros(classes.shape, jnp.bfloat16)
-    for label in range(coeff_table.shape[0]):
-        coeff = jnp.where(labels == label, table[label], coeff)
+    choices = [table[label] for label in range(coeff_table.shape[0])]
+    bit = 0
+    while len(choices) > 1:
+        chosen = (classes & (1 << bit)) != 0
+        pairs = zip(choices[0::2], choices[1::2])
+        choices = [jnp.where(chosen, high, low) for low, high in pairs]
+        bit += 1
+    coeff = jnp.broadcast_to(choices[0], classes.shape)
     stacked = padded_2(
         jnp.stack((solution_in, coeff)).astype(jnp.bfloat16), (("px", 3), ("py", 2)), 1
     )

time: 513 us -> 514 us (level)
  no operation moved by 1% of the time
where the time goes in v15:
time: 514 us; the launch traced here: 509 us
  waiting for transfers between devices  155 us (30%)
  other arithmetic  110 us (21%)
  matrix products  91.7 us (18%)
  starting transfers between devices  79.7 us (16%)
  local copies, waits for them, and re-layouts  43 us (8%)
  blocking collectives  23 us (4%)
  between operations  7.45 us (1%)
    ppermute x12, waiting for transfers between devices, return_lines(): lax.ppermute(part, 'px', [(i, (i + shift) % size) for i in range(size)])  78.7 us
    ppermute x12, waiting for transfers between devices, exchange(): lax.ppermute(part, axis, [(i, (i + shift) % size) for i in range(size)])  56.2 us
    dot_general x4, matrix products, precondition_lines(): jnp.einsum('yj,kji->kyi', eigenvectors, scaled, preferred_element_type=jn...  44.9 us
    ppermute x12, starting transfers between devices, exchange(): lax.ppermute(part, axis, [(i, (i + shift) % size) for i in range(size)])  24.8 us
    dot_general x4, matrix products, precondition_lines(): jnp.einsum('qkyi,qix->kyx', returned, eigenvectors.reshape(across, cols,...  23.9 us
    all_to_all x2, blocking collectives, all_sum(): return jnp.sum(lax.all_to_all(spread, axes, 0, 0, tiled=True), 0)  23 us
    dot_general x4, matrix products, precondition_lines(): jnp.dot(lines.reshape(levels_here * rows, width), eigenvectors, preferred...  22.9 us
    mul x3, other arithmetic, face_sum(): vertical = 0.5 * (coeff[:-1] + coeff[1:]) * (values[:-1] - values[1:])  17.7 us
  transfers between devices with their start and end apart: 36, of which 23 were waited for; matrix products, arithmetic and copies ran while one was open for 25% of the time, Pallas kernels for 0%

profile of v15, /device:TPU:0, one launch (start us, length us, event | category | flops | bytes accessed | tf_op | source)
XLA Modules:
  0.0 509.1 jit_solution(11498828881223503818)
XLA Ops:
  5.5 13.3 %fusion.79 = bf16[1,8,256,512]{3,2,1,0:T(8,128)(2,1)S(1)} fusion(s32[8,256,512]{2,1,0:T(8,128)S(1)} %copy-done.8, bf16[]{:T(256)} %bitcast.16, bf16[]{:T(256)} %bitcast.15, bf16[]{:T(256)} %bitcast.14, bf16[]{:T(256)} %bitcast.13, bf16[]{:T(256)} %bitcast.12, bf16[]{:T(256)} %bitcast.11, bf16[]{:T(256)} %bitcast.10, bf16[]{:T(256)} %bitcast.9, bf16[]{:T(256)} %bitcast.8, ...), kind=kLoop, calls=%fused_computation.142 | loop fusion | flops 24117248 | bytes 6291488 | tf_op jit(solution)/shard_map/stack | solution.py:164
  25.6 4.3 collective-permute-start.1
  37.2 6.8 %fusion.2 = bf16[2,8,258,514]{3,2,1,0:T(8,128)(2,1)S(1)} fusion(bf16[2,8,1,512]{3,2,1,0:T(2,128)(2,1)S(1)} %collective-permute-done.3, bf16[2,8,1,512]{3,2,1,0:T(2,128)(2,1)S(1)} %collective-permute-done, bf16[2,8,256,1]{3,2,1,0:T(8,128)(2,1)} %copy.83, bf16[1,8,256,512]{3,2,1,0:T(8,128)(2,1)} %copy-done.3, ...), kind=kLoop, calls=%fused_computation.13 | loop fusion | flops 33948672 | bytes 8487040 | tf_op jit(solution)/shard_map/concatenate | solution.py:25
  44.7 5.9 %fusion.47 = f32[7,256,512]{2,1,0:T(8,128)} fusion(f32[8,258,514]{2,1,0:T(8,128)S(1)} %get-tuple-element.31, f32[8,258,514]{2,1,0:T(8,128)S(1)} %get-tuple-element.30), kind=kLoop, calls=%fused_computation.83 | loop fusion | flops 3670016 | bytes 18350080 | tf_op jit(solution)/shard_map/mul | solution.py:54
  50.6 11.2 %fusion.34 = f32[8,256,512]{2,1,0:T(8,128)S(1)} fusion(f32[8,256,512]{2,1,0:T(8,128)} %param.7, f32[8,258,514]{2,1,0:T(8,128)S(1)} %get-tuple-element.31, f32[7,256,512]{2,1,0:T(8,128)} %fusion.47, f32[8,258,514]{2,1,0:T(8,128)S(1)} %get-tuple-element.30), kind=kLoop, calls=%fused_computation.54 | loop fusion | flops 23068672 | bytes 54001664 | tf_op jit(solution)/shard_map/sub | solution.py:168
  70.2 4.9 collective-permute-done.4
  75.1 11.1 %collective-permute-done.5 = bf16[1,256,512]{2,1,0:T(8,128)(2,1)S(1)} collective-permute-done((bf16[1,256,512]{2,1,0:T(8,128)(2,1)S(1)}, bf16[1,256,512]{2,1,0:T(8,128)(2,1)S(1)}, u32[]{:S(2)}, u32[]{:S(2)}) %collective-permute-start.5) | collective-permute-done | bytes 262176 | tf_op jit(solution)/shard_map/ppermute | solution.py:76
  89.0 7.2 %collective-permute-start.12 = (bf16[1,256,512]{2,1,0:T(8,128)(2,1)}, bf16[1,256,512]{2,1,0:T(8,128)(2,1)S(1)}, u32[]{:S(2)}, u32[]{:S(2)}) collective-permute-start(bf16[1,256,512]{2,1,0:T(8,128)(2,1)} %get-tuple-element.60), channel_id=1, source_target_pairs={{0,24},{8,0},{16,8},{24,16},{1,25},{9,1},{17,9},{25,17},{2,26},{10... | collective-permute-start | bytes 786440 | tf_op jit(solution)/shard_map/ppermute | solution.py:76
  97.3 5.7 %convolution_convert_fusion.7 = bf16[256,2048]{1,0:T(8,128)(2,1)S(1)} fusion(bf16[2048,2048]{1,0:T(8,128)(2,1)} %param.11, bf16[1,256,2048]{2,1,0:T(8,128)(2,1)S(1)} %constant_dynamic-update-slice_fusion.21), kind=kOutput, calls=%fused_computation.123 | convolution fusion | flops 2148007936 | bytes 10485760 | tf_op jit(solution)/shard_map/dot_general | solution.py:87
  107.7 6.8 %collective-permute-done.10 = bf16[1,256,512]{2,1,0:T(8,128)(2,1)} collective-permute-done((bf16[1,256,512]{2,1,0:T(8,128)(2,1)}, bf16[1,256,512]{2,1,0:T(8,128)(2,1)}, u32[]{:S(2)}, u32[]{:S(2)}) %collective-permute-start.10) | collective-permute-done | bytes 262176 | tf_op jit(solution)/shard_map/ppermute | solution.py:76
  115.5 4.6 collective-permute-done.11
  121.1 5.7 %convolution_convert_fusion.5 = bf16[256,2048]{1,0:T(8,128)(2,1)S(1)} fusion(bf16[2048,2048]{1,0:T(8,128)(2,1)} %param.11, bf16[1,256,2048]{2,1,0:T(8,128)(2,1)S(1)} %constant_dynamic-update-slice_fusion.14), kind=kOutput, calls=%fused_computation.121 | convolution fusion | flops 2148007936 | bytes 10485760 | tf_op jit(solution)/shard_map/dot_general | solution.py:87
  127.8 4.2 all-to-all-start.2
  132.1 11.1 %fusion.65 = bf16[1,2048,256]{1,2,0:T(8,128)(2,1)S(1)} fusion(bf16[2048,2048]{1,0:T(8,128)(2,1)} %param.11, bf16[2048,256]{1,0:T(8,128)(2,1)S(1)} %bitcast.365, f32[]{:T(128)} %bitcast.27, f32[256]{0:T(256)S(1)} %dynamic_slice.114, f32[2048]{0:T(1024)S(1)} %copy-done.10), kind=kOutput, calls=%fused_computation.128 | convolution fusion | flops 4297588736 | bytes 10494980 | tf_op jit(solution)/shard_map/yj,kji->kyi/dot_general | solution.py:101
  147.5 4.4 all-to-all-start.1
  151.9 11.3 %fusion.66 = bf16[1,2048,256]{1,2,0:T(8,128)(2,1)S(1)} fusion(bf16[2048,2048]{1,0:T(8,128)(2,1)} %param.11, bf16[2048,256]{1,0:T(8,128)(2,1)} %bitcast.46, f32[]{:T(128)} %bitcast.49, f32[256]{0:T(256)S(1)} %dynamic_slice.114, f32[2048]{0:T(1024)S(1)} %copy-done.10), kind=kOutput, calls=%fused_computation.129 | convolution fusion | flops 4297588736 | bytes 10494980 | tf_op jit(solution)/shard_map/yj,kji->kyi/dot_general | solution.py:101
  167.7 3.6 all-to-all-start.3
  171.3 6.1 %fusion.64 = bf16[1,258,2048]{2,1,0:T(8,128)(2,1)S(1)} fusion(bf16[8,256,2048]{2,1,0:T(8,128)(2,1)} %bitcast.370, bf16[8,1,258,256]{3,2,1,0:T(8,128)(2,1)} %all-to-all-done.1), kind=kOutput, calls=%fused_computation.127 | convolution fusion | flops 2164789248 | bytes 10502144 | tf_op jit(solution)/shard_map/qkyi,qix->kyx/dot_general | solution.py:109
  183.2 3.7 all-to-all-done.3
  187.0 5.8 %fusion.63 = bf16[1,258,2048]{2,1,0:T(8,128)(2,1)S(1)} fusion(bf16[8,256,2048]{2,1,0:T(8,128)(2,1)} %bitcast.371, bf16[8,1,258,256]{3,2,1,0:T(8,128)(2,1)S(1)} %all-to-all-done.3), kind=kOutput, calls=%fused_computation.126 | convolution fusion | flops 2164789248 | bytes 10502144 | tf_op jit(solution)/shard_map/qkyi,qix->kyx/dot_general | solution.py:109
  199.9 12.0 %collective-permute-done.8 = bf16[1,258,514]{2,1,0:T(8,128)(2,1)} collective-permute-done((bf16[1,258,514]{2,1,0:T(8,128)(2,1)S(1)}, bf16[1,258,514]{2,1,0:T(8,128)(2,1)}, u32[]{:S(2)}, u32[]{:S(2)}) %collective-permute-start.8) | collective-permute-done | bytes 265256 | tf_op jit(solution)/shard_map/ppermute | solution.py:142
  214.3 6.3 %collective-permute-done.13 = bf16[1,258,514]{2,1,0:T(8,128)(2,1)S(1)} collective-permute-done((bf16[1,258,514]{2,1,0:T(8,128)(2,1)S(1)}, bf16[1,258,514]{2,1,0:T(8,128)(2,1)S(1)}, u32[]{:S(2)}, u32[]{:S(2)}) %collective-permute-start.13) | collective-permute-done | bytes 265256 | tf_op jit(solution)/shard_map/ppermute | solution.py:142
  220.6 19.8 %collective-permute-done.14 = bf16[1,258,514]{2,1,0:T(8,128)(2,1)S(1)} collective-permute-done((bf16[1,258,514]{2,1,0:T(8,128)(2,1)S(1)}, bf16[1,258,514]{2,1,0:T(8,128)(2,1)S(1)}, u32[]{:S(2)}, u32[]{:S(2)}) %collective-permute-start.14) | collective-permute-done | bytes 265256 | tf_op jit(solution)/shard_map/ppermute | solution.py:142
  243.5 5.9 %fusion.46 = f32[7,256,512]{2,1,0:T(8,128)} fusion(f32[8,258,514]{2,1,0:T(8,128)S(1)} %fusion.54, f32[8,258,514]{2,1,0:T(8,128)S(1)} %bitcast.361), kind=kLoop, calls=%fused_computation.81 | loop fusion | flops 3670016 | bytes 18350080 | tf_op jit(solution)/shard_map/mul | solution.py:54
  249.4 14.5 %fusion.7 = (f32[]{:T(128)}, f32[]{:T(128)}, f32[8,256,512]{2,1,0:T(8,128)}, bf16[8,256,512]{2,1,0:T(8,128)(2,1)}) fusion(f32[8,256,512]{2,1,0:T(8,128)} %copy-done.1, f32[7,256,512]{2,1,0:T(8,128)} %fusion.46, f32[8,258,514]{2,1,0:T(8,128)S(1)} %fusion.54, f32[8,258,514]{2,1,0:T(8,128)S(1)} %bitcast.361, bf16[4,258,514]{2,1,0:T(8,128)(2,1)} %copy-done.6, ...), kind=kLoop, calls=%fused_computation.18 | loop fusion | flops 28311552 | bytes 58220616 | tf_op jit(solution)/shard_map/reduce_sum | solution.py:176
  265.2 10.4 %all_to_all.52 = f32[32,1,2]{2,1,0:T(1,128)S(1)} all-to-all(f32[32,1,2]{2,1,0:T(1,128)S(1)} %broadcast_in_dim.90), channel_id=1, replica_groups=mesh['px'=4,'py'=8] {'px','py'}, dimensions={0} | all-to-all | bytes 512 | tf_op jit(solution)/shard_map/all_to_all | solution.py:41
  277.6 4.5 multiply_subtract_fusion.1
  286.3 7.3 %collective-permute-done.16 = bf16[1,256,512]{2,1,0:T(8,128)(2,1)S(1)} collective-permute-done((bf16[1,256,512]{2,1,0:T(8,128)(2,1)S(1)}, bf16[1,256,512]{2,1,0:T(8,128)(2,1)S(1)}, u32[]{:S(2)}, u32[]{:S(2)}) %collective-permute-start.16) | collective-permute-done | bytes 262176 | tf_op jit(solution)/shard_map/ppermute | solution.py:76
  293.6 10.2 %collective-permute-done.17 = bf16[1,256,512]{2,1,0:T(8,128)(2,1)S(1)} collective-permute-done((bf16[1,256,512]{2,1,0:T(8,128)(2,1)S(1)}, bf16[1,256,512]{2,1,0:T(8,128)(2,1)S(1)}, u32[]{:S(2)}, u32[]{:S(2)}) %collective-permute-start.17) | collective-permute-done | bytes 262176 | tf_op jit(solution)/shard_map/ppermute | solution.py:76
  305.0 5.0 collective-permute-start.24
  312.1 5.7 %convolution_convert_fusion.3 = bf16[256,2048]{1,0:T(8,128)(2,1)S(1)} fusion(bf16[2048,2048]{1,0:T(8,128)(2,1)} %param.11, bf16[1,256,2048]{2,1,0:T(8,128)(2,1)S(1)} %constant_dynamic-update-slice_fusion.8), kind=kOutput, calls=%fused_computation.119 | convolution fusion | flops 2148007936 | bytes 10485760 | tf_op jit(solution)/shard_map/dot_general | solution.py:87
  322.5 4.9 collective-permute-done.22
  327.4 6.5 %collective-permute-done.23 = bf16[1,256,512]{2,1,0:T(8,128)(2,1)S(1)} collective-permute-done((bf16[1,256,512]{2,1,0:T(8,128)(2,1)S(1)}, bf16[1,256,512]{2,1,0:T(8,128)(2,1)S(1)}, u32[]{:S(2)}, u32[]{:S(2)}) %collective-permute-start.23) | collective-permute-done | bytes 262176 | tf_op jit(solution)/shard_map/ppermute | solution.py:76
  334.0 5.7 %convolution_convert_fusion.1 = bf16[256,2048]{1,0:T(8,128)(2,1)S(1)} fusion(bf16[2048,2048]{1,0:T(8,128)(2,1)} %param.11, bf16[1,256,2048]{2,1,0:T(8,128)(2,1)S(1)} %constant_dynamic-update-slice_fusion), kind=kOutput, calls=%fused_computation.117 | convolution fusion | flops 2148007936 | bytes 10485760 | tf_op jit(solution)/shard_map/dot_general | solution.py:87
  340.8 4.2 all-to-all-start.7
  345.0 11.1 %fusion.67 = bf16[1,2048,256]{1,2,0:T(8,128)(2,1)S(1)} fusion(bf16[2048,2048]{1,0:T(8,128)(2,1)} %param.11, bf16[2048,256]{1,0:T(8,128)(2,1)S(1)} %bitcast.364, f32[]{:T(128)} %bitcast.27, f32[256]{0:T(256)S(1)} %dynamic_slice.114, f32[2048]{0:T(1024)S(1)} %copy-done.10), kind=kOutput, calls=%fused_computation.130 | convolution fusion | flops 4297588736 | bytes 10494980 | tf_op jit(solution)/shard_map/yj,kji->kyi/dot_general | solution.py:101
  360.4 4.4 all-to-all-start.6
  364.9 11.3 %fusion.68 = bf16[1,2048,256]{1,2,0:T(8,128)(2,1)S(1)} fusion(bf16[2048,2048]{1,0:T(8,128)(2,1)} %param.11, bf16[2048,256]{1,0:T(8,128)(2,1)} %bitcast.91, f32[]{:T(128)} %bitcast.49, f32[256]{0:T(256)S(1)} %dynamic_slice.114, f32[2048]{0:T(1024)S(1)} %copy-done.10), kind=kOutput, calls=%fused_computation.131 | convolution fusion | flops 4297588736 | bytes 10494980 | tf_op jit(solution)/shard_map/yj,kji->kyi/dot_general | solution.py:101
  384.2 6.1 %fusion.62 = bf16[1,258,2048]{2,1,0:T(8,128)(2,1)S(1)} fusion(bf16[8,256,2048]{2,1,0:T(8,128)(2,1)} %bitcast.372, bf16[8,1,258,256]{3,2,1,0:T(8,128)(2,1)} %all-to-all-done.6), kind=kOutput, calls=%fused_computation.125 | convolution fusion | flops 2164789248 | bytes 10502144 | tf_op jit(solution)/shard_map/qkyi,qix->kyx/dot_general | solution.py:109
  394.2 5.7 %all-to-all-done.8 = bf16[8,1,258,256]{3,2,1,0:T(8,128)(2,1)S(1)} async-done(((bf16[8,1,258,256]{3,2,1,0:T(8,128)(2,1)}), bf16[8,1,258,256]{3,2,1,0:T(8,128)(2,1)S(1)}, u32[]{:S(2)}, u32[]{:S(2)}) %all-to-all-start.8) | async-done | bytes 1056800 | tf_op jit(solution)/shard_map/all_to_all | solution.py:108
  399.9 5.8 %fusion.61 = bf16[1,258,2048]{2,1,0:T(8,128)(2,1)S(1)} fusion(bf16[8,256,2048]{2,1,0:T(8,128)(2,1)} %bitcast.373, bf16[8,1,258,256]{3,2,1,0:T(8,128)(2,1)S(1)} %all-to-all-done.8), kind=kOutput, calls=%fused_computation.124 | convolution fusion | flops 2164789248 | bytes 10502144 | tf_op jit(solution)/shard_map/qkyi,qix->kyx/dot_general | solution.py:109
  412.2 10.6 %collective-permute-done.20 = bf16[1,258,514]{2,1,0:T(8,128)(2,1)} collective-permute-done((bf16[1,258,514]{2,1,0:T(8,128)(2,1)S(1)}, bf16[1,258,514]{2,1,0:T(8,128)(2,1)}, u32[]{:S(2)}, u32[]{:S(2)}) %collective-permute-start.20) | collective-permute-done | bytes 265256 | tf_op jit(solution)/shard_map/ppermute | solution.py:142
  424.9 6.5 %collective-permute-done.25 = bf16[1,258,514]{2,1,0:T(8,128)(2,1)S(1)} collective-permute-done((bf16[1,258,514]{2,1,0:T(8,128)(2,1)S(1)}, bf16[1,258,514]{2,1,0:T(8,128)(2,1)S(1)}, u32[]{:S(2)}, u32[]{:S(2)}) %collective-permute-start.25) | collective-permute-done | bytes 265256 | tf_op jit(solution)/shard_map/ppermute | solution.py:142
  431.4 20.0 %collective-permute-done.26 = bf16[1,258,514]{2,1,0:T(8,128)(2,1)S(1)} collective-permute-done((bf16[1,258,514]{2,1,0:T(8,128)(2,1)S(1)}, bf16[1,258,514]{2,1,0:T(8,128)(2,1)S(1)}, u32[]{:S(2)}, u32[]{:S(2)}) %collective-permute-start.26) | collective-permute-done | bytes 265256 | tf_op jit(solution)/shard_map/ppermute | solution.py:142
  454.6 5.9 %fusion.45 = f32[7,256,512]{2,1,0:T(8,128)} fusion(f32[8,258,514]{2,1,0:T(8,128)S(1)} %fusion.53, f32[8,258,514]{2,1,0:T(8,128)S(1)} %bitcast.363), kind=kLoop, calls=%fused_computation.79 | loop fusion | flops 3670016 | bytes 18350080 | tf_op jit(solution)/shard_map/mul | solution.py:54
  460.4 15.5 %fusion.5 = (f32[]{:T(128)}, f32[]{:T(128)}, f32[]{:T(128)}, f32[]{:T(128)}, f32[8,256,512]{2,1,0:T(8,128)}, /*index=5*/bf16[8,256,512]{2,1,0:T(8,128)(2,1)}) fusion(bf16[8,256,512]{2,1,0:T(8,128)(2,1)} %get-tuple-element.29, f32[8,256,512]{2,1,0:T(8,128)} %copy-done.2, f32[8,256,512]{2,1,0:T(8,128)} %get-tuple-element.28, f32[7,256,512]{2,1,0:T(8,128)} %fusion.45, ...), kind=kLoop, calls=%fused_computation.16 | loop fusion | flops 33554432 | bytes 64512080 | tf_op jit(solution)/shard_map/reduce_sum | solution.py:184
  478.6 12.5 %all_to_all.53 = f32[32,1,4]{2,1,0:T(1,128)S(1)} all-to-all(f32[32,1,4]{2,1,0:T(1,128)S(1)} %broadcast_in_dim.91), channel_id=1, replica_groups=mesh['px'=4,'py'=8] {'px','py'}, dimensions={0} | all-to-all | bytes 1024 | tf_op jit(solution)/shard_map/all_to_all | solution.py:41
  496.0 12.8 %fusion.10 = (f32[8,256,512]{2,1,0:T(8,128)}, f32[8,256,512]{2,1,0:T(8,128)}, f32[8,256,512]{2,1,0:T(8,128)}) fusion(f32[8,256,512]{2,1,0:T(8,128)} %param.8, bf16[8,256,512]{2,1,0:T(8,128)(2,1)} %get-tuple-element.29, f32[]{:T(128)S(6)} %div.27, f32[]{:T(128)S(6)} %div.23, f32[]{:T(128)S(6)} %div.26, bf16[8,256,512]{2,1,0:T(8,128)(2,1)} %get-tuple-element.27, ...), kind=kLoop, calls=%fused_computation.21 | loop fusion | flops 12582912 | bytes 33554444 | tf_op jit(solution)/shard_map/add | solution.py:196
  (186 shorter events, 112.4 us)
Async XLA Ops:
  2.0 3.5 copy-start.8
  18.7 5.3 %copy-start.3 = (bf16[1,8,256,512]{3,2,1,0:T(8,128)(2,1)}, bf16[1,8,256,512]{3,2,1,0:T(8,128)(2,1)S(1)}, u32[]{:S(2)}) copy-start(bf16[1,8,256,512]{3,2,1,0:T(8,128)(2,1)S(1)} %fusion.79) | copy-start | bytes 6291460
  18.8 18.4 %collective-permute-start = (bf16[2,8,1,512]{3,2,1,0:T(2,128)(2,1)S(1)}, bf16[2,8,1,512]{3,2,1,0:T(2,128)(2,1)S(1)}, u32[]{:S(2)}, u32[]{:S(2)}) collective-permute-start(bf16[2,8,1,512]{3,2,1,0:T(2,128)(2,1)S(1)} %get-tuple-element.34), channel_id=1, source_target_pairs={{0,1},{1,2},{2,3},{3,4},{4,5},{5,6},{6,7},{8,9},{9,10},{10,11},{11... | collective-permute-start | bytes 49160 | tf_op jit(solution)/shard_map/ppermute | solution.py:17
  21.2 16.0 %collective-permute-start.3 = (bf16[2,8,1,512]{3,2,1,0:T(2,128)(2,1)S(1)}, bf16[2,8,1,512]{3,2,1,0:T(2,128)(2,1)S(1)}, u32[]{:S(2)}, u32[]{:S(2)}) collective-permute-start(bf16[2,8,1,512]{3,2,1,0:T(2,128)(2,1)S(1)} %get-tuple-element.35), channel_id=1, source_target_pairs={{1,0},{2,1},{3,2},{4,3},{5,4},{6,5},{7,6},{9,8},{10,9},{11,10},{12... | collective-permute-start | bytes 49160 | tf_op jit(solution)/shard_map/ppermute | solution.py:17
  25.6 6.4 %collective-permute-start.1 = (bf16[2,8,256,1]{2,1,3,0:T(8,128)(2,1)S(1)}, bf16[2,8,256,1]{2,1,3,0:T(8,128)(2,1)S(1)}, u32[]{:S(2)}, u32[]{:S(2)}) collective-permute-start(bf16[2,8,256,1]{2,1,3,0:T(8,128)(2,1)S(1)} %copy.80), channel_id=1, source_target_pairs={{0,8},{8,16},{16,24},{1,9},{9,17},{17,25},{2,10},{10,18},{18,26},{... | collective-permute-start | bytes 24584 | tf_op jit(solution)/shard_map/ppermute | solution.py:17
  30.3 5.5 %collective-permute-start.2 = (bf16[2,8,256,1]{2,1,3,0:T(8,128)(2,1)S(1)}, bf16[2,8,256,1]{2,1,3,0:T(8,128)(2,1)S(1)}, u32[]{:S(2)}, u32[]{:S(2)}) collective-permute-start(bf16[2,8,256,1]{2,1,3,0:T(8,128)(2,1)S(1)} %copy.81), channel_id=1, source_target_pairs={{8,0},{16,8},{24,16},{9,1},{17,9},{25,17},{10,2},{18,10},{26,18},{... | collective-permute-start | bytes 24584 | tf_op jit(solution)/shard_map/ppermute | solution.py:17
  44.7 5.9 %copy-start = (f32[8,258,514]{2,1,0:T(8,128)}, f32[8,258,514]{2,1,0:T(8,128)S(1)}, u32[]{:S(2)}) copy-start(f32[8,258,514]{2,1,0:T(8,128)S(1)} %get-tuple-element.30) | copy-start | bytes 12730756
  61.9 2.0 copy-start.1
  61.9 7.5 %copy-start.10 = (f32[2048]{0:T(1024)S(1)}, f32[2048]{0:T(1024)}, u32[]{:S(2)}) copy-start(f32[2048]{0:T(1024)} %param.12) | copy-start | bytes 24580
  61.9 7.6 %copy-start.9 = (f32[8]{0:T(128)S(1)}, f32[8]{0:T(128)}, u32[]{:S(2)}) copy-start(f32[8]{0:T(128)} %param.13) | copy-start | bytes 100
  63.9 11.2 %collective-permute-start.4 = (bf16[1,256,512]{2,1,0:T(8,128)(2,1)S(1)}, bf16[1,256,512]{2,1,0:T(8,128)(2,1)S(1)}, u32[]{:S(2)}, u32[]{:S(2)}) collective-permute-start(bf16[1,256,512]{2,1,0:T(8,128)(2,1)S(1)} %get-tuple-element.66), channel_id=1, source_target_pairs={{0,8},{8,16},{16,24},{24,0},{1,9},{9,17},{17,25},{25,1},{2,10},{10... | collective-permute-start | bytes 786440 | tf_op jit(solution)/shard_map/ppermute | solution.py:76
  65.5 20.7 %collective-permute-start.5 = (bf16[1,256,512]{2,1,0:T(8,128)(2,1)S(1)}, bf16[1,256,512]{2,1,0:T(8,128)(2,1)S(1)}, u32[]{:S(2)}, u32[]{:S(2)}) collective-permute-start(bf16[1,256,512]{2,1,0:T(8,128)(2,1)S(1)} %get-tuple-element.65), channel_id=1, source_target_pairs={{0,16},{8,24},{16,0},{24,8},{1,17},{9,25},{17,1},{25,9},{2,18},{10... | collective-permute-start | bytes 786440 | tf_op jit(solution)/shard_map/ppermute | solution.py:76
  66.5 19.7 %collective-permute-start.6 = (bf16[1,256,512]{2,1,0:T(8,128)(2,1)S(1)}, bf16[1,256,512]{2,1,0:T(8,128)(2,1)S(1)}, u32[]{:S(2)}, u32[]{:S(2)}) collective-permute-start(bf16[1,256,512]{2,1,0:T(8,128)(2,1)S(1)} %get-tuple-element.64), channel_id=1, source_target_pairs={{0,24},{8,0},{16,8},{24,16},{1,25},{9,1},{17,9},{25,17},{2,26},{10... | collective-permute-start | bytes 786440 | tf_op jit(solution)/shard_map/ppermute | solution.py:76
  89.0 32.0 %collective-permute-start.12 = (bf16[1,256,512]{2,1,0:T(8,128)(2,1)}, bf16[1,256,512]{2,1,0:T(8,128)(2,1)S(1)}, u32[]{:S(2)}, u32[]{:S(2)}) collective-permute-start(bf16[1,256,512]{2,1,0:T(8,128)(2,1)} %get-tuple-element.60), channel_id=1, source_target_pairs={{0,24},{8,0},{16,8},{24,16},{1,25},{9,1},{17,9},{25,17},{2,26},{10... | collective-permute-start | bytes 786440 | tf_op jit(solution)/shard_map/ppermute | solution.py:76
  96.3 23.8 %collective-permute-start.11 = (bf16[1,256,512]{2,1,0:T(8,128)(2,1)}, bf16[1,256,512]{2,1,0:T(8,128)(2,1)}, u32[]{:S(2)}, u32[]{:S(2)}) collective-permute-start(bf16[1,256,512]{2,1,0:T(8,128)(2,1)} %get-tuple-element.61), channel_id=1, source_target_pairs={{0,16},{8,24},{16,0},{24,8},{1,17},{9,25},{17,1},{25,9},{2,18},{10... | collective-permute-start | bytes 786440 | tf_op jit(solution)/shard_map/ppermute | solution.py:76
  96.6 17.9 %collective-permute-start.10 = (bf16[1,256,512]{2,1,0:T(8,128)(2,1)}, bf16[1,256,512]{2,1,0:T(8,128)(2,1)}, u32[]{:S(2)}, u32[]{:S(2)}) collective-permute-start(bf16[1,256,512]{2,1,0:T(8,128)(2,1)} %get-tuple-element.62), channel_id=1, source_target_pairs={{0,8},{8,16},{16,24},{24,0},{1,9},{9,17},{17,25},{25,1},{2,10},{10... | collective-permute-start | bytes 786440 | tf_op jit(solution)/shard_map/ppermute | solution.py:76
  104.1 23.7 %all-to-all-start = ((bf16[8,256,256]{2,1,0:T(8,128)(2,1)}), bf16[8,256,256]{2,1,0:T(8,128)(2,1)S(1)}, u32[]{:S(2)}, u32[]{:S(2)}) async-start(bf16[8,256,256]{2,1,0:T(8,128)(2,1)} %bitcast.359), calls=%async_computation | async-start | bytes 2097152 | tf_op jit(solution)/shard_map/all_to_all | solution.py:91
  127.8 19.7 %all-to-all-start.2 = ((bf16[8,256,256]{2,1,0:T(8,128)(2,1)}), bf16[8,256,256]{2,1,0:T(8,128)(2,1)}, u32[]{:S(2)}, u32[]{:S(2)}) async-start(bf16[8,256,256]{2,1,0:T(8,128)(2,1)} %bitcast.357), calls=%async_computation.2 | async-start | bytes 2097152 | tf_op jit(solution)/shard_map/all_to_all | solution.py:91
  147.5 20.2 %all-to-all-start.1 = ((bf16[8,1,258,256]{3,2,1,0:T(8,128)(2,1)}), bf16[8,1,258,256]{3,2,1,0:T(8,128)(2,1)}, u32[]{:S(2)}, u32[]{:S(2)}) async-start(bf16[8,1,258,256]{3,2,1,0:T(8,128)(2,1)} %copy.85), calls=%async_computation.1 | async-start | bytes 2162688 | tf_op jit(solution)/shard_map/all_to_all | solution.py:108
  167.7 19.3 %all-to-all-start.3 = ((bf16[8,1,258,256]{3,2,1,0:T(8,128)(2,1)}), bf16[8,1,258,256]{3,2,1,0:T(8,128)(2,1)S(1)}, u32[]{:S(2)}, u32[]{:S(2)}) async-start(bf16[8,1,258,256]{3,2,1,0:T(8,128)(2,1)} %copy.87), calls=%async_computation.3 | async-start | bytes 2162688 | tf_op jit(solution)/shard_map/all_to_all | solution.py:108
  178.4 34.6 %collective-permute-start.9 = (bf16[1,258,514]{2,1,0:T(8,128)(2,1)S(1)}, bf16[1,258,514]{2,1,0:T(8,128)(2,1)}, u32[]{:S(2)}, u32[]{:S(2)}) collective-permute-start(bf16[1,258,514]{2,1,0:T(8,128)(2,1)S(1)} %get-tuple-element.44), channel_id=1, source_target_pairs={{0,24},{8,0},{16,8},{24,16},{1,25},{9,1},{17,9},{25,17},{2,26},{10... | collective-permute-start | bytes 795680 | tf_op jit(solution)/shard_map/ppermute | solution.py:142
  178.5 20.4 %collective-permute-start.7 = (bf16[1,258,514]{2,1,0:T(8,128)(2,1)S(1)}, bf16[1,258,514]{2,1,0:T(8,128)(2,1)}, u32[]{:S(2)}, u32[]{:S(2)}) collective-permute-start(bf16[1,258,514]{2,1,0:T(8,128)(2,1)S(1)} %get-tuple-element.45), channel_id=1, source_target_pairs={{0,8},{8,16},{16,24},{24,0},{1,9},{9,17},{17,25},{25,1},{2,10},{10... | collective-permute-start | bytes 795680 | tf_op jit(solution)/shard_map/ppermute | solution.py:142
  180.5 31.4 %collective-permute-start.8 = (bf16[1,258,514]{2,1,0:T(8,128)(2,1)S(1)}, bf16[1,258,514]{2,1,0:T(8,128)(2,1)}, u32[]{:S(2)}, u32[]{:S(2)}) collective-permute-start(bf16[1,258,514]{2,1,0:T(8,128)(2,1)S(1)} %get-tuple-element.46), channel_id=1, source_target_pairs={{0,16},{8,24},{16,0},{24,8},{1,17},{9,25},{17,1},{25,9},{2,18},{10... | collective-permute-start | bytes 795680 | tf_op jit(solution)/shard_map/ppermute | solution.py:142
  193.7 46.7 %collective-permute-start.15 = (bf16[1,258,514]{2,1,0:T(8,128)(2,1)S(1)}, bf16[1,258,514]{2,1,0:T(8,128)(2,1)S(1)}, u32[]{:S(2)}, u32[]{:S(2)}) collective-permute-start(bf16[1,258,514]{2,1,0:T(8,128)(2,1)S(1)} %get-tuple-element.48), channel_id=1, source_target_pairs={{0,24},{8,0},{16,8},{24,16},{1,25},{9,1},{17,9},{25,17},{2,26},{10... | collective-permute-start | bytes 795680 | tf_op jit(solution)/shard_map/ppermute | solution.py:142
  193.8 26.8 %collective-permute-start.13 = (bf16[1,258,514]{2,1,0:T(8,128)(2,1)S(1)}, bf16[1,258,514]{2,1,0:T(8,128)(2,1)S(1)}, u32[]{:S(2)}, u32[]{:S(2)}) collective-permute-start(bf16[1,258,514]{2,1,0:T(8,128)(2,1)S(1)} %get-tuple-element.49), channel_id=1, source_target_pairs={{0,8},{8,16},{16,24},{24,0},{1,9},{9,17},{17,25},{25,1},{2,10},{10... | collective-permute-start | bytes 795680 | tf_op jit(solution)/shard_map/ppermute | solution.py:142
  198.9 41.5 %collective-permute-start.14 = (bf16[1,258,514]{2,1,0:T(8,128)(2,1)S(1)}, bf16[1,258,514]{2,1,0:T(8,128)(2,1)S(1)}, u32[]{:S(2)}, u32[]{:S(2)}) collective-permute-start(bf16[1,258,514]{2,1,0:T(8,128)(2,1)S(1)} %get-tuple-element.50), channel_id=1, source_target_pairs={{0,16},{8,24},{16,0},{24,8},{1,17},{9,25},{17,1},{25,9},{2,18},{10... | collective-permute-start | bytes 795680 | tf_op jit(solution)/shard_map/ppermute | solution.py:142
  211.9 31.6 %slice-start = ((s8[5406720]{0:T(1024)(128)(4,1)}), s8[4194304]{0:T(1024)(128)(4,1)S(1)}, s32[]{:S(2)}) async-start(s8[5406720]{0:T(1024)(128)(4,1)} %bitcast.360), calls=%async_computation.10 | async-start | bytes 8388608
  214.2 26.2 %copy-start.5 = (bf16[4,258,514]{2,1,0:T(8,128)(2,1)}, bf16[4,258,514]{2,1,0:T(8,128)(2,1)S(1)}, u32[]{:S(2)}) copy-start(bf16[4,258,514]{2,1,0:T(8,128)(2,1)S(1)} %constant_dynamic-update-slice_fusion.17) | copy-start | bytes 3182692
  241.6 1.9 slice-start.1
  282.1 21.8 %copy-start.2 = (f32[8,256,512]{2,1,0:T(8,128)}, f32[8,256,512]{2,1,0:T(8,128)S(1)}, u32[]{:S(2)}) copy-start(f32[8,256,512]{2,1,0:T(8,128)S(1)} %multiply_subtract_fusion.1) | copy-start | bytes 12582916
  282.5 11.1 %collective-permute-start.16 = (bf16[1,256,512]{2,1,0:T(8,128)(2,1)S(1)}, bf16[1,256,512]{2,1,0:T(8,128)(2,1)S(1)}, u32[]{:S(2)}, u32[]{:S(2)}) collective-permute-start(bf16[1,256,512]{2,1,0:T(8,128)(2,1)S(1)} %get-tuple-element.58), channel_id=1, source_target_pairs={{0,8},{8,16},{16,24},{24,0},{1,9},{9,17},{17,25},{25,1},{2,10},{10... | collective-permute-start | bytes 786440 | tf_op jit(solution)/shard_map/ppermute | solution.py:76
  283.1 20.7 %collective-permute-start.17 = (bf16[1,256,512]{2,1,0:T(8,128)(2,1)S(1)}, bf16[1,256,512]{2,1,0:T(8,128)(2,1)S(1)}, u32[]{:S(2)}, u32[]{:S(2)}) collective-permute-start(bf16[1,256,512]{2,1,0:T(8,128)(2,1)S(1)} %get-tuple-element.57), channel_id=1, source_target_pairs={{0,16},{8,24},{16,0},{24,8},{1,17},{9,25},{17,1},{25,9},{2,18},{10... | collective-permute-start | bytes 786440 | tf_op jit(solution)/shard_map/ppermute | solution.py:76
  283.6 20.2 %collective-permute-start.18 = (bf16[1,256,512]{2,1,0:T(8,128)(2,1)S(1)}, bf16[1,256,512]{2,1,0:T(8,128)(2,1)S(1)}, u32[]{:S(2)}, u32[]{:S(2)}) collective-permute-start(bf16[1,256,512]{2,1,0:T(8,128)(2,1)S(1)} %get-tuple-element.56), channel_id=1, source_target_pairs={{0,24},{8,0},{16,8},{24,16},{1,25},{9,1},{17,9},{25,17},{2,26},{10... | collective-permute-start | bytes 786440 | tf_op jit(solution)/shard_map/ppermute | solution.py:76
  305.0 29.0 %collective-permute-start.24 = (bf16[1,256,512]{2,1,0:T(8,128)(2,1)S(1)}, bf16[1,256,512]{2,1,0:T(8,128)(2,1)S(1)}, u32[]{:S(2)}, u32[]{:S(2)}) collective-permute-start(bf16[1,256,512]{2,1,0:T(8,128)(2,1)S(1)} %get-tuple-element.52), channel_id=1, source_target_pairs={{0,24},{8,0},{16,8},{24,16},{1,25},{9,1},{17,9},{25,17},{2,26},{10... | collective-permute-start | bytes 786440 | tf_op jit(solution)/shard_map/ppermute | solution.py:76
  310.0 24.0 %collective-permute-start.23 = (bf16[1,256,512]{2,1,0:T(8,128)(2,1)S(1)}, bf16[1,256,512]{2,1,0:T(8,128)(2,1)S(1)}, u32[]{:S(2)}, u32[]{:S(2)}) collective-permute-start(bf16[1,256,512]{2,1,0:T(8,128)(2,1)S(1)} %get-tuple-element.53), channel_id=1, source_target_pairs={{0,16},{8,24},{16,0},{24,8},{1,17},{9,25},{17,1},{25,9},{2,18},{10... | collective-permute-start | bytes 786440 | tf_op jit(solution)/shard_map/ppermute | solution.py:76
  311.7 15.7 %collective-permute-start.22 = (bf16[1,256,512]{2,1,0:T(8,128)(2,1)}, bf16[1,256,512]{2,1,0:T(8,128)(2,1)S(1)}, u32[]{:S(2)}, u32[]{:S(2)}) collective-permute-start(bf16[1,256,512]{2,1,0:T(8,128)(2,1)} %get-tuple-element.54), channel_id=1, source_target_pairs={{0,8},{8,16},{16,24},{24,0},{1,9},{9,17},{17,25},{25,1},{2,10},{10... | collective-permute-start | bytes 786440 | tf_op jit(solution)/shard_map/ppermute | solution.py:76
  319.0 21.8 %all-to-all-start.5 = ((bf16[8,256,256]{2,1,0:T(8,128)(2,1)}), bf16[8,256,256]{2,1,0:T(8,128)(2,1)S(1)}, u32[]{:S(2)}, u32[]{:S(2)}) async-start(bf16[8,256,256]{2,1,0:T(8,128)(2,1)} %bitcast.355), calls=%async_computation.5 | async-start | bytes 2097152 | tf_op jit(solution)/shard_map/all_to_all | solution.py:91
  340.8 19.7 %all-to-all-start.7 = ((bf16[8,256,256]{2,1,0:T(8,128)(2,1)}), bf16[8,256,256]{2,1,0:T(8,128)(2,1)}, u32[]{:S(2)}, u32[]{:S(2)}) async-start(bf16[8,256,256]{2,1,0:T(8,128)(2,1)} %bitcast.353), calls=%async_computation.7 | async-start | bytes 2097152 | tf_op jit(solution)/shard_map/all_to_all | solution.py:91
  360.4 20.2 %all-to-all-start.6 = ((bf16[8,1,258,256]{3,2,1,0:T(8,128)(2,1)}), bf16[8,1,258,256]{3,2,1,0:T(8,128)(2,1)}, u32[]{:S(2)}, u32[]{:S(2)}) async-start(bf16[8,1,258,256]{3,2,1,0:T(8,128)(2,1)} %copy.90), calls=%async_computation.6 | async-start | bytes 2162688 | tf_op jit(solution)/shard_map/all_to_all | solution.py:108
  380.7 19.3 %all-to-all-start.8 = ((bf16[8,1,258,256]{3,2,1,0:T(8,128)(2,1)}), bf16[8,1,258,256]{3,2,1,0:T(8,128)(2,1)S(1)}, u32[]{:S(2)}, u32[]{:S(2)}) async-start(bf16[8,1,258,256]{3,2,1,0:T(8,128)(2,1)} %copy.92), calls=%async_computation.8 | async-start | bytes 2162688 | tf_op jit(solution)/shard_map/all_to_all | solution.py:108
  391.3 32.6 %collective-permute-start.21 = (bf16[1,258,514]{2,1,0:T(8,128)(2,1)S(1)}, bf16[1,258,514]{2,1,0:T(8,128)(2,1)}, u32[]{:S(2)}, u32[]{:S(2)}) collective-permute-start(bf16[1,258,514]{2,1,0:T(8,128)(2,1)S(1)} %get-tuple-element.36), channel_id=1, source_target_pairs={{0,24},{8,0},{16,8},{24,16},{1,25},{9,1},{17,9},{25,17},{2,26},{10... | collective-permute-start | bytes 795680 | tf_op jit(solution)/shard_map/ppermute | solution.py:142
  392.2 17.4 %collective-permute-start.19 = (bf16[1,258,514]{2,1,0:T(8,128)(2,1)S(1)}, bf16[1,258,514]{2,1,0:T(8,128)(2,1)}, u32[]{:S(2)}, u32[]{:S(2)}) collective-permute-start(bf16[1,258,514]{2,1,0:T(8,128)(2,1)S(1)} %get-tuple-element.37), channel_id=1, source_target_pairs={{0,8},{8,16},{16,24},{24,0},{1,9},{9,17},{17,25},{25,1},{2,10},{10... | collective-permute-start | bytes 795680 | tf_op jit(solution)/shard_map/ppermute | solution.py:142
  393.4 29.5 %collective-permute-start.20 = (bf16[1,258,514]{2,1,0:T(8,128)(2,1)S(1)}, bf16[1,258,514]{2,1,0:T(8,128)(2,1)}, u32[]{:S(2)}, u32[]{:S(2)}) collective-permute-start(bf16[1,258,514]{2,1,0:T(8,128)(2,1)S(1)} %get-tuple-element.38), channel_id=1, source_target_pairs={{0,16},{8,24},{16,0},{24,8},{1,17},{9,25},{17,1},{25,9},{2,18},{10... | collective-permute-start | bytes 795680 | tf_op jit(solution)/shard_map/ppermute | solution.py:142
  405.9 48.7 %slice-start.2 = ((s8[5406720]{0:T(1024)(128)(4,1)}), s8[4194304]{0:T(1024)(128)(4,1)S(1)}, s32[]{:S(2)}) async-start(s8[5406720]{0:T(1024)(128)(4,1)} %bitcast.362), calls=%async_computation.12 | async-start | bytes 8388608
  406.7 44.8 %collective-permute-start.27 = (bf16[1,258,514]{2,1,0:T(8,128)(2,1)S(1)}, bf16[1,258,514]{2,1,0:T(8,128)(2,1)S(1)}, u32[]{:S(2)}, u32[]{:S(2)}) collective-permute-start(bf16[1,258,514]{2,1,0:T(8,128)(2,1)S(1)} %get-tuple-element.40), channel_id=1, source_target_pairs={{0,24},{8,0},{16,8},{24,16},{1,25},{9,1},{17,9},{25,17},{2,26},{10... | collective-permute-start | bytes 795680 | tf_op jit(solution)/shard_map/ppermute | solution.py:142
  407.6 23.8 %collective-permute-start.25 = (bf16[1,258,514]{2,1,0:T(8,128)(2,1)S(1)}, bf16[1,258,514]{2,1,0:T(8,128)(2,1)S(1)}, u32[]{:S(2)}, u32[]{:S(2)}) collective-permute-start(bf16[1,258,514]{2,1,0:T(8,128)(2,1)S(1)} %get-tuple-element.41), channel_id=1, source_target_pairs={{0,8},{8,16},{16,24},{24,0},{1,9},{9,17},{17,25},{25,1},{2,10},{10... | collective-permute-start | bytes 795680 | tf_op jit(solution)/shard_map/ppermute | solution.py:142
  409.7 41.8 %collective-permute-start.26 = (bf16[1,258,514]{2,1,0:T(8,128)(2,1)S(1)}, bf16[1,258,514]{2,1,0:T(8,128)(2,1)S(1)}, u32[]{:S(2)}, u32[]{:S(2)}) collective-permute-start(bf16[1,258,514]{2,1,0:T(8,128)(2,1)S(1)} %get-tuple-element.42), channel_id=1, source_target_pairs={{0,16},{8,24},{16,0},{24,8},{1,17},{9,25},{17,1},{25,9},{2,18},{10... | collective-permute-start | bytes 795680 | tf_op jit(solution)/shard_map/ppermute | solution.py:142
  424.9 26.6 %copy-start.7 = (bf16[4,258,514]{2,1,0:T(8,128)(2,1)}, bf16[4,258,514]{2,1,0:T(8,128)(2,1)S(1)}, u32[]{:S(2)}) copy-start(bf16[4,258,514]{2,1,0:T(8,128)(2,1)S(1)} %constant_dynamic-update-slice_fusion.4) | copy-start | bytes 3182692
  (3 other events, 4.1 us)
